TPU v7x, 512 devices: a whole 4x8x8 slice. The times are simulated.
512 devices in a mesh: seq: 128 (over y, z, core), sub: 4 (over x).
Axes of the slice: x: 4, y: 8, z: 8, core: 2. Of those that a mesh axis runs over, the one named last changes fastest.
Arguments:
- linear_query: bfloat16 [32768, 256], P(('seq', 'sub')), may hold values from -6 to 6
- linear_key: bfloat16 [32768, 256], P(('seq', 'sub')), may hold values from -6 to 6
- linear_value: bfloat16 [32768, 2048], P(('seq', 'sub')), may hold values from -6 to 6
- lin_gain: float32 [2048], replicated, may hold values from 0.1 to 1.9
- window_query: bfloat16 [32768, 2048], P(('seq', 'sub')), may hold values from -6 to 6
- window_key: bfloat16 [32768, 2048], P(('seq', 'sub')), may hold values from -6 to 6
- window_value: bfloat16 [32768, 2048], P(('seq', 'sub')), may hold values from -6 to 6
Outputs:
- linear_out: bfloat16 [32768, 2048], P(('seq', 'sub'))
- window_out: bfloat16 [32768, 2048], P(('seq', 'sub'))
All inputs are finite; a program needn't handle non-finite values.
Results may differ from a plain program's by a relative error of at most 0.007.
Values may be sent and summed in bfloat16 or wider, within the bound.
No kernel may reach another device: no remote copies, remote signals or barrier semaphores. Data moves between devices by JAX's collectives and lax.ppermute only.
A program may use at most 128 MiB of HBM per device.

v0:
```python
import math

import jax
import jax.numpy as jnp
from jax import lax
from jax.sharding import PartitionSpec as P

FDIM = 16
VDIM = 128
SDIM = 128
WINDOW = 512


def passed_along(shard, axis, by):
    size = lax.axis_size(axis)
    pairs = [(i, i + by) for i in range(size) if 0 <= i + by < size]
    return lax.ppermute(shard, axis, pairs)


def features(vectors):
    halved = vectors * 0.5
    quadratic = halved[..., :, None] * halved[..., None, :]
    quadratic = quadratic.reshape(halved.shape[:-1] + (halved.shape[-1] * halved.shape[-1],)) * (
        1.0 / math.sqrt(2.0)
    )
    constant = jnp.ones(halved.shape[:-1] + (1,), jnp.float32)
    return jnp.concatenate([constant, halved, quadratic], axis=-1)


def shards(
    linear_query, linear_key, linear_value, lin_gain, window_query, window_key, window_value
):
    rows_dev = linear_query.shape[0]
    sub_count = lax.axis_size("sub")
    seq_count = lax.axis_size("seq")
    device_pos = lax.axis_index("seq") * sub_count + lax.axis_index("sub")
    base_row = device_pos * rows_dev
    reach_dev = WINDOW // rows_dev
    channels = window_key.shape[1]
    head_count = channels // SDIM
    lin_heads = linear_query.shape[1] // FDIM
    stacked = jnp.stack([window_key, window_value])

    def pass_on(turn_index, carry):
        moving, buffer = carry
        moving = passed_along(moving, ("seq", "sub"), 1)
        buffer = lax.dynamic_update_slice_in_dim(
            buffer, moving, (reach_dev - 1 - turn_index) * rows_dev, 1
        )
        return (moving, buffer)

    empty_buf = jnp.zeros((2, reach_dev * rows_dev, channels), jnp.bfloat16)
    moved_last, earlier = lax.fori_loop(0, reach_dev, pass_on, (stacked, empty_buf))
    key_rows = jnp.concatenate([earlier[0], window_key], axis=0).reshape(-1, head_count, SDIM)
    value_rows = jnp.concatenate([earlier[1], window_value], axis=0).reshape(-1, head_count, SDIM)
    query_heads = window_query.reshape(rows_dev, head_count, SDIM)
    scores = jnp.einsum(
        "ihd,jhd->hij", query_heads, key_rows, preferred_element_type=jnp.float32
    ) * (1.0 / math.sqrt(SDIM))
    query_pos = base_row + jnp.arange(rows_dev, dtype=jnp.int32)
    key_pos = (
        base_row - reach_dev * rows_dev + jnp.arange((reach_dev + 1) * rows_dev, dtype=jnp.int32)
    )
    allowed = (
        (key_pos[None, :] <= query_pos[:, None])
        & (key_pos[None, :] > query_pos[:, None] - WINDOW)
        & (key_pos[None, :] >= 0)
    )
    scores = jnp.where(allowed[None], scores, jnp.float32(-1e30))
    row_max = jnp.max(scores, axis=-1, keepdims=True)
    exp_scores = jnp.exp(scores - row_max)
    weights_bf = (exp_scores / jnp.sum(exp_scores, axis=-1, keepdims=True)).astype(jnp.bfloat16)
    mixed = jnp.einsum("hij,jhd->ihd", weights_bf, value_rows, preferred_element_type=jnp.float32)
    window_out = mixed.reshape(rows_dev, channels).astype(jnp.bfloat16)
    query_bf = linear_query.reshape(rows_dev, lin_heads, FDIM)
    key_bf = linear_key.reshape(rows_dev, lin_heads, FDIM)
    query_lin = query_bf.astype(jnp.float32)
    key_lin = key_bf.astype(jnp.float32)
    value_lin = linear_value.astype(jnp.float32).reshape(rows_dev, lin_heads, VDIM)
    local_state = jnp.einsum(
        "jhf,jhe->hfe", features(key_lin), value_lin, precision=lax.Precision.HIGHEST
    )
    seq_levels = (seq_count - 1).bit_length()
    owned = lax.all_to_all(local_state[None], "sub", split_axis=1, concat_axis=0, tiled=True)
    running_inner = jnp.cumsum(owned, axis=0)
    inner_before = running_inner - owned
    chip_total = running_inner[-1]
    running_chip = chip_total
    for level in range(seq_levels):
        running_chip = running_chip + passed_along(running_chip, "seq", 1 << level)
    chips_before = running_chip - chip_total
    slots = inner_before + chips_before[None]
    prefix = lax.all_to_all(slots, "sub", split_axis=0, concat_axis=1, tiled=True)[0]
    from_state = jnp.einsum(
        "ihf,hfe->ihe", features(query_lin), prefix, precision=lax.Precision.HIGHEST
    )
    dot_inner = (
        jnp.einsum("ihd,jhd->hij", query_bf, key_bf, preferred_element_type=jnp.float32) * 0.25
    )
    weight = 1.0 + dot_inner + 0.5 * dot_inner * dot_inner
    causal = (
        jnp.arange(rows_dev, dtype=jnp.int32)[:, None]
        >= jnp.arange(rows_dev, dtype=jnp.int32)[None, :]
    )
    weight = jnp.where(causal[None], weight, jnp.float32(0.0))
    local_sum = jnp.einsum("hij,jhe->ihe", weight, value_lin, precision=lax.Precision.HIGHEST)
    numerator = local_sum + from_state
    inv_rms = lax.rsqrt(jnp.mean(numerator * numerator, axis=-1, keepdims=True) + 1e-05)
    gain_rows = lin_gain.reshape(lin_heads, VDIM)
    linear_out = (
        (numerator * inv_rms * gain_rows).reshape(rows_dev, lin_heads * VDIM).astype(jnp.bfloat16)
    )
    return (linear_out, window_out)


def solution(mesh):
    in_specs = (
        P(("seq", "sub"), None),
        P(("seq", "sub"), None),
        P(("seq", "sub"), None),
        P(),
        P(("seq", "sub"), None),
        P(("seq", "sub"), None),
        P(("seq", "sub"), None),
    )
    out_specs = (P(("seq", "sub"), None), P(("seq", "sub"), None))
    return jax.shard_map(shards, mesh=mesh, in_specs=in_specs, out_specs=out_specs, check_vma=False)
```

profile of v0, /device:TPU:46, one launch (start us, length us, event | category | flops | bytes accessed | tf_op | source)
XLA Modules:
  0.0 400.8 jit_solution(11828196512490582689)
XLA Ops:
  3.7 4.2 %convolution_bitcast_fusion = f32[1,16,273,128]{3,2,1,0:T(8,128)S(1)} fusion(f32[64,16,256]{2,0,1:T(8,128)} %copy.102, f32[64,16,16]{2,0,1:T(8,128)S(1)} %copy.101, f32[273]{0:T(512)S(1)} %pad.9.clone, bf16[64,2048]{1,0:T(8,128)(2,1)S(1)} %copy-done), kind=kOutput, calls=%fused_computation.17 | convolution fusion | flops 429950976 | bytes 3613764 | tf_op jit(solution)/shard_map/jhf,jhe->hfe/dot_general | solution.py:80
  10.2 30.3 %all_to_all.21 = f32[1,16,273,128]{3,0,2,1:T(1,128)S(1)} all-to-all(f32[1,16,273,128]{3,0,2,1:T(1,128)S(1)} %copy.104), channel_id=1, replica_groups=mesh['seq'=128,'sub'=4] {'sub'}, dimensions={1} | all-to-all | bytes 4472832 | tf_op jit(solution)/shard_map/all_to_all | solution.py:84
  43.9 15.3 %collective-permute-done.1 = f32[4,273,128]{2,0,1:T(4,128)S(1)} collective-permute-done((f32[4,273,128]{2,0,1:T(4,128)S(1)}, f32[4,273,128]{2,0,1:T(4,128)S(1)}, u32[]{:S(2)}, u32[]{:S(2)}) %collective-permute-start.1) | collective-permute-done | bytes 559136 | tf_op jit(solution)/shard_map/ppermute | solution.py:17
  61.4 12.5 %collective-permute-done.2 = f32[4,273,128]{2,0,1:T(4,128)S(1)} collective-permute-done((f32[4,273,128]{2,0,1:T(4,128)S(1)}, f32[4,273,128]{2,0,1:T(4,128)S(1)}, u32[]{:S(2)}, u32[]{:S(2)}) %collective-permute-start.2) | collective-permute-done | bytes 559136 | tf_op jit(solution)/shard_map/ppermute | solution.py:17
  77.5 25.4 %collective-permute-done.3 = f32[4,273,128]{2,0,1:T(4,128)} collective-permute-done((f32[4,273,128]{2,0,1:T(4,128)S(1)}, f32[4,273,128]{2,0,1:T(4,128)}, u32[]{:S(2)}, u32[]{:S(2)}) %collective-permute-start.3) | collective-permute-done | bytes 559136 | tf_op jit(solution)/shard_map/ppermute | solution.py:17
  105.1 5.2 %collective-permute-start.4 = (f32[4,273,128]{2,0,1:T(4,128)}, f32[4,273,128]{2,0,1:T(4,128)}, u32[]{:S(2)}, u32[]{:S(2)}) collective-permute-start(f32[4,273,128]{2,0,1:T(4,128)} %copy.111), channel_id=1, source_target_pairs={{0,32},{4,36},{8,40},{12,44},{16,48},{20,52},{24,56},{28,60},{32,6... | collective-permute-start | bytes 1677320 | tf_op jit(solution)/shard_map/ppermute | solution.py:17
  118.1 14.9 %collective-permute-done.4 = f32[4,273,128]{2,0,1:T(4,128)} collective-permute-done((f32[4,273,128]{2,0,1:T(4,128)}, f32[4,273,128]{2,0,1:T(4,128)}, u32[]{:S(2)}, u32[]{:S(2)}) %collective-permute-start.4) | collective-permute-done | bytes 559136 | tf_op jit(solution)/shard_map/ppermute | solution.py:17
  141.1 137.1 %while.15 = (s32[]{:T(128)}, bf16[2,64,2048]{2,1,0:T(8,128)(2,1)}, bf16[2,512,2048]{2,1,0:T(8,128)(2,1)}, s32[]{:T(128)}, s32[]{:T(128)}, /*index=5*/s32[]{:T(128)}, s32[]{:T(128)}, s32[]{:T(128)}) while((s32[]{:T(128)}, bf16[2,64,2048]{2,1,0:T(8,128)(2,1)}, bf16[2,512,2048]{2,1,0:T(8,128)(2,1)}, s32[]{:T(128)}, s32[]{:T(128)}, ...), condition=%wide.region_3.4_spmd, body=%wide.region_2.3_spmd.sunk | while | flops 7 | bytes 4194491 | solution.py:53
  143.0 9.3 %collective-permute-done = bf16[2,64,2048]{2,1,0:T(8,128)(2,1)S(1)} collective-permute-done((bf16[2,64,2048]{2,1,0:T(8,128)(2,1)}, bf16[2,64,2048]{2,1,0:T(8,128)(2,1)S(1)}, u32[]{:S(2)}, u32[]{:S(2)}) %collective-permute-start) | collective-permute-done | bytes 524320 | tf_op jit(solution)/shard_map/while/body/eval_jaxpr/ppermute | solution.py:17
  158.0 11.6 %collective-permute-done = bf16[2,64,2048]{2,1,0:T(8,128)(2,1)S(1)} collective-permute-done((bf16[2,64,2048]{2,1,0:T(8,128)(2,1)}, bf16[2,64,2048]{2,1,0:T(8,128)(2,1)S(1)}, u32[]{:S(2)}, u32[]{:S(2)}) %collective-permute-start) | collective-permute-done | bytes 524320 | tf_op jit(solution)/shard_map/while/body/eval_jaxpr/ppermute | solution.py:17
  173.2 14.7 %collective-permute-done = bf16[2,64,2048]{2,1,0:T(8,128)(2,1)S(1)} collective-permute-done((bf16[2,64,2048]{2,1,0:T(8,128)(2,1)}, bf16[2,64,2048]{2,1,0:T(8,128)(2,1)S(1)}, u32[]{:S(2)}, u32[]{:S(2)}) %collective-permute-start) | collective-permute-done | bytes 524320 | tf_op jit(solution)/shard_map/while/body/eval_jaxpr/ppermute | solution.py:17
  191.5 14.2 %collective-permute-done = bf16[2,64,2048]{2,1,0:T(8,128)(2,1)S(1)} collective-permute-done((bf16[2,64,2048]{2,1,0:T(8,128)(2,1)}, bf16[2,64,2048]{2,1,0:T(8,128)(2,1)S(1)}, u32[]{:S(2)}, u32[]{:S(2)}) %collective-permute-start) | collective-permute-done | bytes 524320 | tf_op jit(solution)/shard_map/while/body/eval_jaxpr/ppermute | solution.py:17
  209.2 14.1 %collective-permute-done = bf16[2,64,2048]{2,1,0:T(8,128)(2,1)S(1)} collective-permute-done((bf16[2,64,2048]{2,1,0:T(8,128)(2,1)}, bf16[2,64,2048]{2,1,0:T(8,128)(2,1)S(1)}, u32[]{:S(2)}, u32[]{:S(2)}) %collective-permute-start) | collective-permute-done | bytes 524320 | tf_op jit(solution)/shard_map/while/body/eval_jaxpr/ppermute | solution.py:17
  226.9 14.1 %collective-permute-done = bf16[2,64,2048]{2,1,0:T(8,128)(2,1)S(1)} collective-permute-done((bf16[2,64,2048]{2,1,0:T(8,128)(2,1)}, bf16[2,64,2048]{2,1,0:T(8,128)(2,1)S(1)}, u32[]{:S(2)}, u32[]{:S(2)}) %collective-permute-start) | collective-permute-done | bytes 524320 | tf_op jit(solution)/shard_map/while/body/eval_jaxpr/ppermute | solution.py:17
  244.6 14.1 %collective-permute-done = bf16[2,64,2048]{2,1,0:T(8,128)(2,1)S(1)} collective-permute-done((bf16[2,64,2048]{2,1,0:T(8,128)(2,1)}, bf16[2,64,2048]{2,1,0:T(8,128)(2,1)S(1)}, u32[]{:S(2)}, u32[]{:S(2)}) %collective-permute-start) | collective-permute-done | bytes 524320 | tf_op jit(solution)/shard_map/while/body/eval_jaxpr/ppermute | solution.py:17
  263.9 12.6 %collective-permute-done = bf16[2,64,2048]{2,1,0:T(8,128)(2,1)S(1)} collective-permute-done((bf16[2,64,2048]{2,1,0:T(8,128)(2,1)}, bf16[2,64,2048]{2,1,0:T(8,128)(2,1)S(1)}, u32[]{:S(2)}, u32[]{:S(2)}) %collective-permute-start) | collective-permute-done | bytes 524320 | tf_op jit(solution)/shard_map/while/body/eval_jaxpr/ppermute | solution.py:17
  278.2 6.3 %copy.124 = bf16[2,512,2048]{1,2,0:T(8,128)(2,1)} copy(bf16[2,512,2048]{2,1,0:T(8,128)(2,1)} %get-tuple-element.66) | data formatting | bytes 8388608 | tf_op jit(solution)/shard_map/while | solution.py:53
  289.3 4.5 %fusion.79 = (bf16[1,512,2048]{1,2,0:T(8,128)(2,1)}, bf16[1,512,2048]{1,2,0:T(8,128)(2,1)}) fusion(bf16[2,512,2048]{1,2,0:T(8,128)(2,1)} %copy.124), kind=kLoop, calls=%fused_computation.91 | loop fusion | bytes 8388608 | tf_op jit(solution)/shard_map/slice | solution.py:54
  297.7 4.0 copy.125
  301.7 28.8 %collective-permute-done.6 = f32[4,273,128]{2,0,1:T(4,128)} collective-permute-done((f32[4,273,128]{2,0,1:T(4,128)}, f32[4,273,128]{2,0,1:T(4,128)}, u32[]{:S(2)}, u32[]{:S(2)}) %collective-permute-start.6) | collective-permute-done | bytes 559136 | tf_op jit(solution)/shard_map/ppermute | solution.py:17
  333.4 24.1 %collective-permute-done.7 = f32[4,273,128]{2,0,1:T(4,128)S(1)} collective-permute-done((f32[4,273,128]{2,0,1:T(4,128)S(1)}, f32[4,273,128]{2,0,1:T(4,128)S(1)}, u32[]{:S(2)}, u32[]{:S(2)}) %collective-permute-start.7) | collective-permute-done | bytes 559136 | tf_op jit(solution)/shard_map/ppermute | solution.py:17
  359.9 7.6 %all-to-all-start.1 = ((f32[4,4,273,128]{3,1,2,0:T(4,128)}), f32[4,4,273,128]{3,1,2,0:T(4,128)}, u32[]{:S(2)}, u32[]{:S(2)}) async-start(f32[4,4,273,128]{3,1,2,0:T(4,128)} %copy.119), calls=%async_computation.1 | async-start | bytes 4472832 | tf_op jit(solution)/shard_map/all_to_all | solution.py:93
  367.7 4.5 %fusion.80 = (f32[16,64]{1,0:T(8,128)S(1)}, f32[16,64,576]{2,1,0:T(8,128)}) fusion(pred[64,576]{1,0:T(8,128)(4,1)S(1)} %and_and_fusion, bf16[64,16,128]{2,0,1:T(8,128)(2,1)S(1)} %copy_bitcast_fusion.3, bf16[512,16,128]{2,0,1:T(8,128)(2,1)} %copy.128, bf16[64,2048]{1,0:T(8,128)(2,1)S(1)} %copy-done.20), kind=kOutput, calls=%fused_computation.92 | convolution fusion | flops 158073408 | bytes 5021696 | tf_op jit(solution)/shard_map/sub | solution.py:71
  376.9 18.4 %all-to-all-done.1 = f32[4,4,273,128]{3,1,2,0:T(4,128)} async-done(((f32[4,4,273,128]{3,1,2,0:T(4,128)}), f32[4,4,273,128]{3,1,2,0:T(4,128)}, u32[]{:S(2)}, u32[]{:S(2)}) %all-to-all-start.1) | async-done | bytes 2236448 | tf_op jit(solution)/shard_map/all_to_all | solution.py:93
  (122 shorter events, 88.9 us)
Async XLA Ops:
  41.8 17.7 %copy-start.1 = (f32[4,4,273,128]{3,2,1,0:T(8,128)}, f32[4,4,273,128]{3,2,1,0:T(8,128)S(1)}, u32[]{:S(2)}) copy-start(f32[4,4,273,128]{3,2,1,0:T(8,128)S(1)} %fusion.85) | copy-start | bytes 6709252
  42.0 17.2 %collective-permute-start.1 = (f32[4,273,128]{2,0,1:T(4,128)S(1)}, f32[4,273,128]{2,0,1:T(4,128)S(1)}, u32[]{:S(2)}, u32[]{:S(2)}) collective-permute-start(f32[4,273,128]{2,0,1:T(4,128)S(1)} %copy.105), channel_id=1, source_target_pairs={{0,4},{4,8},{8,12},{12,16},{16,20},{20,24},{24,28},{28,32},{32,36}... | collective-permute-start | bytes 1677320 | tf_op jit(solution)/shard_map/ppermute | solution.py:17
  59.3 18.1 %copy-start.18 = (bf16[64,256]{1,0:T(8,128)(2,1)S(1)}, bf16[64,256]{1,0:T(8,128)(2,1)}, u32[]{:S(2)}) copy-start(bf16[64,256]{1,0:T(8,128)(2,1)} %param.9) | copy-start | bytes 98308
  59.4 14.4 %collective-permute-start.2 = (f32[4,273,128]{2,0,1:T(4,128)S(1)}, f32[4,273,128]{2,0,1:T(4,128)S(1)}, u32[]{:S(2)}, u32[]{:S(2)}) collective-permute-start(f32[4,273,128]{2,0,1:T(4,128)S(1)} %copy.107), channel_id=1, source_target_pairs={{0,8},{4,12},{8,16},{12,20},{16,24},{20,28},{24,32},{28,36},{32,40... | collective-permute-start | bytes 1677320 | tf_op jit(solution)/shard_map/ppermute | solution.py:17
  74.9 28.0 %collective-permute-start.3 = (f32[4,273,128]{2,0,1:T(4,128)S(1)}, f32[4,273,128]{2,0,1:T(4,128)}, u32[]{:S(2)}, u32[]{:S(2)}) collective-permute-start(f32[4,273,128]{2,0,1:T(4,128)S(1)} %copy.109), channel_id=1, source_target_pairs={{0,16},{4,20},{8,24},{12,28},{16,32},{20,36},{24,40},{28,44},{32,4... | collective-permute-start | bytes 1677320 | tf_op jit(solution)/shard_map/ppermute | solution.py:17
  77.5 32.9 %copy-start.16 = (bf16[64,256]{0,1:T(8,128)(2,1)}, bf16[64,256]{0,1:T(8,128)(2,1)S(1)}, u32[]{:S(2)}) copy-start(bf16[64,256]{0,1:T(8,128)(2,1)S(1)} %copy.98) | copy-start | bytes 98308
  105.1 27.9 %collective-permute-start.4 = (f32[4,273,128]{2,0,1:T(4,128)}, f32[4,273,128]{2,0,1:T(4,128)}, u32[]{:S(2)}, u32[]{:S(2)}) collective-permute-start(f32[4,273,128]{2,0,1:T(4,128)} %copy.111), channel_id=1, source_target_pairs={{0,32},{4,36},{8,40},{12,44},{16,48},{20,52},{24,56},{28,60},{32,6... | collective-permute-start | bytes 1677320 | tf_op jit(solution)/shard_map/ppermute | solution.py:17
  135.9 148.5 %collective-permute-start.5 = (f32[4,273,128]{2,0,1:T(4,128)}, f32[4,273,128]{2,0,1:T(4,128)}, u32[]{:S(2)}, u32[]{:S(2)}) collective-permute-start(f32[4,273,128]{2,0,1:T(4,128)} %copy.113), channel_id=1, source_target_pairs={{0,64},{4,68},{8,72},{12,76},{16,80},{20,84},{24,88},{28,92},{32,9... | collective-permute-start | bytes 1677320 | tf_op jit(solution)/shard_map/ppermute | solution.py:17
  141.1 11.3 %collective-permute-start = (bf16[2,64,2048]{2,1,0:T(8,128)(2,1)}, bf16[2,64,2048]{2,1,0:T(8,128)(2,1)S(1)}, u32[]{:S(2)}, u32[]{:S(2)}) collective-permute-start(bf16[2,64,2048]{2,1,0:T(8,128)(2,1)} %get-tuple-element.109), channel_id=1, source_target_pairs={{0,1},{1,2},{2,3},{3,4},{4,5},{5,6},{6,7},{7,8},{8,9},{9,10},{10,1... | collective-permute-start | bytes 1572872 | tf_op jit(solution)/shard_map/while/body/eval_jaxpr/ppermute | solution.py:17
  154.1 15.5 %collective-permute-start = (bf16[2,64,2048]{2,1,0:T(8,128)(2,1)}, bf16[2,64,2048]{2,1,0:T(8,128)(2,1)S(1)}, u32[]{:S(2)}, u32[]{:S(2)}) collective-permute-start(bf16[2,64,2048]{2,1,0:T(8,128)(2,1)} %get-tuple-element.109), channel_id=1, source_target_pairs={{0,1},{1,2},{2,3},{3,4},{4,5},{5,6},{6,7},{7,8},{8,9},{9,10},{10,1... | collective-permute-start | bytes 1572872 | tf_op jit(solution)/shard_map/while/body/eval_jaxpr/ppermute | solution.py:17
  171.2 16.6 %collective-permute-start = (bf16[2,64,2048]{2,1,0:T(8,128)(2,1)}, bf16[2,64,2048]{2,1,0:T(8,128)(2,1)S(1)}, u32[]{:S(2)}, u32[]{:S(2)}) collective-permute-start(bf16[2,64,2048]{2,1,0:T(8,128)(2,1)} %get-tuple-element.109), channel_id=1, source_target_pairs={{0,1},{1,2},{2,3},{3,4},{4,5},{5,6},{6,7},{7,8},{8,9},{9,10},{10,1... | collective-permute-start | bytes 1572872 | tf_op jit(solution)/shard_map/while/body/eval_jaxpr/ppermute | solution.py:17
  189.5 16.1 %collective-permute-start = (bf16[2,64,2048]{2,1,0:T(8,128)(2,1)}, bf16[2,64,2048]{2,1,0:T(8,128)(2,1)S(1)}, u32[]{:S(2)}, u32[]{:S(2)}) collective-permute-start(bf16[2,64,2048]{2,1,0:T(8,128)(2,1)} %get-tuple-element.109), channel_id=1, source_target_pairs={{0,1},{1,2},{2,3},{3,4},{4,5},{5,6},{6,7},{7,8},{8,9},{9,10},{10,1... | collective-permute-start | bytes 1572872 | tf_op jit(solution)/shard_map/while/body/eval_jaxpr/ppermute | solution.py:17
  207.3 16.0 %collective-permute-start = (bf16[2,64,2048]{2,1,0:T(8,128)(2,1)}, bf16[2,64,2048]{2,1,0:T(8,128)(2,1)S(1)}, u32[]{:S(2)}, u32[]{:S(2)}) collective-permute-start(bf16[2,64,2048]{2,1,0:T(8,128)(2,1)} %get-tuple-element.109), channel_id=1, source_target_pairs={{0,1},{1,2},{2,3},{3,4},{4,5},{5,6},{6,7},{7,8},{8,9},{9,10},{10,1... | collective-permute-start | bytes 1572872 | tf_op jit(solution)/shard_map/while/body/eval_jaxpr/ppermute | solution.py:17
  225.0 16.0 %collective-permute-start = (bf16[2,64,2048]{2,1,0:T(8,128)(2,1)}, bf16[2,64,2048]{2,1,0:T(8,128)(2,1)S(1)}, u32[]{:S(2)}, u32[]{:S(2)}) collective-permute-start(bf16[2,64,2048]{2,1,0:T(8,128)(2,1)} %get-tuple-element.109), channel_id=1, source_target_pairs={{0,1},{1,2},{2,3},{3,4},{4,5},{5,6},{6,7},{7,8},{8,9},{9,10},{10,1... | collective-permute-start | bytes 1572872 | tf_op jit(solution)/shard_map/while/body/eval_jaxpr/ppermute | solution.py:17
  242.7 16.0 %collective-permute-start = (bf16[2,64,2048]{2,1,0:T(8,128)(2,1)}, bf16[2,64,2048]{2,1,0:T(8,128)(2,1)S(1)}, u32[]{:S(2)}, u32[]{:S(2)}) collective-permute-start(bf16[2,64,2048]{2,1,0:T(8,128)(2,1)} %get-tuple-element.109), channel_id=1, source_target_pairs={{0,1},{1,2},{2,3},{3,4},{4,5},{5,6},{6,7},{7,8},{8,9},{9,10},{10,1... | collective-permute-start | bytes 1572872 | tf_op jit(solution)/shard_map/while/body/eval_jaxpr/ppermute | solution.py:17
  260.5 16.0 %collective-permute-start = (bf16[2,64,2048]{2,1,0:T(8,128)(2,1)}, bf16[2,64,2048]{2,1,0:T(8,128)(2,1)S(1)}, u32[]{:S(2)}, u32[]{:S(2)}) collective-permute-start(bf16[2,64,2048]{2,1,0:T(8,128)(2,1)} %get-tuple-element.109), channel_id=1, source_target_pairs={{0,1},{1,2},{2,3},{3,4},{4,5},{5,6},{6,7},{7,8},{8,9},{9,10},{10,1... | collective-permute-start | bytes 1572872 | tf_op jit(solution)/shard_map/while/body/eval_jaxpr/ppermute | solution.py:17
  287.4 43.1 %collective-permute-start.6 = (f32[4,273,128]{2,0,1:T(4,128)}, f32[4,273,128]{2,0,1:T(4,128)}, u32[]{:S(2)}, u32[]{:S(2)}) collective-permute-start(f32[4,273,128]{2,0,1:T(4,128)} %copy.115), channel_id=1, source_target_pairs={{0,128},{4,132},{8,136},{12,140},{16,144},{20,148},{24,152},{28,15... | collective-permute-start | bytes 1677320 | tf_op jit(solution)/shard_map/ppermute | solution.py:17
  297.7 32.8 %copy-start.6 = (f32[4,273,128]{2,1,0:T(8,128)S(1)}, f32[4,273,128]{2,1,0:T(8,128)}, u32[]{:S(2)}) copy-start(f32[4,273,128]{2,1,0:T(8,128)} %copy-done.5) | copy-start | bytes 1677316
  301.7 31.6 %copy-start.13 = (bf16[64,2048]{1,0:T(8,128)(2,1)S(1)}, bf16[64,2048]{1,0:T(8,128)(2,1)}, u32[]{:S(2)}) copy-start(bf16[64,2048]{1,0:T(8,128)(2,1)} %param.15) | copy-start | bytes 786436
  301.7 55.8 %copy-start.2 = (f32[4,4,273,128]{3,2,1,0:T(8,128)S(1)}, f32[4,4,273,128]{3,2,1,0:T(8,128)}, u32[]{:S(2)}) copy-start(f32[4,4,273,128]{3,2,1,0:T(8,128)} %copy-done.1) | copy-start | bytes 6709252
  331.7 25.8 %collective-permute-start.7 = (f32[4,273,128]{2,0,1:T(4,128)S(1)}, f32[4,273,128]{2,0,1:T(4,128)S(1)}, u32[]{:S(2)}, u32[]{:S(2)}) collective-permute-start(f32[4,273,128]{2,0,1:T(4,128)S(1)} %copy.117), channel_id=1, source_target_pairs={{0,256},{4,260},{8,264},{12,268},{16,272},{20,276},{24,280},{28,28... | collective-permute-start | bytes 1677320 | tf_op jit(solution)/shard_map/ppermute | solution.py:17
  359.9 7.8 %copy-start.20 = (bf16[64,2048]{1,0:T(8,128)(2,1)S(1)}, bf16[64,2048]{1,0:T(8,128)(2,1)}, u32[]{:S(2)}) copy-start(bf16[64,2048]{1,0:T(8,128)(2,1)} %param.13) | copy-start | bytes 786436
  359.9 35.4 %all-to-all-start.1 = ((f32[4,4,273,128]{3,1,2,0:T(4,128)}), f32[4,4,273,128]{3,1,2,0:T(4,128)}, u32[]{:S(2)}, u32[]{:S(2)}) async-start(f32[4,4,273,128]{3,1,2,0:T(4,128)} %copy.119), calls=%async_computation.1 | async-start | bytes 4472832 | tf_op jit(solution)/shard_map/all_to_all | solution.py:93
  376.9 20.3 %copy-start.9 = (f32[64,16,16]{2,0,1:T(8,128)S(1)}, f32[64,16,16]{2,0,1:T(8,128)}, u32[]{:S(2)}) copy-start(f32[64,16,16]{2,0,1:T(8,128)} %copy.121) | copy-start | bytes 196612
  (13 other events, 36.2 us)
where the time goes:
time: 402 us; the launch traced here: 401 us
  waiting for transfers between devices  244 us (61%)
  local copies, waits for them, and re-layouts  55.1 us (14%)
  starting transfers between devices  43.9 us (11%)
  blocking collectives  30.3 us (8%)
  matrix products  15.1 us (4%)
  other arithmetic  11.2 us (3%)
    ppermute x15, waiting for transfers between devices, passed_along(): return lax.ppermute(shard, axis, pairs)  226 us
    ppermute x15, starting transfers between devices, passed_along(): return lax.ppermute(shard, axis, pairs)  36.2 us
    all_to_all x1, blocking collectives, shards(): lax.all_to_all(local_state[None], 'sub', split_axis=1, concat_axis=0, til...  30.3 us
    all_to_all x1, waiting for transfers between devices, shards(): lax.all_to_all(slots, 'sub', split_axis=0, concat_axis=1, tiled=True)[0]  18.4 us
  transfers between devices with their start and end apart: 16, of which 15 were waited for; matrix products, arithmetic and copies ran while one was open for 13% of the time, Pallas kernels for 0%

commit v1 on v0

v1 whole, which is shorter than its diff:
```python
import math

import jax
import jax.numpy as jnp
import numpy as np
from jax import lax
from jax.sharding import Mesh
from jax.sharding import PartitionSpec as P

FDIM = 16
VDIM = 128
SDIM = 128
WINDOW = 512
CORES = 2
ALL = ("outer", "core", "sub")
GROUP = ("core", "sub")


def passed_along(shard, axis, by):
    size = lax.axis_size(axis)
    pairs = [(i, i + by) for i in range(size) if 0 <= i + by < size]
    return lax.ppermute(shard, axis, pairs)


def sym_features(vectors, for_query):
    halved = vectors * 0.5
    pieces = [jnp.ones(halved.shape[:-1] + (1,), jnp.float32), halved]
    for a in range(FDIM):
        block = halved[..., a : a + 1] * halved[..., a:]
        if for_query:
            scale = np.ones((FDIM - a,), np.float32)
            scale[0] = 0.5
            block = block * scale
        pieces.append(block)
    return jnp.concatenate(pieces, axis=-1)


def shards(
    linear_query, linear_key, linear_value, lin_gain, window_query, window_key, window_value
):
    rows_dev = linear_query.shape[0]
    dev_count = lax.axis_size(ALL)
    group_count = lax.axis_size(GROUP)
    outer_count = lax.axis_size("outer")
    device_pos = lax.axis_index(ALL)
    base_row = device_pos * rows_dev
    reach_dev = WINDOW // rows_dev
    channels = window_key.shape[1]
    head_count = channels // SDIM
    lin_heads = linear_query.shape[1] // FDIM

    stacked = jnp.stack([window_key, window_value])
    earlier = [passed_along(stacked, ALL, reach_dev - t) for t in range(reach_dev)]
    earlier = jnp.concatenate(earlier, axis=1)
    key_rows = jnp.concatenate([earlier[0], window_key], axis=0).reshape(-1, head_count, SDIM)
    value_rows = jnp.concatenate([earlier[1], window_value], axis=0).reshape(-1, head_count, SDIM)

    query_bf = linear_query.reshape(rows_dev, lin_heads, FDIM)
    key_bf = linear_key.reshape(rows_dev, lin_heads, FDIM)
    query_lin = query_bf.astype(jnp.float32)
    key_lin = key_bf.astype(jnp.float32)
    value_lin = linear_value.astype(jnp.float32).reshape(rows_dev, lin_heads, VDIM)
    local_state = jnp.einsum(
        "jhf,jhe->hfe",
        sym_features(key_lin, False),
        value_lin,
        precision=lax.Precision.HIGHEST,
    )
    owned = lax.all_to_all(local_state[None], GROUP, split_axis=1, concat_axis=0, tiled=True)
    running_inner = jnp.cumsum(owned, axis=0)
    inner_before = running_inner - owned
    group_total = running_inner[-1]
    running = group_total
    for level in range((outer_count - 1).bit_length()):
        running = running + passed_along(running, "outer", 1 << level)
    groups_before = running - group_total
    slots = inner_before + groups_before[None]
    prefix = lax.all_to_all(slots, GROUP, split_axis=0, concat_axis=1, tiled=True)[0]

    query_heads = window_query.reshape(rows_dev, head_count, SDIM)
    scores = jnp.einsum(
        "ihd,jhd->hij", query_heads, key_rows, preferred_element_type=jnp.float32
    ) * (1.0 / math.sqrt(SDIM))
    query_pos = base_row + jnp.arange(rows_dev, dtype=jnp.int32)
    key_pos = (
        base_row - reach_dev * rows_dev + jnp.arange((reach_dev + 1) * rows_dev, dtype=jnp.int32)
    )
    allowed = (
        (key_pos[None, :] <= query_pos[:, None])
        & (key_pos[None, :] > query_pos[:, None] - WINDOW)
        & (key_pos[None, :] >= 0)
    )
    scores = jnp.where(allowed[None], scores, jnp.float32(-1e30))
    row_max = jnp.max(scores, axis=-1, keepdims=True)
    exp_scores = jnp.exp(scores - row_max)
    weights_bf = (exp_scores / jnp.sum(exp_scores, axis=-1, keepdims=True)).astype(jnp.bfloat16)
    mixed = jnp.einsum("hij,jhd->ihd", weights_bf, value_rows, preferred_element_type=jnp.float32)
    window_out = mixed.reshape(rows_dev, channels).astype(jnp.bfloat16)

    from_state = jnp.einsum(
        "ihf,hfe->ihe", sym_features(query_lin, True), prefix, precision=lax.Precision.HIGHEST
    )
    dot_inner = (
        jnp.einsum("ihd,jhd->hij", query_bf, key_bf, preferred_element_type=jnp.float32) * 0.25
    )
    weight = 1.0 + dot_inner + 0.5 * dot_inner * dot_inner
    causal = (
        jnp.arange(rows_dev, dtype=jnp.int32)[:, None]
        >= jnp.arange(rows_dev, dtype=jnp.int32)[None, :]
    )
    weight = jnp.where(causal[None], weight, jnp.float32(0.0))
    local_sum = jnp.einsum("hij,jhe->ihe", weight, value_lin, precision=lax.Precision.HIGHEST)
    numerator = local_sum + from_state
    inv_rms = lax.rsqrt(jnp.mean(numerator * numerator, axis=-1, keepdims=True) + 1e-05)
    gain_rows = lin_gain.reshape(lin_heads, VDIM)
    linear_out = (
        (numerator * inv_rms * gain_rows).reshape(rows_dev, lin_heads * VDIM).astype(jnp.bfloat16)
    )
    return (linear_out, window_out)


def solution(mesh):
    seq_count = mesh.shape["seq"]
    sub_count = mesh.shape["sub"]
    split_mesh = Mesh(
        np.asarray(mesh.devices).reshape(seq_count // CORES, CORES, sub_count), ALL
    )
    rows = P(ALL, None)
    in_specs = (rows, rows, rows, P(), rows, rows, rows)
    out_specs = (rows, rows)
    return jax.shard_map(
        shards, mesh=split_mesh, in_specs=in_specs, out_specs=out_specs, check_vma=False
    )
```

time: 402 us -> 230 us (0.57)
  the two profiles are of different devices: /device:TPU:46 before, /device:TPU:1 now
where the time goes in v1:
time: 230 us; the launch traced here: 227 us
  starting transfers between devices  89.4 us (39%)
  local copies, waits for them, and re-layouts  64.5 us (28%)
  other arithmetic  53 us (23%)
  matrix products  13.9 us (6%)
  waiting for transfers between devices  5.48 us (2%)
    ppermute x14, starting transfers between devices, passed_along(): return lax.ppermute(shard, axis, pairs)  73.8 us
    ppermute x8, local copies, waits for them, and re-layouts, passed_along(): return lax.ppermute(shard, axis, pairs)  19.1 us
    mul x15, other arithmetic, sym_features(): block = block * scale  17.2 us
    mul x15, other arithmetic, sym_features(): block = halved[..., a:a + 1] * halved[..., a:]  16.3 us
    concatenate x2, local copies, waits for them, and re-layouts, sym_features(): return jnp.concatenate(pieces, axis=-1)  13.9 us
    concatenate x1, local copies, waits for them, and re-layouts, shards(): earlier = jnp.concatenate(earlier, axis=1)  10.8 us
    slice x2, other arithmetic, sym_features(): block = halved[..., a:a + 1] * halved[..., a:]  9.59 us
    all_to_all x1, starting transfers between devices, shards(): lax.all_to_all(slots, GROUP, split_axis=0, concat_axis=1, tiled=True)[0]  9.27 us
  transfers between devices with their start and end apart: 16, of which 4 were waited for; matrix products, arithmetic and copies ran while one was open for 53% of the time, Pallas kernels for 0%

profile of v1, /device:TPU:1, one launch (start us, length us, event | category | flops | bytes accessed | tf_op | source)
XLA Modules:
  0.0 227.5 jit_solution(14609232922775666380)
XLA Ops:
  2.6 5.6 %collective-permute-start.6 = (bf16[2,64,2048]{2,1,0:T(8,128)(2,1)}, bf16[2,64,2048]{2,1,0:T(8,128)(2,1)}, u32[]{:S(2)}, u32[]{:S(2)}) collective-permute-start(bf16[2,64,2048]{2,1,0:T(8,128)(2,1)} %pad_maximum_fusion), channel_id=1, source_target_pairs={{0,8},{1,9},{2,10},{3,11},{4,12},{5,13},{6,14},{7,15},{8,16},{9,17... | collective-permute-start | bytes 1572872 | tf_op jit(solution)/shard_map/ppermute | solution.py:22
  8.2 7.1 %collective-permute-start.7 = (bf16[2,64,2048]{2,1,0:T(8,128)(2,1)}, bf16[2,64,2048]{2,1,0:T(8,128)(2,1)}, u32[]{:S(2)}, u32[]{:S(2)}) collective-permute-start(bf16[2,64,2048]{2,1,0:T(8,128)(2,1)} %pad_maximum_fusion), channel_id=1, source_target_pairs={{0,7},{1,8},{2,9},{3,10},{4,11},{5,12},{6,13},{7,14},{8,15},{9,16}... | collective-permute-start | bytes 1572872 | tf_op jit(solution)/shard_map/ppermute | solution.py:22
  15.2 4.5 %collective-permute-start.8 = (bf16[2,64,2048]{2,1,0:T(8,128)(2,1)}, bf16[2,64,2048]{2,1,0:T(8,128)(2,1)}, u32[]{:S(2)}, u32[]{:S(2)}) collective-permute-start(bf16[2,64,2048]{2,1,0:T(8,128)(2,1)} %pad_maximum_fusion), channel_id=1, source_target_pairs={{0,6},{1,7},{2,8},{3,9},{4,10},{5,11},{6,12},{7,13},{8,14},{9,15},... | collective-permute-start | bytes 1572872 | tf_op jit(solution)/shard_map/ppermute | solution.py:22
  23.6 4.1 %slice_reduce_fusion.14 = (f32[64,16]{0,1:T(8,128)S(1)}, f32[64,16]{0,1:T(8,128)S(1)}, f32[64,16]{0,1:T(8,128)S(1)}, f32[64,16]{0,1:T(8,128)S(1)}, f32[64,16]{0,...) fusion(f32[64,16,16]{2,0,1:T(8,128)S(1)} %convert_multiply_fusion.3), kind=kLoop, calls=%fused_computation.76 | loop fusion | flops 2048 | bytes 131072 | tf_op jit(solution)/shard_map/slice | solution.py:29
  44.1 6.7 %concatenate.25 = f32[64,16,153]{2,0,1:T(8,128)S(1)} concatenate(f32[64,16,1]{2,0,1:T(8,128)S(1)} %broadcast.125, f32[64,16,16]{2,0,1:T(8,128)S(1)} %convert_multiply_fusion.3, f32[64,16,16]{2,0,1:T(8,128)} %convert_multiply_fusion.2, f32[64,16,15]{2,0,1:T(8,128)} %slice_multiply_fusion.30, f32[64,16,14]{2,0,1:T(8,128)} %slice_multiply_fusion.29, ...), dimensions={2} | concatenate | bytes 1253376 | tf_op jit(solution)/shard_map/concatenate | solution.py:35
  55.5 6.4 %all-to-all-start = ((f32[1,16,153,128]{3,0,2,1:T(1,128)}), f32[1,16,153,128]{3,0,2,1:T(1,128)S(1)}, u32[]{:S(2)}, u32[]{:S(2)}) async-start(f32[1,16,153,128]{3,0,2,1:T(1,128)} %copy.75), calls=%async_computation | async-start | bytes 2506752 | tf_op jit(solution)/shard_map/all_to_all | solution.py:69
  62.9 5.4 %slice_reduce_fusion = (f32[64,16]{0,1:T(8,128)S(1)}, f32[64,16]{0,1:T(8,128)S(1)}, f32[64,16]{0,1:T(8,128)S(1)}, f32[64,16]{0,1:T(8,128)S(1)}, f32[64,16]{0,1:T...) fusion(f32[64,16,16]{2,0,1:T(8,128)S(1)} %convert_multiply_fusion.1), kind=kLoop, calls=%fused_computation.32 | loop fusion | flops 3072 | bytes 131072 | tf_op jit(solution)/shard_map/slice | solution.py:29
  85.2 3.1 %collective-permute-start = (f32[2,153,128]{2,0,1:T(2,128)S(1)}, f32[2,153,128]{2,0,1:T(2,128)S(1)}, u32[]{:S(2)}, u32[]{:S(2)}) collective-permute-start(f32[2,153,128]{2,0,1:T(2,128)S(1)} %slice_bitcast_fusion), channel_id=1, source_target_pairs={{0,8},{8,16},{16,24},{24,32},{32,40},{40,48},{48,56},{56,64},{64,7... | collective-permute-start | bytes 470024 | tf_op jit(solution)/shard_map/ppermute | solution.py:22
  91.8 5.0 %collective-permute-start.1 = (f32[2,153,128]{2,0,1:T(2,128)S(1)}, f32[2,153,128]{2,0,1:T(2,128)S(1)}, u32[]{:S(2)}, u32[]{:S(2)}) collective-permute-start(f32[2,153,128]{2,0,1:T(2,128)S(1)} %fusion.78), channel_id=1, source_target_pairs={{0,16},{8,24},{16,32},{24,40},{32,48},{40,56},{48,64},{56,72},{64,... | collective-permute-start | bytes 470024 | tf_op jit(solution)/shard_map/ppermute | solution.py:22
  99.6 8.0 %collective-permute-start.2 = (f32[2,153,128]{2,0,1:T(2,128)S(1)}, f32[2,153,128]{2,0,1:T(2,128)S(1)}, u32[]{:S(2)}, u32[]{:S(2)}) collective-permute-start(f32[2,153,128]{2,0,1:T(2,128)S(1)} %add.92), channel_id=1, source_target_pairs={{0,32},{8,40},{16,48},{24,56},{32,64},{40,72},{48,80},{56,88},{64,... | collective-permute-start | bytes 470024 | tf_op jit(solution)/shard_map/ppermute | solution.py:22
  109.8 12.4 %collective-permute-start.3 = (f32[2,153,128]{2,0,1:T(2,128)S(1)}, f32[2,153,128]{2,0,1:T(2,128)}, u32[]{:S(2)}, u32[]{:S(2)}) collective-permute-start(f32[2,153,128]{2,0,1:T(2,128)S(1)} %add.93), channel_id=1, source_target_pairs={{0,64},{8,72},{16,80},{24,88},{32,96},{40,104},{48,112},{56,120},{... | collective-permute-start | bytes 470024 | tf_op jit(solution)/shard_map/ppermute | solution.py:22
  124.7 4.9 %collective-permute-start.4 = (f32[2,153,128]{2,0,1:T(2,128)S(1)}, f32[2,153,128]{2,0,1:T(2,128)S(1)}, u32[]{:S(2)}, u32[]{:S(2)}) collective-permute-start(f32[2,153,128]{2,0,1:T(2,128)S(1)} %add.94), channel_id=1, source_target_pairs={{0,128},{8,136},{16,144},{24,152},{32,160},{40,168},{48,176},{56,1... | collective-permute-start | bytes 470024 | tf_op jit(solution)/shard_map/ppermute | solution.py:22
  130.9 4.3 %collective-permute-start.10 = (bf16[2,64,2048]{2,1,0:T(8,128)(2,1)}, bf16[2,64,2048]{2,1,0:T(8,128)(2,1)}, u32[]{:S(2)}, u32[]{:S(2)}) collective-permute-start(bf16[2,64,2048]{2,1,0:T(8,128)(2,1)} %pad_maximum_fusion), channel_id=1, source_target_pairs={{0,4},{1,5},{2,6},{3,7},{4,8},{5,9},{6,10},{7,11},{8,12},{9,13},{1... | collective-permute-start | bytes 1572872 | tf_op jit(solution)/shard_map/ppermute | solution.py:22
  135.1 4.1 %collective-permute-start.11 = (bf16[2,64,2048]{2,1,0:T(8,128)(2,1)}, bf16[2,64,2048]{2,1,0:T(8,128)(2,1)}, u32[]{:S(2)}, u32[]{:S(2)}) collective-permute-start(bf16[2,64,2048]{2,1,0:T(8,128)(2,1)} %pad_maximum_fusion), channel_id=1, source_target_pairs={{0,3},{1,4},{2,5},{3,6},{4,7},{5,8},{6,9},{7,10},{8,11},{9,12},{10... | collective-permute-start | bytes 1572872 | tf_op jit(solution)/shard_map/ppermute | solution.py:22
  141.5 2.5 %collective-permute-start.13 = (bf16[2,64,2048]{2,1,0:T(8,128)(2,1)}, bf16[2,64,2048]{2,1,0:T(8,128)(2,1)}, u32[]{:S(2)}, u32[]{:S(2)}) collective-permute-start(bf16[2,64,2048]{2,1,0:T(8,128)(2,1)} %pad_maximum_fusion), channel_id=1, source_target_pairs={{0,1},{1,2},{2,3},{3,4},{4,5},{5,6},{6,7},{7,8},{8,9},{9,10},{10,1... | collective-permute-start | bytes 1572872 | tf_op jit(solution)/shard_map/ppermute | solution.py:22
  144.6 7.2 %concatenate.26 = f32[64,16,153]{2,0,1:T(8,128)} concatenate(f32[64,16,1]{2,0,1:T(8,128)} %copy-done.1, f32[64,16,16]{2,0,1:T(8,128)S(1)} %convert_multiply_fusion.1, f32[64,16,16]{2,0,1:T(8,128)} %fusion.20, f32[64,16,15]{2,0,1:T(8,128)} %fusion.35, f32[64,16,14]{2,0,1:T(8,128)} %fusion.34, f32[64,16,13]{2,0,1:T(8,128)} %fusion.33, f32[64,16,12]{2,0,1:T(8,128)} %fusion.32, ...), dimensions={2} | concatenate | bytes 1253376 | tf_op jit(solution)/shard_map/concatenate | solution.py:35
  155.2 8.0 %collective-permute-start.5 = (f32[2,153,128]{2,0,1:T(2,128)S(1)}, f32[2,153,128]{2,0,1:T(2,128)S(1)}, u32[]{:S(2)}, u32[]{:S(2)}) collective-permute-start(f32[2,153,128]{2,0,1:T(2,128)S(1)} %add.95), channel_id=1, source_target_pairs={{0,256},{8,264},{16,272},{24,280},{32,288},{40,296},{48,304},{56,3... | collective-permute-start | bytes 470024 | tf_op jit(solution)/shard_map/ppermute | solution.py:22
  171.1 2.5 %copy.84 = bf16[2,64,2048]{1,2,0:T(8,128)(2,1)} copy(bf16[2,64,2048]{2,1,0:T(8,128)(2,1)} %collective-permute-done.9) | data formatting | bytes 1048576 | tf_op jit(solution)/shard_map/ppermute | solution.py:22
  183.1 10.8 %concatenate.27 = bf16[2,512,2048]{1,2,0:T(8,128)(2,1)} concatenate(bf16[2,64,2048]{1,2,0:T(8,128)(2,1)} %copy.81, bf16[2,64,2048]{1,2,0:T(8,128)(2,1)} %copy.82, bf16[2,64,2048]{1,2,0:T(8,128)(2,1)} %copy.83, bf16[2,64,2048]{1,2,0:T(8,128)(2,1)} %copy.84, bf16[2,64,2048]{1,2,0:T(8,128)(2,1)} %copy.85, bf16[2,64,2048]{1,2,0:T(8,128)(2,1)} %copy.86, bf16[2,64,2048]{1,2,0:T(8,128)(2,1)} %copy.87, ...), dimensions={1} | concatenate | bytes 8388608 | tf_op jit(solution)/shard_map/concatenate | solution.py:54
  196.5 9.3 %all-to-all-start.1 = ((f32[8,2,153,128]{3,1,2,0:T(2,128)}), f32[8,2,153,128]{3,1,2,0:T(2,128)}, u32[]{:S(2)}, u32[]{:S(2)}) async-start(f32[8,2,153,128]{3,1,2,0:T(2,128)} %copy.77), calls=%async_computation.1 | async-start | bytes 2506752 | tf_op jit(solution)/shard_map/all_to_all | solution.py:78
  205.8 3.8 %fusion.79 = (bf16[1,512,2048]{1,2,0:T(8,128)(2,1)}, bf16[1,512,2048]{1,2,0:T(8,128)(2,1)S(1)}) fusion(bf16[2,512,2048]{1,2,0:T(8,128)(2,1)} %concatenate.27), kind=kLoop, calls=%fused_computation.149 | loop fusion | bytes 8388608 | tf_op jit(solution)/shard_map/slice | solution.py:55
  209.6 3.9 %copy.91 = bf16[512,16,128]{2,0,1:T(8,128)(2,1)} copy(bf16[512,16,128]{0,2,1:T(8,128)(2,1)} %bitcast.88) | data formatting | bytes 4194304 | tf_op jit(solution)/shard_map/concatenate | solution.py:55
  213.6 2.5 %copy.89 = bf16[512,16,128]{2,0,1:T(8,128)(2,1)} copy(bf16[512,16,128]{0,2,1:T(8,128)(2,1)S(1)} %bitcast.87) | data formatting | bytes 4194304 | tf_op jit(solution)/shard_map/concatenate | solution.py:56
  216.1 4.4 %fusion.80 = (f32[16,64]{1,0:T(8,128)S(1)}, f32[16,64,576]{2,1,0:T(8,128)}) fusion(pred[64,576]{1,0:T(8,128)(4,1)S(1)} %and_and_fusion, bf16[64,16,128]{2,0,1:T(8,128)(2,1)S(1)} %copy-done.13, bf16[512,16,128]{2,0,1:T(8,128)(2,1)} %copy.91, bf16[64,2048]{1,0:T(8,128)(2,1)S(1)} %copy-done), kind=kOutput, calls=%fused_computation.150 | convolution fusion | flops 158073408 | bytes 5021696 | tf_op jit(solution)/shard_map/sub | solution.py:95
  (159 shorter events, 89.8 us)
Async XLA Ops:
  0.6 215.4 %copy-start = (bf16[64,2048]{1,0:T(8,128)(2,1)S(1)}, bf16[64,2048]{1,0:T(8,128)(2,1)}, u32[]{:S(2)}) copy-start(bf16[64,2048]{1,0:T(8,128)(2,1)} %param.27) | copy-start | bytes 786436
  2.6 128.3 %collective-permute-start.6 = (bf16[2,64,2048]{2,1,0:T(8,128)(2,1)}, bf16[2,64,2048]{2,1,0:T(8,128)(2,1)}, u32[]{:S(2)}, u32[]{:S(2)}) collective-permute-start(bf16[2,64,2048]{2,1,0:T(8,128)(2,1)} %pad_maximum_fusion), channel_id=1, source_target_pairs={{0,8},{1,9},{2,10},{3,11},{4,12},{5,13},{6,14},{7,15},{8,16},{9,17... | collective-permute-start | bytes 1572872 | tf_op jit(solution)/shard_map/ppermute | solution.py:22
  8.2 126.9 %collective-permute-start.7 = (bf16[2,64,2048]{2,1,0:T(8,128)(2,1)}, bf16[2,64,2048]{2,1,0:T(8,128)(2,1)}, u32[]{:S(2)}, u32[]{:S(2)}) collective-permute-start(bf16[2,64,2048]{2,1,0:T(8,128)(2,1)} %pad_maximum_fusion), channel_id=1, source_target_pairs={{0,7},{1,8},{2,9},{3,10},{4,11},{5,12},{6,13},{7,14},{8,15},{9,16}... | collective-permute-start | bytes 1572872 | tf_op jit(solution)/shard_map/ppermute | solution.py:22
  15.2 124.0 %collective-permute-start.8 = (bf16[2,64,2048]{2,1,0:T(8,128)(2,1)}, bf16[2,64,2048]{2,1,0:T(8,128)(2,1)}, u32[]{:S(2)}, u32[]{:S(2)}) collective-permute-start(bf16[2,64,2048]{2,1,0:T(8,128)(2,1)} %pad_maximum_fusion), channel_id=1, source_target_pairs={{0,6},{1,7},{2,8},{3,9},{4,10},{5,11},{6,12},{7,13},{8,14},{9,15},... | collective-permute-start | bytes 1572872 | tf_op jit(solution)/shard_map/ppermute | solution.py:22
  19.8 135.5 %collective-permute-start.9 = (bf16[2,64,2048]{2,1,0:T(8,128)(2,1)}, bf16[2,64,2048]{2,1,0:T(8,128)(2,1)}, u32[]{:S(2)}, u32[]{:S(2)}) collective-permute-start(bf16[2,64,2048]{2,1,0:T(8,128)(2,1)} %pad_maximum_fusion), channel_id=1, source_target_pairs={{0,5},{1,6},{2,7},{3,8},{4,9},{5,10},{6,11},{7,12},{8,13},{9,14},{... | collective-permute-start | bytes 1572872 | tf_op jit(solution)/shard_map/ppermute | solution.py:22
  53.1 8.7 %copy-start.17 = (bf16[64,256]{1,0:T(8,128)(2,1)S(1)}, bf16[64,256]{1,0:T(8,128)(2,1)}, u32[]{:S(2)}) copy-start(bf16[64,256]{1,0:T(8,128)(2,1)} %param.23) | copy-start | bytes 98308
  55.5 29.1 %all-to-all-start = ((f32[1,16,153,128]{3,0,2,1:T(1,128)}), f32[1,16,153,128]{3,0,2,1:T(1,128)S(1)}, u32[]{:S(2)}, u32[]{:S(2)}) async-start(f32[1,16,153,128]{3,0,2,1:T(1,128)} %copy.75), calls=%async_computation | async-start | bytes 2506752 | tf_op jit(solution)/shard_map/all_to_all | solution.py:69
  84.6 12.2 %copy-start.10 = (bf16[64,256]{0,1:T(8,128)(2,1)S(1)}, bf16[64,256]{0,1:T(8,128)(2,1)}, u32[]{:S(2)}) copy-start(bf16[64,256]{0,1:T(8,128)(2,1)} %copy-done.9) | copy-start | bytes 98308
  84.6 12.2 %copy-start.12 = (bf16[64,256]{0,1:T(8,128)(2,1)S(1)}, bf16[64,256]{0,1:T(8,128)(2,1)}, u32[]{:S(2)}) copy-start(bf16[64,256]{0,1:T(8,128)(2,1)} %copy-done.11) | copy-start | bytes 98308
  84.7 22.9 %copy-start.6 = (bf16[64,2048]{1,0:T(8,128)(2,1)S(1)}, bf16[64,2048]{1,0:T(8,128)(2,1)}, u32[]{:S(2)}) copy-start(bf16[64,2048]{1,0:T(8,128)(2,1)} %param.28) | copy-start | bytes 786436
  85.1 37.1 %copy-start.7 = (bf16[64,2048]{1,0:T(8,128)(2,1)S(1)}, bf16[64,2048]{1,0:T(8,128)(2,1)}, u32[]{:S(2)}) copy-start(bf16[64,2048]{1,0:T(8,128)(2,1)} %param.29) | copy-start | bytes 786436
  85.2 6.6 %collective-permute-start = (f32[2,153,128]{2,0,1:T(2,128)S(1)}, f32[2,153,128]{2,0,1:T(2,128)S(1)}, u32[]{:S(2)}, u32[]{:S(2)}) collective-permute-start(f32[2,153,128]{2,0,1:T(2,128)S(1)} %slice_bitcast_fusion), channel_id=1, source_target_pairs={{0,8},{8,16},{16,24},{24,32},{32,40},{40,48},{48,56},{56,64},{64,7... | collective-permute-start | bytes 470024 | tf_op jit(solution)/shard_map/ppermute | solution.py:22
  91.8 7.7 %collective-permute-start.1 = (f32[2,153,128]{2,0,1:T(2,128)S(1)}, f32[2,153,128]{2,0,1:T(2,128)S(1)}, u32[]{:S(2)}, u32[]{:S(2)}) collective-permute-start(f32[2,153,128]{2,0,1:T(2,128)S(1)} %fusion.78), channel_id=1, source_target_pairs={{0,16},{8,24},{16,32},{24,40},{32,48},{40,56},{48,64},{56,72},{64,... | collective-permute-start | bytes 470024 | tf_op jit(solution)/shard_map/ppermute | solution.py:22
  99.6 10.1 %collective-permute-start.2 = (f32[2,153,128]{2,0,1:T(2,128)S(1)}, f32[2,153,128]{2,0,1:T(2,128)S(1)}, u32[]{:S(2)}, u32[]{:S(2)}) collective-permute-start(f32[2,153,128]{2,0,1:T(2,128)S(1)} %add.92), channel_id=1, source_target_pairs={{0,32},{8,40},{16,48},{24,56},{32,64},{40,72},{48,80},{56,88},{64,... | collective-permute-start | bytes 470024 | tf_op jit(solution)/shard_map/ppermute | solution.py:22
  109.8 13.9 %collective-permute-start.3 = (f32[2,153,128]{2,0,1:T(2,128)S(1)}, f32[2,153,128]{2,0,1:T(2,128)}, u32[]{:S(2)}, u32[]{:S(2)}) collective-permute-start(f32[2,153,128]{2,0,1:T(2,128)S(1)} %add.93), channel_id=1, source_target_pairs={{0,64},{8,72},{16,80},{24,88},{32,96},{40,104},{48,112},{56,120},{... | collective-permute-start | bytes 470024 | tf_op jit(solution)/shard_map/ppermute | solution.py:22
  124.7 19.9 %copy-start.8 = (f32[2,153,128]{2,0,1:T(2,128)}, f32[2,153,128]{2,0,1:T(2,128)S(1)}, u32[]{:S(2)}) copy-start(f32[2,153,128]{2,0,1:T(2,128)S(1)} %add.94) | copy-start | bytes 470020
  124.7 16.8 %collective-permute-start.4 = (f32[2,153,128]{2,0,1:T(2,128)S(1)}, f32[2,153,128]{2,0,1:T(2,128)S(1)}, u32[]{:S(2)}, u32[]{:S(2)}) collective-permute-start(f32[2,153,128]{2,0,1:T(2,128)S(1)} %add.94), channel_id=1, source_target_pairs={{0,128},{8,136},{16,144},{24,152},{32,160},{40,168},{48,176},{56,1... | collective-permute-start | bytes 470024 | tf_op jit(solution)/shard_map/ppermute | solution.py:22
  130.9 42.7 %collective-permute-start.10 = (bf16[2,64,2048]{2,1,0:T(8,128)(2,1)}, bf16[2,64,2048]{2,1,0:T(8,128)(2,1)}, u32[]{:S(2)}, u32[]{:S(2)}) collective-permute-start(bf16[2,64,2048]{2,1,0:T(8,128)(2,1)} %pad_maximum_fusion), channel_id=1, source_target_pairs={{0,4},{1,5},{2,6},{3,7},{4,8},{5,9},{6,10},{7,11},{8,12},{9,13},{1... | collective-permute-start | bytes 1572872 | tf_op jit(solution)/shard_map/ppermute | solution.py:22
  135.1 40.8 %collective-permute-start.11 = (bf16[2,64,2048]{2,1,0:T(8,128)(2,1)}, bf16[2,64,2048]{2,1,0:T(8,128)(2,1)}, u32[]{:S(2)}, u32[]{:S(2)}) collective-permute-start(bf16[2,64,2048]{2,1,0:T(8,128)(2,1)} %pad_maximum_fusion), channel_id=1, source_target_pairs={{0,3},{1,4},{2,5},{3,6},{4,7},{5,8},{6,9},{7,10},{8,11},{9,12},{10... | collective-permute-start | bytes 1572872 | tf_op jit(solution)/shard_map/ppermute | solution.py:22
  139.3 39.0 %collective-permute-start.12 = (bf16[2,64,2048]{2,1,0:T(8,128)(2,1)}, bf16[2,64,2048]{2,1,0:T(8,128)(2,1)}, u32[]{:S(2)}, u32[]{:S(2)}) collective-permute-start(bf16[2,64,2048]{2,1,0:T(8,128)(2,1)} %pad_maximum_fusion), channel_id=1, source_target_pairs={{0,2},{1,3},{2,4},{3,5},{4,6},{5,7},{6,8},{7,9},{8,10},{9,11},{10,... | collective-permute-start | bytes 1572872 | tf_op jit(solution)/shard_map/ppermute | solution.py:22
  141.5 39.2 %collective-permute-start.13 = (bf16[2,64,2048]{2,1,0:T(8,128)(2,1)}, bf16[2,64,2048]{2,1,0:T(8,128)(2,1)}, u32[]{:S(2)}, u32[]{:S(2)}) collective-permute-start(bf16[2,64,2048]{2,1,0:T(8,128)(2,1)} %pad_maximum_fusion), channel_id=1, source_target_pairs={{0,1},{1,2},{2,3},{3,4},{4,5},{5,6},{6,7},{7,8},{8,9},{9,10},{10,1... | collective-permute-start | bytes 1572872 | tf_op jit(solution)/shard_map/ppermute | solution.py:22
  144.6 7.2 %copy-start.5 = (bf16[64,2048]{1,0:T(8,128)(2,1)S(1)}, bf16[64,2048]{1,0:T(8,128)(2,1)}, u32[]{:S(2)}) copy-start(bf16[64,2048]{1,0:T(8,128)(2,1)} %param.25) | copy-start | bytes 786436
  155.2 38.7 %collective-permute-start.5 = (f32[2,153,128]{2,0,1:T(2,128)S(1)}, f32[2,153,128]{2,0,1:T(2,128)S(1)}, u32[]{:S(2)}, u32[]{:S(2)}) collective-permute-start(f32[2,153,128]{2,0,1:T(2,128)S(1)} %add.95), channel_id=1, source_target_pairs={{0,256},{8,264},{16,272},{24,280},{32,288},{40,296},{48,304},{56,3... | collective-permute-start | bytes 470024 | tf_op jit(solution)/shard_map/ppermute | solution.py:22
  196.5 27.1 %all-to-all-start.1 = ((f32[8,2,153,128]{3,1,2,0:T(2,128)}), f32[8,2,153,128]{3,1,2,0:T(2,128)}, u32[]{:S(2)}, u32[]{:S(2)}) async-start(f32[8,2,153,128]{3,1,2,0:T(2,128)} %copy.77), calls=%async_computation.1 | async-start | bytes 2506752 | tf_op jit(solution)/shard_map/all_to_all | solution.py:78
  (26 other events, 100.1 us)

commit v2 on v1

--- a/solution.py
+++ b/solution.py
@@ -12,8 +12,19 @@
 SDIM = 128
 WINDOW = 512
 CORES = 2
-ALL = ("outer", "core", "sub")
+ALL = ("y", "z", "core", "sub")
 GROUP = ("core", "sub")
+
+
+def pair_tables(for_query):
+    pairs = [(0, 0)] + [(0, a + 1) for a in range(FDIM)]
+    pairs += [(a + 1, b + 1) for a in range(FDIM) for b in range(a, FDIM)]
+    first = np.zeros((FDIM + 1, len(pairs)), np.float32)
+    second = np.zeros((FDIM + 1, len(pairs)), np.float32)
+    for f, (a, b) in enumerate(pairs):
+        first[a, f] = 0.5 if (for_query and a == b and a > 0) else 1.0
+        second[b, f] = 1.0
+    return first, second
 
 
 def passed_along(shard, axis, by):
@@ -24,15 +35,12 @@
 
 def sym_features(vectors, for_query):
     halved = vectors * 0.5
-    pieces = [jnp.ones(halved.shape[:-1] + (1,), jnp.float32), halved]
-    for a in range(FDIM):
-        block = halved[..., a : a + 1] * halved[..., a:]
-        if for_query:
-            scale = np.ones((FDIM - a,), np.float32)
-            scale[0] = 0.5
-            block = block * scale
-        pieces.append(block)
-    return jnp.concatenate(pieces, axis=-1)
+    ext = jnp.concatenate([jnp.ones(halved.shape[:-1] + (1,), jnp.float32), halved], axis=-1)
+    first, second = pair_tables(for_query)
+    pick = lambda table: jnp.einsum(
+        "jhi,if->jhf", ext, jnp.asarray(table), precision=lax.Precision.HIGHEST
+    )
+    return pick(first) * pick(second)
 
 
 def shards(
@@ -41,7 +49,6 @@
     rows_dev = linear_query.shape[0]
     dev_count = lax.axis_size(ALL)
     group_count = lax.axis_size(GROUP)
-    outer_count = lax.axis_size("outer")
     device_pos = lax.axis_index(ALL)
     base_row = device_pos * rows_dev
     reach_dev = WINDOW // rows_dev
@@ -70,10 +77,14 @@
     running_inner = jnp.cumsum(owned, axis=0)
     inner_before = running_inner - owned
     group_total = running_inner[-1]
-    running = group_total
-    for level in range((outer_count - 1).bit_length()):
-        running = running + passed_along(running, "outer", 1 << level)
-    groups_before = running - group_total
+    along_z = lax.all_gather(group_total, "z")
+    z_before = jnp.arange(along_z.shape[0]) < lax.axis_index("z")
+    line_before = jnp.sum(jnp.where(z_before[:, None, None, None], along_z, 0.0), axis=0)
+    along_y = lax.all_gather(jnp.sum(along_z, axis=0), "y")
+    y_before = jnp.arange(along_y.shape[0]) < lax.axis_index("y")
+    groups_before = line_before + jnp.sum(
+        jnp.where(y_before[:, None, None, None], along_y, 0.0), axis=0
+    )
     slots = inner_before + groups_before[None]
     prefix = lax.all_to_all(slots, GROUP, split_axis=0, concat_axis=1, tiled=True)[0]
 
@@ -122,8 +133,10 @@
 def solution(mesh):
     seq_count = mesh.shape["seq"]
     sub_count = mesh.shape["sub"]
+    lines = seq_count // CORES
+    z_count = math.isqrt(lines)
     split_mesh = Mesh(
-        np.asarray(mesh.devices).reshape(seq_count // CORES, CORES, sub_count), ALL
+        np.asarray(mesh.devices).reshape(lines // z_count, z_count, CORES, sub_count), ALL
     )
     rows = P(ALL, None)
     in_specs = (rows, rows, rows, P(), rows, rows, rows)

time: 230 us -> 229 us (level)
  the two profiles are of different devices: /device:TPU:1 before, /device:TPU:34 now
where the time goes in v2:
time: 229 us; the launch traced here: 227 us
  waiting for transfers between devices  59.8 us (26%)
  local copies, waits for them, and re-layouts  53.6 us (23%)
  starting transfers between devices  47.1 us (21%)
  blocking collectives  21.1 us (9%)
  matrix products  18.4 us (8%)
  between operations  14.5 us (6%)
  other arithmetic  12.4 us (5%)
    all_gather x1, waiting for transfers between devices, shards(): along_z = lax.all_gather(group_total, 'z')  48.4 us
    ppermute x8, starting transfers between devices, passed_along(): return lax.ppermute(shard, axis, pairs)  42.5 us
    all_to_all x1, blocking collectives, shards(): lax.all_to_all(local_state[None], GROUP, split_axis=1, concat_axis=0, til...  21.1 us
    ppermute x8, local copies, waits for them, and re-layouts, passed_along(): return lax.ppermute(shard, axis, pairs)  19.1 us
    ppermute x8, waiting for transfers between devices, passed_along(): return lax.ppermute(shard, axis, pairs)  11.3 us
    concatenate x1, local copies, waits for them, and re-layouts, shards(): earlier = jnp.concatenate(earlier, axis=1)  10.8 us
    dot_general x4, matrix products, sym_features(): jnp.einsum('jhi,if->jhf', ext, jnp.asarray(table), precision=lax.Precisio...  6.6 us
    concatenate x2, local copies, waits for them, and re-layouts, shards(): jnp.concatenate([earlier[0], window_key], axis=0)  4.69 us
  transfers between devices with their start and end apart: 11, of which 2 were waited for; matrix products, arithmetic and copies ran while one was open for 29% of the time, Pallas kernels for 0%

profile of v2, /device:TPU:34, one launch (start us, length us, event | category | flops | bytes accessed | tf_op | source)
XLA Modules:
  0.0 226.8 jit_solution(168994058732046036)
XLA Ops:
  14.5 21.1 %all_to_all.21 = f32[1,16,153,128]{3,0,2,1:T(1,128)S(1)} all-to-all(f32[1,16,153,128]{3,0,2,1:T(1,128)S(1)} %copy.84), channel_id=1, replica_groups=mesh['y'=8,'z'=8,'core'=2,'sub'=4] {'core','sub'}, dimensions={1} | all-to-all | bytes 2506752 | tf_op jit(solution)/shard_map/all_to_all | solution.py:76
  39.7 4.3 %collective-permute-start = (bf16[2,64,2048]{2,1,0:T(8,128)(2,1)}, bf16[2,64,2048]{2,1,0:T(8,128)(2,1)}, u32[]{:S(2)}, u32[]{:S(2)}) collective-permute-start(bf16[2,64,2048]{2,1,0:T(8,128)(2,1)} %pad_maximum_fusion), channel_id=1, source_target_pairs={{0,8},{1,9},{2,10},{3,11},{4,12},{5,13},{6,14},{7,15},{8,16},{9,17... | collective-permute-start | bytes 1572872 | tf_op jit(solution)/shard_map/ppermute | solution.py:33
  44.0 5.7 %collective-permute-start.1 = (bf16[2,64,2048]{2,1,0:T(8,128)(2,1)}, bf16[2,64,2048]{2,1,0:T(8,128)(2,1)}, u32[]{:S(2)}, u32[]{:S(2)}) collective-permute-start(bf16[2,64,2048]{2,1,0:T(8,128)(2,1)} %pad_maximum_fusion), channel_id=1, source_target_pairs={{0,7},{1,8},{2,9},{3,10},{4,11},{5,12},{6,13},{7,14},{8,15},{9,16}... | collective-permute-start | bytes 1572872 | tf_op jit(solution)/shard_map/ppermute | solution.py:33
  49.7 2.6 %collective-permute-start.2 = (bf16[2,64,2048]{2,1,0:T(8,128)(2,1)}, bf16[2,64,2048]{2,1,0:T(8,128)(2,1)}, u32[]{:S(2)}, u32[]{:S(2)}) collective-permute-start(bf16[2,64,2048]{2,1,0:T(8,128)(2,1)} %pad_maximum_fusion), channel_id=1, source_target_pairs={{0,6},{1,7},{2,8},{3,9},{4,10},{5,11},{6,12},{7,13},{8,14},{9,15},... | collective-permute-start | bytes 1572872 | tf_op jit(solution)/shard_map/ppermute | solution.py:33
  52.3 6.1 %collective-permute-start.3 = (bf16[2,64,2048]{2,1,0:T(8,128)(2,1)}, bf16[2,64,2048]{2,1,0:T(8,128)(2,1)}, u32[]{:S(2)}, u32[]{:S(2)}) collective-permute-start(bf16[2,64,2048]{2,1,0:T(8,128)(2,1)} %pad_maximum_fusion), channel_id=1, source_target_pairs={{0,5},{1,6},{2,7},{3,8},{4,9},{5,10},{6,11},{7,12},{8,13},{9,14},{... | collective-permute-start | bytes 1572872 | tf_op jit(solution)/shard_map/ppermute | solution.py:33
  61.2 48.4 %all-gather.4.cloned.1.call-done = f32[8,2,153,128]{3,1,2,0:T(2,128)} async-done(((f32[1,2,153,128]{3,1,2,0:T(2,128)}), f32[8,2,153,128]{3,1,2,0:T(2,128)}) %all-gather.4.cloned.1.call-update) | async-done | bytes 1253392 | tf_op jit(solution)/shard_map/all_gather | solution.py:80
  109.7 2.4 %reduce_sum.46 = f32[2,153,128]{2,0,1:T(2,128)} reduce(f32[8,2,153,128]{3,1,2,0:T(2,128)} %all-gather.4.cloned.1.call-done, f32[]{:T(128)} %constant.16.clone.1), dimensions={0}, to_apply=%region_2.3 | reduce | flops 274176 | bytes 1410052 | tf_op jit(solution)/shard_map/reduce_sum | solution.py:83
  123.5 18.2 %collective-permute-start.6 = (bf16[2,64,2048]{2,1,0:T(8,128)(2,1)}, bf16[2,64,2048]{2,1,0:T(8,128)(2,1)}, u32[]{:S(2)}, u32[]{:S(2)}) collective-permute-start(bf16[2,64,2048]{2,1,0:T(8,128)(2,1)} %pad_maximum_fusion), channel_id=1, source_target_pairs={{0,2},{1,3},{2,4},{3,5},{4,6},{5,7},{6,8},{7,9},{8,10},{9,11},{10,... | collective-permute-start | bytes 1572872 | tf_op jit(solution)/shard_map/ppermute | solution.py:33
  144.7 2.4 %copy.100 = bf16[2,64,2048]{1,2,0:T(8,128)(2,1)} copy(bf16[2,64,2048]{2,1,0:T(8,128)(2,1)} %collective-permute-done.7) | data formatting | bytes 1048576 | tf_op jit(solution)/shard_map/ppermute | solution.py:33
  147.1 2.5 %copy.93 = bf16[2,64,2048]{1,2,0:T(8,128)(2,1)} copy(bf16[2,64,2048]{2,1,0:T(8,128)(2,1)} %collective-permute-done) | data formatting | bytes 1048576 | tf_op jit(solution)/shard_map/ppermute | solution.py:33
  149.5 2.4 %copy.94 = bf16[2,64,2048]{1,2,0:T(8,128)(2,1)} copy(bf16[2,64,2048]{2,1,0:T(8,128)(2,1)} %collective-permute-done.1) | data formatting | bytes 1048576 | tf_op jit(solution)/shard_map/ppermute | solution.py:33
  151.9 2.4 %copy.95 = bf16[2,64,2048]{1,2,0:T(8,128)(2,1)} copy(bf16[2,64,2048]{2,1,0:T(8,128)(2,1)} %collective-permute-done.2) | data formatting | bytes 1048576 | tf_op jit(solution)/shard_map/ppermute | solution.py:33
  154.3 2.4 %copy.96 = bf16[2,64,2048]{1,2,0:T(8,128)(2,1)} copy(bf16[2,64,2048]{2,1,0:T(8,128)(2,1)} %collective-permute-done.3) | data formatting | bytes 1048576 | tf_op jit(solution)/shard_map/ppermute | solution.py:33
  156.7 2.4 %copy.97 = bf16[2,64,2048]{1,2,0:T(8,128)(2,1)} copy(bf16[2,64,2048]{2,1,0:T(8,128)(2,1)} %collective-permute-done.4) | data formatting | bytes 1048576 | tf_op jit(solution)/shard_map/ppermute | solution.py:33
  159.1 2.4 %copy.98 = bf16[2,64,2048]{1,2,0:T(8,128)(2,1)} copy(bf16[2,64,2048]{2,1,0:T(8,128)(2,1)} %collective-permute-done.5) | data formatting | bytes 1048576 | tf_op jit(solution)/shard_map/ppermute | solution.py:33
  161.5 11.3 %collective-permute-done.6 = bf16[2,64,2048]{2,1,0:T(8,128)(2,1)} collective-permute-done((bf16[2,64,2048]{2,1,0:T(8,128)(2,1)}, bf16[2,64,2048]{2,1,0:T(8,128)(2,1)}, u32[]{:S(2)}, u32[]{:S(2)}) %collective-permute-start.6) | collective-permute-done | bytes 524320 | tf_op jit(solution)/shard_map/ppermute | solution.py:33
  172.7 2.4 %copy.99 = bf16[2,64,2048]{1,2,0:T(8,128)(2,1)} copy(bf16[2,64,2048]{2,1,0:T(8,128)(2,1)} %collective-permute-done.6) | data formatting | bytes 1048576 | tf_op jit(solution)/shard_map/ppermute | solution.py:33
  175.1 10.8 %concatenate.27 = bf16[2,512,2048]{1,2,0:T(8,128)(2,1)} concatenate(bf16[2,64,2048]{1,2,0:T(8,128)(2,1)} %copy.93, bf16[2,64,2048]{1,2,0:T(8,128)(2,1)} %copy.94, bf16[2,64,2048]{1,2,0:T(8,128)(2,1)} %copy.95, bf16[2,64,2048]{1,2,0:T(8,128)(2,1)} %copy.96, bf16[2,64,2048]{1,2,0:T(8,128)(2,1)} %copy.97, bf16[2,64,2048]{1,2,0:T(8,128)(2,1)} %copy.98, bf16[2,64,2048]{1,2,0:T(8,128)(2,1)} %copy.99, ...), dimensions={1} | concatenate | bytes 8388608 | tf_op jit(solution)/shard_map/concatenate | solution.py:61
  194.0 4.4 %all-to-all-start.1 = ((f32[8,2,153,128]{3,1,2,0:T(2,128)}), f32[8,2,153,128]{3,1,2,0:T(2,128)}, u32[]{:S(2)}, u32[]{:S(2)}) async-start(f32[8,2,153,128]{3,1,2,0:T(2,128)} %copy.90), calls=%async_computation.1 | async-start | bytes 2506752 | tf_op jit(solution)/shard_map/all_to_all | solution.py:89
  198.5 3.9 %fusion.71 = (bf16[1,512,2048]{1,2,0:T(8,128)(2,1)}, bf16[1,512,2048]{1,2,0:T(8,128)(2,1)S(1)}) fusion(bf16[2,512,2048]{1,2,0:T(8,128)(2,1)} %concatenate.27), kind=kLoop, calls=%fused_computation.84 | loop fusion | bytes 8388608 | tf_op jit(solution)/shard_map/slice | solution.py:62
  202.3 3.9 %copy.103 = bf16[512,16,128]{2,0,1:T(8,128)(2,1)} copy(bf16[512,16,128]{0,2,1:T(8,128)(2,1)} %bitcast.92) | data formatting | bytes 4194304 | tf_op jit(solution)/shard_map/concatenate | solution.py:62
  206.3 2.4 %copy.101 = bf16[512,16,128]{2,0,1:T(8,128)(2,1)} copy(bf16[512,16,128]{0,2,1:T(8,128)(2,1)S(1)} %bitcast.91) | data formatting | bytes 4194304 | tf_op jit(solution)/shard_map/concatenate | solution.py:63
  208.7 4.4 %fusion.72 = (f32[16,64]{1,0:T(8,128)S(1)}, f32[16,64,576]{2,1,0:T(8,128)}) fusion(pred[64,576]{1,0:T(8,128)(4,1)S(1)} %copy-done.10, bf16[64,16,128]{2,0,1:T(8,128)(2,1)S(1)} %copy-done.8, bf16[512,16,128]{2,0,1:T(8,128)(2,1)} %copy.103, bf16[64,2048]{1,0:T(8,128)(2,1)S(1)} %copy-done), kind=kOutput, calls=%fused_computation.85 | convolution fusion | flops 158073408 | bytes 5021696 | tf_op jit(solution)/shard_map/sub | solution.py:106
  213.1 2.4 %fusion.18 = bf16[16,8,8,128]{3,2,1,0:T(8,128)(2,1)S(1)} fusion(bf16[64,16,128]{2,0,1:T(8,128)(2,1)S(1)} %copy-done.7, bf16[512,16,128]{2,0,1:T(8,128)(2,1)S(1)} %copy-done.2, f32[16,64,576]{2,1,0:T(8,128)} %get-tuple-element.7, f32[16,64]{1,0:T(8,128)S(1)} %get-tuple-element.6), kind=kOutput, calls=%fused_computation.27 | convolution fusion | flops 157024256 | bytes 4984832 | tf_op jit(solution)/shard_map/hij,jhd->ihd/dot_general | solution.py:108
  (83 shorter events, 41.1 us)
Async XLA Ops:
  7.2 201.5 %copy-start = (bf16[64,2048]{1,0:T(8,128)(2,1)S(1)}, bf16[64,2048]{1,0:T(8,128)(2,1)}, u32[]{:S(2)}) copy-start(bf16[64,2048]{1,0:T(8,128)(2,1)} %param.15) | copy-start | bytes 786436
  7.2 4.6 %copy-start.3 = (bf16[64,2048]{1,0:T(8,128)(2,1)S(1)}, bf16[64,2048]{1,0:T(8,128)(2,1)}, u32[]{:S(2)}) copy-start(bf16[64,2048]{1,0:T(8,128)(2,1)} %param.13) | copy-start | bytes 786436
  7.2 102.5 %all-gather.4.cloned.1.call-start = ((), (), s32[]{:S(2)}) async-start(), calls=%async_computation.2 | async-start | bytes 1410048 | tf_op jit(solution)/shard_map/all_gather | solution.py:80
  8.2 5.0 %copy-start.6 = (bf16[64,256]{0,1:T(8,128)(2,1)}, bf16[64,256]{0,1:T(8,128)(2,1)S(1)}, u32[]{:S(2)}) copy-start(bf16[64,256]{0,1:T(8,128)(2,1)S(1)} %copy.81) | copy-start | bytes 98308
  36.9 151.4 %all-gather.6.cloned.1.call-start = ((), (), s32[]{:S(2)}) async-start(), calls=%async_computation.3 | async-start | bytes 1474560 | tf_op jit(solution)/shard_map/all_gather | solution.py:83
  37.8 81.8 %collective-permute-start.7 = (bf16[2,64,2048]{2,1,0:T(8,128)(2,1)}, bf16[2,64,2048]{2,1,0:T(8,128)(2,1)}, u32[]{:S(2)}, u32[]{:S(2)}) collective-permute-start(bf16[2,64,2048]{2,1,0:T(8,128)(2,1)} %pad_maximum_fusion), channel_id=1, source_target_pairs={{0,1},{1,2},{2,3},{3,4},{4,5},{5,6},{6,7},{7,8},{8,9},{9,10},{10,1... | collective-permute-start | bytes 1572872 | tf_op jit(solution)/shard_map/ppermute | solution.py:33
  39.7 81.8 %collective-permute-start = (bf16[2,64,2048]{2,1,0:T(8,128)(2,1)}, bf16[2,64,2048]{2,1,0:T(8,128)(2,1)}, u32[]{:S(2)}, u32[]{:S(2)}) collective-permute-start(bf16[2,64,2048]{2,1,0:T(8,128)(2,1)} %pad_maximum_fusion), channel_id=1, source_target_pairs={{0,8},{1,9},{2,10},{3,11},{4,12},{5,13},{6,14},{7,15},{8,16},{9,17... | collective-permute-start | bytes 1572872 | tf_op jit(solution)/shard_map/ppermute | solution.py:33
  44.0 79.4 %collective-permute-start.1 = (bf16[2,64,2048]{2,1,0:T(8,128)(2,1)}, bf16[2,64,2048]{2,1,0:T(8,128)(2,1)}, u32[]{:S(2)}, u32[]{:S(2)}) collective-permute-start(bf16[2,64,2048]{2,1,0:T(8,128)(2,1)} %pad_maximum_fusion), channel_id=1, source_target_pairs={{0,7},{1,8},{2,9},{3,10},{4,11},{5,12},{6,13},{7,14},{8,15},{9,16}... | collective-permute-start | bytes 1572872 | tf_op jit(solution)/shard_map/ppermute | solution.py:33
  49.7 102.1 %collective-permute-start.2 = (bf16[2,64,2048]{2,1,0:T(8,128)(2,1)}, bf16[2,64,2048]{2,1,0:T(8,128)(2,1)}, u32[]{:S(2)}, u32[]{:S(2)}) collective-permute-start(bf16[2,64,2048]{2,1,0:T(8,128)(2,1)} %pad_maximum_fusion), channel_id=1, source_target_pairs={{0,6},{1,7},{2,8},{3,9},{4,10},{5,11},{6,12},{7,13},{8,14},{9,15},... | collective-permute-start | bytes 1572872 | tf_op jit(solution)/shard_map/ppermute | solution.py:33
  52.3 101.9 %collective-permute-start.3 = (bf16[2,64,2048]{2,1,0:T(8,128)(2,1)}, bf16[2,64,2048]{2,1,0:T(8,128)(2,1)}, u32[]{:S(2)}, u32[]{:S(2)}) collective-permute-start(bf16[2,64,2048]{2,1,0:T(8,128)(2,1)} %pad_maximum_fusion), channel_id=1, source_target_pairs={{0,5},{1,6},{2,7},{3,8},{4,9},{5,10},{6,11},{7,12},{8,13},{9,14},{... | collective-permute-start | bytes 1572872 | tf_op jit(solution)/shard_map/ppermute | solution.py:33
  113.7 27.9 %copy-start.11 = (f32[17,153,1]{1,0,2:T(8,128)S(1)}, f32[17,153,1]{1,0,2:T(8,128)}, u32[]{:S(2)}) copy-start(f32[17,153,1]{1,0,2:T(8,128)} %constant.77) | copy-start | bytes 31216
  115.1 27.5 %copy-start.9 = (f32[17,153,1]{1,0,2:T(8,128)S(1)}, f32[17,153,1]{1,0,2:T(8,128)}, u32[]{:S(2)}) copy-start(f32[17,153,1]{1,0,2:T(8,128)} %constant.76) | copy-start | bytes 31216
  119.6 37.1 %collective-permute-start.4 = (bf16[2,64,2048]{2,1,0:T(8,128)(2,1)}, bf16[2,64,2048]{2,1,0:T(8,128)(2,1)}, u32[]{:S(2)}, u32[]{:S(2)}) collective-permute-start(bf16[2,64,2048]{2,1,0:T(8,128)(2,1)} %pad_maximum_fusion), channel_id=1, source_target_pairs={{0,4},{1,5},{2,6},{3,7},{4,8},{5,9},{6,10},{7,11},{8,12},{9,13},{1... | collective-permute-start | bytes 1572872 | tf_op jit(solution)/shard_map/ppermute | solution.py:33
  121.5 37.5 %collective-permute-start.5 = (bf16[2,64,2048]{2,1,0:T(8,128)(2,1)}, bf16[2,64,2048]{2,1,0:T(8,128)(2,1)}, u32[]{:S(2)}, u32[]{:S(2)}) collective-permute-start(bf16[2,64,2048]{2,1,0:T(8,128)(2,1)} %pad_maximum_fusion), channel_id=1, source_target_pairs={{0,3},{1,4},{2,5},{3,6},{4,7},{5,8},{6,9},{7,10},{8,11},{9,12},{10... | collective-permute-start | bytes 1572872 | tf_op jit(solution)/shard_map/ppermute | solution.py:33
  123.5 49.3 %collective-permute-start.6 = (bf16[2,64,2048]{2,1,0:T(8,128)(2,1)}, bf16[2,64,2048]{2,1,0:T(8,128)(2,1)}, u32[]{:S(2)}, u32[]{:S(2)}) collective-permute-start(bf16[2,64,2048]{2,1,0:T(8,128)(2,1)} %pad_maximum_fusion), channel_id=1, source_target_pairs={{0,2},{1,3},{2,4},{3,5},{4,6},{5,7},{6,8},{7,9},{8,10},{9,11},{10,... | collective-permute-start | bytes 1572872 | tf_op jit(solution)/shard_map/ppermute | solution.py:33
  175.1 10.8 %copy-start.14 = (pred[8]{0:T(512)(128)(4,1)S(1)}, pred[8]{0:T(512)(128)(4,1)}, u32[]{:S(2)}) copy-start(pred[8]{0:T(512)(128)(4,1)} %iota_compare_fusion.2) | copy-start | bytes 28
  185.9 4.4 %copy-start.13 = (pred[8]{0:T(512)(128)(4,1)S(1)}, pred[8]{0:T(512)(128)(4,1)}, u32[]{:S(2)}) copy-start(pred[8]{0:T(512)(128)(4,1)} %iota_compare_fusion.1) | copy-start | bytes 28
  194.0 22.2 %all-to-all-start.1 = ((f32[8,2,153,128]{3,1,2,0:T(2,128)}), f32[8,2,153,128]{3,1,2,0:T(2,128)}, u32[]{:S(2)}, u32[]{:S(2)}) async-start(f32[8,2,153,128]{3,1,2,0:T(2,128)} %copy.90), calls=%async_computation.1 | async-start | bytes 2506752 | tf_op jit(solution)/shard_map/all_to_all | solution.py:89
  206.3 2.4 %copy-start.8 = (bf16[64,16,128]{2,0,1:T(8,128)(2,1)S(1)}, bf16[64,16,128]{2,0,1:T(8,128)(2,1)}, u32[]{:S(2)}) copy-start(bf16[64,16,128]{2,0,1:T(8,128)(2,1)} %copy_bitcast_fusion.3) | copy-start | bytes 786436
  206.3 2.4 %copy-start.10 = (pred[64,576]{1,0:T(8,128)(4,1)S(1)}, pred[64,576]{1,0:T(8,128)(4,1)}, u32[]{:S(2)}) copy-start(pred[64,576]{1,0:T(8,128)(4,1)} %and_and_fusion) | copy-start | bytes 110596
  208.7 4.4 %copy-start.2 = (bf16[512,16,128]{2,0,1:T(8,128)(2,1)S(1)}, bf16[512,16,128]{2,0,1:T(8,128)(2,1)}, u32[]{:S(2)}) copy-start(bf16[512,16,128]{2,0,1:T(8,128)(2,1)} %copy.101) | copy-start | bytes 6291460
  208.7 4.4 %copy-start.7 = (bf16[64,16,128]{2,0,1:T(8,128)(2,1)S(1)}, bf16[64,16,128]{2,0,1:T(8,128)(2,1)}, u32[]{:S(2)}) copy-start(bf16[64,16,128]{2,0,1:T(8,128)(2,1)} %copy_bitcast_fusion.2) | copy-start | bytes 786436
  215.4 2.2 copy-start.1
  217.6 1.5 copy-start.12
  (2 other events, 2.5 us)
Sparse Core Ops, SparseCore 0:
  37.0 72.6 all-gather.3
  113.8 50.0 all-gather.5

commit v3 on v2

v3 whole, which is shorter than its diff:
```python
import math

import jax
import jax.numpy as jnp
import numpy as np
from jax import lax
from jax.sharding import Mesh
from jax.sharding import PartitionSpec as P

FDIM = 16
VDIM = 128
SDIM = 128
WINDOW = 512
CORES = 2
FEAT_PAD = 160
ALL = ("y", "z", "core", "sub")
GROUP = ("core", "sub")


def pair_tables(for_query):
    pairs = [(0, 0)] + [(0, a + 1) for a in range(FDIM)]
    pairs += [(a + 1, b + 1) for a in range(FDIM) for b in range(a, FDIM)]
    first = np.zeros((FDIM + 1, FEAT_PAD), np.float32)
    second = np.zeros((FDIM + 1, FEAT_PAD), np.float32)
    for f, (a, b) in enumerate(pairs):
        first[a, f] = 0.5 if (for_query and a == b and a > 0) else 1.0
        second[b, f] = 1.0
    return first, second


def passed_along(shard, axis, by):
    size = lax.axis_size(axis)
    pairs = [(i, i + by) for i in range(size) if 0 <= i + by < size]
    return lax.ppermute(shard, axis, pairs)


def sym_features(vectors, for_query):
    halved = vectors * 0.5
    ext = jnp.concatenate([jnp.ones(halved.shape[:-1] + (1,), jnp.float32), halved], axis=-1)
    first, second = pair_tables(for_query)
    pick = lambda table: jnp.einsum(
        "jhi,if->jhf", ext, jnp.asarray(table), precision=lax.Precision.HIGHEST
    )
    return pick(first) * pick(second)


def groups_before(total):
    z_count = lax.axis_size("z")
    heads, feats, width = total.shape
    dealt = total.reshape(heads, z_count, feats // z_count, width)
    held = lax.all_to_all(dealt, "z", split_axis=1, concat_axis=1, tiled=True)
    running = jnp.cumsum(held, axis=1)
    line_total = running[:, -1]
    along_y = lax.all_gather(line_total, "y")
    y_before = jnp.arange(along_y.shape[0]) < lax.axis_index("y")
    lines_before = jnp.sum(jnp.where(y_before[:, None, None, None], along_y, 0.0), axis=0)
    prefix = running - held + lines_before[:, None]
    back = lax.all_to_all(prefix, "z", split_axis=1, concat_axis=1, tiled=True)
    return back.reshape(heads, feats, width)


def linear_heads(linear_query, linear_key, linear_value, lin_gain):
    rows_dev = linear_query.shape[0]
    group_count = lax.axis_size(GROUP)
    lin_heads = linear_query.shape[1] // FDIM
    own_heads = lin_heads // group_count
    packed = jnp.concatenate(
        [
            linear_query.reshape(rows_dev, group_count, own_heads * FDIM),
            linear_key.reshape(rows_dev, group_count, own_heads * FDIM),
            linear_value.reshape(rows_dev, group_count, own_heads * VDIM),
        ],
        axis=-1,
    )
    got = lax.all_to_all(packed, GROUP, split_axis=1, concat_axis=0, tiled=True)
    rows = got.shape[0]
    got = got.reshape(rows, -1)
    query_bf = got[:, : own_heads * FDIM].reshape(rows, own_heads, FDIM)
    key_bf = got[:, own_heads * FDIM : 2 * own_heads * FDIM].reshape(rows, own_heads, FDIM)
    value_lin = got[:, 2 * own_heads * FDIM :].reshape(rows, own_heads, VDIM).astype(jnp.float32)
    query_lin = query_bf.astype(jnp.float32)
    key_lin = key_bf.astype(jnp.float32)
    total = jnp.einsum(
        "jhf,jhe->hfe", sym_features(key_lin, False), value_lin, precision=lax.Precision.HIGHEST
    )
    before = groups_before(total)
    from_state = jnp.einsum(
        "ihf,hfe->ihe", sym_features(query_lin, True), before, precision=lax.Precision.HIGHEST
    )
    dot_inner = (
        jnp.einsum("ihd,jhd->hij", query_bf, key_bf, preferred_element_type=jnp.float32) * 0.25
    )
    weight = 1.0 + dot_inner + 0.5 * dot_inner * dot_inner
    causal = jnp.arange(rows, dtype=jnp.int32)[:, None] >= jnp.arange(rows, dtype=jnp.int32)[None, :]
    weight = jnp.where(causal[None], weight, jnp.float32(0.0))
    local_sum = jnp.einsum("hij,jhe->ihe", weight, value_lin, precision=lax.Precision.HIGHEST)
    numerator = local_sum + from_state
    inv_rms = lax.rsqrt(jnp.mean(numerator * numerator, axis=-1, keepdims=True) + 1e-05)
    gain_rows = lax.dynamic_slice_in_dim(
        lin_gain.reshape(lin_heads, VDIM), lax.axis_index(GROUP) * own_heads, own_heads, 0
    )
    out = (numerator * inv_rms * gain_rows).astype(jnp.bfloat16)
    out = out.reshape(group_count, rows_dev, own_heads * VDIM)
    back = lax.all_to_all(out, GROUP, split_axis=0, concat_axis=2, tiled=True)
    return back.reshape(rows_dev, lin_heads * VDIM)


def shards(
    linear_query, linear_key, linear_value, lin_gain, window_query, window_key, window_value
):
    rows_dev = linear_query.shape[0]
    dev_count = lax.axis_size(ALL)
    group_count = lax.axis_size(GROUP)
    device_pos = lax.axis_index(ALL)
    base_row = device_pos * rows_dev
    reach_dev = WINDOW // rows_dev
    channels = window_key.shape[1]
    head_count = channels // SDIM
    lin_heads = linear_query.shape[1] // FDIM

    stacked = jnp.stack([window_key, window_value])
    earlier = [passed_along(stacked, ALL, reach_dev - t) for t in range(reach_dev)]
    earlier = jnp.concatenate(earlier, axis=1)
    key_rows = jnp.concatenate([earlier[0], window_key], axis=0).reshape(-1, head_count, SDIM)
    value_rows = jnp.concatenate([earlier[1], window_value], axis=0).reshape(-1, head_count, SDIM)

    query_heads = window_query.reshape(rows_dev, head_count, SDIM)
    scores = jnp.einsum(
        "ihd,jhd->hij", query_heads, key_rows, preferred_element_type=jnp.float32
    ) * (1.0 / math.sqrt(SDIM))
    query_pos = base_row + jnp.arange(rows_dev, dtype=jnp.int32)
    key_pos = (
        base_row - reach_dev * rows_dev + jnp.arange((reach_dev + 1) * rows_dev, dtype=jnp.int32)
    )
    allowed = (
        (key_pos[None, :] <= query_pos[:, None])
        & (key_pos[None, :] > query_pos[:, None] - WINDOW)
        & (key_pos[None, :] >= 0)
    )
    scores = jnp.where(allowed[None], scores, jnp.float32(-1e30))
    row_max = jnp.max(scores, axis=-1, keepdims=True)
    exp_scores = jnp.exp(scores - row_max)
    weights_bf = (exp_scores / jnp.sum(exp_scores, axis=-1, keepdims=True)).astype(jnp.bfloat16)
    mixed = jnp.einsum("hij,jhd->ihd", weights_bf, value_rows, preferred_element_type=jnp.float32)
    window_out = mixed.reshape(rows_dev, channels).astype(jnp.bfloat16)

    linear_out = linear_heads(linear_query, linear_key, linear_value, lin_gain)
    return (linear_out, window_out)


def solution(mesh):
    seq_count = mesh.shape["seq"]
    sub_count = mesh.shape["sub"]
    lines = seq_count // CORES
    z_count = math.isqrt(lines)
    split_mesh = Mesh(
        np.asarray(mesh.devices).reshape(lines // z_count, z_count, CORES, sub_count), ALL
    )
    rows = P(ALL, None)
    in_specs = (rows, rows, rows, P(), rows, rows, rows)
    out_specs = (rows, rows)
    return jax.shard_map(
        shards, mesh=split_mesh, in_specs=in_specs, out_specs=out_specs, check_vma=False
    )
```

time: 229 us -> 189 us (0.83)
  the two profiles are of different devices: /device:TPU:34 before, /device:TPU:1 now
where the time goes in v3:
time: 189 us; the launch traced here: 187 us
  starting transfers between devices  81.4 us (43%)
  local copies, waits for them, and re-layouts  44.6 us (24%)
  blocking collectives  22 us (12%)
  waiting for transfers between devices  16.7 us (9%)
  matrix products  15.7 us (8%)
  other arithmetic  6.05 us (3%)
    ppermute x8, starting transfers between devices, passed_along(): return lax.ppermute(shard, axis, pairs)  33.6 us
    all_to_all x1, starting transfers between devices, groups_before(): held = lax.all_to_all(dealt, 'z', split_axis=1, concat_axis=1, tiled=True)  25.6 us
    all_gather x1, blocking collectives, groups_before(): along_y = lax.all_gather(line_total, 'y')  22 us
    ppermute x8, local copies, waits for them, and re-layouts, passed_along(): return lax.ppermute(shard, axis, pairs)  14.5 us
    all_to_all x1, starting transfers between devices, linear_heads(): back = lax.all_to_all(out, GROUP, split_axis=0, concat_axis=2, tiled=True)  10.9 us
    concatenate x1, local copies, waits for them, and re-layouts, shards(): earlier = jnp.concatenate(earlier, axis=1)  10.8 us
    all_to_all x1, starting transfers between devices, groups_before(): back = lax.all_to_all(prefix, 'z', split_axis=1, concat_axis=1, tiled=True)  6.74 us
    all_to_all x1, waiting for transfers between devices, linear_heads(): got = lax.all_to_all(packed, GROUP, split_axis=1, concat_axis=0, tiled=True)  5.46 us
  transfers between devices with their start and end apart: 12, of which 4 were waited for; matrix products, arithmetic and copies ran while one was open for 31% of the time, Pallas kernels for 0%

profile of v3, /device:TPU:1, one launch (start us, length us, event | category | flops | bytes accessed | tf_op | source)
XLA Modules:
  0.0 187.4 jit_solution(14541325597579867296)
XLA Ops:
  2.7 4.8 %collective-permute-start = (bf16[2,64,2048]{2,1,0:T(8,128)(2,1)}, bf16[2,64,2048]{2,1,0:T(8,128)(2,1)S(1)}, u32[]{:S(2)}, u32[]{:S(2)}) collective-permute-start(bf16[2,64,2048]{2,1,0:T(8,128)(2,1)} %pad_maximum_fusion), channel_id=1, source_target_pairs={{0,8},{1,9},{2,10},{3,11},{4,12},{5,13},{6,14},{7,15},{8,16},{9,17... | collective-permute-start | bytes 1572872 | tf_op jit(solution)/shard_map/ppermute | solution.py:34
  7.5 7.0 %collective-permute-start.1 = (bf16[2,64,2048]{2,1,0:T(8,128)(2,1)}, bf16[2,64,2048]{2,1,0:T(8,128)(2,1)S(1)}, u32[]{:S(2)}, u32[]{:S(2)}) collective-permute-start(bf16[2,64,2048]{2,1,0:T(8,128)(2,1)} %pad_maximum_fusion), channel_id=1, source_target_pairs={{0,7},{1,8},{2,9},{3,10},{4,11},{5,12},{6,13},{7,14},{8,15},{9,16}... | collective-permute-start | bytes 1572872 | tf_op jit(solution)/shard_map/ppermute | solution.py:34
  14.6 4.5 %collective-permute-start.2 = (bf16[2,64,2048]{2,1,0:T(8,128)(2,1)}, bf16[2,64,2048]{2,1,0:T(8,128)(2,1)S(1)}, u32[]{:S(2)}, u32[]{:S(2)}) collective-permute-start(bf16[2,64,2048]{2,1,0:T(8,128)(2,1)} %pad_maximum_fusion), channel_id=1, source_target_pairs={{0,6},{1,7},{2,8},{3,9},{4,10},{5,11},{6,12},{7,13},{8,14},{9,15},... | collective-permute-start | bytes 1572872 | tf_op jit(solution)/shard_map/ppermute | solution.py:34
  19.1 2.5 %collective-permute-start.3 = (bf16[2,64,2048]{2,1,0:T(8,128)(2,1)}, bf16[2,64,2048]{2,1,0:T(8,128)(2,1)}, u32[]{:S(2)}, u32[]{:S(2)}) collective-permute-start(bf16[2,64,2048]{2,1,0:T(8,128)(2,1)} %pad_maximum_fusion), channel_id=1, source_target_pairs={{0,5},{1,6},{2,7},{3,8},{4,9},{5,10},{6,11},{7,12},{8,13},{9,14},{... | collective-permute-start | bytes 1572872 | tf_op jit(solution)/shard_map/ppermute | solution.py:34
  21.6 5.5 %collective-permute-start.4 = (bf16[2,64,2048]{2,1,0:T(8,128)(2,1)}, bf16[2,64,2048]{2,1,0:T(8,128)(2,1)}, u32[]{:S(2)}, u32[]{:S(2)}) collective-permute-start(bf16[2,64,2048]{2,1,0:T(8,128)(2,1)} %pad_maximum_fusion), channel_id=1, source_target_pairs={{0,4},{1,5},{2,6},{3,7},{4,8},{5,9},{6,10},{7,11},{8,12},{9,13},{1... | collective-permute-start | bytes 1572872 | tf_op jit(solution)/shard_map/ppermute | solution.py:34
  31.1 4.5 %all-to-all-start = ((bf16[64,8,320]{2,0,1:T(8,128)(2,1)}), bf16[64,8,320]{2,0,1:T(8,128)(2,1)S(1)}, u32[]{:S(2)}, u32[]{:S(2)}) async-start(bf16[64,8,320]{2,0,1:T(8,128)(2,1)} %pad_maximum_fusion.1), calls=%async_computation | async-start | bytes 786432 | tf_op jit(solution)/shard_map/all_to_all | solution.py:75
  38.1 5.5 %all-to-all-done = bf16[64,8,320]{2,0,1:T(8,128)(2,1)S(1)} async-done(((bf16[64,8,320]{2,0,1:T(8,128)(2,1)}), bf16[64,8,320]{2,0,1:T(8,128)(2,1)S(1)}, u32[]{:S(2)}, u32[]{:S(2)}) %all-to-all-start) | async-done | bytes 327712 | tf_op jit(solution)/shard_map/all_to_all | solution.py:75
  46.8 25.6 %all-to-all-start.1 = ((f32[2,8,20,128]{3,0,2,1:T(2,128)}), f32[2,8,20,128]{3,0,2,1:T(2,128)}, u32[]{:S(2)}, u32[]{:S(2)}) async-start(f32[2,8,20,128]{3,0,2,1:T(2,128)} %bitcast.12), calls=%async_computation.1 | async-start | bytes 327680 | tf_op jit(solution)/shard_map/all_to_all | solution.py:51
  77.6 5.4 %collective-permute-start.7 = (bf16[2,64,2048]{2,1,0:T(8,128)(2,1)}, bf16[2,64,2048]{2,1,0:T(8,128)(2,1)}, u32[]{:S(2)}, u32[]{:S(2)}) collective-permute-start(bf16[2,64,2048]{2,1,0:T(8,128)(2,1)} %pad_maximum_fusion), channel_id=1, source_target_pairs={{0,1},{1,2},{2,3},{3,4},{4,5},{5,6},{6,7},{7,8},{8,9},{9,10},{10,1... | collective-permute-start | bytes 1572872 | tf_op jit(solution)/shard_map/ppermute | solution.py:34
  84.6 2.6 %fusion.9 = f32[2,128,512]{2,1,0:T(8,128)} fusion(bf16[512,2,128]{0,2,1:T(8,128)(2,1)S(1)} %bitcast.98, f32[2,512,512]{2,1,0:T(8,128)S(1)} %fusion.75, pred[512,512]{1,0:T(8,128)(4,1)S(1)} %iota_compare_fusion), kind=kOutput, calls=%fused_computation.12 | convolution fusion | flops 808452096 | bytes 3145728 | tf_op jit(solution)/shard_map/hij,jhe->ihe/dot_general | solution.py:96
  92.0 2.4 %copy.105 = bf16[2,64,2048]{1,2,0:T(8,128)(2,1)} copy(bf16[2,64,2048]{2,1,0:T(8,128)(2,1)} %collective-permute-done.4) | data formatting | bytes 1048576 | tf_op jit(solution)/shard_map/ppermute | solution.py:34
  94.4 3.7 %collective-permute-done.5 = bf16[2,64,2048]{2,1,0:T(8,128)(2,1)} collective-permute-done((bf16[2,64,2048]{2,1,0:T(8,128)(2,1)}, bf16[2,64,2048]{2,1,0:T(8,128)(2,1)}, u32[]{:S(2)}, u32[]{:S(2)}) %collective-permute-start.5) | collective-permute-done | bytes 524320 | tf_op jit(solution)/shard_map/ppermute | solution.py:34
  98.1 2.4 %copy.106 = bf16[2,64,2048]{1,2,0:T(8,128)(2,1)} copy(bf16[2,64,2048]{2,1,0:T(8,128)(2,1)} %collective-permute-done.5) | data formatting | bytes 1048576 | tf_op jit(solution)/shard_map/ppermute | solution.py:34
  100.5 2.4 %copy.107 = bf16[2,64,2048]{1,2,0:T(8,128)(2,1)} copy(bf16[2,64,2048]{2,1,0:T(8,128)(2,1)} %collective-permute-done.6) | data formatting | bytes 1048576 | tf_op jit(solution)/shard_map/ppermute | solution.py:34
  103.0 2.4 %copy.108 = bf16[2,64,2048]{1,2,0:T(8,128)(2,1)} copy(bf16[2,64,2048]{2,1,0:T(8,128)(2,1)} %collective-permute-done.7) | data formatting | bytes 1048576 | tf_op jit(solution)/shard_map/ppermute | solution.py:34
  105.4 10.8 %concatenate.31 = bf16[2,512,2048]{1,2,0:T(8,128)(2,1)} concatenate(bf16[2,64,2048]{1,2,0:T(8,128)(2,1)S(1)} %copy.101, bf16[2,64,2048]{1,2,0:T(8,128)(2,1)S(1)} %copy.102, bf16[2,64,2048]{1,2,0:T(8,128)(2,1)S(1)} %copy.103, bf16[2,64,2048]{1,2,0:T(8,128)(2,1)} %copy.104, bf16[2,64,2048]{1,2,0:T(8,128)(2,1)} %copy.105, bf16[2,64,2048]{1,2,0:T(8,128)(2,1)} %copy.106, ...), dimensions={1} | concatenate | bytes 8388608 | tf_op jit(solution)/shard_map/concatenate | solution.py:123
  116.1 3.9 %fusion.67 = (bf16[1,512,2048]{1,2,0:T(8,128)(2,1)}, bf16[1,512,2048]{1,2,0:T(8,128)(2,1)S(1)}) fusion(bf16[2,512,2048]{1,2,0:T(8,128)(2,1)} %concatenate.31), kind=kLoop, calls=%fused_computation.77 | loop fusion | bytes 8388608 | tf_op jit(solution)/shard_map/slice | solution.py:124
  120.0 3.9 %copy.111 = bf16[512,16,128]{2,0,1:T(8,128)(2,1)} copy(bf16[512,16,128]{0,2,1:T(8,128)(2,1)} %bitcast.90) | data formatting | bytes 4194304 | tf_op jit(solution)/shard_map/concatenate | solution.py:124
  127.3 22.0 %all-gather = f32[16,1,20,128]{3,1,2,0:T(1,128)S(1)} all-gather(f32[2,1,20,128]{3,1,2,0:T(1,128)S(1)} %copy.96), channel_id=2, replica_groups=mesh['y'=8,'z'=8,'core'=2,'sub'=4] {'y'}, dimensions={0}, use_global_device_ids=true | all-gather | bytes 184320 | tf_op jit(solution)/shard_map/all_gather | solution.py:54
  151.1 6.7 %all-to-all-start.2 = ((f32[2,8,20,128]{3,0,2,1:T(2,128)}), f32[2,8,20,128]{3,0,2,1:T(2,128)S(1)}, u32[]{:S(2)}, u32[]{:S(2)}) async-start(f32[2,8,20,128]{3,0,2,1:T(2,128)} %bitcast.88), calls=%async_computation.2 | async-start | bytes 327680 | tf_op jit(solution)/shard_map/all_to_all | solution.py:58
  157.9 4.3 %fusion.69 = (f32[16,64]{1,0:T(8,128)S(1)}, f32[16,64,576]{2,1,0:T(8,128)}) fusion(pred[64,576]{1,0:T(8,128)(4,1)S(1)} %and_and_fusion, bf16[64,16,128]{2,0,1:T(8,128)(2,1)S(1)} %copy-done.7, bf16[512,16,128]{2,0,1:T(8,128)(2,1)} %copy.111, bf16[64,2048]{1,0:T(8,128)(2,1)S(1)} %copy-done), kind=kOutput, calls=%fused_computation.79 | convolution fusion | flops 158073408 | bytes 5021696 | tf_op jit(solution)/shard_map/sub | solution.py:142
  162.2 4.1 %all-to-all-done.2 = f32[2,8,20,128]{3,0,2,1:T(2,128)S(1)} async-done(((f32[2,8,20,128]{3,0,2,1:T(2,128)}), f32[2,8,20,128]{3,0,2,1:T(2,128)S(1)}, u32[]{:S(2)}, u32[]{:S(2)}) %all-to-all-start.2) | async-done | bytes 163872 | tf_op jit(solution)/shard_map/all_to_all | solution.py:58
  169.2 10.9 %all-to-all-start.3 = ((bf16[8,64,256]{2,1,0:T(8,128)(2,1)}), bf16[8,64,256]{2,1,0:T(8,128)(2,1)S(1)}, u32[]{:S(2)}, u32[]{:S(2)}) async-start(bf16[8,64,256]{2,1,0:T(8,128)(2,1)} %reshape.179), calls=%async_computation.3 | async-start | bytes 524288 | tf_op jit(solution)/shard_map/all_to_all | solution.py:104
  183.3 3.4 %all-to-all-done.3 = bf16[8,64,256]{2,1,0:T(8,128)(2,1)S(1)} async-done(((bf16[8,64,256]{2,1,0:T(8,128)(2,1)}), bf16[8,64,256]{2,1,0:T(8,128)(2,1)S(1)}, u32[]{:S(2)}, u32[]{:S(2)}) %all-to-all-start.3) | async-done | bytes 262176 | tf_op jit(solution)/shard_map/all_to_all | solution.py:104
  (81 shorter events, 35.1 us)
Async XLA Ops:
  0.6 157.3 %copy-start = (bf16[64,2048]{1,0:T(8,128)(2,1)S(1)}, bf16[64,2048]{1,0:T(8,128)(2,1)}, u32[]{:S(2)}) copy-start(bf16[64,2048]{1,0:T(8,128)(2,1)} %param.15) | copy-start | bytes 786436
  0.6 35.0 %copy-start.3 = (bf16[64,2048]{1,0:T(8,128)(2,1)S(1)}, bf16[64,2048]{1,0:T(8,128)(2,1)}, u32[]{:S(2)}) copy-start(bf16[64,2048]{1,0:T(8,128)(2,1)} %param.16) | copy-start | bytes 786436
  0.7 36.7 %copy-start.4 = (bf16[64,2048]{1,0:T(8,128)(2,1)S(1)}, bf16[64,2048]{1,0:T(8,128)(2,1)}, u32[]{:S(2)}) copy-start(bf16[64,2048]{1,0:T(8,128)(2,1)} %param.17) | copy-start | bytes 786436
  2.7 71.1 %collective-permute-start = (bf16[2,64,2048]{2,1,0:T(8,128)(2,1)}, bf16[2,64,2048]{2,1,0:T(8,128)(2,1)S(1)}, u32[]{:S(2)}, u32[]{:S(2)}) collective-permute-start(bf16[2,64,2048]{2,1,0:T(8,128)(2,1)} %pad_maximum_fusion), channel_id=1, source_target_pairs={{0,8},{1,9},{2,10},{3,11},{4,12},{5,13},{6,14},{7,15},{8,16},{9,17... | collective-permute-start | bytes 1572872 | tf_op jit(solution)/shard_map/ppermute | solution.py:34
  7.5 68.2 %collective-permute-start.1 = (bf16[2,64,2048]{2,1,0:T(8,128)(2,1)}, bf16[2,64,2048]{2,1,0:T(8,128)(2,1)S(1)}, u32[]{:S(2)}, u32[]{:S(2)}) collective-permute-start(bf16[2,64,2048]{2,1,0:T(8,128)(2,1)} %pad_maximum_fusion), channel_id=1, source_target_pairs={{0,7},{1,8},{2,9},{3,10},{4,11},{5,12},{6,13},{7,14},{8,15},{9,16}... | collective-permute-start | bytes 1572872 | tf_op jit(solution)/shard_map/ppermute | solution.py:34
  14.6 63.1 %collective-permute-start.2 = (bf16[2,64,2048]{2,1,0:T(8,128)(2,1)}, bf16[2,64,2048]{2,1,0:T(8,128)(2,1)S(1)}, u32[]{:S(2)}, u32[]{:S(2)}) collective-permute-start(bf16[2,64,2048]{2,1,0:T(8,128)(2,1)} %pad_maximum_fusion), channel_id=1, source_target_pairs={{0,6},{1,7},{2,8},{3,9},{4,10},{5,11},{6,12},{7,13},{8,14},{9,15},... | collective-permute-start | bytes 1572872 | tf_op jit(solution)/shard_map/ppermute | solution.py:34
  19.1 70.6 %collective-permute-start.3 = (bf16[2,64,2048]{2,1,0:T(8,128)(2,1)}, bf16[2,64,2048]{2,1,0:T(8,128)(2,1)}, u32[]{:S(2)}, u32[]{:S(2)}) collective-permute-start(bf16[2,64,2048]{2,1,0:T(8,128)(2,1)} %pad_maximum_fusion), channel_id=1, source_target_pairs={{0,5},{1,6},{2,7},{3,8},{4,9},{5,10},{6,11},{7,12},{8,13},{9,14},{... | collective-permute-start | bytes 1572872 | tf_op jit(solution)/shard_map/ppermute | solution.py:34
  21.6 70.5 %collective-permute-start.4 = (bf16[2,64,2048]{2,1,0:T(8,128)(2,1)}, bf16[2,64,2048]{2,1,0:T(8,128)(2,1)}, u32[]{:S(2)}, u32[]{:S(2)}) collective-permute-start(bf16[2,64,2048]{2,1,0:T(8,128)(2,1)} %pad_maximum_fusion), channel_id=1, source_target_pairs={{0,4},{1,5},{2,6},{3,7},{4,8},{5,9},{6,10},{7,11},{8,12},{9,13},{1... | collective-permute-start | bytes 1572872 | tf_op jit(solution)/shard_map/ppermute | solution.py:34
  30.1 14.0 %copy-start.10 = (f32[17,160,1]{1,0,2:T(8,128)S(1)}, f32[17,160,1]{1,0,2:T(8,128)}, u32[]{:S(2)}) copy-start(f32[17,160,1]{1,0,2:T(8,128)} %constant.80) | copy-start | bytes 32644
  31.1 13.7 %copy-start.8 = (f32[17,160,1]{1,0,2:T(8,128)S(1)}, f32[17,160,1]{1,0,2:T(8,128)}, u32[]{:S(2)}) copy-start(f32[17,160,1]{1,0,2:T(8,128)} %constant.81) | copy-start | bytes 32644
  31.1 12.5 %all-to-all-start = ((bf16[64,8,320]{2,0,1:T(8,128)(2,1)}), bf16[64,8,320]{2,0,1:T(8,128)(2,1)S(1)}, u32[]{:S(2)}, u32[]{:S(2)}) async-start(bf16[64,8,320]{2,0,1:T(8,128)(2,1)} %pad_maximum_fusion.1), calls=%async_computation | async-start | bytes 786432 | tf_op jit(solution)/shard_map/all_to_all | solution.py:75
  43.9 28.6 %copy-start.9 = (f32[17,160,1]{1,0,2:T(8,128)S(1)}, f32[17,160,1]{1,0,2:T(8,128)}, u32[]{:S(2)}) copy-start(f32[17,160,1]{1,0,2:T(8,128)} %constant.82) | copy-start | bytes 32644
  46.8 79.5 %all-to-all-start.1 = ((f32[2,8,20,128]{3,0,2,1:T(2,128)}), f32[2,8,20,128]{3,0,2,1:T(2,128)}, u32[]{:S(2)}, u32[]{:S(2)}) async-start(f32[2,8,20,128]{3,0,2,1:T(2,128)} %bitcast.12), calls=%async_computation.1 | async-start | bytes 327680 | tf_op jit(solution)/shard_map/all_to_all | solution.py:51
  73.8 24.4 %collective-permute-start.5 = (bf16[2,64,2048]{2,1,0:T(8,128)(2,1)}, bf16[2,64,2048]{2,1,0:T(8,128)(2,1)}, u32[]{:S(2)}, u32[]{:S(2)}) collective-permute-start(bf16[2,64,2048]{2,1,0:T(8,128)(2,1)} %pad_maximum_fusion), channel_id=1, source_target_pairs={{0,3},{1,4},{2,5},{3,6},{4,7},{5,8},{6,9},{7,10},{8,11},{9,12},{10... | collective-permute-start | bytes 1572872 | tf_op jit(solution)/shard_map/ppermute | solution.py:34
  75.7 24.8 %collective-permute-start.6 = (bf16[2,64,2048]{2,1,0:T(8,128)(2,1)}, bf16[2,64,2048]{2,1,0:T(8,128)(2,1)}, u32[]{:S(2)}, u32[]{:S(2)}) collective-permute-start(bf16[2,64,2048]{2,1,0:T(8,128)(2,1)} %pad_maximum_fusion), channel_id=1, source_target_pairs={{0,2},{1,3},{2,4},{3,5},{4,6},{5,7},{6,8},{7,9},{8,10},{9,11},{10,... | collective-permute-start | bytes 1572872 | tf_op jit(solution)/shard_map/ppermute | solution.py:34
  77.6 9.5 %copy-start.5 = (bf16[2,64,2048]{2,1,0:T(8,128)(2,1)}, bf16[2,64,2048]{2,1,0:T(8,128)(2,1)S(1)}, u32[]{:S(2)}) copy-start(bf16[2,64,2048]{2,1,0:T(8,128)(2,1)S(1)} %collective-permute-done.2) | copy-start | bytes 1572868
  77.6 25.3 %collective-permute-start.7 = (bf16[2,64,2048]{2,1,0:T(8,128)(2,1)}, bf16[2,64,2048]{2,1,0:T(8,128)(2,1)}, u32[]{:S(2)}, u32[]{:S(2)}) collective-permute-start(bf16[2,64,2048]{2,1,0:T(8,128)(2,1)} %pad_maximum_fusion), channel_id=1, source_target_pairs={{0,1},{1,2},{2,3},{3,4},{4,5},{5,6},{6,7},{7,8},{8,9},{9,10},{10,1... | collective-permute-start | bytes 1572872 | tf_op jit(solution)/shard_map/ppermute | solution.py:34
  123.9 33.9 %copy-start.7 = (bf16[64,16,128]{2,0,1:T(8,128)(2,1)S(1)}, bf16[64,16,128]{2,0,1:T(8,128)(2,1)}, u32[]{:S(2)}) copy-start(bf16[64,16,128]{2,0,1:T(8,128)(2,1)} %copy_bitcast_fusion.2) | copy-start | bytes 786436
  151.1 15.1 %all-to-all-start.2 = ((f32[2,8,20,128]{3,0,2,1:T(2,128)}), f32[2,8,20,128]{3,0,2,1:T(2,128)S(1)}, u32[]{:S(2)}, u32[]{:S(2)}) async-start(f32[2,8,20,128]{3,0,2,1:T(2,128)} %bitcast.88), calls=%async_computation.2 | async-start | bytes 327680 | tf_op jit(solution)/shard_map/all_to_all | solution.py:58
  157.9 8.4 %copy-start.1 = (f32[512,2,160]{0,2,1:T(8,128)S(1)}, f32[512,2,160]{0,2,1:T(8,128)}, u32[]{:S(2)}) copy-start(f32[512,2,160]{0,2,1:T(8,128)} %convolution_multiply_fusion) | copy-start | bytes 1966084
  162.2 18.0 %copy-start.2 = (bf16[512,16,128]{2,0,1:T(8,128)(2,1)S(1)}, bf16[512,16,128]{2,0,1:T(8,128)(2,1)}, u32[]{:S(2)}) copy-start(bf16[512,16,128]{2,0,1:T(8,128)(2,1)} %copy.109) | copy-start | bytes 6291460
  162.2 18.0 %copy-start.6 = (bf16[64,16,128]{2,0,1:T(8,128)(2,1)S(1)}, bf16[64,16,128]{2,0,1:T(8,128)(2,1)}, u32[]{:S(2)}) copy-start(bf16[64,16,128]{2,0,1:T(8,128)(2,1)} %copy_bitcast_fusion.1) | copy-start | bytes 786436
  169.2 17.5 %all-to-all-start.3 = ((bf16[8,64,256]{2,1,0:T(8,128)(2,1)}), bf16[8,64,256]{2,1,0:T(8,128)(2,1)S(1)}, u32[]{:S(2)}, u32[]{:S(2)}) async-start(bf16[8,64,256]{2,1,0:T(8,128)(2,1)} %reshape.179), calls=%async_computation.3 | async-start | bytes 524288 | tf_op jit(solution)/shard_map/all_to_all | solution.py:104

commit v4 on v3

--- a/solution.py
+++ b/solution.py
@@ -1,9 +1,12 @@
+import functools
 import math
 
 import jax
 import jax.numpy as jnp
 import numpy as np
 from jax import lax
+from jax.experimental import pallas as pl
+from jax.experimental.pallas import tpu as pltpu
 from jax.sharding import Mesh
 from jax.sharding import PartitionSpec as P
 
@@ -42,6 +45,57 @@
         "jhi,if->jhf", ext, jnp.asarray(table), precision=lax.Precision.HIGHEST
     )
     return pick(first) * pick(second)
+
+
+def window_kernel(pos_ref, q_ref, k_ref, v_ref, *refs):
+    reach = len(refs) - 1
+    out_ref = refs[-1]
+    rows = q_ref.shape[0]
+    pos = pos_ref[0]
+    row = lax.broadcasted_iota(jnp.int32, (rows, rows), 0)
+    col = lax.broadcasted_iota(jnp.int32, (rows, rows), 1)
+    here = jnp.zeros((rows, rows), jnp.int32) + pos
+    scale = 1.0 / math.sqrt(SDIM)
+    for head in range(q_ref.shape[1] // SDIM):
+        lanes = pl.ds(head * SDIM, SDIM)
+        query = q_ref[:, lanes]
+        keys = [refs[t][0, :, lanes] for t in range(reach)] + [k_ref[:, lanes]]
+        values = [refs[t][1, :, lanes] for t in range(reach)] + [v_ref[:, lanes]]
+        scores = []
+        for t in range(reach + 1):
+            s = lax.dot_general(query, keys[t], (((1,), (1,)), ((), ())),
+                                preferred_element_type=jnp.float32) * scale
+            if t == reach:
+                ok = col <= row
+            elif t == 0:
+                ok = (col > row) & (here >= reach - t)
+            else:
+                ok = here >= reach - t
+            scores.append(jnp.where(ok, s, jnp.float32(-1e30)))
+        top = functools.reduce(jnp.maximum, [jnp.max(s, axis=1, keepdims=True) for s in scores])
+        expd = [jnp.exp(s - top) for s in scores]
+        total = functools.reduce(jnp.add, [jnp.sum(e, axis=1, keepdims=True) for e in expd])
+        acc = None
+        for t in range(reach + 1):
+            part = lax.dot_general((expd[t] / total).astype(jnp.bfloat16), values[t],
+                                   (((1,), (0,)), ((), ())), preferred_element_type=jnp.float32)
+            acc = part if acc is None else acc + part
+        out_ref[:, lanes] = acc.astype(out_ref.dtype)
+
+def window_attention(pos, query, key, value, earlier):
+    rows, channels = query.shape
+    lanes = 4 * SDIM
+    steps = channels // lanes
+    flat = pl.BlockSpec((rows, lanes), lambda g, p: (0, g))
+    stacked = pl.BlockSpec((2, rows, lanes), lambda g, p: (0, 0, g))
+    return pl.pallas_call(
+        window_kernel,
+        out_shape=jax.ShapeDtypeStruct((rows, channels), jnp.bfloat16),
+        grid_spec=pltpu.PrefetchScalarGridSpec(
+            num_scalar_prefetch=1, grid=(steps,),
+            in_specs=[flat, flat, flat] + [stacked] * len(earlier),
+            out_specs=flat),
+    )(jnp.reshape(pos, (1,)).astype(jnp.int32), query, key, value, *earlier)
 
 
 def groups_before(total):
@@ -120,30 +174,7 @@
 
     stacked = jnp.stack([window_key, window_value])
     earlier = [passed_along(stacked, ALL, reach_dev - t) for t in range(reach_dev)]
-    earlier = jnp.concatenate(earlier, axis=1)
-    key_rows = jnp.concatenate([earlier[0], window_key], axis=0).reshape(-1, head_count, SDIM)
-    value_rows = jnp.concatenate([earlier[1], window_value], axis=0).reshape(-1, head_count, SDIM)
-
-    query_heads = window_query.reshape(rows_dev, head_count, SDIM)
-    scores = jnp.einsum(
-        "ihd,jhd->hij", query_heads, key_rows, preferred_element_type=jnp.float32
-    ) * (1.0 / math.sqrt(SDIM))
-    query_pos = base_row + jnp.arange(rows_dev, dtype=jnp.int32)
-    key_pos = (
-        base_row - reach_dev * rows_dev + jnp.arange((reach_dev + 1) * rows_dev, dtype=jnp.int32)
-    )
-    allowed = (
-        (key_pos[None, :] <= query_pos[:, None])
-        & (key_pos[None, :] > query_pos[:, None] - WINDOW)
-        & (key_pos[None, :] >= 0)
-    )
-    scores = jnp.where(allowed[None], scores, jnp.float32(-1e30))
-    row_max = jnp.max(scores, axis=-1, keepdims=True)
-    exp_scores = jnp.exp(scores - row_max)
-    weights_bf = (exp_scores / jnp.sum(exp_scores, axis=-1, keepdims=True)).astype(jnp.bfloat16)
-    mixed = jnp.einsum("hij,jhd->ihd", weights_bf, value_rows, preferred_element_type=jnp.float32)
-    window_out = mixed.reshape(rows_dev, channels).astype(jnp.bfloat16)
-
+    window_out = window_attention(device_pos, window_query, window_key, window_value, earlier)
     linear_out = linear_heads(linear_query, linear_key, linear_value, lin_gain)
     return (linear_out, window_out)
 

time: 189 us -> 166 us (0.88)
  the two profiles are of different devices: /device:TPU:1 before, /device:TPU:17 now
where the time goes in v4:
time: 166 us; the launch traced here: 165 us
  waiting for transfers between devices  59.6 us (36%)
  starting transfers between devices  56.9 us (34%)
  blocking collectives  19.5 us (12%)
  Pallas kernels  10.5 us (6%)
  local copies, waits for them, and re-layouts  6.96 us (4%)
  matrix products  6.37 us (4%)
  other arithmetic  4.02 us (2%)
    ppermute x8, starting transfers between devices, passed_along(): return lax.ppermute(shard, axis, pairs)  40.2 us
    all_to_all x1, waiting for transfers between devices, linear_heads(): got = lax.all_to_all(packed, GROUP, split_axis=1, concat_axis=0, tiled=True)  30.3 us
    all_gather x1, blocking collectives, groups_before(): along_y = lax.all_gather(line_total, 'y')  19.5 us
    ppermute x8, waiting for transfers between devices, passed_along(): return lax.ppermute(shard, axis, pairs)  15.8 us
    pallas_call x1, Pallas kernels, window_attention(): pl.pallas_call(window_kernel, out_shape=jax.ShapeDtypeStruct((rows, chann...  10.5 us
    all_to_all x1, waiting for transfers between devices, groups_before(): held = lax.all_to_all(dealt, 'z', split_axis=1, concat_axis=1, tiled=True)  6.83 us
    all_to_all x1, waiting for transfers between devices, groups_before(): back = lax.all_to_all(prefix, 'z', split_axis=1, concat_axis=1, tiled=True)  6.69 us
    all_to_all x1, starting transfers between devices, linear_heads(): back = lax.all_to_all(out, GROUP, split_axis=0, concat_axis=2, tiled=True)  5.79 us
  transfers between devices with their start and end apart: 12, of which 4 were waited for; matrix products, arithmetic and copies ran while one was open for 8% of the time, Pallas kernels for 6%

profile of v4, /device:TPU:17, one launch (start us, length us, event | category | flops | bytes accessed | tf_op | source)
XLA Modules:
  0.0 164.8 jit_solution(15280881124531478473)
XLA Ops:
  0.6 1.9 %pad_maximum_fusion = bf16[2,64,2048]{2,1,0:T(8,128)(2,1)} fusion(bf16[1,64,2048]{2,1,0:T(8,128)(2,1)} %bitcast.58, bf16[1,64,2048]{2,1,0:T(8,128)(2,1)} %bitcast.57), kind=kLoop, calls=%fused_computation.17 | loop fusion | flops 262144 | bytes 1048576 | tf_op jit(solution)/shard_map/stack | solution.py:175
  2.5 4.0 %collective-permute-start = (bf16[2,64,2048]{2,1,0:T(8,128)(2,1)}, bf16[2,64,2048]{2,1,0:T(8,128)(2,1)}, u32[]{:S(2)}, u32[]{:S(2)}) collective-permute-start(bf16[2,64,2048]{2,1,0:T(8,128)(2,1)} %pad_maximum_fusion), channel_id=1, source_target_pairs={{0,8},{1,9},{2,10},{3,11},{4,12},{5,13},{6,14},{7,15},{8,16},{9,17... | collective-permute-start | bytes 1572872 | tf_op jit(solution)/shard_map/ppermute | solution.py:37
  6.5 7.0 %collective-permute-start.1 = (bf16[2,64,2048]{2,1,0:T(8,128)(2,1)}, bf16[2,64,2048]{2,1,0:T(8,128)(2,1)}, u32[]{:S(2)}, u32[]{:S(2)}) collective-permute-start(bf16[2,64,2048]{2,1,0:T(8,128)(2,1)} %pad_maximum_fusion), channel_id=1, source_target_pairs={{0,7},{1,8},{2,9},{3,10},{4,11},{5,12},{6,13},{7,14},{8,15},{9,16}... | collective-permute-start | bytes 1572872 | tf_op jit(solution)/shard_map/ppermute | solution.py:37
  13.6 4.5 %collective-permute-start.2 = (bf16[2,64,2048]{2,1,0:T(8,128)(2,1)}, bf16[2,64,2048]{2,1,0:T(8,128)(2,1)}, u32[]{:S(2)}, u32[]{:S(2)}) collective-permute-start(bf16[2,64,2048]{2,1,0:T(8,128)(2,1)} %pad_maximum_fusion), channel_id=1, source_target_pairs={{0,6},{1,7},{2,8},{3,9},{4,10},{5,11},{6,12},{7,13},{8,14},{9,15},... | collective-permute-start | bytes 1572872 | tf_op jit(solution)/shard_map/ppermute | solution.py:37
  18.1 1.9 %collective-permute-start.3 = (bf16[2,64,2048]{2,1,0:T(8,128)(2,1)}, bf16[2,64,2048]{2,1,0:T(8,128)(2,1)}, u32[]{:S(2)}, u32[]{:S(2)}) collective-permute-start(bf16[2,64,2048]{2,1,0:T(8,128)(2,1)} %pad_maximum_fusion), channel_id=1, source_target_pairs={{0,5},{1,6},{2,7},{3,8},{4,9},{5,10},{6,11},{7,12},{8,13},{9,14},{... | collective-permute-start | bytes 1572872 | tf_op jit(solution)/shard_map/ppermute | solution.py:37
  20.0 6.1 %collective-permute-start.4 = (bf16[2,64,2048]{2,1,0:T(8,128)(2,1)}, bf16[2,64,2048]{2,1,0:T(8,128)(2,1)}, u32[]{:S(2)}, u32[]{:S(2)}) collective-permute-start(bf16[2,64,2048]{2,1,0:T(8,128)(2,1)} %pad_maximum_fusion), channel_id=1, source_target_pairs={{0,4},{1,5},{2,6},{3,7},{4,8},{5,9},{6,10},{7,11},{8,12},{9,13},{1... | collective-permute-start | bytes 1572872 | tf_op jit(solution)/shard_map/ppermute | solution.py:37
  26.1 1.0 copy.79
  27.1 0.9 copy.55
  29.1 1.0 pad_maximum_fusion.1
  30.1 3.6 %all-to-all-start = ((bf16[64,8,320]{2,0,1:T(8,128)(2,1)}), bf16[64,8,320]{2,0,1:T(8,128)(2,1)S(1)}, u32[]{:S(2)}, u32[]{:S(2)}) async-start(bf16[64,8,320]{2,0,1:T(8,128)(2,1)} %pad_maximum_fusion.1), calls=%async_computation | async-start | bytes 786432 | tf_op jit(solution)/shard_map/all_to_all | solution.py:129
  33.8 30.3 %all-to-all-done = bf16[64,8,320]{2,0,1:T(8,128)(2,1)S(1)} async-done(((bf16[64,8,320]{2,0,1:T(8,128)(2,1)}), bf16[64,8,320]{2,0,1:T(8,128)(2,1)S(1)}, u32[]{:S(2)}, u32[]{:S(2)}) %all-to-all-start) | async-done | bytes 327712 | tf_op jit(solution)/shard_map/all_to_all | solution.py:129
  68.0 3.9 %all-to-all-start.1 = ((f32[2,8,20,128]{3,0,2,1:T(2,128)}), f32[2,8,20,128]{3,0,2,1:T(2,128)S(1)}, u32[]{:S(2)}, u32[]{:S(2)}) async-start(f32[2,8,20,128]{3,0,2,1:T(2,128)} %bitcast.12), calls=%async_computation.1 | async-start | bytes 327680 | tf_op jit(solution)/shard_map/all_to_all | solution.py:105
  72.0 1.8 %fusion = f32[2,128,512]{2,1,0:T(8,128)S(1)} fusion(bf16[512,2,128]{0,2,1:T(8,128)(2,1)S(1)} %bitcast.56, f32[2,512,512]{2,1,0:T(8,128)S(1)} %fusion.30, pred[512,512]{1,0:T(8,128)(4,1)S(1)} %iota_compare_fusion), kind=kOutput, calls=%fused_computation | convolution fusion | flops 808452096 | bytes 3145728 | tf_op jit(solution)/shard_map/hij,jhe->ihe/dot_general | solution.py:150
  73.7 6.8 %all-to-all-done.1 = f32[2,8,20,128]{3,0,2,1:T(2,128)S(1)} async-done(((f32[2,8,20,128]{3,0,2,1:T(2,128)}), f32[2,8,20,128]{3,0,2,1:T(2,128)S(1)}, u32[]{:S(2)}, u32[]{:S(2)}) %all-to-all-start.1) | async-done | bytes 163872 | tf_op jit(solution)/shard_map/all_to_all | solution.py:105
  80.7 19.5 %all-gather = f32[16,1,20,128]{3,1,2,0:T(1,128)S(1)} all-gather(f32[2,1,20,128]{3,1,2,0:T(1,128)S(1)} %copy.65), channel_id=2, replica_groups=mesh['y'=8,'z'=8,'core'=2,'sub'=4] {'y'}, dimensions={0}, use_global_device_ids=true | all-gather | bytes 184320 | tf_op jit(solution)/shard_map/all_gather | solution.py:108
  101.0 3.4 %all-to-all-start.2 = ((f32[2,8,20,128]{3,0,2,1:T(2,128)}), f32[2,8,20,128]{3,0,2,1:T(2,128)S(1)}, u32[]{:S(2)}, u32[]{:S(2)}) async-start(f32[2,8,20,128]{3,0,2,1:T(2,128)} %bitcast.48), calls=%async_computation.2 | async-start | bytes 327680 | tf_op jit(solution)/shard_map/all_to_all | solution.py:112
  105.9 6.7 %all-to-all-done.2 = f32[2,8,20,128]{3,0,2,1:T(2,128)S(1)} async-done(((f32[2,8,20,128]{3,0,2,1:T(2,128)}), f32[2,8,20,128]{3,0,2,1:T(2,128)S(1)}, u32[]{:S(2)}, u32[]{:S(2)}) %all-to-all-start.2) | async-done | bytes 163872 | tf_op jit(solution)/shard_map/all_to_all | solution.py:112
  113.3 1.9 %collective-permute-start.5 = (bf16[2,64,2048]{2,1,0:T(8,128)(2,1)}, bf16[2,64,2048]{2,1,0:T(8,128)(2,1)S(1)}, u32[]{:S(2)}, u32[]{:S(2)}) collective-permute-start(bf16[2,64,2048]{2,1,0:T(8,128)(2,1)} %pad_maximum_fusion), channel_id=1, source_target_pairs={{0,3},{1,4},{2,5},{3,6},{4,7},{5,8},{6,9},{7,10},{8,11},{9,12},{10... | collective-permute-start | bytes 1572872 | tf_op jit(solution)/shard_map/ppermute | solution.py:37
  115.3 4.4 %collective-permute-start.6 = (bf16[2,64,2048]{2,1,0:T(8,128)(2,1)}, bf16[2,64,2048]{2,1,0:T(8,128)(2,1)S(1)}, u32[]{:S(2)}, u32[]{:S(2)}) collective-permute-start(bf16[2,64,2048]{2,1,0:T(8,128)(2,1)} %pad_maximum_fusion), channel_id=1, source_target_pairs={{0,2},{1,3},{2,4},{3,5},{4,6},{5,7},{6,8},{7,9},{8,10},{9,11},{10,... | collective-permute-start | bytes 1572872 | tf_op jit(solution)/shard_map/ppermute | solution.py:37
  119.7 10.3 %collective-permute-start.7 = (bf16[2,64,2048]{2,1,0:T(8,128)(2,1)}, bf16[2,64,2048]{2,1,0:T(8,128)(2,1)S(1)}, u32[]{:S(2)}, u32[]{:S(2)}) collective-permute-start(bf16[2,64,2048]{2,1,0:T(8,128)(2,1)} %pad_maximum_fusion), channel_id=1, source_target_pairs={{0,1},{1,2},{2,3},{3,4},{4,5},{5,6},{6,7},{7,8},{8,9},{9,10},{10,1... | collective-permute-start | bytes 1572872 | tf_op jit(solution)/shard_map/ppermute | solution.py:37
  130.3 0.9 reshape.81
  131.2 5.8 %all-to-all-start.3 = ((bf16[8,64,256]{2,1,0:T(8,128)(2,1)}), bf16[8,64,256]{2,1,0:T(8,128)(2,1)S(1)}, u32[]{:S(2)}, u32[]{:S(2)}) async-start(bf16[8,64,256]{2,1,0:T(8,128)(2,1)} %reshape.81), calls=%async_computation.3 | async-start | bytes 524288 | tf_op jit(solution)/shard_map/all_to_all | solution.py:158
  137.0 15.8 %collective-permute-done.7.refs_7_ = bf16[2,64,2048]{2,1,0:T(8,128)(2,1)S(1)} collective-permute-done((bf16[2,64,2048]{2,1,0:T(8,128)(2,1)}, bf16[2,64,2048]{2,1,0:T(8,128)(2,1)S(1)}, u32[]{:S(2)}, u32[]{:S(2)}) %collective-permute-start.7) | collective-permute-done | bytes 524320 | tf_op jit(solution)/shard_map/ppermute | solution.py:37
  153.6 10.5 %shard_map.122 = bf16[64,2048]{1,0:T(8,128)(2,1)} custom-call(s32[1]{0:T(128)} %bitcast.20.pos_ref, bf16[64,2048]{1,0:T(8,128)(2,1)} %q_ref.1, bf16[64,2048]{1,0:T(8,128)(2,1)} %k_ref.1, bf16[64,2048]{1,0:T(8,128)(2,1)} %v_ref.1, bf16[2,64,2048]{2,1,0:T(8,128)(2,1)} %collective-permute-done.refs_0_, bf16[2,64,2048]{2,1,0:T(8,128)(2,1)} %collective-permute-done.1.refs_1_, ...), custom_call_target="tpu_custom_call" | custom-call | tf_op jit(solution)/shard_map/pallas_call | solution.py:91
  (53 shorter events, 10.0 us)
Async XLA Ops:
  0.6 33.1 %copy-start = (f32[2048]{0:T(1024)S(1)}, f32[2048]{0:T(1024)}, u32[]{:S(2)}) copy-start(f32[2048]{0:T(1024)} %param.14) | copy-start | bytes 24580
  2.5 110.8 %collective-permute-start = (bf16[2,64,2048]{2,1,0:T(8,128)(2,1)}, bf16[2,64,2048]{2,1,0:T(8,128)(2,1)}, u32[]{:S(2)}, u32[]{:S(2)}) collective-permute-start(bf16[2,64,2048]{2,1,0:T(8,128)(2,1)} %pad_maximum_fusion), channel_id=1, source_target_pairs={{0,8},{1,9},{2,10},{3,11},{4,12},{5,13},{6,14},{7,15},{8,16},{9,17... | collective-permute-start | bytes 1572872 | tf_op jit(solution)/shard_map/ppermute | solution.py:37
  6.5 108.7 %collective-permute-start.1 = (bf16[2,64,2048]{2,1,0:T(8,128)(2,1)}, bf16[2,64,2048]{2,1,0:T(8,128)(2,1)}, u32[]{:S(2)}, u32[]{:S(2)}) collective-permute-start(bf16[2,64,2048]{2,1,0:T(8,128)(2,1)} %pad_maximum_fusion), channel_id=1, source_target_pairs={{0,7},{1,8},{2,9},{3,10},{4,11},{5,12},{6,13},{7,14},{8,15},{9,16}... | collective-permute-start | bytes 1572872 | tf_op jit(solution)/shard_map/ppermute | solution.py:37
  13.6 106.1 %collective-permute-start.2 = (bf16[2,64,2048]{2,1,0:T(8,128)(2,1)}, bf16[2,64,2048]{2,1,0:T(8,128)(2,1)}, u32[]{:S(2)}, u32[]{:S(2)}) collective-permute-start(bf16[2,64,2048]{2,1,0:T(8,128)(2,1)} %pad_maximum_fusion), channel_id=1, source_target_pairs={{0,6},{1,7},{2,8},{3,9},{4,10},{5,11},{6,12},{7,13},{8,14},{9,15},... | collective-permute-start | bytes 1572872 | tf_op jit(solution)/shard_map/ppermute | solution.py:37
  18.1 118.9 %collective-permute-start.3 = (bf16[2,64,2048]{2,1,0:T(8,128)(2,1)}, bf16[2,64,2048]{2,1,0:T(8,128)(2,1)}, u32[]{:S(2)}, u32[]{:S(2)}) collective-permute-start(bf16[2,64,2048]{2,1,0:T(8,128)(2,1)} %pad_maximum_fusion), channel_id=1, source_target_pairs={{0,5},{1,6},{2,7},{3,8},{4,9},{5,10},{6,11},{7,12},{8,13},{9,14},{... | collective-permute-start | bytes 1572872 | tf_op jit(solution)/shard_map/ppermute | solution.py:37
  20.0 117.0 %collective-permute-start.4 = (bf16[2,64,2048]{2,1,0:T(8,128)(2,1)}, bf16[2,64,2048]{2,1,0:T(8,128)(2,1)}, u32[]{:S(2)}, u32[]{:S(2)}) collective-permute-start(bf16[2,64,2048]{2,1,0:T(8,128)(2,1)} %pad_maximum_fusion), channel_id=1, source_target_pairs={{0,4},{1,5},{2,6},{3,7},{4,8},{5,9},{6,10},{7,11},{8,12},{9,13},{1... | collective-permute-start | bytes 1572872 | tf_op jit(solution)/shard_map/ppermute | solution.py:37
  30.1 34.0 %all-to-all-start = ((bf16[64,8,320]{2,0,1:T(8,128)(2,1)}), bf16[64,8,320]{2,0,1:T(8,128)(2,1)S(1)}, u32[]{:S(2)}, u32[]{:S(2)}) async-start(bf16[64,8,320]{2,0,1:T(8,128)(2,1)} %pad_maximum_fusion.1), calls=%async_computation | async-start | bytes 786432 | tf_op jit(solution)/shard_map/all_to_all | solution.py:129
  64.2 1.1 copy-start.6
  64.4 1.6 copy-start.4
  68.0 12.6 %all-to-all-start.1 = ((f32[2,8,20,128]{3,0,2,1:T(2,128)}), f32[2,8,20,128]{3,0,2,1:T(2,128)S(1)}, u32[]{:S(2)}, u32[]{:S(2)}) async-start(f32[2,8,20,128]{3,0,2,1:T(2,128)} %bitcast.12), calls=%async_computation.1 | async-start | bytes 327680 | tf_op jit(solution)/shard_map/all_to_all | solution.py:105
  72.0 32.4 %copy-start.5 = (f32[17,160,1]{1,0,2:T(8,128)S(1)}, f32[17,160,1]{1,0,2:T(8,128)}, u32[]{:S(2)}) copy-start(f32[17,160,1]{1,0,2:T(8,128)} %constant.70) | copy-start | bytes 32644
  101.0 11.6 %all-to-all-start.2 = ((f32[2,8,20,128]{3,0,2,1:T(2,128)}), f32[2,8,20,128]{3,0,2,1:T(2,128)S(1)}, u32[]{:S(2)}, u32[]{:S(2)}) async-start(f32[2,8,20,128]{3,0,2,1:T(2,128)} %bitcast.48), calls=%async_computation.2 | async-start | bytes 327680 | tf_op jit(solution)/shard_map/all_to_all | solution.py:112
  113.3 23.7 %collective-permute-start.5 = (bf16[2,64,2048]{2,1,0:T(8,128)(2,1)}, bf16[2,64,2048]{2,1,0:T(8,128)(2,1)S(1)}, u32[]{:S(2)}, u32[]{:S(2)}) collective-permute-start(bf16[2,64,2048]{2,1,0:T(8,128)(2,1)} %pad_maximum_fusion), channel_id=1, source_target_pairs={{0,3},{1,4},{2,5},{3,6},{4,7},{5,8},{6,9},{7,10},{8,11},{9,12},{10... | collective-permute-start | bytes 1572872 | tf_op jit(solution)/shard_map/ppermute | solution.py:37
  115.3 21.8 %collective-permute-start.6 = (bf16[2,64,2048]{2,1,0:T(8,128)(2,1)}, bf16[2,64,2048]{2,1,0:T(8,128)(2,1)S(1)}, u32[]{:S(2)}, u32[]{:S(2)}) collective-permute-start(bf16[2,64,2048]{2,1,0:T(8,128)(2,1)} %pad_maximum_fusion), channel_id=1, source_target_pairs={{0,2},{1,3},{2,4},{3,5},{4,6},{5,7},{6,8},{7,9},{8,10},{9,11},{10,... | collective-permute-start | bytes 1572872 | tf_op jit(solution)/shard_map/ppermute | solution.py:37
  119.7 33.1 %collective-permute-start.7 = (bf16[2,64,2048]{2,1,0:T(8,128)(2,1)}, bf16[2,64,2048]{2,1,0:T(8,128)(2,1)S(1)}, u32[]{:S(2)}, u32[]{:S(2)}) collective-permute-start(bf16[2,64,2048]{2,1,0:T(8,128)(2,1)} %pad_maximum_fusion), channel_id=1, source_target_pairs={{0,1},{1,2},{2,3},{3,4},{4,5},{5,6},{6,7},{7,8},{8,9},{9,10},{10,1... | collective-permute-start | bytes 1572872 | tf_op jit(solution)/shard_map/ppermute | solution.py:37
  131.2 32.9 %all-to-all-start.3 = ((bf16[8,64,256]{2,1,0:T(8,128)(2,1)}), bf16[8,64,256]{2,1,0:T(8,128)(2,1)S(1)}, u32[]{:S(2)}, u32[]{:S(2)}) async-start(bf16[8,64,256]{2,1,0:T(8,128)(2,1)} %reshape.81), calls=%async_computation.3 | async-start | bytes 524288 | tf_op jit(solution)/shard_map/all_to_all | solution.py:158
  137.0 15.8 %copy-start.1 = (bf16[2,64,2048]{2,1,0:T(8,128)(2,1)}, bf16[2,64,2048]{2,1,0:T(8,128)(2,1)S(1)}, u32[]{:S(2)}) copy-start(bf16[2,64,2048]{2,1,0:T(8,128)(2,1)S(1)} %collective-permute-done.5.refs_5_) | copy-start | bytes 1572868
  137.0 15.8 %copy-start.2 = (bf16[2,64,2048]{2,1,0:T(8,128)(2,1)}, bf16[2,64,2048]{2,1,0:T(8,128)(2,1)S(1)}, u32[]{:S(2)}) copy-start(bf16[2,64,2048]{2,1,0:T(8,128)(2,1)S(1)} %collective-permute-done.6.refs_6_) | copy-start | bytes 1572868
  152.8 0.8 copy-start.3

commit v5 on v4

--- a/solution.py
+++ b/solution.py
@@ -113,7 +113,7 @@
     return back.reshape(heads, feats, width)
 
 
-def linear_heads(linear_query, linear_key, linear_value, lin_gain):
+def linear_heads(linear_query, linear_key, linear_value, lin_gain, held):
     rows_dev = linear_query.shape[0]
     group_count = lax.axis_size(GROUP)
     lin_heads = linear_query.shape[1] // FDIM
@@ -137,7 +137,7 @@
     total = jnp.einsum(
         "jhf,jhe->hfe", sym_features(key_lin, False), value_lin, precision=lax.Precision.HIGHEST
     )
-    before = groups_before(total)
+    before, held = lax.optimization_barrier((groups_before(total), held))
     from_state = jnp.einsum(
         "ihf,hfe->ihe", sym_features(query_lin, True), before, precision=lax.Precision.HIGHEST
     )
@@ -156,7 +156,7 @@
     out = (numerator * inv_rms * gain_rows).astype(jnp.bfloat16)
     out = out.reshape(group_count, rows_dev, own_heads * VDIM)
     back = lax.all_to_all(out, GROUP, split_axis=0, concat_axis=2, tiled=True)
-    return back.reshape(rows_dev, lin_heads * VDIM)
+    return back.reshape(rows_dev, lin_heads * VDIM), held
 
 
 def shards(
@@ -173,9 +173,9 @@
     lin_heads = linear_query.shape[1] // FDIM
 
     stacked = jnp.stack([window_key, window_value])
+    linear_out, stacked = linear_heads(linear_query, linear_key, linear_value, lin_gain, stacked)
     earlier = [passed_along(stacked, ALL, reach_dev - t) for t in range(reach_dev)]
     window_out = window_attention(device_pos, window_query, window_key, window_value, earlier)
-    linear_out = linear_heads(linear_query, linear_key, linear_value, lin_gain)
     return (linear_out, window_out)
 
 

time: 166 us -> 164 us (0.988)
  the two profiles are of different devices: /device:TPU:17 before, /device:TPU:33 now
where the time goes in v5:
time: 164 us; the launch traced here: 163 us
  starting transfers between devices  72.5 us (44%)
  waiting for transfers between devices  41 us (25%)
  blocking collectives  18.3 us (11%)
  Pallas kernels  10.5 us (6%)
  matrix products  9.15 us (6%)
  local copies, waits for them, and re-layouts  7.33 us (4%)
  other arithmetic  3.67 us (2%)
    ppermute x8, starting transfers between devices, passed_along(): return lax.ppermute(shard, axis, pairs)  37.6 us
    all_gather x1, blocking collectives, groups_before(): along_y = lax.all_gather(line_total, 'y')  18.3 us
    all_to_all x1, waiting for transfers between devices, linear_heads(): back = lax.all_to_all(out, GROUP, split_axis=0, concat_axis=2, tiled=True)  17.4 us
    all_to_all x1, starting transfers between devices, linear_heads(): back = lax.all_to_all(out, GROUP, split_axis=0, concat_axis=2, tiled=True)  16.3 us
    pallas_call x1, Pallas kernels, window_attention(): pl.pallas_call(window_kernel, out_shape=jax.ShapeDtypeStruct((rows, chann...  10.5 us
    all_to_all x1, starting transfers between devices, groups_before(): held = lax.all_to_all(dealt, 'z', split_axis=1, concat_axis=1, tiled=True)  10 us
    all_to_all x1, waiting for transfers between devices, groups_before(): held = lax.all_to_all(dealt, 'z', split_axis=1, concat_axis=1, tiled=True)  7.4 us
    all_to_all x1, waiting for transfers between devices, linear_heads(): got = lax.all_to_all(packed, GROUP, split_axis=1, concat_axis=0, tiled=True)  6.31 us
  transfers between devices with their start and end apart: 12, of which 5 were waited for; matrix products, arithmetic and copies ran while one was open for 7% of the time, Pallas kernels for 0%

profile of v5, /device:TPU:33, one launch (start us, length us, event | category | flops | bytes accessed | tf_op | source)
XLA Modules:
  0.0 163.5 jit_solution(11589426987945002592)
XLA Ops:
  0.7 1.0 copy.79
  3.7 1.0 pad_maximum_fusion.1
  4.7 5.1 %all-to-all-start = ((bf16[64,8,320]{2,0,1:T(8,128)(2,1)}), bf16[64,8,320]{2,0,1:T(8,128)(2,1)S(1)}, u32[]{:S(2)}, u32[]{:S(2)}) async-start(bf16[64,8,320]{2,0,1:T(8,128)(2,1)} %pad_maximum_fusion.1), calls=%async_computation | async-start | bytes 786432 | tf_op jit(solution)/shard_map/all_to_all | solution.py:129
  11.5 6.3 %all-to-all-done = bf16[64,8,320]{2,0,1:T(8,128)(2,1)S(1)} async-done(((bf16[64,8,320]{2,0,1:T(8,128)(2,1)}), bf16[64,8,320]{2,0,1:T(8,128)(2,1)S(1)}, u32[]{:S(2)}, u32[]{:S(2)}) %all-to-all-start) | async-done | bytes 327712 | tf_op jit(solution)/shard_map/all_to_all | solution.py:129
  21.2 10.0 %all-to-all-start.1 = ((f32[2,8,20,128]{3,0,2,1:T(2,128)}), f32[2,8,20,128]{3,0,2,1:T(2,128)S(1)}, u32[]{:S(2)}, u32[]{:S(2)}) async-start(f32[2,8,20,128]{3,0,2,1:T(2,128)} %bitcast.12), calls=%async_computation.1 | async-start | bytes 327680 | tf_op jit(solution)/shard_map/all_to_all | solution.py:105
  32.4 7.4 %all-to-all-done.1 = f32[2,8,20,128]{3,0,2,1:T(2,128)S(1)} async-done(((f32[2,8,20,128]{3,0,2,1:T(2,128)}), f32[2,8,20,128]{3,0,2,1:T(2,128)S(1)}, u32[]{:S(2)}, u32[]{:S(2)}) %all-to-all-start.1) | async-done | bytes 163872 | tf_op jit(solution)/shard_map/all_to_all | solution.py:105
  40.0 18.3 %all-gather = f32[16,1,20,128]{3,1,2,0:T(1,128)S(1)} all-gather(f32[2,1,20,128]{3,1,2,0:T(1,128)S(1)} %copy.65), channel_id=2, replica_groups=mesh['y'=8,'z'=8,'core'=2,'sub'=4] {'y'}, dimensions={0}, use_global_device_ids=true | all-gather | bytes 184320 | tf_op jit(solution)/shard_map/all_gather | solution.py:108
  59.1 3.4 %all-to-all-start.2 = ((f32[2,8,20,128]{3,0,2,1:T(2,128)}), f32[2,8,20,128]{3,0,2,1:T(2,128)S(1)}, u32[]{:S(2)}, u32[]{:S(2)}) async-start(f32[2,8,20,128]{3,0,2,1:T(2,128)} %bitcast.48), calls=%async_computation.2 | async-start | bytes 327680 | tf_op jit(solution)/shard_map/all_to_all | solution.py:112
  62.5 3.5 %fusion = f32[2,128,512]{2,1,0:T(8,128)} fusion(bf16[512,2,128]{0,2,1:T(8,128)(2,1)S(1)} %bitcast.56, f32[2,512,512]{2,1,0:T(8,128)S(1)} %fusion.30, pred[512,512]{1,0:T(8,128)(4,1)} %iota_compare_fusion), kind=kOutput, calls=%fused_computation | convolution fusion | flops 808452096 | bytes 3145728 | tf_op jit(solution)/shard_map/hij,jhe->ihe/dot_general | solution.py:150
  66.0 4.6 %all-to-all-done.2 = f32[2,8,20,128]{3,0,2,1:T(2,128)S(1)} async-done(((f32[2,8,20,128]{3,0,2,1:T(2,128)}), f32[2,8,20,128]{3,0,2,1:T(2,128)S(1)}, u32[]{:S(2)}, u32[]{:S(2)}) %all-to-all-start.2) | async-done | bytes 163872 | tf_op jit(solution)/shard_map/all_to_all | solution.py:112
  70.7 2.2 %collective-permute-start = (bf16[2,64,2048]{2,1,0:T(8,128)(2,1)}, bf16[2,64,2048]{2,1,0:T(8,128)(2,1)S(1)}, u32[]{:S(2)}, u32[]{:S(2)}) collective-permute-start(bf16[2,64,2048]{2,1,0:T(8,128)(2,1)} %pad_maximum_fusion), channel_id=1, source_target_pairs={{0,8},{1,9},{2,10},{3,11},{4,12},{5,13},{6,14},{7,15},{8,16},{9,17... | collective-permute-start | bytes 1572872 | tf_op jit(solution)/shard_map/ppermute | solution.py:37
  72.9 13.5 %collective-permute-start.1 = (bf16[2,64,2048]{2,1,0:T(8,128)(2,1)}, bf16[2,64,2048]{2,1,0:T(8,128)(2,1)S(1)}, u32[]{:S(2)}, u32[]{:S(2)}) collective-permute-start(bf16[2,64,2048]{2,1,0:T(8,128)(2,1)} %pad_maximum_fusion), channel_id=1, source_target_pairs={{0,7},{1,8},{2,9},{3,10},{4,11},{5,12},{6,13},{7,14},{8,15},{9,16}... | collective-permute-start | bytes 1572872 | tf_op jit(solution)/shard_map/ppermute | solution.py:37
  86.4 2.9 %collective-permute-start.2 = (bf16[2,64,2048]{2,1,0:T(8,128)(2,1)}, bf16[2,64,2048]{2,1,0:T(8,128)(2,1)S(1)}, u32[]{:S(2)}, u32[]{:S(2)}) collective-permute-start(bf16[2,64,2048]{2,1,0:T(8,128)(2,1)} %pad_maximum_fusion), channel_id=1, source_target_pairs={{0,6},{1,7},{2,8},{3,9},{4,10},{5,11},{6,12},{7,13},{8,14},{9,15},... | collective-permute-start | bytes 1572872 | tf_op jit(solution)/shard_map/ppermute | solution.py:37
  90.0 1.9 %collective-permute-start.3 = (bf16[2,64,2048]{2,1,0:T(8,128)(2,1)}, bf16[2,64,2048]{2,1,0:T(8,128)(2,1)}, u32[]{:S(2)}, u32[]{:S(2)}) collective-permute-start(bf16[2,64,2048]{2,1,0:T(8,128)(2,1)} %pad_maximum_fusion), channel_id=1, source_target_pairs={{0,5},{1,6},{2,7},{3,8},{4,9},{5,10},{6,11},{7,12},{8,13},{9,14},{... | collective-permute-start | bytes 1572872 | tf_op jit(solution)/shard_map/ppermute | solution.py:37
  92.0 2.0 %collective-permute-start.4 = (bf16[2,64,2048]{2,1,0:T(8,128)(2,1)}, bf16[2,64,2048]{2,1,0:T(8,128)(2,1)}, u32[]{:S(2)}, u32[]{:S(2)}) collective-permute-start(bf16[2,64,2048]{2,1,0:T(8,128)(2,1)} %pad_maximum_fusion), channel_id=1, source_target_pairs={{0,4},{1,5},{2,6},{3,7},{4,8},{5,9},{6,10},{7,11},{8,12},{9,13},{1... | collective-permute-start | bytes 1572872 | tf_op jit(solution)/shard_map/ppermute | solution.py:37
  94.0 1.8 %multiply_reduce_fusion = (f32[512,2]{0,1:T(2,128)S(1)}, f32[512,2,128]{0,2,1:T(8,128)S(1)}) fusion(f32[2,128,512]{2,1,0:T(8,128)} %fusion, f32[512,2,160]{0,2,1:T(8,128)S(1)} %convolution_multiply_fusion, f32[2,160,128]{2,0,1:T(2,128)S(1)} %bitcast.60), kind=kOutput, calls=%fused_computation.19 | convolution fusion | flops 252050432 | bytes 1871872 | tf_op jit(solution)/shard_map/ihf,hfe->ihe/dot_general | solution.py:141
  95.8 5.0 %collective-permute-start.5 = (bf16[2,64,2048]{2,1,0:T(8,128)(2,1)S(1)}, bf16[2,64,2048]{2,1,0:T(8,128)(2,1)S(1)}, u32[]{:S(2)}, u32[]{:S(2)}) collective-permute-start(bf16[2,64,2048]{2,1,0:T(8,128)(2,1)S(1)} %copy-done.3), channel_id=1, source_target_pairs={{0,3},{1,4},{2,5},{3,6},{4,7},{5,8},{6,9},{7,10},{8,11},{9,12},{10... | collective-permute-start | bytes 1572872 | tf_op jit(solution)/shard_map/ppermute | solution.py:37
  100.9 2.8 %collective-permute-start.6 = (bf16[2,64,2048]{2,1,0:T(8,128)(2,1)S(1)}, bf16[2,64,2048]{2,1,0:T(8,128)(2,1)S(1)}, u32[]{:S(2)}, u32[]{:S(2)}) collective-permute-start(bf16[2,64,2048]{2,1,0:T(8,128)(2,1)S(1)} %copy-done.3), channel_id=1, source_target_pairs={{0,2},{1,3},{2,4},{3,5},{4,6},{5,7},{6,8},{7,9},{8,10},{9,11},{10,... | collective-permute-start | bytes 1572872 | tf_op jit(solution)/shard_map/ppermute | solution.py:37
  103.7 5.2 %collective-permute-done.2.refs_2_ = bf16[2,64,2048]{2,1,0:T(8,128)(2,1)S(1)} collective-permute-done((bf16[2,64,2048]{2,1,0:T(8,128)(2,1)}, bf16[2,64,2048]{2,1,0:T(8,128)(2,1)S(1)}, u32[]{:S(2)}, u32[]{:S(2)}) %collective-permute-start.2) | collective-permute-done | bytes 524320 | tf_op jit(solution)/shard_map/ppermute | solution.py:37
  108.9 7.3 %collective-permute-start.7 = (bf16[2,64,2048]{2,1,0:T(8,128)(2,1)S(1)}, bf16[2,64,2048]{2,1,0:T(8,128)(2,1)S(1)}, u32[]{:S(2)}, u32[]{:S(2)}) collective-permute-start(bf16[2,64,2048]{2,1,0:T(8,128)(2,1)S(1)} %copy-done.3), channel_id=1, source_target_pairs={{0,1},{1,2},{2,3},{3,4},{4,5},{5,6},{6,7},{7,8},{8,9},{9,10},{10,1... | collective-permute-start | bytes 1572872 | tf_op jit(solution)/shard_map/ppermute | solution.py:37
  116.5 0.9 reshape.81
  117.3 16.3 %all-to-all-start.3 = ((bf16[8,64,256]{2,1,0:T(8,128)(2,1)}), bf16[8,64,256]{2,1,0:T(8,128)(2,1)S(1)}, u32[]{:S(2)}, u32[]{:S(2)}) async-start(bf16[8,64,256]{2,1,0:T(8,128)(2,1)} %reshape.81), calls=%async_computation.3 | async-start | bytes 524288 | tf_op jit(solution)/shard_map/all_to_all | solution.py:158
  133.7 17.4 %all-to-all-done.3 = bf16[8,64,256]{2,1,0:T(8,128)(2,1)S(1)} async-done(((bf16[8,64,256]{2,1,0:T(8,128)(2,1)}), bf16[8,64,256]{2,1,0:T(8,128)(2,1)S(1)}, u32[]{:S(2)}, u32[]{:S(2)}) %all-to-all-start.3) | async-done | bytes 262176 | tf_op jit(solution)/shard_map/all_to_all | solution.py:158
  153.0 10.5 %shard_map.122 = bf16[64,2048]{1,0:T(8,128)(2,1)} custom-call(s32[1]{0:T(128)} %bitcast.22.pos_ref, bf16[64,2048]{1,0:T(8,128)(2,1)} %q_ref.1, bf16[64,2048]{1,0:T(8,128)(2,1)} %k_ref.1, bf16[64,2048]{1,0:T(8,128)(2,1)} %v_ref.1, bf16[2,64,2048]{2,1,0:T(8,128)(2,1)} %copy-done.4, bf16[2,64,2048]{2,1,0:T(8,128)(2,1)} %copy-done.5, ...), custom_call_target="tpu_custom_call" | custom-call | tf_op jit(solution)/shard_map/pallas_call | solution.py:91
  (65 shorter events, 11.9 us)
Async XLA Ops:
  0.6 10.0 %copy-start = (f32[2048]{0:T(1024)S(1)}, f32[2048]{0:T(1024)}, u32[]{:S(2)}) copy-start(f32[2048]{0:T(1024)} %param.14) | copy-start | bytes 24580
  0.6 10.0 %copy-start.2 = (bf16[64,2048]{1,0:T(8,128)(2,1)S(1)}, bf16[64,2048]{1,0:T(8,128)(2,1)}, u32[]{:S(2)}) copy-start(bf16[64,2048]{1,0:T(8,128)(2,1)} %v_ref.1) | copy-start | bytes 786436
  0.7 10.0 %copy-start.1 = (bf16[64,2048]{1,0:T(8,128)(2,1)S(1)}, bf16[64,2048]{1,0:T(8,128)(2,1)}, u32[]{:S(2)}) copy-start(bf16[64,2048]{1,0:T(8,128)(2,1)} %k_ref.1) | copy-start | bytes 786436
  4.7 13.7 %copy-start.12 = (f32[17,160,1]{1,0,2:T(8,128)S(1)}, f32[17,160,1]{1,0,2:T(8,128)}, u32[]{:S(2)}) copy-start(f32[17,160,1]{1,0,2:T(8,128)} %constant.68) | copy-start | bytes 32644
  4.7 13.1 %all-to-all-start = ((bf16[64,8,320]{2,0,1:T(8,128)(2,1)}), bf16[64,8,320]{2,0,1:T(8,128)(2,1)S(1)}, u32[]{:S(2)}, u32[]{:S(2)}) async-start(bf16[64,8,320]{2,0,1:T(8,128)(2,1)} %pad_maximum_fusion.1), calls=%async_computation | async-start | bytes 786432 | tf_op jit(solution)/shard_map/all_to_all | solution.py:129
  9.8 9.3 %copy-start.10 = (f32[17,160,1]{1,0,2:T(8,128)S(1)}, f32[17,160,1]{1,0,2:T(8,128)}, u32[]{:S(2)}) copy-start(f32[17,160,1]{1,0,2:T(8,128)} %constant.69) | copy-start | bytes 32644
  18.3 12.9 %copy-start.11 = (f32[17,160,1]{1,0,2:T(8,128)S(1)}, f32[17,160,1]{1,0,2:T(8,128)}, u32[]{:S(2)}) copy-start(f32[17,160,1]{1,0,2:T(8,128)} %constant.70) | copy-start | bytes 32644
  21.2 18.7 %all-to-all-start.1 = ((f32[2,8,20,128]{3,0,2,1:T(2,128)}), f32[2,8,20,128]{3,0,2,1:T(2,128)S(1)}, u32[]{:S(2)}, u32[]{:S(2)}) async-start(f32[2,8,20,128]{3,0,2,1:T(2,128)} %bitcast.12), calls=%async_computation.1 | async-start | bytes 327680 | tf_op jit(solution)/shard_map/all_to_all | solution.py:105
  59.1 11.6 %all-to-all-start.2 = ((f32[2,8,20,128]{3,0,2,1:T(2,128)}), f32[2,8,20,128]{3,0,2,1:T(2,128)S(1)}, u32[]{:S(2)}, u32[]{:S(2)}) async-start(f32[2,8,20,128]{3,0,2,1:T(2,128)} %bitcast.48), calls=%async_computation.2 | async-start | bytes 327680 | tf_op jit(solution)/shard_map/all_to_all | solution.py:112
  66.0 29.7 %copy-start.3 = (bf16[2,64,2048]{2,1,0:T(8,128)(2,1)S(1)}, bf16[2,64,2048]{2,1,0:T(8,128)(2,1)}, u32[]{:S(2)}) copy-start(bf16[2,64,2048]{2,1,0:T(8,128)(2,1)} %pad_maximum_fusion) | copy-start | bytes 1572868
  70.7 25.1 %collective-permute-start = (bf16[2,64,2048]{2,1,0:T(8,128)(2,1)}, bf16[2,64,2048]{2,1,0:T(8,128)(2,1)S(1)}, u32[]{:S(2)}, u32[]{:S(2)}) collective-permute-start(bf16[2,64,2048]{2,1,0:T(8,128)(2,1)} %pad_maximum_fusion), channel_id=1, source_target_pairs={{0,8},{1,9},{2,10},{3,11},{4,12},{5,13},{6,14},{7,15},{8,16},{9,17... | collective-permute-start | bytes 1572872 | tf_op jit(solution)/shard_map/ppermute | solution.py:37
  72.9 27.9 %collective-permute-start.1 = (bf16[2,64,2048]{2,1,0:T(8,128)(2,1)}, bf16[2,64,2048]{2,1,0:T(8,128)(2,1)S(1)}, u32[]{:S(2)}, u32[]{:S(2)}) collective-permute-start(bf16[2,64,2048]{2,1,0:T(8,128)(2,1)} %pad_maximum_fusion), channel_id=1, source_target_pairs={{0,7},{1,8},{2,9},{3,10},{4,11},{5,12},{6,13},{7,14},{8,15},{9,16}... | collective-permute-start | bytes 1572872 | tf_op jit(solution)/shard_map/ppermute | solution.py:37
  86.4 22.5 %collective-permute-start.2 = (bf16[2,64,2048]{2,1,0:T(8,128)(2,1)}, bf16[2,64,2048]{2,1,0:T(8,128)(2,1)S(1)}, u32[]{:S(2)}, u32[]{:S(2)}) collective-permute-start(bf16[2,64,2048]{2,1,0:T(8,128)(2,1)} %pad_maximum_fusion), channel_id=1, source_target_pairs={{0,6},{1,7},{2,8},{3,9},{4,10},{5,11},{6,12},{7,13},{8,14},{9,15},... | collective-permute-start | bytes 1572872 | tf_op jit(solution)/shard_map/ppermute | solution.py:37
  90.0 61.8 %collective-permute-start.3 = (bf16[2,64,2048]{2,1,0:T(8,128)(2,1)}, bf16[2,64,2048]{2,1,0:T(8,128)(2,1)}, u32[]{:S(2)}, u32[]{:S(2)}) collective-permute-start(bf16[2,64,2048]{2,1,0:T(8,128)(2,1)} %pad_maximum_fusion), channel_id=1, source_target_pairs={{0,5},{1,6},{2,7},{3,8},{4,9},{5,10},{6,11},{7,12},{8,13},{9,14},{... | collective-permute-start | bytes 1572872 | tf_op jit(solution)/shard_map/ppermute | solution.py:37
  92.0 59.9 %collective-permute-start.4 = (bf16[2,64,2048]{2,1,0:T(8,128)(2,1)}, bf16[2,64,2048]{2,1,0:T(8,128)(2,1)}, u32[]{:S(2)}, u32[]{:S(2)}) collective-permute-start(bf16[2,64,2048]{2,1,0:T(8,128)(2,1)} %pad_maximum_fusion), channel_id=1, source_target_pairs={{0,4},{1,5},{2,6},{3,7},{4,8},{5,9},{6,10},{7,11},{8,12},{9,13},{1... | collective-permute-start | bytes 1572872 | tf_op jit(solution)/shard_map/ppermute | solution.py:37
  95.8 56.1 %copy-start.4 = (bf16[2,64,2048]{2,1,0:T(8,128)(2,1)}, bf16[2,64,2048]{2,1,0:T(8,128)(2,1)S(1)}, u32[]{:S(2)}) copy-start(bf16[2,64,2048]{2,1,0:T(8,128)(2,1)S(1)} %collective-permute-done.refs_0_) | copy-start | bytes 1572868
  95.8 56.0 %collective-permute-start.5 = (bf16[2,64,2048]{2,1,0:T(8,128)(2,1)S(1)}, bf16[2,64,2048]{2,1,0:T(8,128)(2,1)S(1)}, u32[]{:S(2)}, u32[]{:S(2)}) collective-permute-start(bf16[2,64,2048]{2,1,0:T(8,128)(2,1)S(1)} %copy-done.3), channel_id=1, source_target_pairs={{0,3},{1,4},{2,5},{3,6},{4,7},{5,8},{6,9},{7,10},{8,11},{9,12},{10... | collective-permute-start | bytes 1572872 | tf_op jit(solution)/shard_map/ppermute | solution.py:37
  100.8 15.3 %copy-start.5 = (bf16[2,64,2048]{2,1,0:T(8,128)(2,1)}, bf16[2,64,2048]{2,1,0:T(8,128)(2,1)S(1)}, u32[]{:S(2)}) copy-start(bf16[2,64,2048]{2,1,0:T(8,128)(2,1)S(1)} %collective-permute-done.1.refs_1_) | copy-start | bytes 1572868
  100.9 51.0 %collective-permute-start.6 = (bf16[2,64,2048]{2,1,0:T(8,128)(2,1)S(1)}, bf16[2,64,2048]{2,1,0:T(8,128)(2,1)S(1)}, u32[]{:S(2)}, u32[]{:S(2)}) collective-permute-start(bf16[2,64,2048]{2,1,0:T(8,128)(2,1)S(1)} %copy-done.3), channel_id=1, source_target_pairs={{0,2},{1,3},{2,4},{3,5},{4,6},{5,7},{6,8},{7,9},{8,10},{9,11},{10,... | collective-permute-start | bytes 1572872 | tf_op jit(solution)/shard_map/ppermute | solution.py:37
  108.9 7.3 %copy-start.6 = (bf16[2,64,2048]{2,1,0:T(8,128)(2,1)}, bf16[2,64,2048]{2,1,0:T(8,128)(2,1)S(1)}, u32[]{:S(2)}) copy-start(bf16[2,64,2048]{2,1,0:T(8,128)(2,1)S(1)} %collective-permute-done.2.refs_2_) | copy-start | bytes 1572868
  108.9 43.0 %collective-permute-start.7 = (bf16[2,64,2048]{2,1,0:T(8,128)(2,1)S(1)}, bf16[2,64,2048]{2,1,0:T(8,128)(2,1)S(1)}, u32[]{:S(2)}, u32[]{:S(2)}) collective-permute-start(bf16[2,64,2048]{2,1,0:T(8,128)(2,1)S(1)} %copy-done.3), channel_id=1, source_target_pairs={{0,1},{1,2},{2,3},{3,4},{4,5},{5,6},{6,7},{7,8},{8,9},{9,10},{10,1... | collective-permute-start | bytes 1572872 | tf_op jit(solution)/shard_map/ppermute | solution.py:37
  117.3 33.7 %all-to-all-start.3 = ((bf16[8,64,256]{2,1,0:T(8,128)(2,1)}), bf16[8,64,256]{2,1,0:T(8,128)(2,1)S(1)}, u32[]{:S(2)}, u32[]{:S(2)}) async-start(bf16[8,64,256]{2,1,0:T(8,128)(2,1)} %reshape.81), calls=%async_computation.3 | async-start | bytes 524288 | tf_op jit(solution)/shard_map/all_to_all | solution.py:158
  151.8 1.0 copy-start.8
  151.9 1.1 copy-start.9
  (1 other events, 0.8 us)

commit v6 on v5

--- a/solution.py
+++ b/solution.py
@@ -105,9 +105,10 @@
     held = lax.all_to_all(dealt, "z", split_axis=1, concat_axis=1, tiled=True)
     running = jnp.cumsum(held, axis=1)
     line_total = running[:, -1]
-    along_y = lax.all_gather(line_total, "y")
-    y_before = jnp.arange(along_y.shape[0]) < lax.axis_index("y")
-    lines_before = jnp.sum(jnp.where(y_before[:, None, None, None], along_y, 0.0), axis=0)
+    lines = line_total
+    for level in range((lax.axis_size("y") - 1).bit_length()):
+        lines = lines + passed_along(lines, "y", 1 << level)
+    lines_before = lines - line_total
     prefix = running - held + lines_before[:, None]
     back = lax.all_to_all(prefix, "z", split_axis=1, concat_axis=1, tiled=True)
     return back.reshape(heads, feats, width)

time: 164 us -> 165 us (level)
  blocking collectives: 18.3 us -> 0 us
  waiting for transfers between devices: 41 us -> 58.9 us
  starting transfers between devices: 72.5 us -> 74.8 us
    all_gather x1 -> x0, blocking collectives: 18.3 us -> none  [groups_before(): along_y = lax.all_gather(line_total, 'y')]
    ppermute x8 -> x11, waiting for transfers between devices: 5.21 us -> 16.9 us  [passed_along(): return lax.ppermute(shard, axis, pairs)]
    ppermute x8 -> x11, starting transfers between devices: 37.6 us -> 42.3 us  [passed_along(): return lax.ppermute(shard, axis, pairs)]
    all_to_all x1, waiting for transfers between devices: 17.4 us -> 20.9 us  [linear_heads(): back = lax.all_to_all(out, GROUP, split_axis=0, concat_axis=2, tiled=True)]
    all_to_all x1, starting transfers between devices: 16.3 us -> 14.1 us  [linear_heads(): back = lax.all_to_all(out, GROUP, split_axis=0, concat_axis=2, tiled=True)]
    unnamed x29 -> x27, local copies, waits for them, and re-layouts: 3.62 us -> 3.6 us
  transfers between devices with their start and end apart: 12 -> 15, of which waited for: 5 -> 8; matrix products, arithmetic and copies ran while one was open for 7% -> 6% of each run, Pallas kernels for 0% -> 0%
where the time goes in v6:
time: 165 us; the launch traced here: 164 us
  starting transfers between devices  74.8 us (45%)
  waiting for transfers between devices  58.9 us (36%)
  Pallas kernels  10.5 us (6%)
  matrix products  8.92 us (5%)
  local copies, waits for them, and re-layouts  7.23 us (4%)
  other arithmetic  2.87 us (2%)
    ppermute x11, starting transfers between devices, passed_along(): return lax.ppermute(shard, axis, pairs)  42.3 us
    all_to_all x1, waiting for transfers between devices, linear_heads(): back = lax.all_to_all(out, GROUP, split_axis=0, concat_axis=2, tiled=True)  20.9 us
    ppermute x11, waiting for transfers between devices, passed_along(): return lax.ppermute(shard, axis, pairs)  16.9 us
    all_to_all x1, starting transfers between devices, linear_heads(): back = lax.all_to_all(out, GROUP, split_axis=0, concat_axis=2, tiled=True)  14.1 us
    pallas_call x1, Pallas kernels, window_attention(): pl.pallas_call(window_kernel, out_shape=jax.ShapeDtypeStruct((rows, chann...  10.5 us
    all_to_all x1, starting transfers between devices, groups_before(): held = lax.all_to_all(dealt, 'z', split_axis=1, concat_axis=1, tiled=True)  10 us
    all_to_all x1, waiting for transfers between devices, linear_heads(): got = lax.all_to_all(packed, GROUP, split_axis=1, concat_axis=0, tiled=True)  7.88 us
    all_to_all x1, waiting for transfers between devices, groups_before(): held = lax.all_to_all(dealt, 'z', split_axis=1, concat_axis=1, tiled=True)  7.64 us
  transfers between devices with their start and end apart: 15, of which 8 were waited for; matrix products, arithmetic and copies ran while one was open for 6% of the time, Pallas kernels for 0%

profile of v6, /device:TPU:33, one launch (start us, length us, event | category | flops | bytes accessed | tf_op | source)
XLA Modules:
  0.0 164.3 jit_solution(225035550697257012)
XLA Ops:
  4.7 5.0 %all-to-all-start = ((bf16[64,8,320]{2,0,1:T(8,128)(2,1)}), bf16[64,8,320]{2,0,1:T(8,128)(2,1)S(1)}, u32[]{:S(2)}, u32[]{:S(2)}) async-start(bf16[64,8,320]{2,0,1:T(8,128)(2,1)} %pad_maximum_fusion.1), calls=%async_computation | async-start | bytes 786432 | tf_op jit(solution)/shard_map/all_to_all | solution.py:130
  9.7 7.9 %all-to-all-done = bf16[64,8,320]{2,0,1:T(8,128)(2,1)S(1)} async-done(((bf16[64,8,320]{2,0,1:T(8,128)(2,1)}), bf16[64,8,320]{2,0,1:T(8,128)(2,1)S(1)}, u32[]{:S(2)}, u32[]{:S(2)}) %all-to-all-start) | async-done | bytes 327712 | tf_op jit(solution)/shard_map/all_to_all | solution.py:130
  20.9 10.0 %all-to-all-start.1 = ((f32[2,8,20,128]{3,0,2,1:T(2,128)}), f32[2,8,20,128]{3,0,2,1:T(2,128)S(1)}, u32[]{:S(2)}, u32[]{:S(2)}) async-start(f32[2,8,20,128]{3,0,2,1:T(2,128)} %bitcast.12), calls=%async_computation.1 | async-start | bytes 327680 | tf_op jit(solution)/shard_map/all_to_all | solution.py:105
  31.9 7.6 %all-to-all-done.1 = f32[2,8,20,128]{3,0,2,1:T(2,128)S(1)} async-done(((f32[2,8,20,128]{3,0,2,1:T(2,128)}), f32[2,8,20,128]{3,0,2,1:T(2,128)S(1)}, u32[]{:S(2)}, u32[]{:S(2)}) %all-to-all-start.1) | async-done | bytes 163872 | tf_op jit(solution)/shard_map/all_to_all | solution.py:105
  39.6 2.3 %collective-permute-start = (f32[2,20,128]{2,0,1:T(2,128)S(1)}, f32[2,20,128]{2,0,1:T(2,128)S(1)}, u32[]{:S(2)}, u32[]{:S(2)}) collective-permute-start(f32[2,20,128]{2,0,1:T(2,128)S(1)} %slice_bitcast_fusion), channel_id=1, source_target_pairs={{0,64},{64,128},{128,192},{192,256},{256,320},{320,384},{384,448},... | collective-permute-start | bytes 61448 | tf_op jit(solution)/shard_map/ppermute | solution.py:37
  42.4 3.0 %collective-permute-done = f32[2,20,128]{2,0,1:T(2,128)S(1)} collective-permute-done((f32[2,20,128]{2,0,1:T(2,128)S(1)}, f32[2,20,128]{2,0,1:T(2,128)S(1)}, u32[]{:S(2)}, u32[]{:S(2)}) %collective-permute-start) | collective-permute-done | bytes 20512 | tf_op jit(solution)/shard_map/ppermute | solution.py:37
  45.4 1.9 %collective-permute-start.1 = (f32[2,20,128]{2,0,1:T(2,128)S(1)}, f32[2,20,128]{2,0,1:T(2,128)S(1)}, u32[]{:S(2)}, u32[]{:S(2)}) collective-permute-start(f32[2,20,128]{2,0,1:T(2,128)S(1)} %fusion.28), channel_id=1, source_target_pairs={{0,128},{64,192},{128,256},{192,320},{256,384},{320,448},{1,129},{... | collective-permute-start | bytes 61448 | tf_op jit(solution)/shard_map/ppermute | solution.py:37
  47.3 4.7 %collective-permute-done.1 = f32[2,20,128]{2,0,1:T(2,128)S(1)} collective-permute-done((f32[2,20,128]{2,0,1:T(2,128)S(1)}, f32[2,20,128]{2,0,1:T(2,128)S(1)}, u32[]{:S(2)}, u32[]{:S(2)}) %collective-permute-start.1) | collective-permute-done | bytes 20512 | tf_op jit(solution)/shard_map/ppermute | solution.py:37
  54.8 5.7 %collective-permute-done.2 = f32[2,20,128]{2,0,1:T(2,128)S(1)} collective-permute-done((f32[2,20,128]{2,0,1:T(2,128)S(1)}, f32[2,20,128]{2,0,1:T(2,128)S(1)}, u32[]{:S(2)}, u32[]{:S(2)}) %collective-permute-start.2) | collective-permute-done | bytes 20512 | tf_op jit(solution)/shard_map/ppermute | solution.py:37
  61.2 3.4 %all-to-all-start.2 = ((f32[2,8,20,128]{3,0,2,1:T(2,128)}), f32[2,8,20,128]{3,0,2,1:T(2,128)S(1)}, u32[]{:S(2)}, u32[]{:S(2)}) async-start(f32[2,8,20,128]{3,0,2,1:T(2,128)} %bitcast.53), calls=%async_computation.2 | async-start | bytes 327680 | tf_op jit(solution)/shard_map/all_to_all | solution.py:113
  64.6 2.6 %fusion = f32[2,128,512]{2,1,0:T(8,128)} fusion(bf16[512,2,128]{0,2,1:T(8,128)(2,1)S(1)} %bitcast.61, f32[2,512,512]{2,1,0:T(8,128)S(1)} %fusion.31, pred[512,512]{1,0:T(8,128)(4,1)S(1)} %iota_compare_fusion), kind=kOutput, calls=%fused_computation | convolution fusion | flops 808452096 | bytes 3145728 | tf_op jit(solution)/shard_map/hij,jhe->ihe/dot_general | solution.py:151
  67.2 5.6 %all-to-all-done.2 = f32[2,8,20,128]{3,0,2,1:T(2,128)S(1)} async-done(((f32[2,8,20,128]{3,0,2,1:T(2,128)}), f32[2,8,20,128]{3,0,2,1:T(2,128)S(1)}, u32[]{:S(2)}, u32[]{:S(2)}) %all-to-all-start.2) | async-done | bytes 163872 | tf_op jit(solution)/shard_map/all_to_all | solution.py:113
  72.8 2.2 %collective-permute-start.3 = (bf16[2,64,2048]{2,1,0:T(8,128)(2,1)}, bf16[2,64,2048]{2,1,0:T(8,128)(2,1)S(1)}, u32[]{:S(2)}, u32[]{:S(2)}) collective-permute-start(bf16[2,64,2048]{2,1,0:T(8,128)(2,1)} %pad_maximum_fusion), channel_id=1, source_target_pairs={{0,8},{1,9},{2,10},{3,11},{4,12},{5,13},{6,14},{7,15},{8,16},{9,17... | collective-permute-start | bytes 1572872 | tf_op jit(solution)/shard_map/ppermute | solution.py:37
  75.0 9.7 %collective-permute-start.4 = (bf16[2,64,2048]{2,1,0:T(8,128)(2,1)}, bf16[2,64,2048]{2,1,0:T(8,128)(2,1)S(1)}, u32[]{:S(2)}, u32[]{:S(2)}) collective-permute-start(bf16[2,64,2048]{2,1,0:T(8,128)(2,1)} %pad_maximum_fusion), channel_id=1, source_target_pairs={{0,7},{1,8},{2,9},{3,10},{4,11},{5,12},{6,13},{7,14},{8,15},{9,16}... | collective-permute-start | bytes 1572872 | tf_op jit(solution)/shard_map/ppermute | solution.py:37
  84.6 3.4 %collective-permute-start.5 = (bf16[2,64,2048]{2,1,0:T(8,128)(2,1)}, bf16[2,64,2048]{2,1,0:T(8,128)(2,1)S(1)}, u32[]{:S(2)}, u32[]{:S(2)}) collective-permute-start(bf16[2,64,2048]{2,1,0:T(8,128)(2,1)} %pad_maximum_fusion), channel_id=1, source_target_pairs={{0,6},{1,7},{2,8},{3,9},{4,10},{5,11},{6,12},{7,13},{8,14},{9,15},... | collective-permute-start | bytes 1572872 | tf_op jit(solution)/shard_map/ppermute | solution.py:37
  88.8 1.9 %collective-permute-start.6 = (bf16[2,64,2048]{2,1,0:T(8,128)(2,1)}, bf16[2,64,2048]{2,1,0:T(8,128)(2,1)S(1)}, u32[]{:S(2)}, u32[]{:S(2)}) collective-permute-start(bf16[2,64,2048]{2,1,0:T(8,128)(2,1)} %pad_maximum_fusion), channel_id=1, source_target_pairs={{0,5},{1,6},{2,7},{3,8},{4,9},{5,10},{6,11},{7,12},{8,13},{9,14},{... | collective-permute-start | bytes 1572872 | tf_op jit(solution)/shard_map/ppermute | solution.py:37
  90.7 2.0 %collective-permute-start.7 = (bf16[2,64,2048]{2,1,0:T(8,128)(2,1)}, bf16[2,64,2048]{2,1,0:T(8,128)(2,1)S(1)}, u32[]{:S(2)}, u32[]{:S(2)}) collective-permute-start(bf16[2,64,2048]{2,1,0:T(8,128)(2,1)} %pad_maximum_fusion), channel_id=1, source_target_pairs={{0,4},{1,5},{2,6},{3,7},{4,8},{5,9},{6,10},{7,11},{8,12},{9,13},{1... | collective-permute-start | bytes 1572872 | tf_op jit(solution)/shard_map/ppermute | solution.py:37
  94.5 4.7 %collective-permute-start.8 = (bf16[2,64,2048]{2,1,0:T(8,128)(2,1)S(1)}, bf16[2,64,2048]{2,1,0:T(8,128)(2,1)S(1)}, u32[]{:S(2)}, u32[]{:S(2)}) collective-permute-start(bf16[2,64,2048]{2,1,0:T(8,128)(2,1)S(1)} %copy-done.3), channel_id=1, source_target_pairs={{0,3},{1,4},{2,5},{3,6},{4,7},{5,8},{6,9},{7,10},{8,11},{9,12},{10... | collective-permute-start | bytes 1572872 | tf_op jit(solution)/shard_map/ppermute | solution.py:37
  99.3 3.4 %collective-permute-start.9 = (bf16[2,64,2048]{2,1,0:T(8,128)(2,1)S(1)}, bf16[2,64,2048]{2,1,0:T(8,128)(2,1)}, u32[]{:S(2)}, u32[]{:S(2)}) collective-permute-start(bf16[2,64,2048]{2,1,0:T(8,128)(2,1)S(1)} %copy-done.3), channel_id=1, source_target_pairs={{0,2},{1,3},{2,4},{3,5},{4,6},{5,7},{6,8},{7,9},{8,10},{9,11},{10,... | collective-permute-start | bytes 1572872 | tf_op jit(solution)/shard_map/ppermute | solution.py:37
  102.7 3.6 %collective-permute-done.5.refs_2_ = bf16[2,64,2048]{2,1,0:T(8,128)(2,1)S(1)} collective-permute-done((bf16[2,64,2048]{2,1,0:T(8,128)(2,1)}, bf16[2,64,2048]{2,1,0:T(8,128)(2,1)S(1)}, u32[]{:S(2)}, u32[]{:S(2)}) %collective-permute-start.5) | collective-permute-done | bytes 524320 | tf_op jit(solution)/shard_map/ppermute | solution.py:37
  106.3 9.5 %collective-permute-start.10 = (bf16[2,64,2048]{2,1,0:T(8,128)(2,1)S(1)}, bf16[2,64,2048]{2,1,0:T(8,128)(2,1)}, u32[]{:S(2)}, u32[]{:S(2)}) collective-permute-start(bf16[2,64,2048]{2,1,0:T(8,128)(2,1)S(1)} %copy-done.3), channel_id=1, source_target_pairs={{0,1},{1,2},{2,3},{3,4},{4,5},{5,6},{6,7},{7,8},{8,9},{9,10},{10,1... | collective-permute-start | bytes 1572872 | tf_op jit(solution)/shard_map/ppermute | solution.py:37
  117.0 14.1 %all-to-all-start.3 = ((bf16[8,64,256]{2,1,0:T(8,128)(2,1)}), bf16[8,64,256]{2,1,0:T(8,128)(2,1)S(1)}, u32[]{:S(2)}, u32[]{:S(2)}) async-start(bf16[8,64,256]{2,1,0:T(8,128)(2,1)} %reshape.77), calls=%async_computation.3 | async-start | bytes 524288 | tf_op jit(solution)/shard_map/all_to_all | solution.py:159
  131.1 20.9 %all-to-all-done.3 = bf16[8,64,256]{2,1,0:T(8,128)(2,1)S(1)} async-done(((bf16[8,64,256]{2,1,0:T(8,128)(2,1)}), bf16[8,64,256]{2,1,0:T(8,128)(2,1)S(1)}, u32[]{:S(2)}, u32[]{:S(2)}) %all-to-all-start.3) | async-done | bytes 262176 | tf_op jit(solution)/shard_map/all_to_all | solution.py:159
  153.8 10.5 %shard_map.122 = bf16[64,2048]{1,0:T(8,128)(2,1)} custom-call(s32[1]{0:T(128)} %bitcast.22.pos_ref, bf16[64,2048]{1,0:T(8,128)(2,1)} %q_ref.1, bf16[64,2048]{1,0:T(8,128)(2,1)} %k_ref.1, bf16[64,2048]{1,0:T(8,128)(2,1)} %v_ref.1, bf16[2,64,2048]{2,1,0:T(8,128)(2,1)} %copy-done.4, bf16[2,64,2048]{2,1,0:T(8,128)(2,1)} %copy-done.5, ...), custom_call_target="tpu_custom_call" | custom-call | tf_op jit(solution)/shard_map/pallas_call | solution.py:91
  (67 shorter events, 17.8 us)
Async XLA Ops:
  0.6 30.3 %copy-start = (f32[2048]{0:T(1024)S(1)}, f32[2048]{0:T(1024)}, u32[]{:S(2)}) copy-start(f32[2048]{0:T(1024)} %param.14) | copy-start | bytes 24580
  2.6 15.5 %copy-start.11 = (f32[17,160,1]{1,0,2:T(8,128)S(1)}, f32[17,160,1]{1,0,2:T(8,128)}, u32[]{:S(2)}) copy-start(f32[17,160,1]{1,0,2:T(8,128)} %constant.68) | copy-start | bytes 32644
  3.7 15.2 %copy-start.10 = (f32[17,160,1]{1,0,2:T(8,128)S(1)}, f32[17,160,1]{1,0,2:T(8,128)}, u32[]{:S(2)}) copy-start(f32[17,160,1]{1,0,2:T(8,128)} %constant.69) | copy-start | bytes 32644
  4.7 12.9 %all-to-all-start = ((bf16[64,8,320]{2,0,1:T(8,128)(2,1)}), bf16[64,8,320]{2,0,1:T(8,128)(2,1)S(1)}, u32[]{:S(2)}, u32[]{:S(2)}) async-start(bf16[64,8,320]{2,0,1:T(8,128)(2,1)} %pad_maximum_fusion.1), calls=%async_computation | async-start | bytes 786432 | tf_op jit(solution)/shard_map/all_to_all | solution.py:130
  18.0 12.9 %copy-start.1 = (bf16[64,2048]{1,0:T(8,128)(2,1)S(1)}, bf16[64,2048]{1,0:T(8,128)(2,1)}, u32[]{:S(2)}) copy-start(bf16[64,2048]{1,0:T(8,128)(2,1)} %k_ref.1) | copy-start | bytes 786436
  18.0 12.9 %copy-start.2 = (bf16[64,2048]{1,0:T(8,128)(2,1)S(1)}, bf16[64,2048]{1,0:T(8,128)(2,1)}, u32[]{:S(2)}) copy-start(bf16[64,2048]{1,0:T(8,128)(2,1)} %v_ref.1) | copy-start | bytes 786436
  20.9 18.7 %all-to-all-start.1 = ((f32[2,8,20,128]{3,0,2,1:T(2,128)}), f32[2,8,20,128]{3,0,2,1:T(2,128)S(1)}, u32[]{:S(2)}, u32[]{:S(2)}) async-start(f32[2,8,20,128]{3,0,2,1:T(2,128)} %bitcast.12), calls=%async_computation.1 | async-start | bytes 327680 | tf_op jit(solution)/shard_map/all_to_all | solution.py:105
  39.6 5.7 %collective-permute-start = (f32[2,20,128]{2,0,1:T(2,128)S(1)}, f32[2,20,128]{2,0,1:T(2,128)S(1)}, u32[]{:S(2)}, u32[]{:S(2)}) collective-permute-start(f32[2,20,128]{2,0,1:T(2,128)S(1)} %slice_bitcast_fusion), channel_id=1, source_target_pairs={{0,64},{64,128},{128,192},{192,256},{256,320},{320,384},{384,448},... | collective-permute-start | bytes 61448 | tf_op jit(solution)/shard_map/ppermute | solution.py:37
  45.4 6.6 %collective-permute-start.1 = (f32[2,20,128]{2,0,1:T(2,128)S(1)}, f32[2,20,128]{2,0,1:T(2,128)S(1)}, u32[]{:S(2)}, u32[]{:S(2)}) collective-permute-start(f32[2,20,128]{2,0,1:T(2,128)S(1)} %fusion.28), channel_id=1, source_target_pairs={{0,128},{64,192},{128,256},{192,320},{256,384},{320,448},{1,129},{... | collective-permute-start | bytes 61448 | tf_op jit(solution)/shard_map/ppermute | solution.py:37
  52.0 8.4 %collective-permute-start.2 = (f32[2,20,128]{2,0,1:T(2,128)S(1)}, f32[2,20,128]{2,0,1:T(2,128)S(1)}, u32[]{:S(2)}, u32[]{:S(2)}) collective-permute-start(f32[2,20,128]{2,0,1:T(2,128)S(1)} %add.64), channel_id=1, source_target_pairs={{0,256},{64,320},{128,384},{192,448},{1,257},{65,321},{129,385},{1... | collective-permute-start | bytes 61448 | tf_op jit(solution)/shard_map/ppermute | solution.py:37
  61.2 11.6 %all-to-all-start.2 = ((f32[2,8,20,128]{3,0,2,1:T(2,128)}), f32[2,8,20,128]{3,0,2,1:T(2,128)S(1)}, u32[]{:S(2)}, u32[]{:S(2)}) async-start(f32[2,8,20,128]{3,0,2,1:T(2,128)} %bitcast.53), calls=%async_computation.2 | async-start | bytes 327680 | tf_op jit(solution)/shard_map/all_to_all | solution.py:113
  67.2 27.4 %copy-start.3 = (bf16[2,64,2048]{2,1,0:T(8,128)(2,1)S(1)}, bf16[2,64,2048]{2,1,0:T(8,128)(2,1)}, u32[]{:S(2)}) copy-start(bf16[2,64,2048]{2,1,0:T(8,128)(2,1)} %pad_maximum_fusion) | copy-start | bytes 1572868
  72.8 21.7 %collective-permute-start.3 = (bf16[2,64,2048]{2,1,0:T(8,128)(2,1)}, bf16[2,64,2048]{2,1,0:T(8,128)(2,1)S(1)}, u32[]{:S(2)}, u32[]{:S(2)}) collective-permute-start(bf16[2,64,2048]{2,1,0:T(8,128)(2,1)} %pad_maximum_fusion), channel_id=1, source_target_pairs={{0,8},{1,9},{2,10},{3,11},{4,12},{5,13},{6,14},{7,15},{8,16},{9,17... | collective-permute-start | bytes 1572872 | tf_op jit(solution)/shard_map/ppermute | solution.py:37
  75.0 24.3 %collective-permute-start.4 = (bf16[2,64,2048]{2,1,0:T(8,128)(2,1)}, bf16[2,64,2048]{2,1,0:T(8,128)(2,1)S(1)}, u32[]{:S(2)}, u32[]{:S(2)}) collective-permute-start(bf16[2,64,2048]{2,1,0:T(8,128)(2,1)} %pad_maximum_fusion), channel_id=1, source_target_pairs={{0,7},{1,8},{2,9},{3,10},{4,11},{5,12},{6,13},{7,14},{8,15},{9,16}... | collective-permute-start | bytes 1572872 | tf_op jit(solution)/shard_map/ppermute | solution.py:37
  84.6 21.7 %collective-permute-start.5 = (bf16[2,64,2048]{2,1,0:T(8,128)(2,1)}, bf16[2,64,2048]{2,1,0:T(8,128)(2,1)S(1)}, u32[]{:S(2)}, u32[]{:S(2)}) collective-permute-start(bf16[2,64,2048]{2,1,0:T(8,128)(2,1)} %pad_maximum_fusion), channel_id=1, source_target_pairs={{0,6},{1,7},{2,8},{3,9},{4,10},{5,11},{6,12},{7,13},{8,14},{9,15},... | collective-permute-start | bytes 1572872 | tf_op jit(solution)/shard_map/ppermute | solution.py:37
  88.8 63.8 %collective-permute-start.6 = (bf16[2,64,2048]{2,1,0:T(8,128)(2,1)}, bf16[2,64,2048]{2,1,0:T(8,128)(2,1)S(1)}, u32[]{:S(2)}, u32[]{:S(2)}) collective-permute-start(bf16[2,64,2048]{2,1,0:T(8,128)(2,1)} %pad_maximum_fusion), channel_id=1, source_target_pairs={{0,5},{1,6},{2,7},{3,8},{4,9},{5,10},{6,11},{7,12},{8,13},{9,14},{... | collective-permute-start | bytes 1572872 | tf_op jit(solution)/shard_map/ppermute | solution.py:37
  90.7 61.9 %collective-permute-start.7 = (bf16[2,64,2048]{2,1,0:T(8,128)(2,1)}, bf16[2,64,2048]{2,1,0:T(8,128)(2,1)S(1)}, u32[]{:S(2)}, u32[]{:S(2)}) collective-permute-start(bf16[2,64,2048]{2,1,0:T(8,128)(2,1)} %pad_maximum_fusion), channel_id=1, source_target_pairs={{0,4},{1,5},{2,6},{3,7},{4,8},{5,9},{6,10},{7,11},{8,12},{9,13},{1... | collective-permute-start | bytes 1572872 | tf_op jit(solution)/shard_map/ppermute | solution.py:37
  94.5 58.2 %copy-start.4 = (bf16[2,64,2048]{2,1,0:T(8,128)(2,1)}, bf16[2,64,2048]{2,1,0:T(8,128)(2,1)S(1)}, u32[]{:S(2)}) copy-start(bf16[2,64,2048]{2,1,0:T(8,128)(2,1)S(1)} %collective-permute-done.3.refs_0_) | copy-start | bytes 1572868
  94.5 58.1 %collective-permute-start.8 = (bf16[2,64,2048]{2,1,0:T(8,128)(2,1)S(1)}, bf16[2,64,2048]{2,1,0:T(8,128)(2,1)S(1)}, u32[]{:S(2)}, u32[]{:S(2)}) collective-permute-start(bf16[2,64,2048]{2,1,0:T(8,128)(2,1)S(1)} %copy-done.3), channel_id=1, source_target_pairs={{0,3},{1,4},{2,5},{3,6},{4,7},{5,8},{6,9},{7,10},{8,11},{9,12},{10... | collective-permute-start | bytes 1572872 | tf_op jit(solution)/shard_map/ppermute | solution.py:37
  99.3 16.5 %copy-start.5 = (bf16[2,64,2048]{2,1,0:T(8,128)(2,1)}, bf16[2,64,2048]{2,1,0:T(8,128)(2,1)S(1)}, u32[]{:S(2)}) copy-start(bf16[2,64,2048]{2,1,0:T(8,128)(2,1)S(1)} %collective-permute-done.4.refs_1_) | copy-start | bytes 1572868
  99.3 53.4 %collective-permute-start.9 = (bf16[2,64,2048]{2,1,0:T(8,128)(2,1)S(1)}, bf16[2,64,2048]{2,1,0:T(8,128)(2,1)}, u32[]{:S(2)}, u32[]{:S(2)}) collective-permute-start(bf16[2,64,2048]{2,1,0:T(8,128)(2,1)S(1)} %copy-done.3), channel_id=1, source_target_pairs={{0,2},{1,3},{2,4},{3,5},{4,6},{5,7},{6,8},{7,9},{8,10},{9,11},{10,... | collective-permute-start | bytes 1572872 | tf_op jit(solution)/shard_map/ppermute | solution.py:37
  106.3 9.5 %copy-start.6 = (bf16[2,64,2048]{2,1,0:T(8,128)(2,1)}, bf16[2,64,2048]{2,1,0:T(8,128)(2,1)S(1)}, u32[]{:S(2)}) copy-start(bf16[2,64,2048]{2,1,0:T(8,128)(2,1)S(1)} %collective-permute-done.5.refs_2_) | copy-start | bytes 1572868
  106.3 46.4 %collective-permute-start.10 = (bf16[2,64,2048]{2,1,0:T(8,128)(2,1)S(1)}, bf16[2,64,2048]{2,1,0:T(8,128)(2,1)}, u32[]{:S(2)}, u32[]{:S(2)}) collective-permute-start(bf16[2,64,2048]{2,1,0:T(8,128)(2,1)S(1)} %copy-done.3), channel_id=1, source_target_pairs={{0,1},{1,2},{2,3},{3,4},{4,5},{5,6},{6,7},{7,8},{8,9},{9,10},{10,1... | collective-permute-start | bytes 1572872 | tf_op jit(solution)/shard_map/ppermute | solution.py:37
  117.0 34.9 %all-to-all-start.3 = ((bf16[8,64,256]{2,1,0:T(8,128)(2,1)}), bf16[8,64,256]{2,1,0:T(8,128)(2,1)S(1)}, u32[]{:S(2)}, u32[]{:S(2)}) async-start(bf16[8,64,256]{2,1,0:T(8,128)(2,1)} %reshape.77), calls=%async_computation.3 | async-start | bytes 524288 | tf_op jit(solution)/shard_map/all_to_all | solution.py:159
  (3 other events, 2.9 us)

commit v7 on v5

--- a/solution.py
+++ b/solution.py
@@ -99,18 +99,14 @@
 
 
 def groups_before(total):
-    z_count = lax.axis_size("z")
-    heads, feats, width = total.shape
-    dealt = total.reshape(heads, z_count, feats // z_count, width)
-    held = lax.all_to_all(dealt, "z", split_axis=1, concat_axis=1, tiled=True)
-    running = jnp.cumsum(held, axis=1)
-    line_total = running[:, -1]
-    along_y = lax.all_gather(line_total, "y")
-    y_before = jnp.arange(along_y.shape[0]) < lax.axis_index("y")
-    lines_before = jnp.sum(jnp.where(y_before[:, None, None, None], along_y, 0.0), axis=0)
-    prefix = running - held + lines_before[:, None]
-    back = lax.all_to_all(prefix, "z", split_axis=1, concat_axis=1, tiled=True)
-    return back.reshape(heads, feats, width)
+    outer = ("y", "z")
+    outer_count = lax.axis_size(outer)
+    shape = total.shape
+    dealt = total.reshape(outer_count, -1, shape[-1])
+    held = lax.all_to_all(dealt, outer, split_axis=0, concat_axis=0, tiled=True)
+    prefix = jnp.cumsum(held, axis=0) - held
+    back = lax.all_to_all(prefix, outer, split_axis=0, concat_axis=0, tiled=True)
+    return back.reshape(shape)
 
 
 def linear_heads(linear_query, linear_key, linear_value, lin_gain, held):

time: 164 us -> 159 us (0.970)
  the two profiles are of different devices: /device:TPU:33 before, /device:TPU:17 now
where the time goes in v7:
time: 159 us; the launch traced here: 158 us
  starting transfers between devices  64.5 us (41%)
  waiting for transfers between devices  63.1 us (40%)
  Pallas kernels  10.5 us (7%)
  matrix products  8.11 us (5%)
  local copies, waits for them, and re-layouts  7.23 us (5%)
  other arithmetic  3.56 us (2%)
    ppermute x8, starting transfers between devices, passed_along(): return lax.ppermute(shard, axis, pairs)  26.6 us
    all_to_all x1, waiting for transfers between devices, linear_heads(): back = lax.all_to_all(out, GROUP, split_axis=0, concat_axis=2, tiled=True)  24.6 us
    all_to_all x1, starting transfers between devices, groups_before(): held = lax.all_to_all(dealt, outer, split_axis=0, concat_axis=0, tiled=True)  16 us
    all_to_all x1, waiting for transfers between devices, groups_before(): held = lax.all_to_all(dealt, outer, split_axis=0, concat_axis=0, tiled=True)  13 us
    ppermute x8, waiting for transfers between devices, passed_along(): return lax.ppermute(shard, axis, pairs)  11.7 us
    all_to_all x1, starting transfers between devices, linear_heads(): back = lax.all_to_all(out, GROUP, split_axis=0, concat_axis=2, tiled=True)  11.6 us
    pallas_call x1, Pallas kernels, window_attention(): pl.pallas_call(window_kernel, out_shape=jax.ShapeDtypeStruct((rows, chann...  10.5 us
    all_to_all x1, waiting for transfers between devices, groups_before(): lax.all_to_all(prefix, outer, split_axis=0, concat_axis=0, tiled=True)  7.53 us
  transfers between devices with their start and end apart: 12, of which 6 were waited for; matrix products, arithmetic and copies ran while one was open for 6% of the time, Pallas kernels for 0%

profile of v7, /device:TPU:17, one launch (start us, length us, event | category | flops | bytes accessed | tf_op | source)
XLA Modules:
  0.0 158.0 jit_solution(4290132151467347733)
XLA Ops:
  0.7 1.0 copy.42
  1.7 0.9 copy.27
  3.7 1.0 pad_maximum_fusion.1
  4.7 5.1 %all-to-all-start = ((bf16[64,8,320]{2,0,1:T(8,128)(2,1)}), bf16[64,8,320]{2,0,1:T(8,128)(2,1)S(1)}, u32[]{:S(2)}, u32[]{:S(2)}) async-start(bf16[64,8,320]{2,0,1:T(8,128)(2,1)} %pad_maximum_fusion.1), calls=%async_computation | async-start | bytes 786432 | tf_op jit(solution)/shard_map/all_to_all | solution.py:125
  11.5 6.3 %all-to-all-done = bf16[64,8,320]{2,0,1:T(8,128)(2,1)S(1)} async-done(((bf16[64,8,320]{2,0,1:T(8,128)(2,1)}), bf16[64,8,320]{2,0,1:T(8,128)(2,1)S(1)}, u32[]{:S(2)}, u32[]{:S(2)}) %all-to-all-start) | async-done | bytes 327712 | tf_op jit(solution)/shard_map/all_to_all | solution.py:125
  21.1 16.0 %all-to-all-start.1 = ((f32[64,5,128]{2,1,0:T(8,128)}), f32[64,5,128]{2,1,0:T(8,128)S(1)}, u32[]{:S(2)}, u32[]{:S(2)}) async-start(f32[64,5,128]{2,1,0:T(8,128)} %reshape.73), calls=%async_computation.1 | async-start | bytes 524288 | tf_op jit(solution)/shard_map/all_to_all | solution.py:106
  37.6 13.0 %all-to-all-done.1 = f32[64,5,128]{2,1,0:T(8,128)S(1)} async-done(((f32[64,5,128]{2,1,0:T(8,128)}), f32[64,5,128]{2,1,0:T(8,128)S(1)}, u32[]{:S(2)}, u32[]{:S(2)}) %all-to-all-start.1) | async-done | bytes 163872 | tf_op jit(solution)/shard_map/all_to_all | solution.py:106
  51.4 5.1 %all-to-all-start.2 = ((f32[64,5,128]{2,1,0:T(8,128)}), f32[64,5,128]{2,1,0:T(8,128)S(1)}, u32[]{:S(2)}, u32[]{:S(2)}) async-start(f32[64,5,128]{2,1,0:T(8,128)} %reduce-window_subtract_fusion), calls=%async_computation.2 | async-start | bytes 524288 | tf_op jit(solution)/shard_map/all_to_all | solution.py:108
  57.3 3.5 %fusion = f32[2,128,512]{2,1,0:T(8,128)} fusion(bf16[512,2,128]{0,2,1:T(8,128)(2,1)S(1)} %bitcast.49, f32[2,512,512]{2,1,0:T(8,128)S(1)} %fusion.28, pred[512,512]{1,0:T(8,128)(4,1)} %iota_compare_fusion), kind=kOutput, calls=%fused_computation | convolution fusion | flops 808452096 | bytes 3145728 | tf_op jit(solution)/shard_map/hij,jhe->ihe/dot_general | solution.py:146
  60.8 7.5 %all-to-all-done.2 = f32[64,5,128]{2,1,0:T(8,128)S(1)} async-done(((f32[64,5,128]{2,1,0:T(8,128)}), f32[64,5,128]{2,1,0:T(8,128)S(1)}, u32[]{:S(2)}, u32[]{:S(2)}) %all-to-all-start.2) | async-done | bytes 163872 | tf_op jit(solution)/shard_map/all_to_all | solution.py:108
  68.4 2.3 %collective-permute-start = (bf16[2,64,2048]{2,1,0:T(8,128)(2,1)}, bf16[2,64,2048]{2,1,0:T(8,128)(2,1)S(1)}, u32[]{:S(2)}, u32[]{:S(2)}) collective-permute-start(bf16[2,64,2048]{2,1,0:T(8,128)(2,1)} %pad_maximum_fusion), channel_id=1, source_target_pairs={{0,8},{1,9},{2,10},{3,11},{4,12},{5,13},{6,14},{7,15},{8,16},{9,17... | collective-permute-start | bytes 1572872 | tf_op jit(solution)/shard_map/ppermute | solution.py:37
  70.7 6.1 %collective-permute-start.1 = (bf16[2,64,2048]{2,1,0:T(8,128)(2,1)}, bf16[2,64,2048]{2,1,0:T(8,128)(2,1)S(1)}, u32[]{:S(2)}, u32[]{:S(2)}) collective-permute-start(bf16[2,64,2048]{2,1,0:T(8,128)(2,1)} %pad_maximum_fusion), channel_id=1, source_target_pairs={{0,7},{1,8},{2,9},{3,10},{4,11},{5,12},{6,13},{7,14},{8,15},{9,16}... | collective-permute-start | bytes 1572872 | tf_op jit(solution)/shard_map/ppermute | solution.py:37
  76.8 3.9 %collective-permute-start.2 = (bf16[2,64,2048]{2,1,0:T(8,128)(2,1)}, bf16[2,64,2048]{2,1,0:T(8,128)(2,1)S(1)}, u32[]{:S(2)}, u32[]{:S(2)}) collective-permute-start(bf16[2,64,2048]{2,1,0:T(8,128)(2,1)} %pad_maximum_fusion), channel_id=1, source_target_pairs={{0,6},{1,7},{2,8},{3,9},{4,10},{5,11},{6,12},{7,13},{8,14},{9,15},... | collective-permute-start | bytes 1572872 | tf_op jit(solution)/shard_map/ppermute | solution.py:37
  81.4 1.9 %collective-permute-start.3 = (bf16[2,64,2048]{2,1,0:T(8,128)(2,1)}, bf16[2,64,2048]{2,1,0:T(8,128)(2,1)S(1)}, u32[]{:S(2)}, u32[]{:S(2)}) collective-permute-start(bf16[2,64,2048]{2,1,0:T(8,128)(2,1)} %pad_maximum_fusion), channel_id=1, source_target_pairs={{0,5},{1,6},{2,7},{3,8},{4,9},{5,10},{6,11},{7,12},{8,13},{9,14},{... | collective-permute-start | bytes 1572872 | tf_op jit(solution)/shard_map/ppermute | solution.py:37
  83.3 1.9 %collective-permute-start.4 = (bf16[2,64,2048]{2,1,0:T(8,128)(2,1)}, bf16[2,64,2048]{2,1,0:T(8,128)(2,1)S(1)}, u32[]{:S(2)}, u32[]{:S(2)}) collective-permute-start(bf16[2,64,2048]{2,1,0:T(8,128)(2,1)} %pad_maximum_fusion), channel_id=1, source_target_pairs={{0,4},{1,5},{2,6},{3,7},{4,8},{5,9},{6,10},{7,11},{8,12},{9,13},{1... | collective-permute-start | bytes 1572872 | tf_op jit(solution)/shard_map/ppermute | solution.py:37
  86.0 4.7 %collective-permute-start.5 = (bf16[2,64,2048]{2,1,0:T(8,128)(2,1)S(1)}, bf16[2,64,2048]{2,1,0:T(8,128)(2,1)S(1)}, u32[]{:S(2)}, u32[]{:S(2)}) collective-permute-start(bf16[2,64,2048]{2,1,0:T(8,128)(2,1)S(1)} %copy-done.4), channel_id=1, source_target_pairs={{0,3},{1,4},{2,5},{3,6},{4,7},{5,8},{6,9},{7,10},{8,11},{9,12},{10... | collective-permute-start | bytes 1572872 | tf_op jit(solution)/shard_map/ppermute | solution.py:37
  90.7 3.8 %collective-permute-done.1.refs_1_ = bf16[2,64,2048]{2,1,0:T(8,128)(2,1)S(1)} collective-permute-done((bf16[2,64,2048]{2,1,0:T(8,128)(2,1)}, bf16[2,64,2048]{2,1,0:T(8,128)(2,1)S(1)}, u32[]{:S(2)}, u32[]{:S(2)}) %collective-permute-start.1) | collective-permute-done | bytes 524320 | tf_op jit(solution)/shard_map/ppermute | solution.py:37
  94.6 3.0 %collective-permute-start.6 = (bf16[2,64,2048]{2,1,0:T(8,128)(2,1)S(1)}, bf16[2,64,2048]{2,1,0:T(8,128)(2,1)}, u32[]{:S(2)}, u32[]{:S(2)}) collective-permute-start(bf16[2,64,2048]{2,1,0:T(8,128)(2,1)S(1)} %copy-done.4), channel_id=1, source_target_pairs={{0,2},{1,3},{2,4},{3,5},{4,6},{5,7},{6,8},{7,9},{8,10},{9,11},{10,... | collective-permute-start | bytes 1572872 | tf_op jit(solution)/shard_map/ppermute | solution.py:37
  97.6 7.8 %collective-permute-done.2.refs_2_ = bf16[2,64,2048]{2,1,0:T(8,128)(2,1)S(1)} collective-permute-done((bf16[2,64,2048]{2,1,0:T(8,128)(2,1)}, bf16[2,64,2048]{2,1,0:T(8,128)(2,1)S(1)}, u32[]{:S(2)}, u32[]{:S(2)}) %collective-permute-start.2) | collective-permute-done | bytes 524320 | tf_op jit(solution)/shard_map/ppermute | solution.py:37
  105.4 2.8 %collective-permute-start.7 = (bf16[2,64,2048]{2,1,0:T(8,128)(2,1)S(1)}, bf16[2,64,2048]{2,1,0:T(8,128)(2,1)}, u32[]{:S(2)}, u32[]{:S(2)}) collective-permute-start(bf16[2,64,2048]{2,1,0:T(8,128)(2,1)S(1)} %copy-done.4), channel_id=1, source_target_pairs={{0,1},{1,2},{2,3},{3,4},{4,5},{5,6},{6,7},{7,8},{8,9},{9,10},{10,1... | collective-permute-start | bytes 1572872 | tf_op jit(solution)/shard_map/ppermute | solution.py:37
  108.5 0.9 reshape.76
  109.4 11.6 %all-to-all-start.3 = ((bf16[8,64,256]{2,1,0:T(8,128)(2,1)}), bf16[8,64,256]{2,1,0:T(8,128)(2,1)S(1)}, u32[]{:S(2)}, u32[]{:S(2)}) async-start(bf16[8,64,256]{2,1,0:T(8,128)(2,1)} %reshape.76), calls=%async_computation.3 | async-start | bytes 524288 | tf_op jit(solution)/shard_map/all_to_all | solution.py:154
  121.1 24.6 %all-to-all-done.3 = bf16[8,64,256]{2,1,0:T(8,128)(2,1)S(1)} async-done(((bf16[8,64,256]{2,1,0:T(8,128)(2,1)}), bf16[8,64,256]{2,1,0:T(8,128)(2,1)S(1)}, u32[]{:S(2)}, u32[]{:S(2)}) %all-to-all-start.3) | async-done | bytes 262176 | tf_op jit(solution)/shard_map/all_to_all | solution.py:154
  147.6 10.5 %shard_map.122 = bf16[64,2048]{1,0:T(8,128)(2,1)} custom-call(s32[1]{0:T(128)} %bitcast.19.pos_ref, bf16[64,2048]{1,0:T(8,128)(2,1)} %q_ref.1, bf16[64,2048]{1,0:T(8,128)(2,1)} %k_ref.1, bf16[64,2048]{1,0:T(8,128)(2,1)} %v_ref.1, bf16[2,64,2048]{2,1,0:T(8,128)(2,1)} %copy-done.5, bf16[2,64,2048]{2,1,0:T(8,128)(2,1)} %copy-done.6, ...), custom_call_target="tpu_custom_call" | custom-call | tf_op jit(solution)/shard_map/pallas_call | solution.py:91
  (61 shorter events, 11.6 us)
Async XLA Ops:
  0.6 10.0 %copy-start = (f32[2048]{0:T(1024)S(1)}, f32[2048]{0:T(1024)}, u32[]{:S(2)}) copy-start(f32[2048]{0:T(1024)} %param.14) | copy-start | bytes 24580
  0.6 10.0 %copy-start.2 = (bf16[64,2048]{1,0:T(8,128)(2,1)S(1)}, bf16[64,2048]{1,0:T(8,128)(2,1)}, u32[]{:S(2)}) copy-start(bf16[64,2048]{1,0:T(8,128)(2,1)} %v_ref.1) | copy-start | bytes 786436
  0.7 10.0 %copy-start.1 = (bf16[64,2048]{1,0:T(8,128)(2,1)S(1)}, bf16[64,2048]{1,0:T(8,128)(2,1)}, u32[]{:S(2)}) copy-start(bf16[64,2048]{1,0:T(8,128)(2,1)} %k_ref.1) | copy-start | bytes 786436
  4.7 13.7 %copy-start.13 = (f32[17,160,1]{1,0,2:T(8,128)S(1)}, f32[17,160,1]{1,0,2:T(8,128)}, u32[]{:S(2)}) copy-start(f32[17,160,1]{1,0,2:T(8,128)} %constant.68) | copy-start | bytes 32644
  4.7 13.1 %all-to-all-start = ((bf16[64,8,320]{2,0,1:T(8,128)(2,1)}), bf16[64,8,320]{2,0,1:T(8,128)(2,1)S(1)}, u32[]{:S(2)}, u32[]{:S(2)}) async-start(bf16[64,8,320]{2,0,1:T(8,128)(2,1)} %pad_maximum_fusion.1), calls=%async_computation | async-start | bytes 786432 | tf_op jit(solution)/shard_map/all_to_all | solution.py:125
  9.9 9.3 %copy-start.11 = (f32[17,160,1]{1,0,2:T(8,128)S(1)}, f32[17,160,1]{1,0,2:T(8,128)}, u32[]{:S(2)}) copy-start(f32[17,160,1]{1,0,2:T(8,128)} %constant.69) | copy-start | bytes 32644
  21.1 35.4 %copy-start.12 = (f32[17,160,1]{1,0,2:T(8,128)S(1)}, f32[17,160,1]{1,0,2:T(8,128)}, u32[]{:S(2)}) copy-start(f32[17,160,1]{1,0,2:T(8,128)} %constant.70) | copy-start | bytes 32644
  21.1 29.5 %all-to-all-start.1 = ((f32[64,5,128]{2,1,0:T(8,128)}), f32[64,5,128]{2,1,0:T(8,128)S(1)}, u32[]{:S(2)}, u32[]{:S(2)}) async-start(f32[64,5,128]{2,1,0:T(8,128)} %reshape.73), calls=%async_computation.1 | async-start | bytes 524288 | tf_op jit(solution)/shard_map/all_to_all | solution.py:106
  51.4 16.9 %all-to-all-start.2 = ((f32[64,5,128]{2,1,0:T(8,128)}), f32[64,5,128]{2,1,0:T(8,128)S(1)}, u32[]{:S(2)}, u32[]{:S(2)}) async-start(f32[64,5,128]{2,1,0:T(8,128)} %reduce-window_subtract_fusion), calls=%async_computation.2 | async-start | bytes 524288 | tf_op jit(solution)/shard_map/all_to_all | solution.py:108
  60.8 24.4 %copy-start.3 = (f32[2,128,512]{2,1,0:T(8,128)S(1)}, f32[2,128,512]{2,1,0:T(8,128)}, u32[]{:S(2)}) copy-start(f32[2,128,512]{2,1,0:T(8,128)} %fusion) | copy-start | bytes 1572868
  60.8 25.2 %copy-start.4 = (bf16[2,64,2048]{2,1,0:T(8,128)(2,1)S(1)}, bf16[2,64,2048]{2,1,0:T(8,128)(2,1)}, u32[]{:S(2)}) copy-start(bf16[2,64,2048]{2,1,0:T(8,128)(2,1)} %pad_maximum_fusion) | copy-start | bytes 1572868
  68.4 17.6 %collective-permute-start = (bf16[2,64,2048]{2,1,0:T(8,128)(2,1)}, bf16[2,64,2048]{2,1,0:T(8,128)(2,1)S(1)}, u32[]{:S(2)}, u32[]{:S(2)}) collective-permute-start(bf16[2,64,2048]{2,1,0:T(8,128)(2,1)} %pad_maximum_fusion), channel_id=1, source_target_pairs={{0,8},{1,9},{2,10},{3,11},{4,12},{5,13},{6,14},{7,15},{8,16},{9,17... | collective-permute-start | bytes 1572872 | tf_op jit(solution)/shard_map/ppermute | solution.py:37
  70.7 23.9 %collective-permute-start.1 = (bf16[2,64,2048]{2,1,0:T(8,128)(2,1)}, bf16[2,64,2048]{2,1,0:T(8,128)(2,1)S(1)}, u32[]{:S(2)}, u32[]{:S(2)}) collective-permute-start(bf16[2,64,2048]{2,1,0:T(8,128)(2,1)} %pad_maximum_fusion), channel_id=1, source_target_pairs={{0,7},{1,8},{2,9},{3,10},{4,11},{5,12},{6,13},{7,14},{8,15},{9,16}... | collective-permute-start | bytes 1572872 | tf_op jit(solution)/shard_map/ppermute | solution.py:37
  76.8 28.6 %collective-permute-start.2 = (bf16[2,64,2048]{2,1,0:T(8,128)(2,1)}, bf16[2,64,2048]{2,1,0:T(8,128)(2,1)S(1)}, u32[]{:S(2)}, u32[]{:S(2)}) collective-permute-start(bf16[2,64,2048]{2,1,0:T(8,128)(2,1)} %pad_maximum_fusion), channel_id=1, source_target_pairs={{0,6},{1,7},{2,8},{3,9},{4,10},{5,11},{6,12},{7,13},{8,14},{9,15},... | collective-permute-start | bytes 1572872 | tf_op jit(solution)/shard_map/ppermute | solution.py:37
  81.4 65.0 %collective-permute-start.3 = (bf16[2,64,2048]{2,1,0:T(8,128)(2,1)}, bf16[2,64,2048]{2,1,0:T(8,128)(2,1)S(1)}, u32[]{:S(2)}, u32[]{:S(2)}) collective-permute-start(bf16[2,64,2048]{2,1,0:T(8,128)(2,1)} %pad_maximum_fusion), channel_id=1, source_target_pairs={{0,5},{1,6},{2,7},{3,8},{4,9},{5,10},{6,11},{7,12},{8,13},{9,14},{... | collective-permute-start | bytes 1572872 | tf_op jit(solution)/shard_map/ppermute | solution.py:37
  83.3 63.1 %collective-permute-start.4 = (bf16[2,64,2048]{2,1,0:T(8,128)(2,1)}, bf16[2,64,2048]{2,1,0:T(8,128)(2,1)S(1)}, u32[]{:S(2)}, u32[]{:S(2)}) collective-permute-start(bf16[2,64,2048]{2,1,0:T(8,128)(2,1)} %pad_maximum_fusion), channel_id=1, source_target_pairs={{0,4},{1,5},{2,6},{3,7},{4,8},{5,9},{6,10},{7,11},{8,12},{9,13},{1... | collective-permute-start | bytes 1572872 | tf_op jit(solution)/shard_map/ppermute | solution.py:37
  86.0 22.2 %copy-start.5 = (bf16[2,64,2048]{2,1,0:T(8,128)(2,1)}, bf16[2,64,2048]{2,1,0:T(8,128)(2,1)S(1)}, u32[]{:S(2)}) copy-start(bf16[2,64,2048]{2,1,0:T(8,128)(2,1)S(1)} %collective-permute-done.refs_0_) | copy-start | bytes 1572868
  86.0 60.4 %collective-permute-start.5 = (bf16[2,64,2048]{2,1,0:T(8,128)(2,1)S(1)}, bf16[2,64,2048]{2,1,0:T(8,128)(2,1)S(1)}, u32[]{:S(2)}, u32[]{:S(2)}) collective-permute-start(bf16[2,64,2048]{2,1,0:T(8,128)(2,1)S(1)} %copy-done.4), channel_id=1, source_target_pairs={{0,3},{1,4},{2,5},{3,6},{4,7},{5,8},{6,9},{7,10},{8,11},{9,12},{10... | collective-permute-start | bytes 1572872 | tf_op jit(solution)/shard_map/ppermute | solution.py:37
  94.6 13.7 %copy-start.6 = (bf16[2,64,2048]{2,1,0:T(8,128)(2,1)}, bf16[2,64,2048]{2,1,0:T(8,128)(2,1)S(1)}, u32[]{:S(2)}) copy-start(bf16[2,64,2048]{2,1,0:T(8,128)(2,1)S(1)} %collective-permute-done.1.refs_1_) | copy-start | bytes 1572868
  94.6 51.9 %collective-permute-start.6 = (bf16[2,64,2048]{2,1,0:T(8,128)(2,1)S(1)}, bf16[2,64,2048]{2,1,0:T(8,128)(2,1)}, u32[]{:S(2)}, u32[]{:S(2)}) collective-permute-start(bf16[2,64,2048]{2,1,0:T(8,128)(2,1)S(1)} %copy-done.4), channel_id=1, source_target_pairs={{0,2},{1,3},{2,4},{3,5},{4,6},{5,7},{6,8},{7,9},{8,10},{9,11},{10,... | collective-permute-start | bytes 1572872 | tf_op jit(solution)/shard_map/ppermute | solution.py:37
  105.4 2.8 %copy-start.7 = (bf16[2,64,2048]{2,1,0:T(8,128)(2,1)}, bf16[2,64,2048]{2,1,0:T(8,128)(2,1)S(1)}, u32[]{:S(2)}) copy-start(bf16[2,64,2048]{2,1,0:T(8,128)(2,1)S(1)} %collective-permute-done.2.refs_2_) | copy-start | bytes 1572868
  105.4 41.0 %collective-permute-start.7 = (bf16[2,64,2048]{2,1,0:T(8,128)(2,1)S(1)}, bf16[2,64,2048]{2,1,0:T(8,128)(2,1)}, u32[]{:S(2)}, u32[]{:S(2)}) collective-permute-start(bf16[2,64,2048]{2,1,0:T(8,128)(2,1)S(1)} %copy-done.4), channel_id=1, source_target_pairs={{0,1},{1,2},{2,3},{3,4},{4,5},{5,6},{6,7},{7,8},{8,9},{9,10},{10,1... | collective-permute-start | bytes 1572872 | tf_op jit(solution)/shard_map/ppermute | solution.py:37
  109.4 36.3 %all-to-all-start.3 = ((bf16[8,64,256]{2,1,0:T(8,128)(2,1)}), bf16[8,64,256]{2,1,0:T(8,128)(2,1)S(1)}, u32[]{:S(2)}, u32[]{:S(2)}) async-start(bf16[8,64,256]{2,1,0:T(8,128)(2,1)} %reshape.76), calls=%async_computation.3 | async-start | bytes 524288 | tf_op jit(solution)/shard_map/all_to_all | solution.py:154
  146.4 1.1 copy-start.10
  (2 other events, 1.8 us)

commit v8 on v7

--- a/solution.py
+++ b/solution.py
@@ -123,6 +123,7 @@
         axis=-1,
     )
     got = lax.all_to_all(packed, GROUP, split_axis=1, concat_axis=0, tiled=True)
+    got, held = lax.optimization_barrier((got, held))
     rows = got.shape[0]
     got = got.reshape(rows, -1)
     query_bf = got[:, : own_heads * FDIM].reshape(rows, own_heads, FDIM)
@@ -133,7 +134,7 @@
     total = jnp.einsum(
         "jhf,jhe->hfe", sym_features(key_lin, False), value_lin, precision=lax.Precision.HIGHEST
     )
-    before, held = lax.optimization_barrier((groups_before(total), held))
+    before = groups_before(total)
     from_state = jnp.einsum(
         "ihf,hfe->ihe", sym_features(query_lin, True), before, precision=lax.Precision.HIGHEST
     )

time: 159 us -> 152 us (0.956)
  the two profiles are of different devices: /device:TPU:17 before, /device:TPU:9 now
where the time goes in v8:
time: 152 us; the launch traced here: 151 us
  starting transfers between devices  77.7 us (51%)
  waiting for transfers between devices  47.6 us (31%)
  Pallas kernels  10.5 us (7%)
  matrix products  6.35 us (4%)
  local copies, waits for them, and re-layouts  6.15 us (4%)
  other arithmetic  2.05 us (1%)
    ppermute x8, starting transfers between devices, passed_along(): return lax.ppermute(shard, axis, pairs)  44.6 us
    all_to_all x1, waiting for transfers between devices, groups_before(): lax.all_to_all(prefix, outer, split_axis=0, concat_axis=0, tiled=True)  22.2 us
    ppermute x8, waiting for transfers between devices, passed_along(): return lax.ppermute(shard, axis, pairs)  17.6 us
    all_to_all x1, starting transfers between devices, groups_before(): held = lax.all_to_all(dealt, outer, split_axis=0, concat_axis=0, tiled=True)  16 us
    pallas_call x1, Pallas kernels, window_attention(): pl.pallas_call(window_kernel, out_shape=jax.ShapeDtypeStruct((rows, chann...  10.5 us
    all_to_all x1, waiting for transfers between devices, linear_heads(): got = lax.all_to_all(packed, GROUP, split_axis=1, concat_axis=0, tiled=True)  7.77 us
    all_to_all x1, starting transfers between devices, groups_before(): lax.all_to_all(prefix, outer, split_axis=0, concat_axis=0, tiled=True)  7.6 us
    all_to_all x1, starting transfers between devices, linear_heads(): got = lax.all_to_all(packed, GROUP, split_axis=1, concat_axis=0, tiled=True)  5.1 us
  transfers between devices with their start and end apart: 12, of which 5 were waited for; matrix products, arithmetic and copies ran while one was open for 4% of the time, Pallas kernels for 7%

profile of v8, /device:TPU:9, one launch (start us, length us, event | category | flops | bytes accessed | tf_op | source)
XLA Modules:
  0.0 151.4 jit_solution(12022232121605736062)
XLA Ops:
  0.7 1.0 copy.42
  1.7 0.9 copy.26
  2.7 0.9 copy.27
  3.7 1.0 pad_maximum_fusion.1
  4.7 5.1 %all-to-all-start = ((bf16[64,8,320]{2,0,1:T(8,128)(2,1)}), bf16[64,8,320]{2,0,1:T(8,128)(2,1)S(1)}, u32[]{:S(2)}, u32[]{:S(2)}) async-start(bf16[64,8,320]{2,0,1:T(8,128)(2,1)} %pad_maximum_fusion.1), calls=%async_computation | async-start | bytes 786432 | tf_op jit(solution)/shard_map/all_to_all | solution.py:125
  10.0 7.8 %all-to-all-done = bf16[64,8,320]{2,0,1:T(8,128)(2,1)S(1)} async-done(((bf16[64,8,320]{2,0,1:T(8,128)(2,1)}), bf16[64,8,320]{2,0,1:T(8,128)(2,1)S(1)}, u32[]{:S(2)}, u32[]{:S(2)}) %all-to-all-start) | async-done | bytes 327712 | tf_op jit(solution)/shard_map/all_to_all | solution.py:125
  21.0 16.0 %all-to-all-start.1 = ((f32[64,5,128]{2,1,0:T(8,128)}), f32[64,5,128]{2,1,0:T(8,128)S(1)}, u32[]{:S(2)}, u32[]{:S(2)}) async-start(f32[64,5,128]{2,1,0:T(8,128)} %reshape.72), calls=%async_computation.1 | async-start | bytes 524288 | tf_op jit(solution)/shard_map/all_to_all | solution.py:106
  37.6 3.1 %collective-permute-start = (bf16[2,64,2048]{2,1,0:T(8,128)(2,1)S(1)}, bf16[2,64,2048]{2,1,0:T(8,128)(2,1)S(1)}, u32[]{:S(2)}, u32[]{:S(2)}) collective-permute-start(bf16[2,64,2048]{2,1,0:T(8,128)(2,1)S(1)} %pad_maximum_fusion), channel_id=1, source_target_pairs={{0,8},{1,9},{2,10},{3,11},{4,12},{5,13},{6,14},{7,15},{8,16},{9,17... | collective-permute-start | bytes 1572872 | tf_op jit(solution)/shard_map/ppermute | solution.py:37
  40.7 5.4 %collective-permute-start.1 = (bf16[2,64,2048]{2,1,0:T(8,128)(2,1)S(1)}, bf16[2,64,2048]{2,1,0:T(8,128)(2,1)S(1)}, u32[]{:S(2)}, u32[]{:S(2)}) collective-permute-start(bf16[2,64,2048]{2,1,0:T(8,128)(2,1)S(1)} %pad_maximum_fusion), channel_id=1, source_target_pairs={{0,7},{1,8},{2,9},{3,10},{4,11},{5,12},{6,13},{7,14},{8,15},{9,16}... | collective-permute-start | bytes 1572872 | tf_op jit(solution)/shard_map/ppermute | solution.py:37
  46.1 3.8 %collective-permute-start.2 = (bf16[2,64,2048]{2,1,0:T(8,128)(2,1)S(1)}, bf16[2,64,2048]{2,1,0:T(8,128)(2,1)}, u32[]{:S(2)}, u32[]{:S(2)}) collective-permute-start(bf16[2,64,2048]{2,1,0:T(8,128)(2,1)S(1)} %pad_maximum_fusion), channel_id=1, source_target_pairs={{0,6},{1,7},{2,8},{3,9},{4,10},{5,11},{6,12},{7,13},{8,14},{9,15},... | collective-permute-start | bytes 1572872 | tf_op jit(solution)/shard_map/ppermute | solution.py:37
  49.9 1.9 %collective-permute-start.3 = (bf16[2,64,2048]{2,1,0:T(8,128)(2,1)S(1)}, bf16[2,64,2048]{2,1,0:T(8,128)(2,1)}, u32[]{:S(2)}, u32[]{:S(2)}) collective-permute-start(bf16[2,64,2048]{2,1,0:T(8,128)(2,1)S(1)} %pad_maximum_fusion), channel_id=1, source_target_pairs={{0,5},{1,6},{2,7},{3,8},{4,9},{5,10},{6,11},{7,12},{8,13},{9,14},{... | collective-permute-start | bytes 1572872 | tf_op jit(solution)/shard_map/ppermute | solution.py:37
  51.9 3.9 %collective-permute-start.4 = (bf16[2,64,2048]{2,1,0:T(8,128)(2,1)S(1)}, bf16[2,64,2048]{2,1,0:T(8,128)(2,1)}, u32[]{:S(2)}, u32[]{:S(2)}) collective-permute-start(bf16[2,64,2048]{2,1,0:T(8,128)(2,1)S(1)} %pad_maximum_fusion), channel_id=1, source_target_pairs={{0,4},{1,5},{2,6},{3,7},{4,8},{5,9},{6,10},{7,11},{8,12},{9,13},{1... | collective-permute-start | bytes 1572872 | tf_op jit(solution)/shard_map/ppermute | solution.py:37
  55.8 1.8 %fusion = f32[2,128,512]{2,1,0:T(8,128)S(1)} fusion(bf16[512,2,128]{0,2,1:T(8,128)(2,1)S(1)} %bitcast.50, f32[2,512,512]{2,1,0:T(8,128)S(1)} %fusion.28, pred[512,512]{1,0:T(8,128)(4,1)S(1)} %iota_compare_fusion), kind=kOutput, calls=%fused_computation | convolution fusion | flops 808452096 | bytes 3145728 | tf_op jit(solution)/shard_map/hij,jhe->ihe/dot_general | solution.py:147
  58.4 7.6 %all-to-all-start.2 = ((f32[64,5,128]{2,1,0:T(8,128)}), f32[64,5,128]{2,1,0:T(8,128)S(1)}, u32[]{:S(2)}, u32[]{:S(2)}) async-start(f32[64,5,128]{2,1,0:T(8,128)} %reduce-window_subtract_fusion), calls=%async_computation.2 | async-start | bytes 524288 | tf_op jit(solution)/shard_map/all_to_all | solution.py:108
  67.5 22.2 %all-to-all-done.2 = f32[64,5,128]{2,1,0:T(8,128)S(1)} async-done(((f32[64,5,128]{2,1,0:T(8,128)}), f32[64,5,128]{2,1,0:T(8,128)S(1)}, u32[]{:S(2)}, u32[]{:S(2)}) %all-to-all-start.2) | async-done | bytes 163872 | tf_op jit(solution)/shard_map/all_to_all | solution.py:108
  90.5 22.0 %collective-permute-start.5 = (bf16[2,64,2048]{2,1,0:T(8,128)(2,1)S(1)}, bf16[2,64,2048]{2,1,0:T(8,128)(2,1)S(1)}, u32[]{:S(2)}, u32[]{:S(2)}) collective-permute-start(bf16[2,64,2048]{2,1,0:T(8,128)(2,1)S(1)} %pad_maximum_fusion), channel_id=1, source_target_pairs={{0,3},{1,4},{2,5},{3,6},{4,7},{5,8},{6,9},{7,10},{8,11},{9,12},{10... | collective-permute-start | bytes 1572872 | tf_op jit(solution)/shard_map/ppermute | solution.py:37
  112.6 1.9 %collective-permute-start.6 = (bf16[2,64,2048]{2,1,0:T(8,128)(2,1)S(1)}, bf16[2,64,2048]{2,1,0:T(8,128)(2,1)S(1)}, u32[]{:S(2)}, u32[]{:S(2)}) collective-permute-start(bf16[2,64,2048]{2,1,0:T(8,128)(2,1)S(1)} %pad_maximum_fusion), channel_id=1, source_target_pairs={{0,2},{1,3},{2,4},{3,5},{4,6},{5,7},{6,8},{7,9},{8,10},{9,11},{10,... | collective-permute-start | bytes 1572872 | tf_op jit(solution)/shard_map/ppermute | solution.py:37
  114.5 2.5 %collective-permute-start.7 = (bf16[2,64,2048]{2,1,0:T(8,128)(2,1)S(1)}, bf16[2,64,2048]{2,1,0:T(8,128)(2,1)}, u32[]{:S(2)}, u32[]{:S(2)}) collective-permute-start(bf16[2,64,2048]{2,1,0:T(8,128)(2,1)S(1)} %pad_maximum_fusion), channel_id=1, source_target_pairs={{0,1},{1,2},{2,3},{3,4},{4,5},{5,6},{6,7},{7,8},{8,9},{9,10},{10,1... | collective-permute-start | bytes 1572872 | tf_op jit(solution)/shard_map/ppermute | solution.py:37
  117.3 0.9 reshape.75
  118.2 4.3 %all-to-all-start.3 = ((bf16[8,64,256]{2,1,0:T(8,128)(2,1)}), bf16[8,64,256]{2,1,0:T(8,128)(2,1)S(1)}, u32[]{:S(2)}, u32[]{:S(2)}) async-start(bf16[8,64,256]{2,1,0:T(8,128)(2,1)} %reshape.75), calls=%async_computation.3 | async-start | bytes 524288 | tf_op jit(solution)/shard_map/all_to_all | solution.py:155
  122.5 10.0 %collective-permute-done.5.refs_5_ = bf16[2,64,2048]{2,1,0:T(8,128)(2,1)S(1)} collective-permute-done((bf16[2,64,2048]{2,1,0:T(8,128)(2,1)S(1)}, bf16[2,64,2048]{2,1,0:T(8,128)(2,1)S(1)}, u32[]{:S(2)}, u32[]{:S(2)}) %collective-permute-start.5) | collective-permute-done | bytes 524320 | tf_op jit(solution)/shard_map/ppermute | solution.py:37
  132.6 2.9 %collective-permute-done.6.refs_6_ = bf16[2,64,2048]{2,1,0:T(8,128)(2,1)S(1)} collective-permute-done((bf16[2,64,2048]{2,1,0:T(8,128)(2,1)S(1)}, bf16[2,64,2048]{2,1,0:T(8,128)(2,1)S(1)}, u32[]{:S(2)}, u32[]{:S(2)}) %collective-permute-start.6) | collective-permute-done | bytes 524320 | tf_op jit(solution)/shard_map/ppermute | solution.py:37
  135.5 4.6 %collective-permute-done.7.refs_7_ = bf16[2,64,2048]{2,1,0:T(8,128)(2,1)} collective-permute-done((bf16[2,64,2048]{2,1,0:T(8,128)(2,1)S(1)}, bf16[2,64,2048]{2,1,0:T(8,128)(2,1)}, u32[]{:S(2)}, u32[]{:S(2)}) %collective-permute-start.7) | collective-permute-done | bytes 524320 | tf_op jit(solution)/shard_map/ppermute | solution.py:37
  140.1 10.5 %shard_map.122 = bf16[64,2048]{1,0:T(8,128)(2,1)} custom-call(s32[1]{0:T(128)} %bitcast.18.pos_ref, bf16[64,2048]{1,0:T(8,128)(2,1)} %q_ref.1, bf16[64,2048]{1,0:T(8,128)(2,1)} %k_ref.1, bf16[64,2048]{1,0:T(8,128)(2,1)} %v_ref.1, bf16[2,64,2048]{2,1,0:T(8,128)(2,1)} %copy-done.3, bf16[2,64,2048]{2,1,0:T(8,128)(2,1)} %copy-done.4, ...), custom_call_target="tpu_custom_call" | custom-call | tf_op jit(solution)/shard_map/pallas_call | solution.py:91
  (53 shorter events, 8.1 us)
Async XLA Ops:
  0.6 9.3 %copy-start = (f32[2048]{0:T(1024)S(1)}, f32[2048]{0:T(1024)}, u32[]{:S(2)}) copy-start(f32[2048]{0:T(1024)} %param.14) | copy-start | bytes 24580
  0.6 9.3 %copy-start.1 = (bf16[64,2048]{1,0:T(8,128)(2,1)S(1)}, bf16[64,2048]{1,0:T(8,128)(2,1)}, u32[]{:S(2)}) copy-start(bf16[64,2048]{1,0:T(8,128)(2,1)} %k_ref.1) | copy-start | bytes 786436
  0.7 9.3 %copy-start.2 = (bf16[64,2048]{1,0:T(8,128)(2,1)S(1)}, bf16[64,2048]{1,0:T(8,128)(2,1)}, u32[]{:S(2)}) copy-start(bf16[64,2048]{1,0:T(8,128)(2,1)} %v_ref.1) | copy-start | bytes 786436
  4.7 13.6 %copy-start.9 = (f32[17,160,1]{1,0,2:T(8,128)S(1)}, f32[17,160,1]{1,0,2:T(8,128)}, u32[]{:S(2)}) copy-start(f32[17,160,1]{1,0,2:T(8,128)} %constant.68) | copy-start | bytes 32644
  4.7 13.1 %all-to-all-start = ((bf16[64,8,320]{2,0,1:T(8,128)(2,1)}), bf16[64,8,320]{2,0,1:T(8,128)(2,1)S(1)}, u32[]{:S(2)}, u32[]{:S(2)}) async-start(bf16[64,8,320]{2,0,1:T(8,128)(2,1)} %pad_maximum_fusion.1), calls=%async_computation | async-start | bytes 786432 | tf_op jit(solution)/shard_map/all_to_all | solution.py:125
  9.8 9.2 %copy-start.7 = (f32[17,160,1]{1,0,2:T(8,128)S(1)}, f32[17,160,1]{1,0,2:T(8,128)}, u32[]{:S(2)}) copy-start(f32[17,160,1]{1,0,2:T(8,128)} %constant.69) | copy-start | bytes 32644
  21.0 36.6 %all-to-all-start.1 = ((f32[64,5,128]{2,1,0:T(8,128)}), f32[64,5,128]{2,1,0:T(8,128)S(1)}, u32[]{:S(2)}, u32[]{:S(2)}) async-start(f32[64,5,128]{2,1,0:T(8,128)} %reshape.72), calls=%async_computation.1 | async-start | bytes 524288 | tf_op jit(solution)/shard_map/all_to_all | solution.py:106
  37.6 28.4 %copy-start.8 = (f32[17,160,1]{1,0,2:T(8,128)S(1)}, f32[17,160,1]{1,0,2:T(8,128)}, u32[]{:S(2)}) copy-start(f32[17,160,1]{1,0,2:T(8,128)} %constant.70) | copy-start | bytes 32644
  37.6 52.8 %collective-permute-start = (bf16[2,64,2048]{2,1,0:T(8,128)(2,1)S(1)}, bf16[2,64,2048]{2,1,0:T(8,128)(2,1)S(1)}, u32[]{:S(2)}, u32[]{:S(2)}) collective-permute-start(bf16[2,64,2048]{2,1,0:T(8,128)(2,1)S(1)} %pad_maximum_fusion), channel_id=1, source_target_pairs={{0,8},{1,9},{2,10},{3,11},{4,12},{5,13},{6,14},{7,15},{8,16},{9,17... | collective-permute-start | bytes 1572872 | tf_op jit(solution)/shard_map/ppermute | solution.py:37
  40.7 71.8 %collective-permute-start.1 = (bf16[2,64,2048]{2,1,0:T(8,128)(2,1)S(1)}, bf16[2,64,2048]{2,1,0:T(8,128)(2,1)S(1)}, u32[]{:S(2)}, u32[]{:S(2)}) collective-permute-start(bf16[2,64,2048]{2,1,0:T(8,128)(2,1)S(1)} %pad_maximum_fusion), channel_id=1, source_target_pairs={{0,7},{1,8},{2,9},{3,10},{4,11},{5,12},{6,13},{7,14},{8,15},{9,16}... | collective-permute-start | bytes 1572872 | tf_op jit(solution)/shard_map/ppermute | solution.py:37
  46.1 68.4 %collective-permute-start.2 = (bf16[2,64,2048]{2,1,0:T(8,128)(2,1)S(1)}, bf16[2,64,2048]{2,1,0:T(8,128)(2,1)}, u32[]{:S(2)}, u32[]{:S(2)}) collective-permute-start(bf16[2,64,2048]{2,1,0:T(8,128)(2,1)S(1)} %pad_maximum_fusion), channel_id=1, source_target_pairs={{0,6},{1,7},{2,8},{3,9},{4,10},{5,11},{6,12},{7,13},{8,14},{9,15},... | collective-permute-start | bytes 1572872 | tf_op jit(solution)/shard_map/ppermute | solution.py:37
  49.9 72.6 %collective-permute-start.3 = (bf16[2,64,2048]{2,1,0:T(8,128)(2,1)S(1)}, bf16[2,64,2048]{2,1,0:T(8,128)(2,1)}, u32[]{:S(2)}, u32[]{:S(2)}) collective-permute-start(bf16[2,64,2048]{2,1,0:T(8,128)(2,1)S(1)} %pad_maximum_fusion), channel_id=1, source_target_pairs={{0,5},{1,6},{2,7},{3,8},{4,9},{5,10},{6,11},{7,12},{8,13},{9,14},{... | collective-permute-start | bytes 1572872 | tf_op jit(solution)/shard_map/ppermute | solution.py:37
  51.9 70.6 %collective-permute-start.4 = (bf16[2,64,2048]{2,1,0:T(8,128)(2,1)S(1)}, bf16[2,64,2048]{2,1,0:T(8,128)(2,1)}, u32[]{:S(2)}, u32[]{:S(2)}) collective-permute-start(bf16[2,64,2048]{2,1,0:T(8,128)(2,1)S(1)} %pad_maximum_fusion), channel_id=1, source_target_pairs={{0,4},{1,5},{2,6},{3,7},{4,8},{5,9},{6,10},{7,11},{8,12},{9,13},{1... | collective-permute-start | bytes 1572872 | tf_op jit(solution)/shard_map/ppermute | solution.py:37
  58.4 31.3 %all-to-all-start.2 = ((f32[64,5,128]{2,1,0:T(8,128)}), f32[64,5,128]{2,1,0:T(8,128)S(1)}, u32[]{:S(2)}, u32[]{:S(2)}) async-start(f32[64,5,128]{2,1,0:T(8,128)} %reduce-window_subtract_fusion), calls=%async_computation.2 | async-start | bytes 524288 | tf_op jit(solution)/shard_map/all_to_all | solution.py:108
  90.5 49.6 %copy-start.3 = (bf16[2,64,2048]{2,1,0:T(8,128)(2,1)}, bf16[2,64,2048]{2,1,0:T(8,128)(2,1)S(1)}, u32[]{:S(2)}) copy-start(bf16[2,64,2048]{2,1,0:T(8,128)(2,1)S(1)} %collective-permute-done.refs_0_) | copy-start | bytes 1572868
  90.5 42.1 %collective-permute-start.5 = (bf16[2,64,2048]{2,1,0:T(8,128)(2,1)S(1)}, bf16[2,64,2048]{2,1,0:T(8,128)(2,1)S(1)}, u32[]{:S(2)}, u32[]{:S(2)}) collective-permute-start(bf16[2,64,2048]{2,1,0:T(8,128)(2,1)S(1)} %pad_maximum_fusion), channel_id=1, source_target_pairs={{0,3},{1,4},{2,5},{3,6},{4,7},{5,8},{6,9},{7,10},{8,11},{9,12},{10... | collective-permute-start | bytes 1572872 | tf_op jit(solution)/shard_map/ppermute | solution.py:37
  112.6 27.5 %copy-start.4 = (bf16[2,64,2048]{2,1,0:T(8,128)(2,1)}, bf16[2,64,2048]{2,1,0:T(8,128)(2,1)S(1)}, u32[]{:S(2)}) copy-start(bf16[2,64,2048]{2,1,0:T(8,128)(2,1)S(1)} %collective-permute-done.1.refs_1_) | copy-start | bytes 1572868
  112.6 22.9 %collective-permute-start.6 = (bf16[2,64,2048]{2,1,0:T(8,128)(2,1)S(1)}, bf16[2,64,2048]{2,1,0:T(8,128)(2,1)S(1)}, u32[]{:S(2)}, u32[]{:S(2)}) collective-permute-start(bf16[2,64,2048]{2,1,0:T(8,128)(2,1)S(1)} %pad_maximum_fusion), channel_id=1, source_target_pairs={{0,2},{1,3},{2,4},{3,5},{4,6},{5,7},{6,8},{7,9},{8,10},{9,11},{10,... | collective-permute-start | bytes 1572872 | tf_op jit(solution)/shard_map/ppermute | solution.py:37
  114.5 25.6 %collective-permute-start.7 = (bf16[2,64,2048]{2,1,0:T(8,128)(2,1)S(1)}, bf16[2,64,2048]{2,1,0:T(8,128)(2,1)}, u32[]{:S(2)}, u32[]{:S(2)}) collective-permute-start(bf16[2,64,2048]{2,1,0:T(8,128)(2,1)S(1)} %pad_maximum_fusion), channel_id=1, source_target_pairs={{0,1},{1,2},{2,3},{3,4},{4,5},{5,6},{6,7},{7,8},{8,9},{9,10},{10,1... | collective-permute-start | bytes 1572872 | tf_op jit(solution)/shard_map/ppermute | solution.py:37
  118.2 32.5 %all-to-all-start.3 = ((bf16[8,64,256]{2,1,0:T(8,128)(2,1)}), bf16[8,64,256]{2,1,0:T(8,128)(2,1)S(1)}, u32[]{:S(2)}, u32[]{:S(2)}) async-start(bf16[8,64,256]{2,1,0:T(8,128)(2,1)} %reshape.75), calls=%async_computation.3 | async-start | bytes 524288 | tf_op jit(solution)/shard_map/all_to_all | solution.py:155
  132.6 7.5 %copy-start.5 = (bf16[2,64,2048]{2,1,0:T(8,128)(2,1)}, bf16[2,64,2048]{2,1,0:T(8,128)(2,1)S(1)}, u32[]{:S(2)}) copy-start(bf16[2,64,2048]{2,1,0:T(8,128)(2,1)S(1)} %collective-permute-done.5.refs_5_) | copy-start | bytes 1572868
  135.5 4.6 %copy-start.6 = (bf16[2,64,2048]{2,1,0:T(8,128)(2,1)}, bf16[2,64,2048]{2,1,0:T(8,128)(2,1)S(1)}, u32[]{:S(2)}) copy-start(bf16[2,64,2048]{2,1,0:T(8,128)(2,1)S(1)} %collective-permute-done.6.refs_6_) | copy-start | bytes 1572868

commit v9 on v8

--- a/solution.py
+++ b/solution.py
@@ -1,4 +1,3 @@
-import functools
 import math
 
 import jax
@@ -51,36 +50,23 @@
     reach = len(refs) - 1
     out_ref = refs[-1]
     rows = q_ref.shape[0]
-    pos = pos_ref[0]
-    row = lax.broadcasted_iota(jnp.int32, (rows, rows), 0)
-    col = lax.broadcasted_iota(jnp.int32, (rows, rows), 1)
-    here = jnp.zeros((rows, rows), jnp.int32) + pos
+    span = (reach + 1) * rows
+    row = lax.broadcasted_iota(jnp.int32, (rows, span), 0)
+    rel = lax.broadcasted_iota(jnp.int32, (rows, span), 1) - reach * rows
+    first = jnp.zeros((rows, span), jnp.int32) + pos_ref[0] * rows
+    allowed = (rel <= row) & (rel > row - WINDOW) & (first + rel >= 0)
     scale = 1.0 / math.sqrt(SDIM)
     for head in range(q_ref.shape[1] // SDIM):
         lanes = pl.ds(head * SDIM, SDIM)
-        query = q_ref[:, lanes]
-        keys = [refs[t][0, :, lanes] for t in range(reach)] + [k_ref[:, lanes]]
-        values = [refs[t][1, :, lanes] for t in range(reach)] + [v_ref[:, lanes]]
-        scores = []
-        for t in range(reach + 1):
-            s = lax.dot_general(query, keys[t], (((1,), (1,)), ((), ())),
-                                preferred_element_type=jnp.float32) * scale
-            if t == reach:
-                ok = col <= row
-            elif t == 0:
-                ok = (col > row) & (here >= reach - t)
-            else:
-                ok = here >= reach - t
-            scores.append(jnp.where(ok, s, jnp.float32(-1e30)))
-        top = functools.reduce(jnp.maximum, [jnp.max(s, axis=1, keepdims=True) for s in scores])
-        expd = [jnp.exp(s - top) for s in scores]
-        total = functools.reduce(jnp.add, [jnp.sum(e, axis=1, keepdims=True) for e in expd])
-        acc = None
-        for t in range(reach + 1):
-            part = lax.dot_general((expd[t] / total).astype(jnp.bfloat16), values[t],
-                                   (((1,), (0,)), ((), ())), preferred_element_type=jnp.float32)
-            acc = part if acc is None else acc + part
-        out_ref[:, lanes] = acc.astype(out_ref.dtype)
+        keys = jnp.concatenate([refs[t][0, :, lanes] for t in range(reach)] + [k_ref[:, lanes]], axis=0)
+        values = jnp.concatenate([refs[t][1, :, lanes] for t in range(reach)] + [v_ref[:, lanes]], axis=0)
+        scores = lax.dot_general(q_ref[:, lanes], keys, (((1,), (1,)), ((), ())),
+                                 preferred_element_type=jnp.float32) * scale
+        scores = jnp.where(allowed, scores, jnp.float32(-1e30))
+        expd = jnp.exp(scores - jnp.max(scores, axis=1, keepdims=True))
+        probs = (expd / jnp.sum(expd, axis=1, keepdims=True)).astype(jnp.bfloat16)
+        out_ref[:, lanes] = lax.dot_general(probs, values, (((1,), (0,)), ((), ())),
+                                            preferred_element_type=jnp.float32).astype(out_ref.dtype)
 
 def window_attention(pos, query, key, value, earlier):
     rows, channels = query.shape

time: 152 us -> 150 us (0.987)
  Pallas kernels: 10.5 us -> 8.53 us
    pallas_call x1, Pallas kernels: 10.5 us -> 8.53 us  [window_attention(): pl.pallas_call(window_kernel, out_shape=jax.ShapeDtypeStruct((rows, chann...]
  transfers between devices with their start and end apart: 12 -> 12, of which waited for: 5 -> 5; matrix products, arithmetic and copies ran while one was open for 4% -> 4% of each run, Pallas kernels for 7% -> 6%
where the time goes in v9:
time: 150 us; the launch traced here: 149 us
  starting transfers between devices  77.7 us (52%)
  waiting for transfers between devices  47.6 us (32%)
  Pallas kernels  8.53 us (6%)
  matrix products  6.35 us (4%)
  local copies, waits for them, and re-layouts  6.15 us (4%)
  other arithmetic  2.05 us (1%)
    ppermute x8, starting transfers between devices, passed_along(): return lax.ppermute(shard, axis, pairs)  44.6 us
    all_to_all x1, waiting for transfers between devices, groups_before(): lax.all_to_all(prefix, outer, split_axis=0, concat_axis=0, tiled=True)  22.2 us
    ppermute x8, waiting for transfers between devices, passed_along(): return lax.ppermute(shard, axis, pairs)  17.6 us
    all_to_all x1, starting transfers between devices, groups_before(): held = lax.all_to_all(dealt, outer, split_axis=0, concat_axis=0, tiled=True)  16 us
    pallas_call x1, Pallas kernels, window_attention(): pl.pallas_call(window_kernel, out_shape=jax.ShapeDtypeStruct((rows, chann...  8.53 us
    all_to_all x1, waiting for transfers between devices, linear_heads(): got = lax.all_to_all(packed, GROUP, split_axis=1, concat_axis=0, tiled=True)  7.77 us
    all_to_all x1, starting transfers between devices, groups_before(): lax.all_to_all(prefix, outer, split_axis=0, concat_axis=0, tiled=True)  7.6 us
    all_to_all x1, starting transfers between devices, linear_heads(): got = lax.all_to_all(packed, GROUP, split_axis=1, concat_axis=0, tiled=True)  5.1 us
  transfers between devices with their start and end apart: 12, of which 5 were waited for; matrix products, arithmetic and copies ran while one was open for 4% of the time, Pallas kernels for 6%

profile of v9, /device:TPU:9, one launch (start us, length us, event | category | flops | bytes accessed | tf_op | source)
XLA Modules:
  0.0 149.4 jit_solution(140211556662263484)
XLA Ops:
  0.7 1.0 copy.42
  1.7 0.9 copy.26
  2.7 0.9 copy.27
  3.7 1.0 pad_maximum_fusion.1
  4.7 5.1 %all-to-all-start = ((bf16[64,8,320]{2,0,1:T(8,128)(2,1)}), bf16[64,8,320]{2,0,1:T(8,128)(2,1)S(1)}, u32[]{:S(2)}, u32[]{:S(2)}) async-start(bf16[64,8,320]{2,0,1:T(8,128)(2,1)} %pad_maximum_fusion.1), calls=%async_computation | async-start | bytes 786432 | tf_op jit(solution)/shard_map/all_to_all | solution.py:111
  10.0 7.8 %all-to-all-done = bf16[64,8,320]{2,0,1:T(8,128)(2,1)S(1)} async-done(((bf16[64,8,320]{2,0,1:T(8,128)(2,1)}), bf16[64,8,320]{2,0,1:T(8,128)(2,1)S(1)}, u32[]{:S(2)}, u32[]{:S(2)}) %all-to-all-start) | async-done | bytes 327712 | tf_op jit(solution)/shard_map/all_to_all | solution.py:111
  21.0 16.0 %all-to-all-start.1 = ((f32[64,5,128]{2,1,0:T(8,128)}), f32[64,5,128]{2,1,0:T(8,128)S(1)}, u32[]{:S(2)}, u32[]{:S(2)}) async-start(f32[64,5,128]{2,1,0:T(8,128)} %reshape.72), calls=%async_computation.1 | async-start | bytes 524288 | tf_op jit(solution)/shard_map/all_to_all | solution.py:92
  37.6 3.1 %collective-permute-start = (bf16[2,64,2048]{2,1,0:T(8,128)(2,1)S(1)}, bf16[2,64,2048]{2,1,0:T(8,128)(2,1)S(1)}, u32[]{:S(2)}, u32[]{:S(2)}) collective-permute-start(bf16[2,64,2048]{2,1,0:T(8,128)(2,1)S(1)} %pad_maximum_fusion), channel_id=1, source_target_pairs={{0,8},{1,9},{2,10},{3,11},{4,12},{5,13},{6,14},{7,15},{8,16},{9,17... | collective-permute-start | bytes 1572872 | tf_op jit(solution)/shard_map/ppermute | solution.py:36
  40.7 5.4 %collective-permute-start.1 = (bf16[2,64,2048]{2,1,0:T(8,128)(2,1)S(1)}, bf16[2,64,2048]{2,1,0:T(8,128)(2,1)S(1)}, u32[]{:S(2)}, u32[]{:S(2)}) collective-permute-start(bf16[2,64,2048]{2,1,0:T(8,128)(2,1)S(1)} %pad_maximum_fusion), channel_id=1, source_target_pairs={{0,7},{1,8},{2,9},{3,10},{4,11},{5,12},{6,13},{7,14},{8,15},{9,16}... | collective-permute-start | bytes 1572872 | tf_op jit(solution)/shard_map/ppermute | solution.py:36
  46.1 3.8 %collective-permute-start.2 = (bf16[2,64,2048]{2,1,0:T(8,128)(2,1)S(1)}, bf16[2,64,2048]{2,1,0:T(8,128)(2,1)}, u32[]{:S(2)}, u32[]{:S(2)}) collective-permute-start(bf16[2,64,2048]{2,1,0:T(8,128)(2,1)S(1)} %pad_maximum_fusion), channel_id=1, source_target_pairs={{0,6},{1,7},{2,8},{3,9},{4,10},{5,11},{6,12},{7,13},{8,14},{9,15},... | collective-permute-start | bytes 1572872 | tf_op jit(solution)/shard_map/ppermute | solution.py:36
  49.9 1.9 %collective-permute-start.3 = (bf16[2,64,2048]{2,1,0:T(8,128)(2,1)S(1)}, bf16[2,64,2048]{2,1,0:T(8,128)(2,1)}, u32[]{:S(2)}, u32[]{:S(2)}) collective-permute-start(bf16[2,64,2048]{2,1,0:T(8,128)(2,1)S(1)} %pad_maximum_fusion), channel_id=1, source_target_pairs={{0,5},{1,6},{2,7},{3,8},{4,9},{5,10},{6,11},{7,12},{8,13},{9,14},{... | collective-permute-start | bytes 1572872 | tf_op jit(solution)/shard_map/ppermute | solution.py:36
  51.9 3.9 %collective-permute-start.4 = (bf16[2,64,2048]{2,1,0:T(8,128)(2,1)S(1)}, bf16[2,64,2048]{2,1,0:T(8,128)(2,1)}, u32[]{:S(2)}, u32[]{:S(2)}) collective-permute-start(bf16[2,64,2048]{2,1,0:T(8,128)(2,1)S(1)} %pad_maximum_fusion), channel_id=1, source_target_pairs={{0,4},{1,5},{2,6},{3,7},{4,8},{5,9},{6,10},{7,11},{8,12},{9,13},{1... | collective-permute-start | bytes 1572872 | tf_op jit(solution)/shard_map/ppermute | solution.py:36
  55.8 1.8 %fusion = f32[2,128,512]{2,1,0:T(8,128)S(1)} fusion(bf16[512,2,128]{0,2,1:T(8,128)(2,1)S(1)} %bitcast.50, f32[2,512,512]{2,1,0:T(8,128)S(1)} %fusion.28, pred[512,512]{1,0:T(8,128)(4,1)S(1)} %iota_compare_fusion), kind=kOutput, calls=%fused_computation | convolution fusion | flops 808452096 | bytes 3145728 | tf_op jit(solution)/shard_map/hij,jhe->ihe/dot_general | solution.py:133
  58.4 7.6 %all-to-all-start.2 = ((f32[64,5,128]{2,1,0:T(8,128)}), f32[64,5,128]{2,1,0:T(8,128)S(1)}, u32[]{:S(2)}, u32[]{:S(2)}) async-start(f32[64,5,128]{2,1,0:T(8,128)} %reduce-window_subtract_fusion), calls=%async_computation.2 | async-start | bytes 524288 | tf_op jit(solution)/shard_map/all_to_all | solution.py:94
  67.5 22.2 %all-to-all-done.2 = f32[64,5,128]{2,1,0:T(8,128)S(1)} async-done(((f32[64,5,128]{2,1,0:T(8,128)}), f32[64,5,128]{2,1,0:T(8,128)S(1)}, u32[]{:S(2)}, u32[]{:S(2)}) %all-to-all-start.2) | async-done | bytes 163872 | tf_op jit(solution)/shard_map/all_to_all | solution.py:94
  90.5 22.0 %collective-permute-start.5 = (bf16[2,64,2048]{2,1,0:T(8,128)(2,1)S(1)}, bf16[2,64,2048]{2,1,0:T(8,128)(2,1)S(1)}, u32[]{:S(2)}, u32[]{:S(2)}) collective-permute-start(bf16[2,64,2048]{2,1,0:T(8,128)(2,1)S(1)} %pad_maximum_fusion), channel_id=1, source_target_pairs={{0,3},{1,4},{2,5},{3,6},{4,7},{5,8},{6,9},{7,10},{8,11},{9,12},{10... | collective-permute-start | bytes 1572872 | tf_op jit(solution)/shard_map/ppermute | solution.py:36
  112.6 1.9 %collective-permute-start.6 = (bf16[2,64,2048]{2,1,0:T(8,128)(2,1)S(1)}, bf16[2,64,2048]{2,1,0:T(8,128)(2,1)S(1)}, u32[]{:S(2)}, u32[]{:S(2)}) collective-permute-start(bf16[2,64,2048]{2,1,0:T(8,128)(2,1)S(1)} %pad_maximum_fusion), channel_id=1, source_target_pairs={{0,2},{1,3},{2,4},{3,5},{4,6},{5,7},{6,8},{7,9},{8,10},{9,11},{10,... | collective-permute-start | bytes 1572872 | tf_op jit(solution)/shard_map/ppermute | solution.py:36
  114.5 2.5 %collective-permute-start.7 = (bf16[2,64,2048]{2,1,0:T(8,128)(2,1)S(1)}, bf16[2,64,2048]{2,1,0:T(8,128)(2,1)}, u32[]{:S(2)}, u32[]{:S(2)}) collective-permute-start(bf16[2,64,2048]{2,1,0:T(8,128)(2,1)S(1)} %pad_maximum_fusion), channel_id=1, source_target_pairs={{0,1},{1,2},{2,3},{3,4},{4,5},{5,6},{6,7},{7,8},{8,9},{9,10},{10,1... | collective-permute-start | bytes 1572872 | tf_op jit(solution)/shard_map/ppermute | solution.py:36
  117.3 0.9 reshape.75
  118.2 4.3 %all-to-all-start.3 = ((bf16[8,64,256]{2,1,0:T(8,128)(2,1)}), bf16[8,64,256]{2,1,0:T(8,128)(2,1)S(1)}, u32[]{:S(2)}, u32[]{:S(2)}) async-start(bf16[8,64,256]{2,1,0:T(8,128)(2,1)} %reshape.75), calls=%async_computation.3 | async-start | bytes 524288 | tf_op jit(solution)/shard_map/all_to_all | solution.py:141
  122.5 10.0 %collective-permute-done.5.refs_5_ = bf16[2,64,2048]{2,1,0:T(8,128)(2,1)S(1)} collective-permute-done((bf16[2,64,2048]{2,1,0:T(8,128)(2,1)S(1)}, bf16[2,64,2048]{2,1,0:T(8,128)(2,1)S(1)}, u32[]{:S(2)}, u32[]{:S(2)}) %collective-permute-start.5) | collective-permute-done | bytes 524320 | tf_op jit(solution)/shard_map/ppermute | solution.py:36
  132.6 2.9 %collective-permute-done.6.refs_6_ = bf16[2,64,2048]{2,1,0:T(8,128)(2,1)S(1)} collective-permute-done((bf16[2,64,2048]{2,1,0:T(8,128)(2,1)S(1)}, bf16[2,64,2048]{2,1,0:T(8,128)(2,1)S(1)}, u32[]{:S(2)}, u32[]{:S(2)}) %collective-permute-start.6) | collective-permute-done | bytes 524320 | tf_op jit(solution)/shard_map/ppermute | solution.py:36
  135.5 4.6 %collective-permute-done.7.refs_7_ = bf16[2,64,2048]{2,1,0:T(8,128)(2,1)} collective-permute-done((bf16[2,64,2048]{2,1,0:T(8,128)(2,1)S(1)}, bf16[2,64,2048]{2,1,0:T(8,128)(2,1)}, u32[]{:S(2)}, u32[]{:S(2)}) %collective-permute-start.7) | collective-permute-done | bytes 524320 | tf_op jit(solution)/shard_map/ppermute | solution.py:36
  140.1 8.5 %shard_map.122 = bf16[64,2048]{1,0:T(8,128)(2,1)} custom-call(s32[1]{0:T(128)} %bitcast.18.pos_ref, bf16[64,2048]{1,0:T(8,128)(2,1)} %q_ref.1, bf16[64,2048]{1,0:T(8,128)(2,1)} %k_ref.1, bf16[64,2048]{1,0:T(8,128)(2,1)} %v_ref.1, bf16[2,64,2048]{2,1,0:T(8,128)(2,1)} %copy-done.3, bf16[2,64,2048]{2,1,0:T(8,128)(2,1)} %copy-done.4, ...), custom_call_target="tpu_custom_call" | custom-call | tf_op jit(solution)/shard_map/pallas_call | solution.py:77
  (53 shorter events, 8.1 us)
Async XLA Ops:
  0.6 9.3 %copy-start = (f32[2048]{0:T(1024)S(1)}, f32[2048]{0:T(1024)}, u32[]{:S(2)}) copy-start(f32[2048]{0:T(1024)} %param.14) | copy-start | bytes 24580
  0.6 9.3 %copy-start.1 = (bf16[64,2048]{1,0:T(8,128)(2,1)S(1)}, bf16[64,2048]{1,0:T(8,128)(2,1)}, u32[]{:S(2)}) copy-start(bf16[64,2048]{1,0:T(8,128)(2,1)} %k_ref.1) | copy-start | bytes 786436
  0.7 9.3 %copy-start.2 = (bf16[64,2048]{1,0:T(8,128)(2,1)S(1)}, bf16[64,2048]{1,0:T(8,128)(2,1)}, u32[]{:S(2)}) copy-start(bf16[64,2048]{1,0:T(8,128)(2,1)} %v_ref.1) | copy-start | bytes 786436
  4.7 13.6 %copy-start.9 = (f32[17,160,1]{1,0,2:T(8,128)S(1)}, f32[17,160,1]{1,0,2:T(8,128)}, u32[]{:S(2)}) copy-start(f32[17,160,1]{1,0,2:T(8,128)} %constant.68) | copy-start | bytes 32644
  4.7 13.1 %all-to-all-start = ((bf16[64,8,320]{2,0,1:T(8,128)(2,1)}), bf16[64,8,320]{2,0,1:T(8,128)(2,1)S(1)}, u32[]{:S(2)}, u32[]{:S(2)}) async-start(bf16[64,8,320]{2,0,1:T(8,128)(2,1)} %pad_maximum_fusion.1), calls=%async_computation | async-start | bytes 786432 | tf_op jit(solution)/shard_map/all_to_all | solution.py:111
  9.8 9.2 %copy-start.7 = (f32[17,160,1]{1,0,2:T(8,128)S(1)}, f32[17,160,1]{1,0,2:T(8,128)}, u32[]{:S(2)}) copy-start(f32[17,160,1]{1,0,2:T(8,128)} %constant.69) | copy-start | bytes 32644
  21.0 36.6 %all-to-all-start.1 = ((f32[64,5,128]{2,1,0:T(8,128)}), f32[64,5,128]{2,1,0:T(8,128)S(1)}, u32[]{:S(2)}, u32[]{:S(2)}) async-start(f32[64,5,128]{2,1,0:T(8,128)} %reshape.72), calls=%async_computation.1 | async-start | bytes 524288 | tf_op jit(solution)/shard_map/all_to_all | solution.py:92
  37.6 28.4 %copy-start.8 = (f32[17,160,1]{1,0,2:T(8,128)S(1)}, f32[17,160,1]{1,0,2:T(8,128)}, u32[]{:S(2)}) copy-start(f32[17,160,1]{1,0,2:T(8,128)} %constant.70) | copy-start | bytes 32644
  37.6 52.8 %collective-permute-start = (bf16[2,64,2048]{2,1,0:T(8,128)(2,1)S(1)}, bf16[2,64,2048]{2,1,0:T(8,128)(2,1)S(1)}, u32[]{:S(2)}, u32[]{:S(2)}) collective-permute-start(bf16[2,64,2048]{2,1,0:T(8,128)(2,1)S(1)} %pad_maximum_fusion), channel_id=1, source_target_pairs={{0,8},{1,9},{2,10},{3,11},{4,12},{5,13},{6,14},{7,15},{8,16},{9,17... | collective-permute-start | bytes 1572872 | tf_op jit(solution)/shard_map/ppermute | solution.py:36
  40.7 71.8 %collective-permute-start.1 = (bf16[2,64,2048]{2,1,0:T(8,128)(2,1)S(1)}, bf16[2,64,2048]{2,1,0:T(8,128)(2,1)S(1)}, u32[]{:S(2)}, u32[]{:S(2)}) collective-permute-start(bf16[2,64,2048]{2,1,0:T(8,128)(2,1)S(1)} %pad_maximum_fusion), channel_id=1, source_target_pairs={{0,7},{1,8},{2,9},{3,10},{4,11},{5,12},{6,13},{7,14},{8,15},{9,16}... | collective-permute-start | bytes 1572872 | tf_op jit(solution)/shard_map/ppermute | solution.py:36
  46.1 68.4 %collective-permute-start.2 = (bf16[2,64,2048]{2,1,0:T(8,128)(2,1)S(1)}, bf16[2,64,2048]{2,1,0:T(8,128)(2,1)}, u32[]{:S(2)}, u32[]{:S(2)}) collective-permute-start(bf16[2,64,2048]{2,1,0:T(8,128)(2,1)S(1)} %pad_maximum_fusion), channel_id=1, source_target_pairs={{0,6},{1,7},{2,8},{3,9},{4,10},{5,11},{6,12},{7,13},{8,14},{9,15},... | collective-permute-start | bytes 1572872 | tf_op jit(solution)/shard_map/ppermute | solution.py:36
  49.9 72.6 %collective-permute-start.3 = (bf16[2,64,2048]{2,1,0:T(8,128)(2,1)S(1)}, bf16[2,64,2048]{2,1,0:T(8,128)(2,1)}, u32[]{:S(2)}, u32[]{:S(2)}) collective-permute-start(bf16[2,64,2048]{2,1,0:T(8,128)(2,1)S(1)} %pad_maximum_fusion), channel_id=1, source_target_pairs={{0,5},{1,6},{2,7},{3,8},{4,9},{5,10},{6,11},{7,12},{8,13},{9,14},{... | collective-permute-start | bytes 1572872 | tf_op jit(solution)/shard_map/ppermute | solution.py:36
  51.9 70.6 %collective-permute-start.4 = (bf16[2,64,2048]{2,1,0:T(8,128)(2,1)S(1)}, bf16[2,64,2048]{2,1,0:T(8,128)(2,1)}, u32[]{:S(2)}, u32[]{:S(2)}) collective-permute-start(bf16[2,64,2048]{2,1,0:T(8,128)(2,1)S(1)} %pad_maximum_fusion), channel_id=1, source_target_pairs={{0,4},{1,5},{2,6},{3,7},{4,8},{5,9},{6,10},{7,11},{8,12},{9,13},{1... | collective-permute-start | bytes 1572872 | tf_op jit(solution)/shard_map/ppermute | solution.py:36
  58.4 31.3 %all-to-all-start.2 = ((f32[64,5,128]{2,1,0:T(8,128)}), f32[64,5,128]{2,1,0:T(8,128)S(1)}, u32[]{:S(2)}, u32[]{:S(2)}) async-start(f32[64,5,128]{2,1,0:T(8,128)} %reduce-window_subtract_fusion), calls=%async_computation.2 | async-start | bytes 524288 | tf_op jit(solution)/shard_map/all_to_all | solution.py:94
  90.5 49.6 %copy-start.3 = (bf16[2,64,2048]{2,1,0:T(8,128)(2,1)}, bf16[2,64,2048]{2,1,0:T(8,128)(2,1)S(1)}, u32[]{:S(2)}) copy-start(bf16[2,64,2048]{2,1,0:T(8,128)(2,1)S(1)} %collective-permute-done.refs_0_) | copy-start | bytes 1572868
  90.5 42.1 %collective-permute-start.5 = (bf16[2,64,2048]{2,1,0:T(8,128)(2,1)S(1)}, bf16[2,64,2048]{2,1,0:T(8,128)(2,1)S(1)}, u32[]{:S(2)}, u32[]{:S(2)}) collective-permute-start(bf16[2,64,2048]{2,1,0:T(8,128)(2,1)S(1)} %pad_maximum_fusion), channel_id=1, source_target_pairs={{0,3},{1,4},{2,5},{3,6},{4,7},{5,8},{6,9},{7,10},{8,11},{9,12},{10... | collective-permute-start | bytes 1572872 | tf_op jit(solution)/shard_map/ppermute | solution.py:36
  112.6 27.5 %copy-start.4 = (bf16[2,64,2048]{2,1,0:T(8,128)(2,1)}, bf16[2,64,2048]{2,1,0:T(8,128)(2,1)S(1)}, u32[]{:S(2)}) copy-start(bf16[2,64,2048]{2,1,0:T(8,128)(2,1)S(1)} %collective-permute-done.1.refs_1_) | copy-start | bytes 1572868
  112.6 22.9 %collective-permute-start.6 = (bf16[2,64,2048]{2,1,0:T(8,128)(2,1)S(1)}, bf16[2,64,2048]{2,1,0:T(8,128)(2,1)S(1)}, u32[]{:S(2)}, u32[]{:S(2)}) collective-permute-start(bf16[2,64,2048]{2,1,0:T(8,128)(2,1)S(1)} %pad_maximum_fusion), channel_id=1, source_target_pairs={{0,2},{1,3},{2,4},{3,5},{4,6},{5,7},{6,8},{7,9},{8,10},{9,11},{10,... | collective-permute-start | bytes 1572872 | tf_op jit(solution)/shard_map/ppermute | solution.py:36
  114.5 25.6 %collective-permute-start.7 = (bf16[2,64,2048]{2,1,0:T(8,128)(2,1)S(1)}, bf16[2,64,2048]{2,1,0:T(8,128)(2,1)}, u32[]{:S(2)}, u32[]{:S(2)}) collective-permute-start(bf16[2,64,2048]{2,1,0:T(8,128)(2,1)S(1)} %pad_maximum_fusion), channel_id=1, source_target_pairs={{0,1},{1,2},{2,3},{3,4},{4,5},{5,6},{6,7},{7,8},{8,9},{9,10},{10,1... | collective-permute-start | bytes 1572872 | tf_op jit(solution)/shard_map/ppermute | solution.py:36
  118.2 30.5 %all-to-all-start.3 = ((bf16[8,64,256]{2,1,0:T(8,128)(2,1)}), bf16[8,64,256]{2,1,0:T(8,128)(2,1)S(1)}, u32[]{:S(2)}, u32[]{:S(2)}) async-start(bf16[8,64,256]{2,1,0:T(8,128)(2,1)} %reshape.75), calls=%async_computation.3 | async-start | bytes 524288 | tf_op jit(solution)/shard_map/all_to_all | solution.py:141
  132.6 7.5 %copy-start.5 = (bf16[2,64,2048]{2,1,0:T(8,128)(2,1)}, bf16[2,64,2048]{2,1,0:T(8,128)(2,1)S(1)}, u32[]{:S(2)}) copy-start(bf16[2,64,2048]{2,1,0:T(8,128)(2,1)S(1)} %collective-permute-done.5.refs_5_) | copy-start | bytes 1572868
  135.5 4.6 %copy-start.6 = (bf16[2,64,2048]{2,1,0:T(8,128)(2,1)}, bf16[2,64,2048]{2,1,0:T(8,128)(2,1)S(1)}, u32[]{:S(2)}) copy-start(bf16[2,64,2048]{2,1,0:T(8,128)(2,1)S(1)} %collective-permute-done.6.refs_6_) | copy-start | bytes 1572868

commit v10 on v9

--- a/solution.py
+++ b/solution.py
@@ -109,7 +109,6 @@
         axis=-1,
     )
     got = lax.all_to_all(packed, GROUP, split_axis=1, concat_axis=0, tiled=True)
-    got, held = lax.optimization_barrier((got, held))
     rows = got.shape[0]
     got = got.reshape(rows, -1)
     query_bf = got[:, : own_heads * FDIM].reshape(rows, own_heads, FDIM)

time: 150 us -> 148 us (0.987)
  waiting for transfers between devices: 47.6 us -> 44.8 us
    all_to_all x1, waiting for transfers between devices: 0.01 us -> 15.9 us  [groups_before(): held = lax.all_to_all(dealt, outer, split_axis=0, concat_axis=0, tiled=True)]
    all_to_all x1, waiting for transfers between devices: 22.2 us -> 10.5 us  [groups_before(): lax.all_to_all(prefix, outer, split_axis=0, concat_axis=0, tiled=True)]
    all_to_all x1, waiting for transfers between devices: 7.77 us -> 0.01 us  [linear_heads(): got = lax.all_to_all(packed, GROUP, split_axis=1, concat_axis=0, tiled=True)]
    ppermute x8, starting transfers between devices: 44.6 us -> 51.1 us  [passed_along(): return lax.ppermute(shard, axis, pairs)]
    all_to_all x1, starting transfers between devices: 16 us -> 10.3 us  [groups_before(): held = lax.all_to_all(dealt, outer, split_axis=0, concat_axis=0, tiled=True)]
  transfers between devices with their start and end apart: 12 -> 12, of which waited for: 5 -> 5; matrix products, arithmetic and copies ran while one was open for 4% -> 7% of each run, Pallas kernels for 6% -> 6%
where the time goes in v10:
time: 148 us; the launch traced here: 147 us
  starting transfers between devices  78.5 us (53%)
  waiting for transfers between devices  44.8 us (30%)
  Pallas kernels  8.53 us (6%)
  matrix products  6.37 us (4%)
  local copies, waits for them, and re-layouts  6.15 us (4%)
  other arithmetic  2.06 us (1%)
    ppermute x8, starting transfers between devices, passed_along(): return lax.ppermute(shard, axis, pairs)  51.1 us
    ppermute x8, waiting for transfers between devices, passed_along(): return lax.ppermute(shard, axis, pairs)  18.4 us
    all_to_all x1, waiting for transfers between devices, groups_before(): held = lax.all_to_all(dealt, outer, split_axis=0, concat_axis=0, tiled=True)  15.9 us
    all_to_all x1, waiting for transfers between devices, groups_before(): lax.all_to_all(prefix, outer, split_axis=0, concat_axis=0, tiled=True)  10.5 us
    all_to_all x1, starting transfers between devices, groups_before(): held = lax.all_to_all(dealt, outer, split_axis=0, concat_axis=0, tiled=True)  10.3 us
    pallas_call x1, Pallas kernels, window_attention(): pl.pallas_call(window_kernel, out_shape=jax.ShapeDtypeStruct((rows, chann...  8.53 us
    all_to_all x1, starting transfers between devices, groups_before(): lax.all_to_all(prefix, outer, split_axis=0, concat_axis=0, tiled=True)  7.64 us
    all_to_all x1, starting transfers between devices, linear_heads(): got = lax.all_to_all(packed, GROUP, split_axis=1, concat_axis=0, tiled=True)  5.1 us
  transfers between devices with their start and end apart: 12, of which 5 were waited for; matrix products, arithmetic and copies ran while one was open for 7% of the time, Pallas kernels for 6%

profile of v10, /device:TPU:9, one launch (start us, length us, event | category | flops | bytes accessed | tf_op | source)
XLA Modules:
  0.0 147.4 jit_solution(18350115292039859576)
XLA Ops:
  0.7 1.0 copy.42
  1.7 0.9 copy.26
  2.7 0.9 copy.27
  3.7 1.0 pad_maximum_fusion.1
  4.7 5.1 %all-to-all-start = ((bf16[64,8,320]{2,0,1:T(8,128)(2,1)}), bf16[64,8,320]{2,0,1:T(8,128)(2,1)S(1)}, u32[]{:S(2)}, u32[]{:S(2)}) async-start(bf16[64,8,320]{2,0,1:T(8,128)(2,1)} %pad_maximum_fusion.1), calls=%async_computation | async-start | bytes 786432 | tf_op jit(solution)/shard_map/all_to_all | solution.py:111
  9.9 4.0 %collective-permute-start = (bf16[2,64,2048]{2,1,0:T(8,128)(2,1)S(1)}, bf16[2,64,2048]{2,1,0:T(8,128)(2,1)S(1)}, u32[]{:S(2)}, u32[]{:S(2)}) collective-permute-start(bf16[2,64,2048]{2,1,0:T(8,128)(2,1)S(1)} %pad_maximum_fusion), channel_id=1, source_target_pairs={{0,8},{1,9},{2,10},{3,11},{4,12},{5,13},{6,14},{7,15},{8,16},{9,17... | collective-permute-start | bytes 1572872 | tf_op jit(solution)/shard_map/ppermute | solution.py:36
  13.9 6.8 %collective-permute-start.1 = (bf16[2,64,2048]{2,1,0:T(8,128)(2,1)S(1)}, bf16[2,64,2048]{2,1,0:T(8,128)(2,1)S(1)}, u32[]{:S(2)}, u32[]{:S(2)}) collective-permute-start(bf16[2,64,2048]{2,1,0:T(8,128)(2,1)S(1)} %pad_maximum_fusion), channel_id=1, source_target_pairs={{0,7},{1,8},{2,9},{3,10},{4,11},{5,12},{6,13},{7,14},{8,15},{9,16}... | collective-permute-start | bytes 1572872 | tf_op jit(solution)/shard_map/ppermute | solution.py:36
  20.8 4.6 %collective-permute-start.2 = (bf16[2,64,2048]{2,1,0:T(8,128)(2,1)S(1)}, bf16[2,64,2048]{2,1,0:T(8,128)(2,1)}, u32[]{:S(2)}, u32[]{:S(2)}) collective-permute-start(bf16[2,64,2048]{2,1,0:T(8,128)(2,1)S(1)} %pad_maximum_fusion), channel_id=1, source_target_pairs={{0,6},{1,7},{2,8},{3,9},{4,10},{5,11},{6,12},{7,13},{8,14},{9,15},... | collective-permute-start | bytes 1572872 | tf_op jit(solution)/shard_map/ppermute | solution.py:36
  25.4 2.0 %collective-permute-start.3 = (bf16[2,64,2048]{2,1,0:T(8,128)(2,1)S(1)}, bf16[2,64,2048]{2,1,0:T(8,128)(2,1)}, u32[]{:S(2)}, u32[]{:S(2)}) collective-permute-start(bf16[2,64,2048]{2,1,0:T(8,128)(2,1)S(1)} %pad_maximum_fusion), channel_id=1, source_target_pairs={{0,5},{1,6},{2,7},{3,8},{4,9},{5,10},{6,11},{7,12},{8,13},{9,14},{... | collective-permute-start | bytes 1572872 | tf_op jit(solution)/shard_map/ppermute | solution.py:36
  27.3 6.0 %collective-permute-start.4 = (bf16[2,64,2048]{2,1,0:T(8,128)(2,1)S(1)}, bf16[2,64,2048]{2,1,0:T(8,128)(2,1)}, u32[]{:S(2)}, u32[]{:S(2)}) collective-permute-start(bf16[2,64,2048]{2,1,0:T(8,128)(2,1)S(1)} %pad_maximum_fusion), channel_id=1, source_target_pairs={{0,4},{1,5},{2,6},{3,7},{4,8},{5,9},{6,10},{7,11},{8,12},{9,13},{1... | collective-permute-start | bytes 1572872 | tf_op jit(solution)/shard_map/ppermute | solution.py:36
  36.7 10.3 %all-to-all-start.1 = ((f32[64,5,128]{2,1,0:T(8,128)}), f32[64,5,128]{2,1,0:T(8,128)S(1)}, u32[]{:S(2)}, u32[]{:S(2)}) async-start(f32[64,5,128]{2,1,0:T(8,128)} %reshape.73), calls=%async_computation.1 | async-start | bytes 524288 | tf_op jit(solution)/shard_map/all_to_all | solution.py:92
  47.6 1.8 %fusion = f32[2,128,512]{2,1,0:T(8,128)S(1)} fusion(bf16[512,2,128]{0,2,1:T(8,128)(2,1)S(1)} %bitcast.49, f32[2,512,512]{2,1,0:T(8,128)S(1)} %fusion.28, pred[512,512]{1,0:T(8,128)(4,1)S(1)} %iota_compare_fusion), kind=kOutput, calls=%fused_computation | convolution fusion | flops 808452096 | bytes 3145728 | tf_op jit(solution)/shard_map/hij,jhe->ihe/dot_general | solution.py:132
  49.3 15.9 %all-to-all-done.1 = f32[64,5,128]{2,1,0:T(8,128)S(1)} async-done(((f32[64,5,128]{2,1,0:T(8,128)}), f32[64,5,128]{2,1,0:T(8,128)S(1)}, u32[]{:S(2)}, u32[]{:S(2)}) %all-to-all-start.1) | async-done | bytes 163872 | tf_op jit(solution)/shard_map/all_to_all | solution.py:92
  66.0 7.6 %all-to-all-start.2 = ((f32[64,5,128]{2,1,0:T(8,128)}), f32[64,5,128]{2,1,0:T(8,128)S(1)}, u32[]{:S(2)}, u32[]{:S(2)}) async-start(f32[64,5,128]{2,1,0:T(8,128)} %reduce-window_subtract_fusion), calls=%async_computation.2 | async-start | bytes 524288 | tf_op jit(solution)/shard_map/all_to_all | solution.py:94
  75.1 10.5 %all-to-all-done.2 = f32[64,5,128]{2,1,0:T(8,128)S(1)} async-done(((f32[64,5,128]{2,1,0:T(8,128)}), f32[64,5,128]{2,1,0:T(8,128)S(1)}, u32[]{:S(2)}, u32[]{:S(2)}) %all-to-all-start.2) | async-done | bytes 163872 | tf_op jit(solution)/shard_map/all_to_all | solution.py:94
  86.5 23.3 %collective-permute-start.5 = (bf16[2,64,2048]{2,1,0:T(8,128)(2,1)S(1)}, bf16[2,64,2048]{2,1,0:T(8,128)(2,1)S(1)}, u32[]{:S(2)}, u32[]{:S(2)}) collective-permute-start(bf16[2,64,2048]{2,1,0:T(8,128)(2,1)S(1)} %pad_maximum_fusion), channel_id=1, source_target_pairs={{0,3},{1,4},{2,5},{3,6},{4,7},{5,8},{6,9},{7,10},{8,11},{9,12},{10... | collective-permute-start | bytes 1572872 | tf_op jit(solution)/shard_map/ppermute | solution.py:36
  109.8 1.9 %collective-permute-start.6 = (bf16[2,64,2048]{2,1,0:T(8,128)(2,1)S(1)}, bf16[2,64,2048]{2,1,0:T(8,128)(2,1)S(1)}, u32[]{:S(2)}, u32[]{:S(2)}) collective-permute-start(bf16[2,64,2048]{2,1,0:T(8,128)(2,1)S(1)} %pad_maximum_fusion), channel_id=1, source_target_pairs={{0,2},{1,3},{2,4},{3,5},{4,6},{5,7},{6,8},{7,9},{8,10},{9,11},{10,... | collective-permute-start | bytes 1572872 | tf_op jit(solution)/shard_map/ppermute | solution.py:36
  111.8 2.5 %collective-permute-start.7 = (bf16[2,64,2048]{2,1,0:T(8,128)(2,1)S(1)}, bf16[2,64,2048]{2,1,0:T(8,128)(2,1)}, u32[]{:S(2)}, u32[]{:S(2)}) collective-permute-start(bf16[2,64,2048]{2,1,0:T(8,128)(2,1)S(1)} %pad_maximum_fusion), channel_id=1, source_target_pairs={{0,1},{1,2},{2,3},{3,4},{4,5},{5,6},{6,7},{7,8},{8,9},{9,10},{10,1... | collective-permute-start | bytes 1572872 | tf_op jit(solution)/shard_map/ppermute | solution.py:36
  114.6 0.9 reshape.76
  115.4 4.3 %all-to-all-start.3 = ((bf16[8,64,256]{2,1,0:T(8,128)(2,1)}), bf16[8,64,256]{2,1,0:T(8,128)(2,1)S(1)}, u32[]{:S(2)}, u32[]{:S(2)}) async-start(bf16[8,64,256]{2,1,0:T(8,128)(2,1)} %reshape.76), calls=%async_computation.3 | async-start | bytes 524288 | tf_op jit(solution)/shard_map/all_to_all | solution.py:140
  119.8 10.8 %collective-permute-done.5.refs_5_ = bf16[2,64,2048]{2,1,0:T(8,128)(2,1)S(1)} collective-permute-done((bf16[2,64,2048]{2,1,0:T(8,128)(2,1)S(1)}, bf16[2,64,2048]{2,1,0:T(8,128)(2,1)S(1)}, u32[]{:S(2)}, u32[]{:S(2)}) %collective-permute-start.5) | collective-permute-done | bytes 524320 | tf_op jit(solution)/shard_map/ppermute | solution.py:36
  130.6 1.9 %collective-permute-done.6.refs_6_ = bf16[2,64,2048]{2,1,0:T(8,128)(2,1)S(1)} collective-permute-done((bf16[2,64,2048]{2,1,0:T(8,128)(2,1)S(1)}, bf16[2,64,2048]{2,1,0:T(8,128)(2,1)S(1)}, u32[]{:S(2)}, u32[]{:S(2)}) %collective-permute-start.6) | collective-permute-done | bytes 524320 | tf_op jit(solution)/shard_map/ppermute | solution.py:36
  132.5 5.6 %collective-permute-done.7.refs_7_ = bf16[2,64,2048]{2,1,0:T(8,128)(2,1)} collective-permute-done((bf16[2,64,2048]{2,1,0:T(8,128)(2,1)S(1)}, bf16[2,64,2048]{2,1,0:T(8,128)(2,1)}, u32[]{:S(2)}, u32[]{:S(2)}) %collective-permute-start.7) | collective-permute-done | bytes 524320 | tf_op jit(solution)/shard_map/ppermute | solution.py:36
  138.2 8.5 %shard_map.122 = bf16[64,2048]{1,0:T(8,128)(2,1)} custom-call(s32[1]{0:T(128)} %bitcast.17.pos_ref, bf16[64,2048]{1,0:T(8,128)(2,1)} %q_ref.1, bf16[64,2048]{1,0:T(8,128)(2,1)} %k_ref.1, bf16[64,2048]{1,0:T(8,128)(2,1)} %v_ref.1, bf16[2,64,2048]{2,1,0:T(8,128)(2,1)} %copy-done.3, bf16[2,64,2048]{2,1,0:T(8,128)(2,1)} %copy-done.4, ...), custom_call_target="tpu_custom_call" | custom-call | tf_op jit(solution)/shard_map/pallas_call | solution.py:77
  (53 shorter events, 8.2 us)
Async XLA Ops:
  0.6 32.7 %copy-start = (f32[2048]{0:T(1024)S(1)}, f32[2048]{0:T(1024)}, u32[]{:S(2)}) copy-start(f32[2048]{0:T(1024)} %param.14) | copy-start | bytes 24580
  0.6 9.2 %copy-start.1 = (bf16[64,2048]{1,0:T(8,128)(2,1)S(1)}, bf16[64,2048]{1,0:T(8,128)(2,1)}, u32[]{:S(2)}) copy-start(bf16[64,2048]{1,0:T(8,128)(2,1)} %k_ref.1) | copy-start | bytes 786436
  0.7 9.2 %copy-start.2 = (bf16[64,2048]{1,0:T(8,128)(2,1)S(1)}, bf16[64,2048]{1,0:T(8,128)(2,1)}, u32[]{:S(2)}) copy-start(bf16[64,2048]{1,0:T(8,128)(2,1)} %v_ref.1) | copy-start | bytes 786436
  4.7 29.3 %copy-start.9 = (f32[17,160,1]{1,0,2:T(8,128)S(1)}, f32[17,160,1]{1,0,2:T(8,128)}, u32[]{:S(2)}) copy-start(f32[17,160,1]{1,0,2:T(8,128)} %constant.68) | copy-start | bytes 32644
  4.7 28.7 %all-to-all-start = ((bf16[64,8,320]{2,0,1:T(8,128)(2,1)}), bf16[64,8,320]{2,0,1:T(8,128)(2,1)S(1)}, u32[]{:S(2)}, u32[]{:S(2)}) async-start(bf16[64,8,320]{2,0,1:T(8,128)(2,1)} %pad_maximum_fusion.1), calls=%async_computation | async-start | bytes 786432 | tf_op jit(solution)/shard_map/all_to_all | solution.py:111
  9.9 24.9 %copy-start.7 = (f32[17,160,1]{1,0,2:T(8,128)S(1)}, f32[17,160,1]{1,0,2:T(8,128)}, u32[]{:S(2)}) copy-start(f32[17,160,1]{1,0,2:T(8,128)} %constant.69) | copy-start | bytes 32644
  9.9 76.5 %collective-permute-start = (bf16[2,64,2048]{2,1,0:T(8,128)(2,1)S(1)}, bf16[2,64,2048]{2,1,0:T(8,128)(2,1)S(1)}, u32[]{:S(2)}, u32[]{:S(2)}) collective-permute-start(bf16[2,64,2048]{2,1,0:T(8,128)(2,1)S(1)} %pad_maximum_fusion), channel_id=1, source_target_pairs={{0,8},{1,9},{2,10},{3,11},{4,12},{5,13},{6,14},{7,15},{8,16},{9,17... | collective-permute-start | bytes 1572872 | tf_op jit(solution)/shard_map/ppermute | solution.py:36
  13.9 95.9 %collective-permute-start.1 = (bf16[2,64,2048]{2,1,0:T(8,128)(2,1)S(1)}, bf16[2,64,2048]{2,1,0:T(8,128)(2,1)S(1)}, u32[]{:S(2)}, u32[]{:S(2)}) collective-permute-start(bf16[2,64,2048]{2,1,0:T(8,128)(2,1)S(1)} %pad_maximum_fusion), channel_id=1, source_target_pairs={{0,7},{1,8},{2,9},{3,10},{4,11},{5,12},{6,13},{7,14},{8,15},{9,16}... | collective-permute-start | bytes 1572872 | tf_op jit(solution)/shard_map/ppermute | solution.py:36
  20.8 91.0 %collective-permute-start.2 = (bf16[2,64,2048]{2,1,0:T(8,128)(2,1)S(1)}, bf16[2,64,2048]{2,1,0:T(8,128)(2,1)}, u32[]{:S(2)}, u32[]{:S(2)}) collective-permute-start(bf16[2,64,2048]{2,1,0:T(8,128)(2,1)S(1)} %pad_maximum_fusion), channel_id=1, source_target_pairs={{0,6},{1,7},{2,8},{3,9},{4,10},{5,11},{6,12},{7,13},{8,14},{9,15},... | collective-permute-start | bytes 1572872 | tf_op jit(solution)/shard_map/ppermute | solution.py:36
  25.4 94.4 %collective-permute-start.3 = (bf16[2,64,2048]{2,1,0:T(8,128)(2,1)S(1)}, bf16[2,64,2048]{2,1,0:T(8,128)(2,1)}, u32[]{:S(2)}, u32[]{:S(2)}) collective-permute-start(bf16[2,64,2048]{2,1,0:T(8,128)(2,1)S(1)} %pad_maximum_fusion), channel_id=1, source_target_pairs={{0,5},{1,6},{2,7},{3,8},{4,9},{5,10},{6,11},{7,12},{8,13},{9,14},{... | collective-permute-start | bytes 1572872 | tf_op jit(solution)/shard_map/ppermute | solution.py:36
  27.3 92.5 %collective-permute-start.4 = (bf16[2,64,2048]{2,1,0:T(8,128)(2,1)S(1)}, bf16[2,64,2048]{2,1,0:T(8,128)(2,1)}, u32[]{:S(2)}, u32[]{:S(2)}) collective-permute-start(bf16[2,64,2048]{2,1,0:T(8,128)(2,1)S(1)} %pad_maximum_fusion), channel_id=1, source_target_pairs={{0,4},{1,5},{2,6},{3,7},{4,8},{5,9},{6,10},{7,11},{8,12},{9,13},{1... | collective-permute-start | bytes 1572872 | tf_op jit(solution)/shard_map/ppermute | solution.py:36
  36.7 28.5 %all-to-all-start.1 = ((f32[64,5,128]{2,1,0:T(8,128)}), f32[64,5,128]{2,1,0:T(8,128)S(1)}, u32[]{:S(2)}, u32[]{:S(2)}) async-start(f32[64,5,128]{2,1,0:T(8,128)} %reshape.73), calls=%async_computation.1 | async-start | bytes 524288 | tf_op jit(solution)/shard_map/all_to_all | solution.py:92
  47.5 26.1 %copy-start.8 = (f32[17,160,1]{1,0,2:T(8,128)S(1)}, f32[17,160,1]{1,0,2:T(8,128)}, u32[]{:S(2)}) copy-start(f32[17,160,1]{1,0,2:T(8,128)} %constant.70) | copy-start | bytes 32644
  66.0 19.7 %all-to-all-start.2 = ((f32[64,5,128]{2,1,0:T(8,128)}), f32[64,5,128]{2,1,0:T(8,128)S(1)}, u32[]{:S(2)}, u32[]{:S(2)}) async-start(f32[64,5,128]{2,1,0:T(8,128)} %reduce-window_subtract_fusion), calls=%async_computation.2 | async-start | bytes 524288 | tf_op jit(solution)/shard_map/all_to_all | solution.py:94
  86.5 51.7 %copy-start.3 = (bf16[2,64,2048]{2,1,0:T(8,128)(2,1)}, bf16[2,64,2048]{2,1,0:T(8,128)(2,1)S(1)}, u32[]{:S(2)}) copy-start(bf16[2,64,2048]{2,1,0:T(8,128)(2,1)S(1)} %collective-permute-done.refs_0_) | copy-start | bytes 1572868
  86.5 44.2 %collective-permute-start.5 = (bf16[2,64,2048]{2,1,0:T(8,128)(2,1)S(1)}, bf16[2,64,2048]{2,1,0:T(8,128)(2,1)S(1)}, u32[]{:S(2)}, u32[]{:S(2)}) collective-permute-start(bf16[2,64,2048]{2,1,0:T(8,128)(2,1)S(1)} %pad_maximum_fusion), channel_id=1, source_target_pairs={{0,3},{1,4},{2,5},{3,6},{4,7},{5,8},{6,9},{7,10},{8,11},{9,12},{10... | collective-permute-start | bytes 1572872 | tf_op jit(solution)/shard_map/ppermute | solution.py:36
  109.8 28.3 %copy-start.4 = (bf16[2,64,2048]{2,1,0:T(8,128)(2,1)}, bf16[2,64,2048]{2,1,0:T(8,128)(2,1)S(1)}, u32[]{:S(2)}) copy-start(bf16[2,64,2048]{2,1,0:T(8,128)(2,1)S(1)} %collective-permute-done.1.refs_1_) | copy-start | bytes 1572868
  109.8 22.7 %collective-permute-start.6 = (bf16[2,64,2048]{2,1,0:T(8,128)(2,1)S(1)}, bf16[2,64,2048]{2,1,0:T(8,128)(2,1)S(1)}, u32[]{:S(2)}, u32[]{:S(2)}) collective-permute-start(bf16[2,64,2048]{2,1,0:T(8,128)(2,1)S(1)} %pad_maximum_fusion), channel_id=1, source_target_pairs={{0,2},{1,3},{2,4},{3,5},{4,6},{5,7},{6,8},{7,9},{8,10},{9,11},{10,... | collective-permute-start | bytes 1572872 | tf_op jit(solution)/shard_map/ppermute | solution.py:36
  111.8 26.4 %collective-permute-start.7 = (bf16[2,64,2048]{2,1,0:T(8,128)(2,1)S(1)}, bf16[2,64,2048]{2,1,0:T(8,128)(2,1)}, u32[]{:S(2)}, u32[]{:S(2)}) collective-permute-start(bf16[2,64,2048]{2,1,0:T(8,128)(2,1)S(1)} %pad_maximum_fusion), channel_id=1, source_target_pairs={{0,1},{1,2},{2,3},{3,4},{4,5},{5,6},{6,7},{7,8},{8,9},{9,10},{10,1... | collective-permute-start | bytes 1572872 | tf_op jit(solution)/shard_map/ppermute | solution.py:36
  115.4 31.3 %all-to-all-start.3 = ((bf16[8,64,256]{2,1,0:T(8,128)(2,1)}), bf16[8,64,256]{2,1,0:T(8,128)(2,1)S(1)}, u32[]{:S(2)}, u32[]{:S(2)}) async-start(bf16[8,64,256]{2,1,0:T(8,128)(2,1)} %reshape.76), calls=%async_computation.3 | async-start | bytes 524288 | tf_op jit(solution)/shard_map/all_to_all | solution.py:140
  130.6 7.5 %copy-start.5 = (bf16[2,64,2048]{2,1,0:T(8,128)(2,1)}, bf16[2,64,2048]{2,1,0:T(8,128)(2,1)S(1)}, u32[]{:S(2)}) copy-start(bf16[2,64,2048]{2,1,0:T(8,128)(2,1)S(1)} %collective-permute-done.5.refs_5_) | copy-start | bytes 1572868
  132.5 5.7 %copy-start.6 = (bf16[2,64,2048]{2,1,0:T(8,128)(2,1)}, bf16[2,64,2048]{2,1,0:T(8,128)(2,1)S(1)}, u32[]{:S(2)}) copy-start(bf16[2,64,2048]{2,1,0:T(8,128)(2,1)S(1)} %collective-permute-done.6.refs_6_) | copy-start | bytes 1572868

commit v11 on v10

--- a/solution.py
+++ b/solution.py
@@ -68,20 +68,31 @@
         out_ref[:, lanes] = lax.dot_general(probs, values, (((1,), (0,)), ((), ())),
                                             preferred_element_type=jnp.float32).astype(out_ref.dtype)
 
-def window_attention(pos, query, key, value, earlier):
+def window_attention(pos, query, key, value, arrived, picks):
     rows, channels = query.shape
     lanes = 4 * SDIM
     steps = channels // lanes
     flat = pl.BlockSpec((rows, lanes), lambda g, p: (0, g))
-    stacked = pl.BlockSpec((2, rows, lanes), lambda g, p: (0, 0, g))
+    picked = [
+        pl.BlockSpec((None, 2, rows, lanes), lambda g, p, half=half: (half, 0, 0, g))
+        for _, half in picks
+    ]
     return pl.pallas_call(
         window_kernel,
         out_shape=jax.ShapeDtypeStruct((rows, channels), jnp.bfloat16),
         grid_spec=pltpu.PrefetchScalarGridSpec(
-            num_scalar_prefetch=1, grid=(steps,),
-            in_specs=[flat, flat, flat] + [stacked] * len(earlier),
-            out_specs=flat),
-    )(jnp.reshape(pos, (1,)).astype(jnp.int32), query, key, value, *earlier)
+            num_scalar_prefetch=1,
+            grid=(steps,),
+            in_specs=[flat, flat, flat] + picked,
+            out_specs=flat,
+        ),
+    )(
+        jnp.reshape(pos, (1,)).astype(jnp.int32),
+        query,
+        key,
+        value,
+        *[arrived[i] for i, _ in picks],
+    )
 
 
 def groups_before(total):
@@ -156,8 +167,17 @@
 
     stacked = jnp.stack([window_key, window_value])
     linear_out, stacked = linear_heads(linear_query, linear_key, linear_value, lin_gain, stacked)
-    earlier = [passed_along(stacked, ALL, reach_dev - t) for t in range(reach_dev)]
-    window_out = window_attention(device_pos, window_query, window_key, window_value, earlier)
+    half = reach_dev // 2
+    relayed = passed_along(stacked, ALL, half)
+    pair = jnp.stack([stacked, relayed])
+    arrived = [passed_along(pair, ALL, k) for k in range(1, half + 1)]
+    picks = []
+    for t in range(reach_dev):
+        distance = reach_dev - t
+        picks.append((distance - half - 1, 1) if distance > half else (distance - 1, 0))
+    window_out = window_attention(
+        device_pos, window_query, window_key, window_value, arrived, picks
+    )
     return (linear_out, window_out)
 
 

time: 148 us -> 133 us (0.90)
  starting transfers between devices: 78.5 us -> 50.2 us
  matrix products: 6.37 us -> 11.2 us
  local copies, waits for them, and re-layouts: 6.15 us -> 10.1 us
  other arithmetic: 2.06 us -> 5.73 us
    all_to_all x1, waiting for transfers between devices: 0.01 us -> 35.2 us  [linear_heads(): back = lax.all_to_all(out, GROUP, split_axis=0, concat_axis=2, tiled=True)]
    ppermute x8 -> x5, starting transfers between devices: 51.1 us -> 16.3 us  [passed_along(): return lax.ppermute(shard, axis, pairs)]
    ppermute x8 -> x5, waiting for transfers between devices: 18.4 us -> 0.01 us  [passed_along(): return lax.ppermute(shard, axis, pairs)]
    all_to_all x1, waiting for transfers between devices: 10.5 us -> 0.01 us  [groups_before(): lax.all_to_all(prefix, outer, split_axis=0, concat_axis=0, tiled=True)]
    all_to_all x1, waiting for transfers between devices: 15.9 us -> 8.13 us  [groups_before(): held = lax.all_to_all(dealt, outer, split_axis=0, concat_axis=0, tiled=True)]
    all_to_all x1, starting transfers between devices: 10.3 us -> 16.4 us  [groups_before(): held = lax.all_to_all(dealt, outer, split_axis=0, concat_axis=0, tiled=True)]
    another operation x1 -> x2, other arithmetic: 0.05 us -> 3.03 us  [shards(): pair = jnp.stack([stacked, relayed])]
    dot_general x4, matrix products: 2.93 us -> 5.69 us  [sym_features(): jnp.einsum('jhi,if->jhf', ext, jnp.asarray(table), precision=lax.Precisio...]
  transfers between devices with their start and end apart: 12 -> 9, of which waited for: 5 -> 3; matrix products, arithmetic and copies ran while one was open for 7% -> 16% of each run, Pallas kernels for 6% -> 0%
where the time goes in v11:
time: 133 us; the launch traced here: 132 us
  starting transfers between devices  50.2 us (38%)
  waiting for transfers between devices  45.7 us (34%)
  matrix products  11.2 us (8%)
  local copies, waits for them, and re-layouts  10.1 us (8%)
  Pallas kernels  8.51 us (6%)
  other arithmetic  5.73 us (4%)
    all_to_all x1, waiting for transfers between devices, linear_heads(): back = lax.all_to_all(out, GROUP, split_axis=0, concat_axis=2, tiled=True)  35.2 us
    all_to_all x1, starting transfers between devices, groups_before(): held = lax.all_to_all(dealt, outer, split_axis=0, concat_axis=0, tiled=True)  16.4 us
    ppermute x5, starting transfers between devices, passed_along(): return lax.ppermute(shard, axis, pairs)  16.3 us
    pallas_call x1, Pallas kernels, window_attention(): pl.pallas_call(window_kernel, out_shape=jax.ShapeDtypeStruct((rows, chann...  8.51 us
    all_to_all x1, waiting for transfers between devices, groups_before(): held = lax.all_to_all(dealt, outer, split_axis=0, concat_axis=0, tiled=True)  8.13 us
    all_to_all x1, starting transfers between devices, groups_before(): lax.all_to_all(prefix, outer, split_axis=0, concat_axis=0, tiled=True)  6.51 us
    all_to_all x1, starting transfers between devices, linear_heads(): back = lax.all_to_all(out, GROUP, split_axis=0, concat_axis=2, tiled=True)  6.07 us
    dot_general x4, matrix products, sym_features(): jnp.einsum('jhi,if->jhf', ext, jnp.asarray(table), precision=lax.Precisio...  5.69 us
  transfers between devices with their start and end apart: 9, of which 3 were waited for; matrix products, arithmetic and copies ran while one was open for 16% of the time, Pallas kernels for 0%

profile of v11, /device:TPU:9, one launch (start us, length us, event | category | flops | bytes accessed | tf_op | source)
XLA Modules:
  0.0 132.4 jit_solution(8397136605277702156)
XLA Ops:
  0.7 1.0 copy.42
  1.7 0.9 copy.26
  3.7 1.0 pad_maximum_fusion.2
  4.7 5.0 %all-to-all-start = ((bf16[64,8,320]{2,0,1:T(8,128)(2,1)}), bf16[64,8,320]{2,0,1:T(8,128)(2,1)S(1)}, u32[]{:S(2)}, u32[]{:S(2)}) async-start(bf16[64,8,320]{2,0,1:T(8,128)(2,1)} %pad_maximum_fusion.2), calls=%async_computation | async-start | bytes 786432 | tf_op jit(solution)/shard_map/all_to_all | solution.py:122
  9.7 0.9 fusion.27
  10.6 3.9 %collective-permute-start = (bf16[2,64,2048]{2,1,0:T(8,128)(2,1)}, bf16[2,64,2048]{2,1,0:T(8,128)(2,1)}, u32[]{:S(2)}, u32[]{:S(2)}) collective-permute-start(bf16[2,64,2048]{2,1,0:T(8,128)(2,1)} %get-tuple-element.3), channel_id=1, source_target_pairs={{0,4},{1,5},{2,6},{3,7},{4,8},{5,9},{6,10},{7,11},{8,12},{9,13},{1... | collective-permute-start | bytes 1572872 | tf_op jit(solution)/shard_map/ppermute | solution.py:36
  15.3 2.4 %all-to-all-done = bf16[64,8,320]{2,0,1:T(8,128)(2,1)S(1)} async-done(((bf16[64,8,320]{2,0,1:T(8,128)(2,1)}), bf16[64,8,320]{2,0,1:T(8,128)(2,1)S(1)}, u32[]{:S(2)}, u32[]{:S(2)}) %all-to-all-start) | async-done | bytes 327712 | tf_op jit(solution)/shard_map/all_to_all | solution.py:122
  21.5 16.4 %all-to-all-start.1 = ((f32[64,5,128]{2,1,0:T(8,128)}), f32[64,5,128]{2,1,0:T(8,128)S(1)}, u32[]{:S(2)}, u32[]{:S(2)}) async-start(f32[64,5,128]{2,1,0:T(8,128)} %reshape.73), calls=%async_computation.1 | async-start | bytes 524288 | tf_op jit(solution)/shard_map/all_to_all | solution.py:103
  37.9 1.6 %fusion.14 = f32[512,2,160]{0,2,1:T(8,128)} fusion(f32[17,160,1]{1,0,2:T(8,128)S(1)} %copy-done.8, f32[512,2,16]{0,2,1:T(8,128)S(1)} %convert_multiply_fusion), kind=kOutput, calls=%fused_computation.25 | convolution fusion | flops 33423360 | bytes 731776 | tf_op jit(solution)/shard_map/jhi,if->jhf/dot_general | solution.py:43
  39.5 2.6 %fusion = f32[2,128,512]{2,1,0:T(8,128)} fusion(bf16[512,2,128]{0,2,1:T(8,128)(2,1)S(1)} %bitcast.54, f32[2,512,512]{2,1,0:T(8,128)S(1)} %fusion.29, pred[512,512]{1,0:T(8,128)(4,1)S(1)} %copy-done.6), kind=kOutput, calls=%fused_computation | convolution fusion | flops 808452096 | bytes 3145728 | tf_op jit(solution)/shard_map/hij,jhe->ihe/dot_general | solution.py:143
  42.1 8.1 %all-to-all-done.1 = f32[64,5,128]{2,1,0:T(8,128)S(1)} async-done(((f32[64,5,128]{2,1,0:T(8,128)}), f32[64,5,128]{2,1,0:T(8,128)S(1)}, u32[]{:S(2)}, u32[]{:S(2)}) %all-to-all-start.1) | async-done | bytes 163872 | tf_op jit(solution)/shard_map/all_to_all | solution.py:103
  51.0 6.5 %all-to-all-start.2 = ((f32[64,5,128]{2,1,0:T(8,128)}), f32[64,5,128]{2,1,0:T(8,128)S(1)}, u32[]{:S(2)}, u32[]{:S(2)}) async-start(f32[64,5,128]{2,1,0:T(8,128)} %reduce-window_subtract_fusion), calls=%async_computation.2 | async-start | bytes 524288 | tf_op jit(solution)/shard_map/all_to_all | solution.py:105
  57.5 2.1 %pad_maximum_fusion = bf16[2,2,64,2048]{3,2,1,0:T(8,128)(2,1)} fusion(bf16[1,2,64,2048]{3,2,1,0:T(8,128)(2,1)} %bitcast.21, bf16[1,2,64,2048]{3,2,1,0:T(8,128)(2,1)S(1)} %get-tuple-element.2), kind=kLoop, calls=%fused_computation.11 | loop fusion | flops 524288 | bytes 2097152 | tf_op jit(solution)/shard_map/stack | solution.py:172
  59.6 4.6 %collective-permute-start.1 = (bf16[2,2,64,2048]{3,2,1,0:T(8,128)(2,1)}, bf16[2,2,64,2048]{3,2,1,0:T(8,128)(2,1)S(1)}, u32[]{:S(2)}, u32[]{:S(2)}) collective-permute-start(bf16[2,2,64,2048]{3,2,1,0:T(8,128)(2,1)} %pad_maximum_fusion), channel_id=1, source_target_pairs={{0,4},{1,5},{2,6},{3,7},{4,8},{5,9},{6,10},{7,11},{8,12},{9,13},{1... | collective-permute-start | bytes 3145736 | tf_op jit(solution)/shard_map/ppermute | solution.py:36
  64.2 3.0 %collective-permute-start.2 = (bf16[2,2,64,2048]{3,2,1,0:T(8,128)(2,1)}, bf16[2,2,64,2048]{3,2,1,0:T(8,128)(2,1)S(1)}, u32[]{:S(2)}, u32[]{:S(2)}) collective-permute-start(bf16[2,2,64,2048]{3,2,1,0:T(8,128)(2,1)} %pad_maximum_fusion), channel_id=1, source_target_pairs={{0,3},{1,4},{2,5},{3,6},{4,7},{5,8},{6,9},{7,10},{8,11},{9,12},{10... | collective-permute-start | bytes 3145736 | tf_op jit(solution)/shard_map/ppermute | solution.py:36
  67.1 2.9 %collective-permute-start.3 = (bf16[2,2,64,2048]{3,2,1,0:T(8,128)(2,1)}, bf16[2,2,64,2048]{3,2,1,0:T(8,128)(2,1)S(1)}, u32[]{:S(2)}, u32[]{:S(2)}) collective-permute-start(bf16[2,2,64,2048]{3,2,1,0:T(8,128)(2,1)} %pad_maximum_fusion), channel_id=1, source_target_pairs={{0,2},{1,3},{2,4},{3,5},{4,6},{5,7},{6,8},{7,9},{8,10},{9,11},{10,... | collective-permute-start | bytes 3145736 | tf_op jit(solution)/shard_map/ppermute | solution.py:36
  70.1 1.9 %collective-permute-start.4 = (bf16[2,2,64,2048]{3,2,1,0:T(8,128)(2,1)}, bf16[2,2,64,2048]{3,2,1,0:T(8,128)(2,1)}, u32[]{:S(2)}, u32[]{:S(2)}) collective-permute-start(bf16[2,2,64,2048]{3,2,1,0:T(8,128)(2,1)} %pad_maximum_fusion), channel_id=1, source_target_pairs={{0,1},{1,2},{2,3},{3,4},{4,5},{5,6},{6,7},{7,8},{8,9},{9,10},{10,1... | collective-permute-start | bytes 3145736 | tf_op jit(solution)/shard_map/ppermute | solution.py:36
  72.0 2.7 %convolution_multiply_fusion = f32[512,2,160]{0,2,1:T(8,128)} fusion(f32[512,2,160]{0,2,1:T(8,128)} %fusion.14, f32[17,160,1]{1,0,2:T(8,128)S(1)} %copy-done.7, f32[512,2,16]{0,2,1:T(8,128)S(1)} %convert_multiply_fusion), kind=kOutput, calls=%fused_computation.7 | convolution fusion | flops 33587200 | bytes 1387136 | tf_op jit(solution)/shard_map/jhi,if->jhf/dot_general | solution.py:43
  75.4 2.0 %multiply_reduce_fusion = (f32[512,2]{0,1:T(2,128)S(1)}, f32[512,2,128]{0,2,1:T(8,128)S(1)}) fusion(f32[2,128,512]{2,1,0:T(8,128)} %fusion, f32[2,160,128]{2,1,0:T(8,128)} %reshape.74, f32[512,2,160]{0,2,1:T(8,128)} %convolution_multiply_fusion), kind=kOutput, calls=%fused_computation.21 | convolution fusion | flops 252050432 | bytes 1871872 | tf_op jit(solution)/shard_map/ihf,hfe->ihe/dot_general | solution.py:134
  78.4 1.8 %reshape.76 = bf16[8,64,256]{2,1,0:T(8,128)(2,1)} reshape(bf16[512,2,128]{2,1,0:T(2,128)(2,1)} %copy.35) | data formatting | bytes 524288 | tf_op jit(solution)/shard_map/reshape | solution.py:150
  80.2 6.1 %all-to-all-start.3 = ((bf16[8,64,256]{2,1,0:T(8,128)(2,1)}), bf16[8,64,256]{2,1,0:T(8,128)(2,1)S(1)}, u32[]{:S(2)}, u32[]{:S(2)}) async-start(bf16[8,64,256]{2,1,0:T(8,128)(2,1)} %reshape.76), calls=%async_computation.3 | async-start | bytes 524288 | tf_op jit(solution)/shard_map/all_to_all | solution.py:151
  86.3 35.2 %all-to-all-done.3 = bf16[8,64,256]{2,1,0:T(8,128)(2,1)S(1)} async-done(((bf16[8,64,256]{2,1,0:T(8,128)(2,1)}), bf16[8,64,256]{2,1,0:T(8,128)(2,1)S(1)}, u32[]{:S(2)}, u32[]{:S(2)}) %all-to-all-start.3) | async-done | bytes 262176 | tf_op jit(solution)/shard_map/all_to_all | solution.py:151
  122.3 0.9 copy-done.1
  123.9 8.5 %shard_map.122 = bf16[64,2048]{1,0:T(8,128)(2,1)} custom-call(s32[1]{0:T(128)} %bitcast.17.pos_ref, bf16[64,2048]{1,0:T(8,128)(2,1)} %q_ref.1, bf16[64,2048]{1,0:T(8,128)(2,1)} %k_ref.1, bf16[64,2048]{1,0:T(8,128)(2,1)} %v_ref.1, bf16[2,2,64,2048]{3,2,1,0:T(8,128)(2,1)} %copy-done.1, bf16[2,2,64,2048]{3,2,1,0:T(8,128)(2,1)} %copy-done.2, ...), custom_call_target="tpu_custom_call" | custom-call | tf_op jit(solution)/shard_map/pallas_call | solution.py:80
  (48 shorter events, 9.6 us)
Async XLA Ops:
  0.6 13.9 %copy-start = (f32[2048]{0:T(1024)S(1)}, f32[2048]{0:T(1024)}, u32[]{:S(2)}) copy-start(f32[2048]{0:T(1024)} %param.14) | copy-start | bytes 24580
  0.6 9.1 %copy-start.4 = (bf16[64,2048]{1,0:T(8,128)(2,1)S(1)}, bf16[64,2048]{1,0:T(8,128)(2,1)}, u32[]{:S(2)}) copy-start(bf16[64,2048]{1,0:T(8,128)(2,1)} %k_ref.1) | copy-start | bytes 786436
  0.7 9.1 %copy-start.5 = (bf16[64,2048]{1,0:T(8,128)(2,1)S(1)}, bf16[64,2048]{1,0:T(8,128)(2,1)}, u32[]{:S(2)}) copy-start(bf16[64,2048]{1,0:T(8,128)(2,1)} %v_ref.1) | copy-start | bytes 786436
  4.7 12.9 %all-to-all-start = ((bf16[64,8,320]{2,0,1:T(8,128)(2,1)}), bf16[64,8,320]{2,0,1:T(8,128)(2,1)S(1)}, u32[]{:S(2)}, u32[]{:S(2)}) async-start(bf16[64,8,320]{2,0,1:T(8,128)(2,1)} %pad_maximum_fusion.2), calls=%async_computation | async-start | bytes 786432 | tf_op jit(solution)/shard_map/all_to_all | solution.py:122
  10.6 46.9 %collective-permute-start = (bf16[2,64,2048]{2,1,0:T(8,128)(2,1)}, bf16[2,64,2048]{2,1,0:T(8,128)(2,1)}, u32[]{:S(2)}, u32[]{:S(2)}) collective-permute-start(bf16[2,64,2048]{2,1,0:T(8,128)(2,1)} %get-tuple-element.3), channel_id=1, source_target_pairs={{0,4},{1,5},{2,6},{3,7},{4,8},{5,9},{6,10},{7,11},{8,12},{9,13},{1... | collective-permute-start | bytes 1572872 | tf_op jit(solution)/shard_map/ppermute | solution.py:36
  17.7 1.1 copy-start.9
  17.9 1.6 %copy-start.7 = (f32[17,160,1]{1,0,2:T(8,128)S(1)}, f32[17,160,1]{1,0,2:T(8,128)}, u32[]{:S(2)}) copy-start(f32[17,160,1]{1,0,2:T(8,128)} %constant.69) | copy-start | bytes 32644
  18.8 19.1 %copy-start.8 = (f32[17,160,1]{1,0,2:T(8,128)S(1)}, f32[17,160,1]{1,0,2:T(8,128)}, u32[]{:S(2)}) copy-start(f32[17,160,1]{1,0,2:T(8,128)} %constant.70) | copy-start | bytes 32644
  20.3 19.2 %copy-start.6 = (pred[512,512]{1,0:T(8,128)(4,1)S(1)}, pred[512,512]{1,0:T(8,128)(4,1)}, u32[]{:S(2)}) copy-start(pred[512,512]{1,0:T(8,128)(4,1)} %iota_compare_fusion) | copy-start | bytes 786436
  21.5 28.7 %all-to-all-start.1 = ((f32[64,5,128]{2,1,0:T(8,128)}), f32[64,5,128]{2,1,0:T(8,128)S(1)}, u32[]{:S(2)}, u32[]{:S(2)}) async-start(f32[64,5,128]{2,1,0:T(8,128)} %reshape.73), calls=%async_computation.1 | async-start | bytes 524288 | tf_op jit(solution)/shard_map/all_to_all | solution.py:103
  51.0 23.7 %all-to-all-start.2 = ((f32[64,5,128]{2,1,0:T(8,128)}), f32[64,5,128]{2,1,0:T(8,128)S(1)}, u32[]{:S(2)}, u32[]{:S(2)}) async-start(f32[64,5,128]{2,1,0:T(8,128)} %reduce-window_subtract_fusion), calls=%async_computation.2 | async-start | bytes 524288 | tf_op jit(solution)/shard_map/all_to_all | solution.py:105
  59.6 62.6 %collective-permute-start.1 = (bf16[2,2,64,2048]{3,2,1,0:T(8,128)(2,1)}, bf16[2,2,64,2048]{3,2,1,0:T(8,128)(2,1)S(1)}, u32[]{:S(2)}, u32[]{:S(2)}) collective-permute-start(bf16[2,2,64,2048]{3,2,1,0:T(8,128)(2,1)} %pad_maximum_fusion), channel_id=1, source_target_pairs={{0,4},{1,5},{2,6},{3,7},{4,8},{5,9},{6,10},{7,11},{8,12},{9,13},{1... | collective-permute-start | bytes 3145736 | tf_op jit(solution)/shard_map/ppermute | solution.py:36
  64.2 58.0 %collective-permute-start.2 = (bf16[2,2,64,2048]{3,2,1,0:T(8,128)(2,1)}, bf16[2,2,64,2048]{3,2,1,0:T(8,128)(2,1)S(1)}, u32[]{:S(2)}, u32[]{:S(2)}) collective-permute-start(bf16[2,2,64,2048]{3,2,1,0:T(8,128)(2,1)} %pad_maximum_fusion), channel_id=1, source_target_pairs={{0,3},{1,4},{2,5},{3,6},{4,7},{5,8},{6,9},{7,10},{8,11},{9,12},{10... | collective-permute-start | bytes 3145736 | tf_op jit(solution)/shard_map/ppermute | solution.py:36
  67.1 55.1 %collective-permute-start.3 = (bf16[2,2,64,2048]{3,2,1,0:T(8,128)(2,1)}, bf16[2,2,64,2048]{3,2,1,0:T(8,128)(2,1)S(1)}, u32[]{:S(2)}, u32[]{:S(2)}) collective-permute-start(bf16[2,2,64,2048]{3,2,1,0:T(8,128)(2,1)} %pad_maximum_fusion), channel_id=1, source_target_pairs={{0,2},{1,3},{2,4},{3,5},{4,6},{5,7},{6,8},{7,9},{8,10},{9,11},{10,... | collective-permute-start | bytes 3145736 | tf_op jit(solution)/shard_map/ppermute | solution.py:36
  70.1 52.2 %collective-permute-start.4 = (bf16[2,2,64,2048]{3,2,1,0:T(8,128)(2,1)}, bf16[2,2,64,2048]{3,2,1,0:T(8,128)(2,1)}, u32[]{:S(2)}, u32[]{:S(2)}) collective-permute-start(bf16[2,2,64,2048]{3,2,1,0:T(8,128)(2,1)} %pad_maximum_fusion), channel_id=1, source_target_pairs={{0,1},{1,2},{2,3},{3,4},{4,5},{5,6},{6,7},{7,8},{8,9},{9,10},{10,1... | collective-permute-start | bytes 3145736 | tf_op jit(solution)/shard_map/ppermute | solution.py:36
  80.2 41.3 %all-to-all-start.3 = ((bf16[8,64,256]{2,1,0:T(8,128)(2,1)}), bf16[8,64,256]{2,1,0:T(8,128)(2,1)S(1)}, u32[]{:S(2)}, u32[]{:S(2)}) async-start(bf16[8,64,256]{2,1,0:T(8,128)(2,1)} %reshape.76), calls=%async_computation.3 | async-start | bytes 524288 | tf_op jit(solution)/shard_map/all_to_all | solution.py:151
  122.2 1.0 copy-start.1
  122.2 1.3 copy-start.2
  122.2 1.7 %copy-start.3 = (bf16[2,2,64,2048]{3,2,1,0:T(8,128)(2,1)}, bf16[2,2,64,2048]{3,2,1,0:T(8,128)(2,1)S(1)}, u32[]{:S(2)}) copy-start(bf16[2,2,64,2048]{3,2,1,0:T(8,128)(2,1)S(1)} %collective-permute-done.3.refs_2_.refs_6_) | copy-start | bytes 3145732

commit v12 on v11

--- a/solution.py
+++ b/solution.py
@@ -73,8 +73,11 @@
     lanes = 4 * SDIM
     steps = channels // lanes
     flat = pl.BlockSpec((rows, lanes), lambda g, p: (0, g))
+    single = pl.BlockSpec((2, rows, lanes), lambda g, p: (0, 0, g))
     picked = [
-        pl.BlockSpec((None, 2, rows, lanes), lambda g, p, half=half: (half, 0, 0, g))
+        single
+        if half is None
+        else pl.BlockSpec((None, 2, rows, lanes), lambda g, p, half=half: (half, 0, 0, g))
         for _, half in picks
     ]
     return pl.pallas_call(
@@ -170,11 +173,19 @@
     half = reach_dev // 2
     relayed = passed_along(stacked, ALL, half)
     pair = jnp.stack([stacked, relayed])
-    arrived = [passed_along(pair, ALL, k) for k in range(1, half + 1)]
+    arrived = [passed_along(pair, ALL, k) for k in range(1, half)]
+    arrived += [relayed, passed_along(relayed, ALL, half)]
     picks = []
     for t in range(reach_dev):
         distance = reach_dev - t
-        picks.append((distance - half - 1, 1) if distance > half else (distance - 1, 0))
+        if distance == reach_dev:
+            picks.append((half, None))
+        elif distance == half:
+            picks.append((half - 1, None))
+        elif distance > half:
+            picks.append((distance - half - 1, 1))
+        else:
+            picks.append((distance - 1, 0))
     window_out = window_attention(
         device_pos, window_query, window_key, window_value, arrived, picks
     )

time: 133 us -> 133 us (level)
  the two profiles are of different devices: /device:TPU:9 before, /device:TPU:1 now
where the time goes in v12:
time: 133 us; the launch traced here: 132 us
  starting transfers between devices  48.7 us (37%)
  waiting for transfers between devices  40.3 us (30%)
  matrix products  15.1 us (11%)
  local copies, waits for them, and re-layouts  12.6 us (9%)
  Pallas kernels  8.51 us (6%)
  other arithmetic  5.47 us (4%)
    all_to_all x1, waiting for transfers between devices, linear_heads(): back = lax.all_to_all(out, GROUP, split_axis=0, concat_axis=2, tiled=True)  28.4 us
    ppermute x5, starting transfers between devices, passed_along(): return lax.ppermute(shard, axis, pairs)  14.8 us
    all_to_all x1, starting transfers between devices, groups_before(): held = lax.all_to_all(dealt, outer, split_axis=0, concat_axis=0, tiled=True)  12.1 us
    all_to_all x1, starting transfers between devices, linear_heads(): got = lax.all_to_all(packed, GROUP, split_axis=1, concat_axis=0, tiled=True)  10.3 us
    pallas_call x1, Pallas kernels, window_attention(): pl.pallas_call(window_kernel, out_shape=jax.ShapeDtypeStruct((rows, chann...  8.51 us
    dot_general x4, matrix products, sym_features(): jnp.einsum('jhi,if->jhf', ext, jnp.asarray(table), precision=lax.Precisio...  7.97 us
    all_to_all x1, waiting for transfers between devices, groups_before(): held = lax.all_to_all(dealt, outer, split_axis=0, concat_axis=0, tiled=True)  7.57 us
    all_to_all x1, starting transfers between devices, linear_heads(): back = lax.all_to_all(out, GROUP, split_axis=0, concat_axis=2, tiled=True)  5.96 us
  transfers between devices with their start and end apart: 9, of which 3 were waited for; matrix products, arithmetic and copies ran while one was open for 20% of the time, Pallas kernels for 0%

profile of v12, /device:TPU:1, one launch (start us, length us, event | category | flops | bytes accessed | tf_op | source)
XLA Modules:
  0.0 131.6 jit_solution(18300828510306313039)
XLA Ops:
  3.7 1.0 pad_maximum_fusion.2
  4.7 10.3 %all-to-all-start = ((bf16[64,8,320]{2,0,1:T(8,128)(2,1)}), bf16[64,8,320]{2,0,1:T(8,128)(2,1)S(1)}, u32[]{:S(2)}, u32[]{:S(2)}) async-start(bf16[64,8,320]{2,0,1:T(8,128)(2,1)} %pad_maximum_fusion.2), calls=%async_computation | async-start | bytes 786432 | tf_op jit(solution)/shard_map/all_to_all | solution.py:125
  15.9 1.9 %collective-permute-start = (bf16[2,64,2048]{2,1,0:T(8,128)(2,1)}, bf16[2,64,2048]{2,1,0:T(8,128)(2,1)S(1)}, u32[]{:S(2)}, u32[]{:S(2)}) collective-permute-start(bf16[2,64,2048]{2,1,0:T(8,128)(2,1)} %get-tuple-element.3), channel_id=1, source_target_pairs={{0,4},{1,5},{2,6},{3,7},{4,8},{5,9},{6,10},{7,11},{8,12},{9,13},{1... | collective-permute-start | bytes 1572872 | tf_op jit(solution)/shard_map/ppermute | solution.py:36
  18.6 4.4 %all-to-all-done = bf16[64,8,320]{2,0,1:T(8,128)(2,1)S(1)} async-done(((bf16[64,8,320]{2,0,1:T(8,128)(2,1)}), bf16[64,8,320]{2,0,1:T(8,128)(2,1)S(1)}, u32[]{:S(2)}, u32[]{:S(2)}) %all-to-all-start) | async-done | bytes 327712 | tf_op jit(solution)/shard_map/all_to_all | solution.py:125
  26.1 1.5 %fusion.17 = f32[512,2,160]{0,2,1:T(8,128)S(1)} fusion(f32[17,160,1]{1,0,2:T(8,128)} %constant.68, f32[512,2,16]{0,2,1:T(8,128)S(1)} %convert_multiply_fusion.1), kind=kOutput, calls=%fused_computation.28 | convolution fusion | flops 33423360 | bytes 731776 | tf_op jit(solution)/shard_map/jhi,if->jhf/dot_general | solution.py:43
  27.6 1.5 %convolution_multiply_fusion.1 = f32[512,2,160]{0,2,1:T(8,128)S(1)} fusion(f32[512,2,160]{0,2,1:T(8,128)S(1)} %fusion.17, f32[17,160,1]{1,0,2:T(8,128)} %constant.69, f32[512,2,16]{0,2,1:T(8,128)S(1)} %convert_multiply_fusion.1), kind=kOutput, calls=%fused_computation.8 | convolution fusion | flops 33587200 | bytes 1387136 | tf_op jit(solution)/shard_map/jhi,if->jhf/dot_general | solution.py:43
  29.1 1.1 fusion.30
  30.2 1.6 %reshape.73 = f32[64,5,128]{2,1,0:T(8,128)} reshape(f32[2,160,128]{2,1,0:T(8,128)} %fusion.30) | data formatting | bytes 327680 | tf_op jit(solution)/shard_map/reshape | solution.py:105
  31.9 12.1 %all-to-all-start.1 = ((f32[64,5,128]{2,1,0:T(8,128)}), f32[64,5,128]{2,1,0:T(8,128)S(1)}, u32[]{:S(2)}, u32[]{:S(2)}) async-start(f32[64,5,128]{2,1,0:T(8,128)} %reshape.73), calls=%async_computation.1 | async-start | bytes 524288 | tf_op jit(solution)/shard_map/all_to_all | solution.py:106
  44.0 2.3 %fusion.14 = f32[512,2,160]{0,2,1:T(8,128)} fusion(f32[17,160,1]{1,0,2:T(8,128)} %constant.70, f32[512,2,16]{0,2,1:T(8,128)S(1)} %convert_multiply_fusion), kind=kOutput, calls=%fused_computation.25 | convolution fusion | flops 33423360 | bytes 731776 | tf_op jit(solution)/shard_map/jhi,if->jhf/dot_general | solution.py:43
  46.3 3.6 %fusion = f32[2,128,512]{2,1,0:T(8,128)} fusion(bf16[512,2,128]{0,2,1:T(8,128)(2,1)} %bitcast.54, f32[2,512,512]{2,1,0:T(8,128)S(1)} %fusion.29, pred[512,512]{1,0:T(8,128)(4,1)} %iota_compare_fusion), kind=kOutput, calls=%fused_computation | convolution fusion | flops 808452096 | bytes 3145728 | tf_op jit(solution)/shard_map/hij,jhe->ihe/dot_general | solution.py:146
  49.9 7.6 %all-to-all-done.1 = f32[64,5,128]{2,1,0:T(8,128)S(1)} async-done(((f32[64,5,128]{2,1,0:T(8,128)}), f32[64,5,128]{2,1,0:T(8,128)S(1)}, u32[]{:S(2)}, u32[]{:S(2)}) %all-to-all-start.1) | async-done | bytes 163872 | tf_op jit(solution)/shard_map/all_to_all | solution.py:106
  58.3 5.5 %all-to-all-start.2 = ((f32[64,5,128]{2,1,0:T(8,128)}), f32[64,5,128]{2,1,0:T(8,128)}, u32[]{:S(2)}, u32[]{:S(2)}) async-start(f32[64,5,128]{2,1,0:T(8,128)} %reduce-window_subtract_fusion), calls=%async_computation.2 | async-start | bytes 524288 | tf_op jit(solution)/shard_map/all_to_all | solution.py:108
  63.8 1.1 pad_maximum_fusion
  65.0 2.4 %collective-permute-start.2 = (bf16[2,2,64,2048]{3,2,1,0:T(8,128)(2,1)}, bf16[2,2,64,2048]{3,2,1,0:T(8,128)(2,1)S(1)}, u32[]{:S(2)}, u32[]{:S(2)}) collective-permute-start(bf16[2,2,64,2048]{3,2,1,0:T(8,128)(2,1)} %pad_maximum_fusion), channel_id=1, source_target_pairs={{0,3},{1,4},{2,5},{3,6},{4,7},{5,8},{6,9},{7,10},{8,11},{9,12},{10... | collective-permute-start | bytes 3145736 | tf_op jit(solution)/shard_map/ppermute | solution.py:36
  67.4 6.4 %collective-permute-start.3 = (bf16[2,2,64,2048]{3,2,1,0:T(8,128)(2,1)}, bf16[2,2,64,2048]{3,2,1,0:T(8,128)(2,1)S(1)}, u32[]{:S(2)}, u32[]{:S(2)}) collective-permute-start(bf16[2,2,64,2048]{3,2,1,0:T(8,128)(2,1)} %pad_maximum_fusion), channel_id=1, source_target_pairs={{0,2},{1,3},{2,4},{3,5},{4,6},{5,7},{6,8},{7,9},{8,10},{9,11},{10,... | collective-permute-start | bytes 3145736 | tf_op jit(solution)/shard_map/ppermute | solution.py:36
  73.9 1.9 %collective-permute-start.4 = (bf16[2,2,64,2048]{3,2,1,0:T(8,128)(2,1)}, bf16[2,2,64,2048]{3,2,1,0:T(8,128)(2,1)S(1)}, u32[]{:S(2)}, u32[]{:S(2)}) collective-permute-start(bf16[2,2,64,2048]{3,2,1,0:T(8,128)(2,1)} %pad_maximum_fusion), channel_id=1, source_target_pairs={{0,1},{1,2},{2,3},{3,4},{4,5},{5,6},{6,7},{7,8},{8,9},{9,10},{10,1... | collective-permute-start | bytes 3145736 | tf_op jit(solution)/shard_map/ppermute | solution.py:36
  75.8 2.7 %convolution_multiply_fusion = f32[512,2,160]{0,2,1:T(8,128)} fusion(f32[512,2,160]{0,2,1:T(8,128)} %fusion.14, f32[17,160,1]{1,0,2:T(8,128)S(1)} %copy-done.9, f32[512,2,16]{0,2,1:T(8,128)S(1)} %convert_multiply_fusion), kind=kOutput, calls=%fused_computation.7 | convolution fusion | flops 33587200 | bytes 1387136 | tf_op jit(solution)/shard_map/jhi,if->jhf/dot_general | solution.py:43
  78.5 2.1 %collective-permute-start.1 = (bf16[2,64,2048]{2,1,0:T(8,128)(2,1)}, bf16[2,64,2048]{2,1,0:T(8,128)(2,1)}, u32[]{:S(2)}, u32[]{:S(2)}) collective-permute-start(bf16[2,64,2048]{2,1,0:T(8,128)(2,1)} %copy-done.4), channel_id=1, source_target_pairs={{0,4},{1,5},{2,6},{3,7},{4,8},{5,9},{6,10},{7,11},{8,12},{9,13},{1... | collective-permute-start | bytes 1572872 | tf_op jit(solution)/shard_map/ppermute | solution.py:36
  81.6 2.0 %multiply_reduce_fusion = (f32[512,2]{0,1:T(2,128)S(1)}, f32[512,2,128]{0,2,1:T(8,128)S(1)}) fusion(f32[2,128,512]{2,1,0:T(8,128)} %fusion, f32[2,160,128]{2,1,0:T(8,128)S(1)} %reshape.74, f32[512,2,160]{0,2,1:T(8,128)} %convolution_multiply_fusion), kind=kOutput, calls=%fused_computation.21 | convolution fusion | flops 252050432 | bytes 1871872 | tf_op jit(solution)/shard_map/ihf,hfe->ihe/dot_general | solution.py:137
  84.6 1.8 %reshape.76 = bf16[8,64,256]{2,1,0:T(8,128)(2,1)} reshape(bf16[512,2,128]{2,1,0:T(2,128)(2,1)} %copy.35) | data formatting | bytes 524288 | tf_op jit(solution)/shard_map/reshape | solution.py:153
  86.4 6.0 %all-to-all-start.3 = ((bf16[8,64,256]{2,1,0:T(8,128)(2,1)}), bf16[8,64,256]{2,1,0:T(8,128)(2,1)S(1)}, u32[]{:S(2)}, u32[]{:S(2)}) async-start(bf16[8,64,256]{2,1,0:T(8,128)(2,1)} %reshape.76), calls=%async_computation.3 | async-start | bytes 524288 | tf_op jit(solution)/shard_map/all_to_all | solution.py:154
  92.4 28.4 %all-to-all-done.3 = bf16[8,64,256]{2,1,0:T(8,128)(2,1)S(1)} async-done(((bf16[8,64,256]{2,1,0:T(8,128)(2,1)}), bf16[8,64,256]{2,1,0:T(8,128)(2,1)S(1)}, u32[]{:S(2)}, u32[]{:S(2)}) %all-to-all-start.3) | async-done | bytes 262176 | tf_op jit(solution)/shard_map/all_to_all | solution.py:154
  123.1 8.5 %shard_map.122 = bf16[64,2048]{1,0:T(8,128)(2,1)} custom-call(s32[1]{0:T(128)} %bitcast.17.pos_ref, bf16[64,2048]{1,0:T(8,128)(2,1)} %q_ref.1, bf16[64,2048]{1,0:T(8,128)(2,1)} %k_ref.1, bf16[64,2048]{1,0:T(8,128)(2,1)} %v_ref.1, bf16[2,64,2048]{2,1,0:T(8,128)(2,1)} %collective-permute-done.1.refs_0_, bf16[2,2,64,2048]{3,2,1,0:T(8,128)(2,1)} %copy-done.1, ...), custom_call_target="tpu_custom_call" | custom-call | tf_op jit(solution)/shard_map/pallas_call | solution.py:83
  (48 shorter events, 12.9 us)
Async XLA Ops:
  0.6 17.2 %copy-start = (f32[2048]{0:T(1024)S(1)}, f32[2048]{0:T(1024)}, u32[]{:S(2)}) copy-start(f32[2048]{0:T(1024)} %param.14) | copy-start | bytes 24580
  0.6 14.4 %copy-start.5 = (bf16[64,2048]{1,0:T(8,128)(2,1)S(1)}, bf16[64,2048]{1,0:T(8,128)(2,1)}, u32[]{:S(2)}) copy-start(bf16[64,2048]{1,0:T(8,128)(2,1)} %k_ref.1) | copy-start | bytes 786436
  0.7 14.3 %copy-start.6 = (bf16[64,2048]{1,0:T(8,128)(2,1)S(1)}, bf16[64,2048]{1,0:T(8,128)(2,1)}, u32[]{:S(2)}) copy-start(bf16[64,2048]{1,0:T(8,128)(2,1)} %v_ref.1) | copy-start | bytes 786436
  4.7 18.2 %all-to-all-start = ((bf16[64,8,320]{2,0,1:T(8,128)(2,1)}), bf16[64,8,320]{2,0,1:T(8,128)(2,1)S(1)}, u32[]{:S(2)}, u32[]{:S(2)}) async-start(bf16[64,8,320]{2,0,1:T(8,128)(2,1)} %pad_maximum_fusion.2), calls=%async_computation | async-start | bytes 786432 | tf_op jit(solution)/shard_map/all_to_all | solution.py:125
  15.9 48.0 %collective-permute-start = (bf16[2,64,2048]{2,1,0:T(8,128)(2,1)}, bf16[2,64,2048]{2,1,0:T(8,128)(2,1)S(1)}, u32[]{:S(2)}, u32[]{:S(2)}) collective-permute-start(bf16[2,64,2048]{2,1,0:T(8,128)(2,1)} %get-tuple-element.3), channel_id=1, source_target_pairs={{0,4},{1,5},{2,6},{3,7},{4,8},{5,9},{6,10},{7,11},{8,12},{9,13},{1... | collective-permute-start | bytes 1572872 | tf_op jit(solution)/shard_map/ppermute | solution.py:36
  23.4 0.6 copy-start.8
  26.1 3.0 %copy-start.7 = (bf16[512,256]{0,1:T(8,128)(2,1)S(1)}, bf16[512,256]{0,1:T(8,128)(2,1)}, u32[]{:S(2)}) copy-start(bf16[512,256]{0,1:T(8,128)(2,1)} %copy.31) | copy-start | bytes 786436
  31.9 25.6 %all-to-all-start.1 = ((f32[64,5,128]{2,1,0:T(8,128)}), f32[64,5,128]{2,1,0:T(8,128)S(1)}, u32[]{:S(2)}, u32[]{:S(2)}) async-start(f32[64,5,128]{2,1,0:T(8,128)} %reshape.73), calls=%async_computation.1 | async-start | bytes 524288 | tf_op jit(solution)/shard_map/all_to_all | solution.py:106
  49.9 25.9 %copy-start.9 = (f32[17,160,1]{1,0,2:T(8,128)S(1)}, f32[17,160,1]{1,0,2:T(8,128)}, u32[]{:S(2)}) copy-start(f32[17,160,1]{1,0,2:T(8,128)} %constant.69) | copy-start | bytes 32644
  58.3 22.3 %all-to-all-start.2 = ((f32[64,5,128]{2,1,0:T(8,128)}), f32[64,5,128]{2,1,0:T(8,128)}, u32[]{:S(2)}, u32[]{:S(2)}) async-start(f32[64,5,128]{2,1,0:T(8,128)} %reduce-window_subtract_fusion), calls=%async_computation.2 | async-start | bytes 524288 | tf_op jit(solution)/shard_map/all_to_all | solution.py:108
  63.8 3.6 %copy-start.4 = (bf16[2,64,2048]{2,1,0:T(8,128)(2,1)}, bf16[2,64,2048]{2,1,0:T(8,128)(2,1)S(1)}, u32[]{:S(2)}) copy-start(bf16[2,64,2048]{2,1,0:T(8,128)(2,1)S(1)} %collective-permute-done.refs_4_) | copy-start | bytes 1572868
  65.0 56.5 %collective-permute-start.2 = (bf16[2,2,64,2048]{3,2,1,0:T(8,128)(2,1)}, bf16[2,2,64,2048]{3,2,1,0:T(8,128)(2,1)S(1)}, u32[]{:S(2)}, u32[]{:S(2)}) collective-permute-start(bf16[2,2,64,2048]{3,2,1,0:T(8,128)(2,1)} %pad_maximum_fusion), channel_id=1, source_target_pairs={{0,3},{1,4},{2,5},{3,6},{4,7},{5,8},{6,9},{7,10},{8,11},{9,12},{10... | collective-permute-start | bytes 3145736 | tf_op jit(solution)/shard_map/ppermute | solution.py:36
  67.4 54.0 %collective-permute-start.3 = (bf16[2,2,64,2048]{3,2,1,0:T(8,128)(2,1)}, bf16[2,2,64,2048]{3,2,1,0:T(8,128)(2,1)S(1)}, u32[]{:S(2)}, u32[]{:S(2)}) collective-permute-start(bf16[2,2,64,2048]{3,2,1,0:T(8,128)(2,1)} %pad_maximum_fusion), channel_id=1, source_target_pairs={{0,2},{1,3},{2,4},{3,5},{4,6},{5,7},{6,8},{7,9},{8,10},{9,11},{10,... | collective-permute-start | bytes 3145736 | tf_op jit(solution)/shard_map/ppermute | solution.py:36
  73.9 47.6 %collective-permute-start.4 = (bf16[2,2,64,2048]{3,2,1,0:T(8,128)(2,1)}, bf16[2,2,64,2048]{3,2,1,0:T(8,128)(2,1)S(1)}, u32[]{:S(2)}, u32[]{:S(2)}) collective-permute-start(bf16[2,2,64,2048]{3,2,1,0:T(8,128)(2,1)} %pad_maximum_fusion), channel_id=1, source_target_pairs={{0,1},{1,2},{2,3},{3,4},{4,5},{5,6},{6,7},{7,8},{8,9},{9,10},{10,1... | collective-permute-start | bytes 3145736 | tf_op jit(solution)/shard_map/ppermute | solution.py:36
  78.5 43.0 %collective-permute-start.1 = (bf16[2,64,2048]{2,1,0:T(8,128)(2,1)}, bf16[2,64,2048]{2,1,0:T(8,128)(2,1)}, u32[]{:S(2)}, u32[]{:S(2)}) collective-permute-start(bf16[2,64,2048]{2,1,0:T(8,128)(2,1)} %copy-done.4), channel_id=1, source_target_pairs={{0,4},{1,5},{2,6},{3,7},{4,8},{5,9},{6,10},{7,11},{8,12},{9,13},{1... | collective-permute-start | bytes 1572872 | tf_op jit(solution)/shard_map/ppermute | solution.py:36
  86.4 34.3 %all-to-all-start.3 = ((bf16[8,64,256]{2,1,0:T(8,128)(2,1)}), bf16[8,64,256]{2,1,0:T(8,128)(2,1)S(1)}, u32[]{:S(2)}, u32[]{:S(2)}) async-start(bf16[8,64,256]{2,1,0:T(8,128)(2,1)} %reshape.76), calls=%async_computation.3 | async-start | bytes 524288 | tf_op jit(solution)/shard_map/all_to_all | solution.py:154
  121.5 1.0 copy-start.1
  121.5 1.3 copy-start.2
  121.5 1.6 %copy-start.3 = (bf16[2,2,64,2048]{3,2,1,0:T(8,128)(2,1)}, bf16[2,2,64,2048]{3,2,1,0:T(8,128)(2,1)S(1)}, u32[]{:S(2)}) copy-start(bf16[2,2,64,2048]{3,2,1,0:T(8,128)(2,1)S(1)} %collective-permute-done.4.refs_3_.refs_7_) | copy-start | bytes 3145732

commit v13 on v12

--- a/solution.py
+++ b/solution.py
@@ -122,6 +122,7 @@
         ],
         axis=-1,
     )
+    packed, held = lax.optimization_barrier((packed, held))
     got = lax.all_to_all(packed, GROUP, split_axis=1, concat_axis=0, tiled=True)
     rows = got.shape[0]
     got = got.reshape(rows, -1)
@@ -169,9 +170,9 @@
     lin_heads = linear_query.shape[1] // FDIM
 
     stacked = jnp.stack([window_key, window_value])
-    linear_out, stacked = linear_heads(linear_query, linear_key, linear_value, lin_gain, stacked)
     half = reach_dev // 2
     relayed = passed_along(stacked, ALL, half)
+    linear_out, relayed = linear_heads(linear_query, linear_key, linear_value, lin_gain, relayed)
     pair = jnp.stack([stacked, relayed])
     arrived = [passed_along(pair, ALL, k) for k in range(1, half)]
     arrived += [relayed, passed_along(relayed, ALL, half)]

time: 133 us -> 128 us (0.962)
  waiting for transfers between devices: 40.3 us -> 21.9 us
  starting transfers between devices: 48.7 us -> 65 us
  matrix products: 15.1 us -> 12.3 us
    all_to_all x1, waiting for transfers between devices: 28.4 us -> 0.01 us  [linear_heads(): back = lax.all_to_all(out, GROUP, split_axis=0, concat_axis=2, tiled=True)]
    all_to_all x1, starting transfers between devices: 5.96 us -> 19.5 us  [linear_heads(): back = lax.all_to_all(out, GROUP, split_axis=0, concat_axis=2, tiled=True)]
    all_to_all x1, waiting for transfers between devices: 0.01 us -> 10.1 us  [groups_before(): lax.all_to_all(prefix, outer, split_axis=0, concat_axis=0, tiled=True)]
    all_to_all x1, starting transfers between devices: 10.3 us -> 4.41 us  [linear_heads(): got = lax.all_to_all(packed, GROUP, split_axis=1, concat_axis=0, tiled=True)]
    ppermute x5, starting transfers between devices: 14.8 us -> 20.1 us  [passed_along(): return lax.ppermute(shard, axis, pairs)]
    all_to_all x1, waiting for transfers between devices: 4.36 us -> 0.01 us  [linear_heads(): got = lax.all_to_all(packed, GROUP, split_axis=1, concat_axis=0, tiled=True)]
    all_to_all x1, starting transfers between devices: 12.1 us -> 15.8 us  [groups_before(): held = lax.all_to_all(dealt, outer, split_axis=0, concat_axis=0, tiled=True)]
    ppermute x5, waiting for transfers between devices: 0.01 us -> 2.81 us  [passed_along(): return lax.ppermute(shard, axis, pairs)]
  transfers between devices with their start and end apart: 9 -> 9, of which waited for: 3 -> 3; matrix products, arithmetic and copies ran while one was open for 20% -> 21% of each run, Pallas kernels for 0% -> 7%
where the time goes in v13:
time: 128 us; the launch traced here: 127 us
  starting transfers between devices  65 us (51%)
  waiting for transfers between devices  21.9 us (17%)
  local copies, waits for them, and re-layouts  13.8 us (11%)
  matrix products  12.3 us (10%)
  Pallas kernels  8.51 us (7%)
  other arithmetic  4.91 us (4%)
    ppermute x5, starting transfers between devices, passed_along(): return lax.ppermute(shard, axis, pairs)  20.1 us
    all_to_all x1, starting transfers between devices, linear_heads(): back = lax.all_to_all(out, GROUP, split_axis=0, concat_axis=2, tiled=True)  19.5 us
    all_to_all x1, starting transfers between devices, groups_before(): held = lax.all_to_all(dealt, outer, split_axis=0, concat_axis=0, tiled=True)  15.8 us
    all_to_all x1, waiting for transfers between devices, groups_before(): lax.all_to_all(prefix, outer, split_axis=0, concat_axis=0, tiled=True)  10.1 us
    all_to_all x1, waiting for transfers between devices, groups_before(): held = lax.all_to_all(dealt, outer, split_axis=0, concat_axis=0, tiled=True)  9.04 us
    pallas_call x1, Pallas kernels, window_attention(): pl.pallas_call(window_kernel, out_shape=jax.ShapeDtypeStruct((rows, chann...  8.51 us
    dot_general x4, matrix products, sym_features(): jnp.einsum('jhi,if->jhf', ext, jnp.asarray(table), precision=lax.Precisio...  5.28 us
    all_to_all x1, starting transfers between devices, groups_before(): lax.all_to_all(prefix, outer, split_axis=0, concat_axis=0, tiled=True)  5.19 us
  transfers between devices with their start and end apart: 9, of which 3 were waited for; matrix products, arithmetic and copies ran while one was open for 21% of the time, Pallas kernels for 7%

profile of v13, /device:TPU:1, one launch (start us, length us, event | category | flops | bytes accessed | tf_op | source)
XLA Modules:
  0.0 127.4 jit_solution(2760822516035474490)
XLA Ops:
  0.7 1.1 fusion.27
  1.8 5.4 %collective-permute-start = (bf16[2,64,2048]{2,1,0:T(8,128)(2,1)S(1)}, bf16[2,64,2048]{2,1,0:T(8,128)(2,1)S(1)}, u32[]{:S(2)}, u32[]{:S(2)}) collective-permute-start(bf16[2,64,2048]{2,1,0:T(8,128)(2,1)S(1)} %get-tuple-element.7), channel_id=1, source_target_pairs={{0,4},{1,5},{2,6},{3,7},{4,8},{5,9},{6,10},{7,11},{8,12},{9,13},{1... | collective-permute-start | bytes 1572872 | tf_op jit(solution)/shard_map/ppermute | solution.py:36
  10.5 2.8 %collective-permute-done.refs_4_ = bf16[2,64,2048]{2,1,0:T(8,128)(2,1)S(1)} collective-permute-done((bf16[2,64,2048]{2,1,0:T(8,128)(2,1)S(1)}, bf16[2,64,2048]{2,1,0:T(8,128)(2,1)S(1)}, u32[]{:S(2)}, u32[]{:S(2)}) %collective-permute-start) | collective-permute-done | bytes 524320 | tf_op jit(solution)/shard_map/ppermute | solution.py:36
  13.3 4.4 %all-to-all-start = ((bf16[64,8,320]{2,0,1:T(8,128)(2,1)}), bf16[64,8,320]{2,0,1:T(8,128)(2,1)S(1)}, u32[]{:S(2)}, u32[]{:S(2)}) async-start(bf16[64,8,320]{2,0,1:T(8,128)(2,1)} %pad_maximum_fusion.2), calls=%async_computation | async-start | bytes 786432 | tf_op jit(solution)/shard_map/all_to_all | solution.py:126
  17.7 1.1 pad_maximum_fusion
  18.8 4.5 %collective-permute-start.2 = (bf16[2,2,64,2048]{3,2,1,0:T(8,128)(2,1)}, bf16[2,2,64,2048]{3,2,1,0:T(8,128)(2,1)S(1)}, u32[]{:S(2)}, u32[]{:S(2)}) collective-permute-start(bf16[2,2,64,2048]{3,2,1,0:T(8,128)(2,1)} %pad_maximum_fusion), channel_id=1, source_target_pairs={{0,3},{1,4},{2,5},{3,6},{4,7},{5,8},{6,9},{7,10},{8,11},{9,12},{10... | collective-permute-start | bytes 3145736 | tf_op jit(solution)/shard_map/ppermute | solution.py:36
  23.3 4.9 %collective-permute-start.3 = (bf16[2,2,64,2048]{3,2,1,0:T(8,128)(2,1)}, bf16[2,2,64,2048]{3,2,1,0:T(8,128)(2,1)S(1)}, u32[]{:S(2)}, u32[]{:S(2)}) collective-permute-start(bf16[2,2,64,2048]{3,2,1,0:T(8,128)(2,1)} %pad_maximum_fusion), channel_id=1, source_target_pairs={{0,2},{1,3},{2,4},{3,5},{4,6},{5,7},{6,8},{7,9},{8,10},{9,11},{10,... | collective-permute-start | bytes 3145736 | tf_op jit(solution)/shard_map/ppermute | solution.py:36
  28.3 2.5 %collective-permute-start.4 = (bf16[2,2,64,2048]{3,2,1,0:T(8,128)(2,1)}, bf16[2,2,64,2048]{3,2,1,0:T(8,128)(2,1)S(1)}, u32[]{:S(2)}, u32[]{:S(2)}) collective-permute-start(bf16[2,2,64,2048]{3,2,1,0:T(8,128)(2,1)} %pad_maximum_fusion), channel_id=1, source_target_pairs={{0,1},{1,2},{2,3},{3,4},{4,5},{5,6},{6,7},{7,8},{8,9},{9,10},{10,1... | collective-permute-start | bytes 3145736 | tf_op jit(solution)/shard_map/ppermute | solution.py:36
  30.7 2.8 %collective-permute-start.1 = (bf16[2,64,2048]{2,1,0:T(8,128)(2,1)}, bf16[2,64,2048]{2,1,0:T(8,128)(2,1)}, u32[]{:S(2)}, u32[]{:S(2)}) collective-permute-start(bf16[2,64,2048]{2,1,0:T(8,128)(2,1)} %copy-done.4), channel_id=1, source_target_pairs={{0,4},{1,5},{2,6},{3,7},{4,8},{5,9},{6,10},{7,11},{8,12},{9,13},{1... | collective-permute-start | bytes 1572872 | tf_op jit(solution)/shard_map/ppermute | solution.py:36
  37.9 1.5 %fusion.17 = f32[512,2,160]{0,2,1:T(8,128)S(1)} fusion(f32[17,160,1]{1,0,2:T(8,128)} %constant.68, f32[512,2,16]{0,2,1:T(8,128)S(1)} %convert_multiply_fusion.1), kind=kOutput, calls=%fused_computation.28 | convolution fusion | flops 33423360 | bytes 731776 | tf_op jit(solution)/shard_map/jhi,if->jhf/dot_general | solution.py:43
  39.4 1.5 %convolution_multiply_fusion.1 = f32[512,2,160]{0,2,1:T(8,128)S(1)} fusion(f32[512,2,160]{0,2,1:T(8,128)S(1)} %fusion.17, f32[17,160,1]{1,0,2:T(8,128)} %constant.69, f32[512,2,16]{0,2,1:T(8,128)S(1)} %convert_multiply_fusion.1), kind=kOutput, calls=%fused_computation.8 | convolution fusion | flops 33587200 | bytes 1387136 | tf_op jit(solution)/shard_map/jhi,if->jhf/dot_general | solution.py:43
  40.8 1.1 fusion.30
  42.0 1.6 %reshape.73 = f32[64,5,128]{2,1,0:T(8,128)} reshape(f32[2,160,128]{2,1,0:T(8,128)} %fusion.30) | data formatting | bytes 327680 | tf_op jit(solution)/shard_map/reshape | solution.py:105
  43.6 15.8 %all-to-all-start.1 = ((f32[64,5,128]{2,1,0:T(8,128)}), f32[64,5,128]{2,1,0:T(8,128)S(1)}, u32[]{:S(2)}, u32[]{:S(2)}) async-start(f32[64,5,128]{2,1,0:T(8,128)} %reshape.73), calls=%async_computation.1 | async-start | bytes 524288 | tf_op jit(solution)/shard_map/all_to_all | solution.py:106
  60.1 1.3 %fusion.29 = f32[2,512,512]{2,1,0:T(8,128)S(1)} fusion(bf16[512,2,16]{0,2,1:T(8,128)(2,1)} %bitcast.58, bf16[512,2,16]{0,2,1:T(8,128)(2,1)} %bitcast.57), kind=kOutput, calls=%fused_computation.44 | convolution fusion | flops 16777216 | bytes 2162688 | tf_op jit(solution)/shard_map/ihd,jhd->hij/dot_general | solution.py:142
  61.5 2.6 %fusion = f32[2,128,512]{2,1,0:T(8,128)} fusion(bf16[512,2,128]{0,2,1:T(8,128)(2,1)S(1)} %bitcast.55, f32[2,512,512]{2,1,0:T(8,128)S(1)} %fusion.29, pred[512,512]{1,0:T(8,128)(4,1)S(1)} %copy-done.10), kind=kOutput, calls=%fused_computation | convolution fusion | flops 808452096 | bytes 3145728 | tf_op jit(solution)/shard_map/hij,jhe->ihe/dot_general | solution.py:147
  64.0 9.0 %all-to-all-done.1 = f32[64,5,128]{2,1,0:T(8,128)S(1)} async-done(((f32[64,5,128]{2,1,0:T(8,128)}), f32[64,5,128]{2,1,0:T(8,128)S(1)}, u32[]{:S(2)}, u32[]{:S(2)}) %all-to-all-start.1) | async-done | bytes 163872 | tf_op jit(solution)/shard_map/all_to_all | solution.py:106
  73.8 5.2 %all-to-all-start.2 = ((f32[64,5,128]{2,1,0:T(8,128)}), f32[64,5,128]{2,1,0:T(8,128)S(1)}, u32[]{:S(2)}, u32[]{:S(2)}) async-start(f32[64,5,128]{2,1,0:T(8,128)} %reduce-window_subtract_fusion), calls=%async_computation.2 | async-start | bytes 524288 | tf_op jit(solution)/shard_map/all_to_all | solution.py:108
  79.8 1.6 %convolution_multiply_fusion = f32[512,2,160]{0,2,1:T(8,128)} fusion(f32[512,2,160]{0,2,1:T(8,128)S(1)} %fusion.14, f32[17,160,1]{1,0,2:T(8,128)S(1)} %copy-done.11, f32[512,2,16]{0,2,1:T(8,128)S(1)} %convert_multiply_fusion), kind=kOutput, calls=%fused_computation.7 | convolution fusion | flops 33587200 | bytes 1387136 | tf_op jit(solution)/shard_map/jhi,if->jhf/dot_general | solution.py:43
  81.4 10.1 %all-to-all-done.2 = f32[64,5,128]{2,1,0:T(8,128)S(1)} async-done(((f32[64,5,128]{2,1,0:T(8,128)}), f32[64,5,128]{2,1,0:T(8,128)S(1)}, u32[]{:S(2)}, u32[]{:S(2)}) %all-to-all-start.2) | async-done | bytes 163872 | tf_op jit(solution)/shard_map/all_to_all | solution.py:108
  92.1 2.0 %multiply_reduce_fusion = (f32[512,2]{0,1:T(2,128)S(1)}, f32[512,2,128]{0,2,1:T(8,128)S(1)}) fusion(f32[2,128,512]{2,1,0:T(8,128)} %fusion, f32[2,160,128]{2,1,0:T(8,128)} %reshape.74, f32[512,2,160]{0,2,1:T(8,128)} %convolution_multiply_fusion), kind=kOutput, calls=%fused_computation.21 | convolution fusion | flops 252050432 | bytes 1871872 | tf_op jit(solution)/shard_map/ihf,hfe->ihe/dot_general | solution.py:138
  95.2 1.8 %reshape.76 = bf16[8,64,256]{2,1,0:T(8,128)(2,1)} reshape(bf16[512,2,128]{2,1,0:T(2,128)(2,1)} %copy.35) | data formatting | bytes 524288 | tf_op jit(solution)/shard_map/reshape | solution.py:154
  97.0 19.5 %all-to-all-start.3 = ((bf16[8,64,256]{2,1,0:T(8,128)(2,1)}), bf16[8,64,256]{2,1,0:T(8,128)(2,1)S(1)}, u32[]{:S(2)}, u32[]{:S(2)}) async-start(bf16[8,64,256]{2,1,0:T(8,128)(2,1)} %reshape.76), calls=%async_computation.3 | async-start | bytes 524288 | tf_op jit(solution)/shard_map/all_to_all | solution.py:155
  118.2 8.5 %shard_map.122 = bf16[64,2048]{1,0:T(8,128)(2,1)} custom-call(s32[1]{0:T(128)} %bitcast.19.pos_ref, bf16[64,2048]{1,0:T(8,128)(2,1)} %q_ref.1, bf16[64,2048]{1,0:T(8,128)(2,1)} %k_ref.1, bf16[64,2048]{1,0:T(8,128)(2,1)} %v_ref.1, bf16[2,64,2048]{2,1,0:T(8,128)(2,1)} %collective-permute-done.1.refs_0_, bf16[2,2,64,2048]{3,2,1,0:T(8,128)(2,1)} %copy-done.1, ...), custom_call_target="tpu_custom_call" | custom-call | tf_op jit(solution)/shard_map/pallas_call | solution.py:83
  (58 shorter events, 13.8 us)
Async XLA Ops:
  0.6 17.1 %copy-start = (f32[2048]{0:T(1024)S(1)}, f32[2048]{0:T(1024)}, u32[]{:S(2)}) copy-start(f32[2048]{0:T(1024)} %param.14) | copy-start | bytes 24580
  0.6 7.5 %copy-start.12 = (bf16[64,256]{1,0:T(8,128)(2,1)S(1)}, bf16[64,256]{1,0:T(8,128)(2,1)}, u32[]{:S(2)}) copy-start(bf16[64,256]{1,0:T(8,128)(2,1)} %param.11) | copy-start | bytes 98308
  0.7 7.8 %copy-start.13 = (bf16[64,256]{1,0:T(8,128)(2,1)S(1)}, bf16[64,256]{1,0:T(8,128)(2,1)}, u32[]{:S(2)}) copy-start(bf16[64,256]{1,0:T(8,128)(2,1)} %param.12) | copy-start | bytes 98308
  1.8 11.5 %collective-permute-start = (bf16[2,64,2048]{2,1,0:T(8,128)(2,1)S(1)}, bf16[2,64,2048]{2,1,0:T(8,128)(2,1)S(1)}, u32[]{:S(2)}, u32[]{:S(2)}) collective-permute-start(bf16[2,64,2048]{2,1,0:T(8,128)(2,1)S(1)} %get-tuple-element.7), channel_id=1, source_target_pairs={{0,4},{1,5},{2,6},{3,7},{4,8},{5,9},{6,10},{7,11},{8,12},{9,13},{1... | collective-permute-start | bytes 1572872 | tf_op jit(solution)/shard_map/ppermute | solution.py:36
  13.3 4.4 %copy-start.4 = (bf16[2,64,2048]{2,1,0:T(8,128)(2,1)}, bf16[2,64,2048]{2,1,0:T(8,128)(2,1)S(1)}, u32[]{:S(2)}) copy-start(bf16[2,64,2048]{2,1,0:T(8,128)(2,1)S(1)} %collective-permute-done.refs_4_) | copy-start | bytes 1572868
  13.3 20.3 %all-to-all-start = ((bf16[64,8,320]{2,0,1:T(8,128)(2,1)}), bf16[64,8,320]{2,0,1:T(8,128)(2,1)S(1)}, u32[]{:S(2)}, u32[]{:S(2)}) async-start(bf16[64,8,320]{2,0,1:T(8,128)(2,1)} %pad_maximum_fusion.2), calls=%async_computation | async-start | bytes 786432 | tf_op jit(solution)/shard_map/all_to_all | solution.py:126
  18.8 97.7 %collective-permute-start.2 = (bf16[2,2,64,2048]{3,2,1,0:T(8,128)(2,1)}, bf16[2,2,64,2048]{3,2,1,0:T(8,128)(2,1)S(1)}, u32[]{:S(2)}, u32[]{:S(2)}) collective-permute-start(bf16[2,2,64,2048]{3,2,1,0:T(8,128)(2,1)} %pad_maximum_fusion), channel_id=1, source_target_pairs={{0,3},{1,4},{2,5},{3,6},{4,7},{5,8},{6,9},{7,10},{8,11},{9,12},{10... | collective-permute-start | bytes 3145736 | tf_op jit(solution)/shard_map/ppermute | solution.py:36
  23.3 93.2 %collective-permute-start.3 = (bf16[2,2,64,2048]{3,2,1,0:T(8,128)(2,1)}, bf16[2,2,64,2048]{3,2,1,0:T(8,128)(2,1)S(1)}, u32[]{:S(2)}, u32[]{:S(2)}) collective-permute-start(bf16[2,2,64,2048]{3,2,1,0:T(8,128)(2,1)} %pad_maximum_fusion), channel_id=1, source_target_pairs={{0,2},{1,3},{2,4},{3,5},{4,6},{5,7},{6,8},{7,9},{8,10},{9,11},{10,... | collective-permute-start | bytes 3145736 | tf_op jit(solution)/shard_map/ppermute | solution.py:36
  28.3 88.3 %collective-permute-start.4 = (bf16[2,2,64,2048]{3,2,1,0:T(8,128)(2,1)}, bf16[2,2,64,2048]{3,2,1,0:T(8,128)(2,1)S(1)}, u32[]{:S(2)}, u32[]{:S(2)}) collective-permute-start(bf16[2,2,64,2048]{3,2,1,0:T(8,128)(2,1)} %pad_maximum_fusion), channel_id=1, source_target_pairs={{0,1},{1,2},{2,3},{3,4},{4,5},{5,6},{6,7},{7,8},{8,9},{9,10},{10,1... | collective-permute-start | bytes 3145736 | tf_op jit(solution)/shard_map/ppermute | solution.py:36
  30.7 85.8 %collective-permute-start.1 = (bf16[2,64,2048]{2,1,0:T(8,128)(2,1)}, bf16[2,64,2048]{2,1,0:T(8,128)(2,1)}, u32[]{:S(2)}, u32[]{:S(2)}) collective-permute-start(bf16[2,64,2048]{2,1,0:T(8,128)(2,1)} %copy-done.4), channel_id=1, source_target_pairs={{0,4},{1,5},{2,6},{3,7},{4,8},{5,9},{6,10},{7,11},{8,12},{9,13},{1... | collective-permute-start | bytes 1572872 | tf_op jit(solution)/shard_map/ppermute | solution.py:36
  36.1 0.6 copy-start.8
  37.9 5.8 %copy-start.5 = (bf16[512,256]{0,1:T(8,128)(2,1)}, bf16[512,256]{0,1:T(8,128)(2,1)S(1)}, u32[]{:S(2)}) copy-start(bf16[512,256]{0,1:T(8,128)(2,1)S(1)} %copy.31) | copy-start | bytes 786436
  40.8 18.5 %copy-start.7 = (bf16[512,32]{1,0:T(8,128)(2,1)S(1)}, bf16[512,32]{1,0:T(8,128)(2,1)}, u32[]{:S(2)}) copy-start(bf16[512,32]{1,0:T(8,128)(2,1)} %get-tuple-element.9) | copy-start | bytes 98308
  43.6 29.5 %all-to-all-start.1 = ((f32[64,5,128]{2,1,0:T(8,128)}), f32[64,5,128]{2,1,0:T(8,128)S(1)}, u32[]{:S(2)}, u32[]{:S(2)}) async-start(f32[64,5,128]{2,1,0:T(8,128)} %reshape.73), calls=%async_computation.1 | async-start | bytes 524288 | tf_op jit(solution)/shard_map/all_to_all | solution.py:106
  60.1 1.3 %copy-start.9 = (bf16[512,32]{0,1:T(8,128)(2,1)S(1)}, bf16[512,32]{0,1:T(8,128)(2,1)}, u32[]{:S(2)}) copy-start(bf16[512,32]{0,1:T(8,128)(2,1)} %copy.32) | copy-start | bytes 98308
  60.1 1.3 %copy-start.6 = (bf16[512,256]{0,1:T(8,128)(2,1)S(1)}, bf16[512,256]{0,1:T(8,128)(2,1)}, u32[]{:S(2)}) copy-start(bf16[512,256]{0,1:T(8,128)(2,1)} %copy-done.5) | copy-start | bytes 786436
  60.1 1.4 %copy-start.10 = (pred[512,512]{1,0:T(8,128)(4,1)S(1)}, pred[512,512]{1,0:T(8,128)(4,1)}, u32[]{:S(2)}) copy-start(pred[512,512]{1,0:T(8,128)(4,1)} %iota_compare_fusion) | copy-start | bytes 786436
  61.4 17.6 %copy-start.14 = (f32[17,160,1]{1,0,2:T(8,128)S(1)}, f32[17,160,1]{1,0,2:T(8,128)}, u32[]{:S(2)}) copy-start(f32[17,160,1]{1,0,2:T(8,128)} %constant.70) | copy-start | bytes 32644
  61.5 18.3 %copy-start.11 = (f32[17,160,1]{1,0,2:T(8,128)S(1)}, f32[17,160,1]{1,0,2:T(8,128)}, u32[]{:S(2)}) copy-start(f32[17,160,1]{1,0,2:T(8,128)} %constant.69) | copy-start | bytes 32644
  73.8 17.6 %all-to-all-start.2 = ((f32[64,5,128]{2,1,0:T(8,128)}), f32[64,5,128]{2,1,0:T(8,128)S(1)}, u32[]{:S(2)}, u32[]{:S(2)}) async-start(f32[64,5,128]{2,1,0:T(8,128)} %reduce-window_subtract_fusion), calls=%async_computation.2 | async-start | bytes 524288 | tf_op jit(solution)/shard_map/all_to_all | solution.py:108
  97.0 29.7 %all-to-all-start.3 = ((bf16[8,64,256]{2,1,0:T(8,128)(2,1)}), bf16[8,64,256]{2,1,0:T(8,128)(2,1)S(1)}, u32[]{:S(2)}, u32[]{:S(2)}) async-start(bf16[8,64,256]{2,1,0:T(8,128)(2,1)} %reshape.76), calls=%async_computation.3 | async-start | bytes 524288 | tf_op jit(solution)/shard_map/all_to_all | solution.py:155
  116.5 1.0 copy-start.1
  116.6 1.3 %copy-start.2 = (bf16[2,2,64,2048]{3,2,1,0:T(8,128)(2,1)}, bf16[2,2,64,2048]{3,2,1,0:T(8,128)(2,1)S(1)}, u32[]{:S(2)}) copy-start(bf16[2,2,64,2048]{3,2,1,0:T(8,128)(2,1)S(1)} %collective-permute-done.3.refs_2_.refs_6_) | copy-start | bytes 3145732
  116.6 1.6 %copy-start.3 = (bf16[2,2,64,2048]{3,2,1,0:T(8,128)(2,1)}, bf16[2,2,64,2048]{3,2,1,0:T(8,128)(2,1)S(1)}, u32[]{:S(2)}) copy-start(bf16[2,2,64,2048]{3,2,1,0:T(8,128)(2,1)S(1)} %collective-permute-done.4.refs_3_.refs_7_) | copy-start | bytes 3145732

commit v14 on v13

--- a/solution.py
+++ b/solution.py
@@ -15,8 +15,9 @@
 WINDOW = 512
 CORES = 2
 FEAT_PAD = 160
-ALL = ("y", "z", "core", "sub")
-GROUP = ("core", "sub")
+ALL = ("y", "z", "pair", "core", "sub")
+GROUP = ("pair", "core", "sub")
+LINES_PER_GROUP = 2
 
 
 def pair_tables(for_query):
@@ -199,7 +200,14 @@
     lines = seq_count // CORES
     z_count = math.isqrt(lines)
     split_mesh = Mesh(
-        np.asarray(mesh.devices).reshape(lines // z_count, z_count, CORES, sub_count), ALL
+        np.asarray(mesh.devices).reshape(
+            lines // z_count,
+            z_count // LINES_PER_GROUP,
+            LINES_PER_GROUP,
+            CORES,
+            sub_count,
+        ),
+        ALL,
     )
     rows = P(ALL, None)
     in_specs = (rows, rows, rows, P(), rows, rows, rows)

time: 128 us -> 121 us (0.945)
  local copies, waits for them, and re-layouts: 13.8 us -> 8.88 us
  starting transfers between devices: 65 us -> 60.3 us
  matrix products: 12.3 us -> 14.9 us
    slice x5 -> x0, local copies, waits for them, and re-layouts: 4.37 us -> none  [the longest x2 1.93 us: linear_heads(): got[:, 2 * own_heads * FDIM:].reshape(rows, own_heads, VDIM)]
    reshape x3 -> x0, local copies, waits for them, and re-layouts: 4.14 us -> none  [the longest x1 1.82 us: linear_heads(): out = out.reshape(group_count, rows_dev, own_heads * VDIM)]
    all_to_all x1, starting transfers between devices: 19.5 us -> 16.6 us  [linear_heads(): back = lax.all_to_all(out, GROUP, split_axis=0, concat_axis=2, tiled=True)]
    dot_general x0 -> x2, local copies, waits for them, and re-layouts: none -> 2.87 us  [linear_heads(): jnp.einsum('jhf,jhe->hfe', sym_features(key_lin, False), value_lin, preci...]
    all_to_all x1, starting transfers between devices: 4.41 us -> 6.73 us  [linear_heads(): got = lax.all_to_all(packed, GROUP, split_axis=1, concat_axis=0, tiled=True)]
    ppermute x5, starting transfers between devices: 20.1 us -> 18 us  [passed_along(): return lax.ppermute(shard, axis, pairs)]
    dot_general x4, matrix products: 5.28 us -> 7.13 us  [sym_features(): jnp.einsum('jhi,if->jhf', ext, jnp.asarray(table), precision=lax.Precisio...]
    all_to_all x1, waiting for transfers between devices: 10.1 us -> 8.36 us  [groups_before(): lax.all_to_all(prefix, outer, split_axis=0, concat_axis=0, tiled=True)]
  transfers between devices with their start and end apart: 9 -> 9, of which waited for: 3 -> 3; matrix products, arithmetic and copies ran while one was open for 21% -> 22% of each run, Pallas kernels for 7% -> 7%
where the time goes in v14:
time: 121 us; the launch traced here: 120 us
  starting transfers between devices  60.3 us (50%)
  waiting for transfers between devices  20.7 us (17%)
  matrix products  14.9 us (12%)
  local copies, waits for them, and re-layouts  8.88 us (7%)
  Pallas kernels  8.51 us (7%)
  other arithmetic  5.43 us (4%)
    ppermute x5, starting transfers between devices, passed_along(): return lax.ppermute(shard, axis, pairs)  18 us
    all_to_all x1, starting transfers between devices, linear_heads(): back = lax.all_to_all(out, GROUP, split_axis=0, concat_axis=2, tiled=True)  16.6 us
    all_to_all x1, starting transfers between devices, groups_before(): held = lax.all_to_all(dealt, outer, split_axis=0, concat_axis=0, tiled=True)  15.1 us
    all_to_all x1, waiting for transfers between devices, groups_before(): held = lax.all_to_all(dealt, outer, split_axis=0, concat_axis=0, tiled=True)  9.65 us
    pallas_call x1, Pallas kernels, window_attention(): pl.pallas_call(window_kernel, out_shape=jax.ShapeDtypeStruct((rows, chann...  8.51 us
    all_to_all x1, waiting for transfers between devices, groups_before(): lax.all_to_all(prefix, outer, split_axis=0, concat_axis=0, tiled=True)  8.36 us
    dot_general x4, matrix products, sym_features(): jnp.einsum('jhi,if->jhf', ext, jnp.asarray(table), precision=lax.Precisio...  7.13 us
    all_to_all x1, starting transfers between devices, linear_heads(): got = lax.all_to_all(packed, GROUP, split_axis=1, concat_axis=0, tiled=True)  6.73 us
  transfers between devices with their start and end apart: 9, of which 3 were waited for; matrix products, arithmetic and copies ran while one was open for 22% of the time, Pallas kernels for 7%

profile of v14, /device:TPU:1, one launch (start us, length us, event | category | flops | bytes accessed | tf_op | source)
XLA Modules:
  0.0 119.6 jit_solution(11089413552621434293)
XLA Ops:
  0.6 1.1 fusion.40
  1.8 5.4 %collective-permute-start = (bf16[2,64,2048]{2,1,0:T(8,128)(2,1)S(1)}, bf16[2,64,2048]{2,1,0:T(8,128)(2,1)}, u32[]{:S(2)}, u32[]{:S(2)}) collective-permute-start(bf16[2,64,2048]{2,1,0:T(8,128)(2,1)S(1)} %get-tuple-element.7), channel_id=1, source_target_pairs={{0,4},{1,5},{2,6},{3,7},{4,8},{5,9},{6,10},{7,11},{8,12},{9,13},{1... | collective-permute-start | bytes 1572872 | tf_op jit(solution)/shard_map/ppermute | solution.py:37
  9.4 1.2 %pad_maximum_fusion.1 = bf16[64,16,160]{2,0,1:T(8,128)(2,1)} fusion(bf16[64,16,128]{2,0,1:T(8,128)(2,1)S(1)} %copy_bitcast_fusion.1, bf16[64,16,16]{2,0,1:T(8,128)(2,1)S(1)} %copy.44, bf16[64,16,16]{2,0,1:T(8,128)(2,1)S(1)} %copy.43), kind=kLoop, calls=%fused_computation.21 | loop fusion | flops 983040 | bytes 655360 | tf_op jit(solution)/shard_map/concatenate | solution.py:118
  10.6 2.7 %collective-permute-done.refs_4_ = bf16[2,64,2048]{2,1,0:T(8,128)(2,1)} collective-permute-done((bf16[2,64,2048]{2,1,0:T(8,128)(2,1)S(1)}, bf16[2,64,2048]{2,1,0:T(8,128)(2,1)}, u32[]{:S(2)}, u32[]{:S(2)}) %collective-permute-start) | collective-permute-done | bytes 524320 | tf_op jit(solution)/shard_map/ppermute | solution.py:37
  13.3 6.7 %all-to-all-start = ((bf16[64,16,160]{2,0,1:T(8,128)(2,1)}), bf16[64,16,160]{2,0,1:T(8,128)(2,1)S(1)}, u32[]{:S(2)}, u32[]{:S(2)}) async-start(bf16[64,16,160]{2,0,1:T(8,128)(2,1)} %pad_maximum_fusion.1), calls=%async_computation | async-start | bytes 1048576 | tf_op jit(solution)/shard_map/all_to_all | solution.py:127
  20.7 3.5 %collective-permute-start.1 = (bf16[2,64,2048]{2,1,0:T(8,128)(2,1)}, bf16[2,64,2048]{2,1,0:T(8,128)(2,1)}, u32[]{:S(2)}, u32[]{:S(2)}) collective-permute-start(bf16[2,64,2048]{2,1,0:T(8,128)(2,1)} %collective-permute-done.refs_4_), channel_id=1, source_target_pairs={{0,4},{1,5},{2,6},{3,7},{4,8},{5,9},{6,10},{7,11},{8,12},{9,13},{1... | collective-permute-start | bytes 1572872 | tf_op jit(solution)/shard_map/ppermute | solution.py:37
  24.3 2.1 %pad_maximum_fusion = bf16[2,2,64,2048]{3,2,1,0:T(8,128)(2,1)} fusion(bf16[1,2,64,2048]{3,2,1,0:T(8,128)(2,1)} %bitcast.24, bf16[1,2,64,2048]{3,2,1,0:T(8,128)(2,1)S(1)} %get-tuple-element.6), kind=kLoop, calls=%fused_computation.18 | loop fusion | flops 524288 | bytes 2097152 | tf_op jit(solution)/shard_map/stack | solution.py:177
  26.4 4.3 %collective-permute-start.2 = (bf16[2,2,64,2048]{3,2,1,0:T(8,128)(2,1)}, bf16[2,2,64,2048]{3,2,1,0:T(8,128)(2,1)S(1)}, u32[]{:S(2)}, u32[]{:S(2)}) collective-permute-start(bf16[2,2,64,2048]{3,2,1,0:T(8,128)(2,1)} %pad_maximum_fusion), channel_id=1, source_target_pairs={{0,3},{1,4},{2,5},{3,6},{4,7},{5,8},{6,9},{7,10},{8,11},{9,12},{10... | collective-permute-start | bytes 3145736 | tf_op jit(solution)/shard_map/ppermute | solution.py:37
  30.7 2.3 %collective-permute-start.3 = (bf16[2,2,64,2048]{3,2,1,0:T(8,128)(2,1)}, bf16[2,2,64,2048]{3,2,1,0:T(8,128)(2,1)S(1)}, u32[]{:S(2)}, u32[]{:S(2)}) collective-permute-start(bf16[2,2,64,2048]{3,2,1,0:T(8,128)(2,1)} %pad_maximum_fusion), channel_id=1, source_target_pairs={{0,2},{1,3},{2,4},{3,5},{4,6},{5,7},{6,8},{7,9},{8,10},{9,11},{10,... | collective-permute-start | bytes 3145736 | tf_op jit(solution)/shard_map/ppermute | solution.py:37
  33.0 2.5 %collective-permute-start.4 = (bf16[2,2,64,2048]{3,2,1,0:T(8,128)(2,1)}, bf16[2,2,64,2048]{3,2,1,0:T(8,128)(2,1)}, u32[]{:S(2)}, u32[]{:S(2)}) collective-permute-start(bf16[2,2,64,2048]{3,2,1,0:T(8,128)(2,1)} %pad_maximum_fusion), channel_id=1, source_target_pairs={{0,1},{1,2},{2,3},{3,4},{4,5},{5,6},{6,7},{7,8},{8,9},{9,10},{10,1... | collective-permute-start | bytes 3145736 | tf_op jit(solution)/shard_map/ppermute | solution.py:37
  36.5 3.0 %fusion = f32[128,1024]{1,0:T(8,128)} fusion(f32[1024,1024]{1,0:T(8,128)S(1)} %fusion.27, bf16[1024,160]{1,0:T(8,128)(2,1)S(1)} %bitcast.62), kind=kOutput, calls=%fused_computation | convolution fusion | flops 1617952768 | bytes 4980736 | tf_op jit(solution)/shard_map/hij,jhe->ihe/dot_general | solution.py:148
  40.4 1.8 %fusion.11 = f32[160,1024]{1,0:T(8,128)} fusion(f32[1024,160]{0,1:T(8,128)S(1)} %fusion.19, f32[17,160]{1,0:T(8,128)S(1)} %copy-done.3, f32[1024,1,16]{2,0,1:T(8,128)S(1)} %get-tuple-element.9), kind=kOutput, calls=%fused_computation.14 | convolution fusion | flops 33587200 | bytes 1387136 | tf_op jit(solution)/shard_map/jhi,if->jhf/dot_general | solution.py:44
  42.2 2.2 %dot_general.30 = f32[32,5,1024]{2,1,0:T(8,128)} reshape(f32[160,1024]{1,0:T(8,128)} %fusion.11) | data formatting | bytes 1310720 | tf_op jit(solution)/shard_map/jhf,jhe->hfe/dot_general | solution.py:135
  44.3 2.0 %fusion.13 = f32[32,5,128]{2,0,1:T(8,128)S(1)} fusion(f32[32,5,1024]{2,1,0:T(8,128)} %dot_general.30, bf16[1024,160]{1,0:T(8,128)(2,1)S(1)} %bitcast.63), kind=kOutput, calls=%fused_computation.19 | convolution fusion | flops 251658240 | bytes 999424 | tf_op jit(solution)/shard_map/jhf,jhe->hfe/dot_general | solution.py:135
  47.1 15.1 %all-to-all-start.1 = ((f32[32,5,128]{2,1,0:T(8,128)}), f32[32,5,128]{2,1,0:T(8,128)S(1)}, u32[]{:S(2)}, u32[]{:S(2)}) async-start(f32[32,5,128]{2,1,0:T(8,128)} %copy.47), calls=%async_computation.1 | async-start | bytes 262144 | tf_op jit(solution)/shard_map/all_to_all | solution.py:107
  62.2 1.7 %fusion.16 = f32[1024,160]{0,1:T(8,128)} fusion(f32[17,160]{1,0:T(8,128)S(1)} %copy-done.4, f32[1024,1,16]{2,0,1:T(8,128)S(1)} %get-tuple-element.8), kind=kOutput, calls=%fused_computation.24 | convolution fusion | flops 33423360 | bytes 731776 | tf_op jit(solution)/shard_map/jhi,if->jhf/dot_general | solution.py:44
  63.9 9.6 %all-to-all-done.1 = f32[32,5,128]{2,1,0:T(8,128)S(1)} async-done(((f32[32,5,128]{2,1,0:T(8,128)}), f32[32,5,128]{2,1,0:T(8,128)S(1)}, u32[]{:S(2)}, u32[]{:S(2)}) %all-to-all-start.1) | async-done | bytes 81952 | tf_op jit(solution)/shard_map/all_to_all | solution.py:107
  74.2 3.9 %all-to-all-start.2 = ((f32[32,5,128]{2,1,0:T(8,128)}), f32[32,5,128]{2,1,0:T(8,128)S(1)}, u32[]{:S(2)}, u32[]{:S(2)}) async-start(f32[32,5,128]{2,1,0:T(8,128)} %reduce-window_subtract_fusion), calls=%async_computation.2 | async-start | bytes 262144 | tf_op jit(solution)/shard_map/all_to_all | solution.py:109
  78.1 2.8 %convolution_multiply_fusion = f32[1024,160]{0,1:T(8,128)} fusion(f32[1024,160]{0,1:T(8,128)} %fusion.16, f32[17,160]{1,0:T(8,128)S(1)} %copy-done.3, f32[1024,1,16]{2,0,1:T(8,128)S(1)} %get-tuple-element.8), kind=kOutput, calls=%fused_computation.12 | convolution fusion | flops 33587200 | bytes 1387136 | tf_op jit(solution)/shard_map/jhi,if->jhf/dot_general | solution.py:44
  80.9 8.4 %all-to-all-done.2 = f32[32,5,128]{2,1,0:T(8,128)S(1)} async-done(((f32[32,5,128]{2,1,0:T(8,128)}), f32[32,5,128]{2,1,0:T(8,128)S(1)}, u32[]{:S(2)}, u32[]{:S(2)}) %all-to-all-start.2) | async-done | bytes 81952 | tf_op jit(solution)/shard_map/all_to_all | solution.py:109
  89.3 1.9 %multiply_reduce_fusion = (f32[1024]{0:T(1024)S(1)}, f32[1,128,1024]{2,1,0:T(8,128)S(1)}) fusion(f32[128,1024]{1,0:T(8,128)} %fusion, f32[160,128]{1,0:T(8,128)S(1)} %reshape.105, f32[1024,160]{0,1:T(8,128)} %convolution_multiply_fusion), kind=kOutput, calls=%fused_computation.30 | convolution fusion | flops 252050432 | bytes 1789952 | tf_op jit(solution)/shard_map/ihf,hfe->ihe/dot_general | solution.py:139
  92.1 16.6 %all-to-all-start.3 = ((bf16[16,64,128]{2,1,0:T(8,128)(2,1)}), bf16[16,64,128]{2,1,0:T(8,128)(2,1)S(1)}, u32[]{:S(2)}, u32[]{:S(2)}) async-start(bf16[16,64,128]{2,1,0:T(8,128)(2,1)} %bitcast.19), calls=%async_computation.3 | async-start | bytes 524288 | tf_op jit(solution)/shard_map/all_to_all | solution.py:156
  108.8 1.0 copy-done.1
  110.1 8.5 %shard_map.122 = bf16[64,2048]{1,0:T(8,128)(2,1)} custom-call(s32[1]{0:T(128)} %bitcast.22.pos_ref, bf16[64,2048]{1,0:T(8,128)(2,1)} %q_ref.1, bf16[64,2048]{1,0:T(8,128)(2,1)} %k_ref.1, bf16[64,2048]{1,0:T(8,128)(2,1)} %v_ref.1, bf16[2,64,2048]{2,1,0:T(8,128)(2,1)} %collective-permute-done.1.refs_0_, bf16[2,2,64,2048]{3,2,1,0:T(8,128)(2,1)} %copy-done.1, ...), custom_call_target="tpu_custom_call" | custom-call | tf_op jit(solution)/shard_map/pallas_call | solution.py:84
  (34 shorter events, 8.4 us)
Async XLA Ops:
  0.6 8.7 %copy-start = (bf16[64,2048]{1,0:T(8,128)(2,1)S(1)}, bf16[64,2048]{1,0:T(8,128)(2,1)}, u32[]{:S(2)}) copy-start(bf16[64,2048]{1,0:T(8,128)(2,1)} %param.13) | copy-start | bytes 786436
  1.8 11.5 %collective-permute-start = (bf16[2,64,2048]{2,1,0:T(8,128)(2,1)S(1)}, bf16[2,64,2048]{2,1,0:T(8,128)(2,1)}, u32[]{:S(2)}, u32[]{:S(2)}) collective-permute-start(bf16[2,64,2048]{2,1,0:T(8,128)(2,1)S(1)} %get-tuple-element.7), channel_id=1, source_target_pairs={{0,4},{1,5},{2,6},{3,7},{4,8},{5,9},{6,10},{7,11},{8,12},{9,13},{1... | collective-permute-start | bytes 1572872 | tf_op jit(solution)/shard_map/ppermute | solution.py:37
  13.3 22.2 %all-to-all-start = ((bf16[64,16,160]{2,0,1:T(8,128)(2,1)}), bf16[64,16,160]{2,0,1:T(8,128)(2,1)S(1)}, u32[]{:S(2)}, u32[]{:S(2)}) async-start(bf16[64,16,160]{2,0,1:T(8,128)(2,1)} %pad_maximum_fusion.1), calls=%async_computation | async-start | bytes 1048576 | tf_op jit(solution)/shard_map/all_to_all | solution.py:127
  20.7 88.0 %collective-permute-start.1 = (bf16[2,64,2048]{2,1,0:T(8,128)(2,1)}, bf16[2,64,2048]{2,1,0:T(8,128)(2,1)}, u32[]{:S(2)}, u32[]{:S(2)}) collective-permute-start(bf16[2,64,2048]{2,1,0:T(8,128)(2,1)} %collective-permute-done.refs_4_), channel_id=1, source_target_pairs={{0,4},{1,5},{2,6},{3,7},{4,8},{5,9},{6,10},{7,11},{8,12},{9,13},{1... | collective-permute-start | bytes 1572872 | tf_op jit(solution)/shard_map/ppermute | solution.py:37
  26.4 82.4 %collective-permute-start.2 = (bf16[2,2,64,2048]{3,2,1,0:T(8,128)(2,1)}, bf16[2,2,64,2048]{3,2,1,0:T(8,128)(2,1)S(1)}, u32[]{:S(2)}, u32[]{:S(2)}) collective-permute-start(bf16[2,2,64,2048]{3,2,1,0:T(8,128)(2,1)} %pad_maximum_fusion), channel_id=1, source_target_pairs={{0,3},{1,4},{2,5},{3,6},{4,7},{5,8},{6,9},{7,10},{8,11},{9,12},{10... | collective-permute-start | bytes 3145736 | tf_op jit(solution)/shard_map/ppermute | solution.py:37
  30.7 78.1 %collective-permute-start.3 = (bf16[2,2,64,2048]{3,2,1,0:T(8,128)(2,1)}, bf16[2,2,64,2048]{3,2,1,0:T(8,128)(2,1)S(1)}, u32[]{:S(2)}, u32[]{:S(2)}) collective-permute-start(bf16[2,2,64,2048]{3,2,1,0:T(8,128)(2,1)} %pad_maximum_fusion), channel_id=1, source_target_pairs={{0,2},{1,3},{2,4},{3,5},{4,6},{5,7},{6,8},{7,9},{8,10},{9,11},{10,... | collective-permute-start | bytes 3145736 | tf_op jit(solution)/shard_map/ppermute | solution.py:37
  33.0 75.7 %collective-permute-start.4 = (bf16[2,2,64,2048]{3,2,1,0:T(8,128)(2,1)}, bf16[2,2,64,2048]{3,2,1,0:T(8,128)(2,1)}, u32[]{:S(2)}, u32[]{:S(2)}) collective-permute-start(bf16[2,2,64,2048]{3,2,1,0:T(8,128)(2,1)} %pad_maximum_fusion), channel_id=1, source_target_pairs={{0,1},{1,2},{2,3},{3,4},{4,5},{5,6},{6,7},{7,8},{8,9},{9,10},{10,1... | collective-permute-start | bytes 3145736 | tf_op jit(solution)/shard_map/ppermute | solution.py:37
  36.5 3.1 %copy-start.5 = (f32[17,160]{1,0:T(8,128)S(1)}, f32[17,160]{1,0:T(8,128)}, u32[]{:S(2)}) copy-start(f32[17,160]{1,0:T(8,128)} %constant.57.clone) | copy-start | bytes 32644
  36.5 3.9 %copy-start.3 = (f32[17,160]{1,0:T(8,128)S(1)}, f32[17,160]{1,0:T(8,128)}, u32[]{:S(2)}) copy-start(f32[17,160]{1,0:T(8,128)} %constant.58.clone) | copy-start | bytes 32644
  39.5 22.6 %copy-start.4 = (f32[17,160]{1,0:T(8,128)S(1)}, f32[17,160]{1,0:T(8,128)}, u32[]{:S(2)}) copy-start(f32[17,160]{1,0:T(8,128)} %constant.59.clone) | copy-start | bytes 32644
  47.1 26.4 %all-to-all-start.1 = ((f32[32,5,128]{2,1,0:T(8,128)}), f32[32,5,128]{2,1,0:T(8,128)S(1)}, u32[]{:S(2)}, u32[]{:S(2)}) async-start(f32[32,5,128]{2,1,0:T(8,128)} %copy.47), calls=%async_computation.1 | async-start | bytes 262144 | tf_op jit(solution)/shard_map/all_to_all | solution.py:107
  74.2 15.0 %all-to-all-start.2 = ((f32[32,5,128]{2,1,0:T(8,128)}), f32[32,5,128]{2,1,0:T(8,128)S(1)}, u32[]{:S(2)}, u32[]{:S(2)}) async-start(f32[32,5,128]{2,1,0:T(8,128)} %reduce-window_subtract_fusion), calls=%async_computation.2 | async-start | bytes 262144 | tf_op jit(solution)/shard_map/all_to_all | solution.py:109
  92.1 26.5 %all-to-all-start.3 = ((bf16[16,64,128]{2,1,0:T(8,128)(2,1)}), bf16[16,64,128]{2,1,0:T(8,128)(2,1)S(1)}, u32[]{:S(2)}, u32[]{:S(2)}) async-start(bf16[16,64,128]{2,1,0:T(8,128)(2,1)} %bitcast.19), calls=%async_computation.3 | async-start | bytes 524288 | tf_op jit(solution)/shard_map/all_to_all | solution.py:156
  108.7 1.0 copy-start.1
  108.8 1.3 %copy-start.2 = (bf16[2,2,64,2048]{3,2,1,0:T(8,128)(2,1)}, bf16[2,2,64,2048]{3,2,1,0:T(8,128)(2,1)S(1)}, u32[]{:S(2)}) copy-start(bf16[2,2,64,2048]{3,2,1,0:T(8,128)(2,1)S(1)} %collective-permute-done.3.refs_2_.refs_6_) | copy-start | bytes 3145732

commit v15 on v14

--- a/solution.py
+++ b/solution.py
@@ -110,7 +110,7 @@
     return back.reshape(shape)
 
 
-def linear_heads(linear_query, linear_key, linear_value, lin_gain, held):
+def linear_heads(linear_query, linear_key, linear_value, lin_gain, held, finish):
     rows_dev = linear_query.shape[0]
     group_count = lax.axis_size(GROUP)
     lin_heads = linear_query.shape[1] // FDIM
@@ -136,6 +136,7 @@
         "jhf,jhe->hfe", sym_features(key_lin, False), value_lin, precision=lax.Precision.HIGHEST
     )
     before = groups_before(total)
+    before, finished = lax.optimization_barrier((before, finish(held)))
     from_state = jnp.einsum(
         "ihf,hfe->ihe", sym_features(query_lin, True), before, precision=lax.Precision.HIGHEST
     )
@@ -154,7 +155,7 @@
     out = (numerator * inv_rms * gain_rows).astype(jnp.bfloat16)
     out = out.reshape(group_count, rows_dev, own_heads * VDIM)
     back = lax.all_to_all(out, GROUP, split_axis=0, concat_axis=2, tiled=True)
-    return back.reshape(rows_dev, lin_heads * VDIM), held
+    return back.reshape(rows_dev, lin_heads * VDIM), finished
 
 
 def shards(
@@ -173,23 +174,28 @@
     stacked = jnp.stack([window_key, window_value])
     half = reach_dev // 2
     relayed = passed_along(stacked, ALL, half)
-    linear_out, relayed = linear_heads(linear_query, linear_key, linear_value, lin_gain, relayed)
-    pair = jnp.stack([stacked, relayed])
-    arrived = [passed_along(pair, ALL, k) for k in range(1, half)]
-    arrived += [relayed, passed_along(relayed, ALL, half)]
-    picks = []
-    for t in range(reach_dev):
-        distance = reach_dev - t
-        if distance == reach_dev:
-            picks.append((half, None))
-        elif distance == half:
-            picks.append((half - 1, None))
-        elif distance > half:
-            picks.append((distance - half - 1, 1))
-        else:
-            picks.append((distance - 1, 0))
-    window_out = window_attention(
-        device_pos, window_query, window_key, window_value, arrived, picks
+
+    def finish(relayed):
+        pair = jnp.stack([stacked, relayed])
+        arrived = [passed_along(pair, ALL, k) for k in range(1, half)]
+        arrived += [relayed, passed_along(relayed, ALL, half)]
+        picks = []
+        for t in range(reach_dev):
+            distance = reach_dev - t
+            if distance == reach_dev:
+                picks.append((half, None))
+            elif distance == half:
+                picks.append((half - 1, None))
+            elif distance > half:
+                picks.append((distance - half - 1, 1))
+            else:
+                picks.append((distance - 1, 0))
+        return window_attention(
+            device_pos, window_query, window_key, window_value, arrived, picks
+        )
+
+    linear_out, window_out = linear_heads(
+        linear_query, linear_key, linear_value, lin_gain, relayed, finish
     )
     return (linear_out, window_out)
 

time: 121 us -> 130 us (1.074)
  blocking collectives: 0 us -> 23.2 us
  starting transfers between devices: 60.3 us -> 48 us
  waiting for transfers between devices: 20.7 us -> 15.6 us
  matrix products: 14.9 us -> 18.7 us
    all_to_all x0 -> x1, blocking collectives: none -> 23.2 us  [linear_heads(): back = lax.all_to_all(out, GROUP, split_axis=0, concat_axis=2, tiled=True)]
    all_to_all x1 -> x0, starting transfers between devices: 16.6 us -> none  [linear_heads(): back = lax.all_to_all(out, GROUP, split_axis=0, concat_axis=2, tiled=True)]
    all_to_all x1, waiting for transfers between devices: 9.65 us -> 4.38 us  [groups_before(): held = lax.all_to_all(dealt, outer, split_axis=0, concat_axis=0, tiled=True)]
    all_to_all x1, starting transfers between devices: 3.86 us -> 7.24 us  [groups_before(): lax.all_to_all(prefix, outer, split_axis=0, concat_axis=0, tiled=True)]
    dot_general x1, matrix products: 3.04 us -> 5.21 us  [linear_heads(): jnp.einsum('hij,jhe->ihe', weight, value_lin, precision=lax.Precision.HIG...]
    dot_general x1, matrix products: 0.79 us -> 2.76 us  [linear_heads(): jnp.einsum('ihd,jhd->hij', query_bf, key_bf, preferred_element_type=jnp.f...]
    unnamed x15 -> x19, local copies, waits for them, and re-layouts: 3.87 us -> 3.85 us
  transfers between devices with their start and end apart: 9 -> 8, of which waited for: 3 -> 3; matrix products, arithmetic and copies ran while one was open for 22% -> 21% of each run, Pallas kernels for 7% -> 0%
where the time goes in v15:
time: 130 us; the launch traced here: 129 us
  starting transfers between devices  48 us (37%)
  blocking collectives  23.2 us (18%)
  matrix products  18.7 us (14%)
  waiting for transfers between devices  15.6 us (12%)
  local copies, waits for them, and re-layouts  8.84 us (7%)
  Pallas kernels  8.6 us (7%)
  other arithmetic  5.48 us (4%)
    all_to_all x1, blocking collectives, linear_heads(): back = lax.all_to_all(out, GROUP, split_axis=0, concat_axis=2, tiled=True)  23.2 us
    ppermute x5, starting transfers between devices, passed_along(): return lax.ppermute(shard, axis, pairs)  18.9 us
    all_to_all x1, starting transfers between devices, groups_before(): held = lax.all_to_all(dealt, outer, split_axis=0, concat_axis=0, tiled=True)  15.1 us
    pallas_call x1, Pallas kernels, window_attention(): pl.pallas_call(window_kernel, out_shape=jax.ShapeDtypeStruct((rows, chann...  8.6 us
    all_to_all x1, waiting for transfers between devices, groups_before(): lax.all_to_all(prefix, outer, split_axis=0, concat_axis=0, tiled=True)  8.6 us
    all_to_all x1, starting transfers between devices, groups_before(): lax.all_to_all(prefix, outer, split_axis=0, concat_axis=0, tiled=True)  7.24 us
    dot_general x4, matrix products, sym_features(): jnp.einsum('jhi,if->jhf', ext, jnp.asarray(table), precision=lax.Precisio...  7.11 us
    all_to_all x1, starting transfers between devices, linear_heads(): got = lax.all_to_all(packed, GROUP, split_axis=1, concat_axis=0, tiled=True)  6.73 us
  transfers between devices with their start and end apart: 8, of which 3 were waited for; matrix products, arithmetic and copies ran while one was open for 21% of the time, Pallas kernels for 0%

profile of v15, /device:TPU:1, one launch (start us, length us, event | category | flops | bytes accessed | tf_op | source)
XLA Modules:
  0.0 129.3 jit_solution(15740592891700169015)
XLA Ops:
  0.6 1.1 fusion.41
  1.8 5.4 %collective-permute-start = (bf16[2,64,2048]{2,1,0:T(8,128)(2,1)S(1)}, bf16[2,64,2048]{2,1,0:T(8,128)(2,1)}, u32[]{:S(2)}, u32[]{:S(2)}) collective-permute-start(bf16[2,64,2048]{2,1,0:T(8,128)(2,1)S(1)} %get-tuple-element.11), channel_id=1, source_target_pairs={{0,4},{1,5},{2,6},{3,7},{4,8},{5,9},{6,10},{7,11},{8,12},{9,13},{1... | collective-permute-start | bytes 1572872 | tf_op jit(solution)/shard_map/ppermute | solution.py:37
  9.4 1.2 pad_maximum_fusion.1
  10.6 2.6 %collective-permute-done.refs_4_ = bf16[2,64,2048]{2,1,0:T(8,128)(2,1)} collective-permute-done((bf16[2,64,2048]{2,1,0:T(8,128)(2,1)S(1)}, bf16[2,64,2048]{2,1,0:T(8,128)(2,1)}, u32[]{:S(2)}, u32[]{:S(2)}) %collective-permute-start) | collective-permute-done | bytes 524320 | tf_op jit(solution)/shard_map/ppermute | solution.py:37
  13.3 6.7 %all-to-all-start = ((bf16[64,16,160]{2,0,1:T(8,128)(2,1)}), bf16[64,16,160]{2,0,1:T(8,128)(2,1)S(1)}, u32[]{:S(2)}, u32[]{:S(2)}) async-start(bf16[64,16,160]{2,0,1:T(8,128)(2,1)} %pad_maximum_fusion.1), calls=%async_computation | async-start | bytes 1048576 | tf_op jit(solution)/shard_map/all_to_all | solution.py:127
  20.7 2.2 %pad_maximum_fusion = bf16[2,2,64,2048]{3,2,1,0:T(8,128)(2,1)} fusion(bf16[1,2,64,2048]{3,2,1,0:T(8,128)(2,1)} %bitcast.15, bf16[1,2,64,2048]{3,2,1,0:T(8,128)(2,1)S(1)} %get-tuple-element.10), kind=kLoop, calls=%fused_computation.18 | loop fusion | flops 524288 | bytes 2097152 | tf_op jit(solution)/shard_map/stack | solution.py:179
  22.9 4.6 %collective-permute-start.2 = (bf16[2,2,64,2048]{3,2,1,0:T(8,128)(2,1)}, bf16[2,2,64,2048]{3,2,1,0:T(8,128)(2,1)S(1)}, u32[]{:S(2)}, u32[]{:S(2)}) collective-permute-start(bf16[2,2,64,2048]{3,2,1,0:T(8,128)(2,1)} %pad_maximum_fusion), channel_id=1, source_target_pairs={{0,3},{1,4},{2,5},{3,6},{4,7},{5,8},{6,9},{7,10},{8,11},{9,12},{10... | collective-permute-start | bytes 3145736 | tf_op jit(solution)/shard_map/ppermute | solution.py:37
  27.5 3.6 %collective-permute-start.3 = (bf16[2,2,64,2048]{3,2,1,0:T(8,128)(2,1)}, bf16[2,2,64,2048]{3,2,1,0:T(8,128)(2,1)S(1)}, u32[]{:S(2)}, u32[]{:S(2)}) collective-permute-start(bf16[2,2,64,2048]{3,2,1,0:T(8,128)(2,1)} %pad_maximum_fusion), channel_id=1, source_target_pairs={{0,2},{1,3},{2,4},{3,5},{4,6},{5,7},{6,8},{7,9},{8,10},{9,11},{10,... | collective-permute-start | bytes 3145736 | tf_op jit(solution)/shard_map/ppermute | solution.py:37
  31.1 2.5 %collective-permute-start.4 = (bf16[2,2,64,2048]{3,2,1,0:T(8,128)(2,1)}, bf16[2,2,64,2048]{3,2,1,0:T(8,128)(2,1)}, u32[]{:S(2)}, u32[]{:S(2)}) collective-permute-start(bf16[2,2,64,2048]{3,2,1,0:T(8,128)(2,1)} %pad_maximum_fusion), channel_id=1, source_target_pairs={{0,1},{1,2},{2,3},{3,4},{4,5},{5,6},{6,7},{7,8},{8,9},{9,10},{10,1... | collective-permute-start | bytes 3145736 | tf_op jit(solution)/shard_map/ppermute | solution.py:37
  33.6 2.8 %collective-permute-start.1 = (bf16[2,64,2048]{2,1,0:T(8,128)(2,1)}, bf16[2,64,2048]{2,1,0:T(8,128)(2,1)}, u32[]{:S(2)}, u32[]{:S(2)}) collective-permute-start(bf16[2,64,2048]{2,1,0:T(8,128)(2,1)} %collective-permute-done.refs_4_), channel_id=1, source_target_pairs={{0,4},{1,5},{2,6},{3,7},{4,8},{5,9},{6,10},{7,11},{8,12},{9,13},{1... | collective-permute-start | bytes 1572872 | tf_op jit(solution)/shard_map/ppermute | solution.py:37
  36.6 2.8 %fusion.27 = f32[1024,1024]{1,0:T(8,128)} fusion(bf16[1024,160]{1,0:T(8,128)(2,1)S(1)} %bitcast.65), kind=kOutput, calls=%fused_computation.41 | convolution fusion | flops 33554432 | bytes 4521984 | tf_op jit(solution)/shard_map/ihd,jhd->hij/dot_general | solution.py:144
  40.2 1.7 %fusion.11 = f32[160,1024]{1,0:T(8,128)} fusion(f32[1024,160]{0,1:T(8,128)S(1)} %fusion.19, f32[17,160]{1,0:T(8,128)S(1)} %copy-done.5, f32[1024,1,16]{2,0,1:T(8,128)S(1)} %get-tuple-element.12), kind=kOutput, calls=%fused_computation.14 | convolution fusion | flops 33587200 | bytes 1387136 | tf_op jit(solution)/shard_map/jhi,if->jhf/dot_general | solution.py:44
  42.0 2.2 %dot_general.30 = f32[32,5,1024]{2,1,0:T(8,128)} reshape(f32[160,1024]{1,0:T(8,128)} %fusion.11) | data formatting | bytes 1310720 | tf_op jit(solution)/shard_map/jhf,jhe->hfe/dot_general | solution.py:135
  44.1 2.0 %fusion.13 = f32[32,5,128]{2,0,1:T(8,128)S(1)} fusion(f32[32,5,1024]{2,1,0:T(8,128)} %dot_general.30, bf16[1024,160]{1,0:T(8,128)(2,1)S(1)} %bitcast.66), kind=kOutput, calls=%fused_computation.19 | convolution fusion | flops 251658240 | bytes 999424 | tf_op jit(solution)/shard_map/jhf,jhe->hfe/dot_general | solution.py:135
  46.9 15.1 %all-to-all-start.1 = ((f32[32,5,128]{2,1,0:T(8,128)}), f32[32,5,128]{2,1,0:T(8,128)S(1)}, u32[]{:S(2)}, u32[]{:S(2)}) async-start(f32[32,5,128]{2,1,0:T(8,128)} %copy.47), calls=%async_computation.1 | async-start | bytes 262144 | tf_op jit(solution)/shard_map/all_to_all | solution.py:107
  62.0 5.2 %fusion = f32[128,1024]{1,0:T(8,128)} fusion(f32[1024,1024]{1,0:T(8,128)} %fusion.27, bf16[1024,160]{1,0:T(8,128)(2,1)S(1)} %bitcast.67), kind=kOutput, calls=%fused_computation | convolution fusion | flops 1617952768 | bytes 4980736 | tf_op jit(solution)/shard_map/hij,jhe->ihe/dot_general | solution.py:149
  67.2 1.7 %fusion.16 = f32[1024,160]{0,1:T(8,128)} fusion(f32[17,160]{1,0:T(8,128)S(1)} %copy-done.6, f32[1024,1,16]{2,0,1:T(8,128)S(1)} %get-tuple-element.13), kind=kOutput, calls=%fused_computation.24 | convolution fusion | flops 33423360 | bytes 731776 | tf_op jit(solution)/shard_map/jhi,if->jhf/dot_general | solution.py:44
  68.9 4.4 %all-to-all-done.1 = f32[32,5,128]{2,1,0:T(8,128)S(1)} async-done(((f32[32,5,128]{2,1,0:T(8,128)}), f32[32,5,128]{2,1,0:T(8,128)S(1)}, u32[]{:S(2)}, u32[]{:S(2)}) %all-to-all-start.1) | async-done | bytes 81952 | tf_op jit(solution)/shard_map/all_to_all | solution.py:107
  74.0 7.2 %all-to-all-start.2 = ((f32[32,5,128]{2,1,0:T(8,128)}), f32[32,5,128]{2,1,0:T(8,128)S(1)}, u32[]{:S(2)}, u32[]{:S(2)}) async-start(f32[32,5,128]{2,1,0:T(8,128)} %reduce-window_subtract_fusion), calls=%async_computation.2 | async-start | bytes 262144 | tf_op jit(solution)/shard_map/all_to_all | solution.py:109
  81.2 2.8 %convolution_multiply_fusion = f32[1024,160]{0,1:T(8,128)} fusion(f32[1024,160]{0,1:T(8,128)} %fusion.16, f32[17,160]{1,0:T(8,128)} %constant.58.clone, f32[1024,1,16]{2,0,1:T(8,128)S(1)} %get-tuple-element.13), kind=kOutput, calls=%fused_computation.12 | convolution fusion | flops 33587200 | bytes 1387136 | tf_op jit(solution)/shard_map/jhi,if->jhf/dot_general | solution.py:44
  84.0 8.6 %all-to-all-done.2 = f32[32,5,128]{2,1,0:T(8,128)S(1)} async-done(((f32[32,5,128]{2,1,0:T(8,128)}), f32[32,5,128]{2,1,0:T(8,128)S(1)}, u32[]{:S(2)}, u32[]{:S(2)}) %all-to-all-start.2) | async-done | bytes 81952 | tf_op jit(solution)/shard_map/all_to_all | solution.py:109
  94.6 8.6 %shard_map.122 = bf16[64,2048]{1,0:T(8,128)(2,1)} custom-call(s32[1]{0:T(128)} %bitcast.13.pos_ref, bf16[64,2048]{1,0:T(8,128)(2,1)} %q_ref.1, bf16[64,2048]{1,0:T(8,128)(2,1)} %k_ref.1, bf16[64,2048]{1,0:T(8,128)(2,1)} %v_ref.1, bf16[2,64,2048]{2,1,0:T(8,128)(2,1)} %collective-permute-done.1.refs_0_, bf16[2,2,64,2048]{3,2,1,0:T(8,128)(2,1)} %copy-done.1, ...), custom_call_target="tpu_custom_call" | custom-call | tf_op jit(solution)/shard_map/pallas_call | solution.py:84
  103.3 1.6 %multiply_reduce_fusion = (f32[1024]{0:T(1024)S(1)}, f32[1,128,1024]{2,1,0:T(8,128)S(1)}) fusion(f32[128,1024]{1,0:T(8,128)S(1)} %copy-done.4, f32[1024,160]{0,1:T(8,128)S(1)} %copy-done.3, f32[1,160,128]{2,1,0:T(8,128)} %reshape.106), kind=kOutput, calls=%fused_computation.30 | convolution fusion | flops 252050432 | bytes 1789952 | tf_op jit(solution)/shard_map/ihf,hfe->ihe/dot_general | solution.py:140
  105.1 23.2 %all_to_all.40 = bf16[16,64,128]{2,1,0:T(8,128)(2,1)S(1)} all-to-all(bf16[16,64,128]{2,1,0:T(8,128)(2,1)S(1)} %bitcast.70), channel_id=1, replica_groups=mesh['y'=8,'z'=4,'pair'=2,'core'=2,'sub'=4] {'pair','core','sub'}, dimensions={0} | all-to-all | bytes 524288 | tf_op jit(solution)/shard_map/all_to_all | solution.py:157
  (37 shorter events, 8.5 us)
Async XLA Ops:
  0.6 8.7 %copy-start = (bf16[64,2048]{1,0:T(8,128)(2,1)S(1)}, bf16[64,2048]{1,0:T(8,128)(2,1)}, u32[]{:S(2)}) copy-start(bf16[64,2048]{1,0:T(8,128)(2,1)} %param.13) | copy-start | bytes 786436
  1.8 11.5 %collective-permute-start = (bf16[2,64,2048]{2,1,0:T(8,128)(2,1)S(1)}, bf16[2,64,2048]{2,1,0:T(8,128)(2,1)}, u32[]{:S(2)}, u32[]{:S(2)}) collective-permute-start(bf16[2,64,2048]{2,1,0:T(8,128)(2,1)S(1)} %get-tuple-element.11), channel_id=1, source_target_pairs={{0,4},{1,5},{2,6},{3,7},{4,8},{5,9},{6,10},{7,11},{8,12},{9,13},{1... | collective-permute-start | bytes 1572872 | tf_op jit(solution)/shard_map/ppermute | solution.py:37
  13.3 23.1 %all-to-all-start = ((bf16[64,16,160]{2,0,1:T(8,128)(2,1)}), bf16[64,16,160]{2,0,1:T(8,128)(2,1)S(1)}, u32[]{:S(2)}, u32[]{:S(2)}) async-start(bf16[64,16,160]{2,0,1:T(8,128)(2,1)} %pad_maximum_fusion.1), calls=%async_computation | async-start | bytes 1048576 | tf_op jit(solution)/shard_map/all_to_all | solution.py:127
  20.7 18.6 %copy-start.7 = (f32[17,160]{1,0:T(8,128)S(1)}, f32[17,160]{1,0:T(8,128)}, u32[]{:S(2)}) copy-start(f32[17,160]{1,0:T(8,128)} %constant.57.clone) | copy-start | bytes 32644
  22.9 17.4 %copy-start.5 = (f32[17,160]{1,0:T(8,128)S(1)}, f32[17,160]{1,0:T(8,128)}, u32[]{:S(2)}) copy-start(f32[17,160]{1,0:T(8,128)} %constant.58.clone) | copy-start | bytes 32644
  22.9 70.4 %collective-permute-start.2 = (bf16[2,2,64,2048]{3,2,1,0:T(8,128)(2,1)}, bf16[2,2,64,2048]{3,2,1,0:T(8,128)(2,1)S(1)}, u32[]{:S(2)}, u32[]{:S(2)}) collective-permute-start(bf16[2,2,64,2048]{3,2,1,0:T(8,128)(2,1)} %pad_maximum_fusion), channel_id=1, source_target_pairs={{0,3},{1,4},{2,5},{3,6},{4,7},{5,8},{6,9},{7,10},{8,11},{9,12},{10... | collective-permute-start | bytes 3145736 | tf_op jit(solution)/shard_map/ppermute | solution.py:37
  27.5 65.8 %collective-permute-start.3 = (bf16[2,2,64,2048]{3,2,1,0:T(8,128)(2,1)}, bf16[2,2,64,2048]{3,2,1,0:T(8,128)(2,1)S(1)}, u32[]{:S(2)}, u32[]{:S(2)}) collective-permute-start(bf16[2,2,64,2048]{3,2,1,0:T(8,128)(2,1)} %pad_maximum_fusion), channel_id=1, source_target_pairs={{0,2},{1,3},{2,4},{3,5},{4,6},{5,7},{6,8},{7,9},{8,10},{9,11},{10,... | collective-permute-start | bytes 3145736 | tf_op jit(solution)/shard_map/ppermute | solution.py:37
  31.1 62.2 %collective-permute-start.4 = (bf16[2,2,64,2048]{3,2,1,0:T(8,128)(2,1)}, bf16[2,2,64,2048]{3,2,1,0:T(8,128)(2,1)}, u32[]{:S(2)}, u32[]{:S(2)}) collective-permute-start(bf16[2,2,64,2048]{3,2,1,0:T(8,128)(2,1)} %pad_maximum_fusion), channel_id=1, source_target_pairs={{0,1},{1,2},{2,3},{3,4},{4,5},{5,6},{6,7},{7,8},{8,9},{9,10},{10,1... | collective-permute-start | bytes 3145736 | tf_op jit(solution)/shard_map/ppermute | solution.py:37
  33.6 59.7 %collective-permute-start.1 = (bf16[2,64,2048]{2,1,0:T(8,128)(2,1)}, bf16[2,64,2048]{2,1,0:T(8,128)(2,1)}, u32[]{:S(2)}, u32[]{:S(2)}) collective-permute-start(bf16[2,64,2048]{2,1,0:T(8,128)(2,1)} %collective-permute-done.refs_4_), channel_id=1, source_target_pairs={{0,4},{1,5},{2,6},{3,7},{4,8},{5,9},{6,10},{7,11},{8,12},{9,13},{1... | collective-permute-start | bytes 1572872 | tf_op jit(solution)/shard_map/ppermute | solution.py:37
  46.9 26.4 %all-to-all-start.1 = ((f32[32,5,128]{2,1,0:T(8,128)}), f32[32,5,128]{2,1,0:T(8,128)S(1)}, u32[]{:S(2)}, u32[]{:S(2)}) async-start(f32[32,5,128]{2,1,0:T(8,128)} %copy.47), calls=%async_computation.1 | async-start | bytes 262144 | tf_op jit(solution)/shard_map/all_to_all | solution.py:107
  62.0 5.2 %copy-start.6 = (f32[17,160]{1,0:T(8,128)S(1)}, f32[17,160]{1,0:T(8,128)}, u32[]{:S(2)}) copy-start(f32[17,160]{1,0:T(8,128)} %constant.59.clone) | copy-start | bytes 32644
  74.0 18.7 %all-to-all-start.2 = ((f32[32,5,128]{2,1,0:T(8,128)}), f32[32,5,128]{2,1,0:T(8,128)S(1)}, u32[]{:S(2)}, u32[]{:S(2)}) async-start(f32[32,5,128]{2,1,0:T(8,128)} %reduce-window_subtract_fusion), calls=%async_computation.2 | async-start | bytes 262144 | tf_op jit(solution)/shard_map/all_to_all | solution.py:109
  93.3 1.0 copy-start.1
  93.3 1.3 %copy-start.2 = (bf16[2,2,64,2048]{3,2,1,0:T(8,128)(2,1)}, bf16[2,2,64,2048]{3,2,1,0:T(8,128)(2,1)S(1)}, u32[]{:S(2)}) copy-start(bf16[2,2,64,2048]{3,2,1,0:T(8,128)(2,1)S(1)} %collective-permute-done.3.refs_2_.refs_6_) | copy-start | bytes 3145732
  94.6 8.6 %copy-start.3 = (f32[1024,160]{0,1:T(8,128)S(1)}, f32[1024,160]{0,1:T(8,128)}, u32[]{:S(2)}) copy-start(f32[1024,160]{0,1:T(8,128)} %convolution_multiply_fusion) | copy-start | bytes 1966084
  94.6 8.6 %copy-start.4 = (f32[128,1024]{1,0:T(8,128)S(1)}, f32[128,1024]{1,0:T(8,128)}, u32[]{:S(2)}) copy-start(f32[128,1024]{1,0:T(8,128)} %fusion) | copy-start | bytes 1572868

commit v16 on v14

--- a/solution.py
+++ b/solution.py
@@ -135,6 +135,7 @@
     total = jnp.einsum(
         "jhf,jhe->hfe", sym_features(key_lin, False), value_lin, precision=lax.Precision.HIGHEST
     )
+    total, held = lax.optimization_barrier((total, held))
     before = groups_before(total)
     from_state = jnp.einsum(
         "ihf,hfe->ihe", sym_features(query_lin, True), before, precision=lax.Precision.HIGHEST

time: 121 us -> 143 us (1.18)
  waiting for transfers between devices: 20.7 us -> 36 us
  starting transfers between devices: 60.3 us -> 69.5 us
  matrix products: 14.9 us -> 13.1 us
    all_to_all x1, waiting for transfers between devices: 0.01 us -> 10.2 us  [linear_heads(): got = lax.all_to_all(packed, GROUP, split_axis=1, concat_axis=0, tiled=True)]
    all_to_all x1, starting transfers between devices: 16.6 us -> 24.9 us  [linear_heads(): back = lax.all_to_all(out, GROUP, split_axis=0, concat_axis=2, tiled=True)]
    all_to_all x1, waiting for transfers between devices: 0.01 us -> 7.57 us  [linear_heads(): back = lax.all_to_all(out, GROUP, split_axis=0, concat_axis=2, tiled=True)]
    all_to_all x1, waiting for transfers between devices: 9.65 us -> 5.22 us  [groups_before(): held = lax.all_to_all(dealt, outer, split_axis=0, concat_axis=0, tiled=True)]
    dot_general x4, matrix products: 7.13 us -> 2.9 us  [sym_features(): jnp.einsum('jhi,if->jhf', ext, jnp.asarray(table), precision=lax.Precisio...]
    dot_general x2 -> x0, local copies, waits for them, and re-layouts: 2.87 us -> none  [linear_heads(): jnp.einsum('jhf,jhe->hfe', sym_features(key_lin, False), value_lin, preci...]
    all_to_all x1, starting transfers between devices: 3.86 us -> 6.53 us  [groups_before(): lax.all_to_all(prefix, outer, split_axis=0, concat_axis=0, tiled=True)]
    all_to_all x1, waiting for transfers between devices: 8.36 us -> 10.7 us  [groups_before(): lax.all_to_all(prefix, outer, split_axis=0, concat_axis=0, tiled=True)]
  transfers between devices with their start and end apart: 9 -> 9, of which waited for: 3 -> 5; matrix products, arithmetic and copies ran while one was open for 22% -> 13% of each run, Pallas kernels for 7% -> 0%
where the time goes in v16:
time: 143 us; the launch traced here: 142 us
  starting transfers between devices  69.5 us (49%)
  waiting for transfers between devices  36 us (25%)
  matrix products  13.1 us (9%)
  local copies, waits for them, and re-layouts  9.28 us (6%)
  Pallas kernels  8.51 us (6%)
  other arithmetic  4.53 us (3%)
    all_to_all x1, starting transfers between devices, linear_heads(): back = lax.all_to_all(out, GROUP, split_axis=0, concat_axis=2, tiled=True)  24.9 us
    ppermute x5, starting transfers between devices, passed_along(): return lax.ppermute(shard, axis, pairs)  16.3 us
    all_to_all x1, starting transfers between devices, groups_before(): held = lax.all_to_all(dealt, outer, split_axis=0, concat_axis=0, tiled=True)  15.1 us
    all_to_all x1, waiting for transfers between devices, groups_before(): lax.all_to_all(prefix, outer, split_axis=0, concat_axis=0, tiled=True)  10.7 us
    all_to_all x1, waiting for transfers between devices, linear_heads(): got = lax.all_to_all(packed, GROUP, split_axis=1, concat_axis=0, tiled=True)  10.2 us
    pallas_call x1, Pallas kernels, window_attention(): pl.pallas_call(window_kernel, out_shape=jax.ShapeDtypeStruct((rows, chann...  8.51 us
    all_to_all x1, waiting for transfers between devices, linear_heads(): back = lax.all_to_all(out, GROUP, split_axis=0, concat_axis=2, tiled=True)  7.57 us
    all_to_all x1, starting transfers between devices, linear_heads(): got = lax.all_to_all(packed, GROUP, split_axis=1, concat_axis=0, tiled=True)  6.73 us
  transfers between devices with their start and end apart: 9, of which 5 were waited for; matrix products, arithmetic and copies ran while one was open for 13% of the time, Pallas kernels for 0%

profile of v16, /device:TPU:1, one launch (start us, length us, event | category | flops | bytes accessed | tf_op | source)
XLA Modules:
  0.0 141.9 jit_solution(3513957936410253710)
XLA Ops:
  0.7 1.1 fusion.36
  1.8 5.4 %collective-permute-start = (bf16[2,64,2048]{2,1,0:T(8,128)(2,1)S(1)}, bf16[2,64,2048]{2,1,0:T(8,128)(2,1)}, u32[]{:S(2)}, u32[]{:S(2)}) collective-permute-start(bf16[2,64,2048]{2,1,0:T(8,128)(2,1)S(1)} %get-tuple-element.11), channel_id=1, source_target_pairs={{0,4},{1,5},{2,6},{3,7},{4,8},{5,9},{6,10},{7,11},{8,12},{9,13},{1... | collective-permute-start | bytes 1572872 | tf_op jit(solution)/shard_map/ppermute | solution.py:37
  9.5 1.0 copy.46
  10.9 2.4 %collective-permute-done.refs_4_ = bf16[2,64,2048]{2,1,0:T(8,128)(2,1)} collective-permute-done((bf16[2,64,2048]{2,1,0:T(8,128)(2,1)S(1)}, bf16[2,64,2048]{2,1,0:T(8,128)(2,1)}, u32[]{:S(2)}, u32[]{:S(2)}) %collective-permute-start) | collective-permute-done | bytes 524320 | tf_op jit(solution)/shard_map/ppermute | solution.py:37
  13.3 1.0 copy.38
  14.2 6.7 %all-to-all-start = ((bf16[64,16,160]{2,0,1:T(8,128)(2,1)}), bf16[64,16,160]{2,0,1:T(8,128)(2,1)S(1)}, u32[]{:S(2)}, u32[]{:S(2)}) async-start(bf16[64,16,160]{2,0,1:T(8,128)(2,1)} %copy.38), calls=%async_computation | async-start | bytes 1048576 | tf_op jit(solution)/shard_map/all_to_all | solution.py:127
  21.0 10.2 %all-to-all-done = bf16[64,16,160]{2,0,1:T(8,128)(2,1)S(1)} async-done(((bf16[64,16,160]{2,0,1:T(8,128)(2,1)}), bf16[64,16,160]{2,0,1:T(8,128)(2,1)S(1)}, u32[]{:S(2)}, u32[]{:S(2)}) %all-to-all-start) | async-done | bytes 327712 | tf_op jit(solution)/shard_map/all_to_all | solution.py:127
  33.5 2.2 %pad_maximum_fusion = bf16[2,2,64,2048]{3,2,1,0:T(8,128)(2,1)} fusion(bf16[1,2,64,2048]{3,2,1,0:T(8,128)(2,1)} %bitcast.23, bf16[1,2,64,2048]{3,2,1,0:T(8,128)(2,1)S(1)} %get-tuple-element.10), kind=kLoop, calls=%fused_computation.18 | loop fusion | flops 524288 | bytes 2097152 | tf_op jit(solution)/shard_map/stack | solution.py:178
  35.6 2.5 %collective-permute-start.2 = (bf16[2,2,64,2048]{3,2,1,0:T(8,128)(2,1)}, bf16[2,2,64,2048]{3,2,1,0:T(8,128)(2,1)S(1)}, u32[]{:S(2)}, u32[]{:S(2)}) collective-permute-start(bf16[2,2,64,2048]{3,2,1,0:T(8,128)(2,1)} %pad_maximum_fusion), channel_id=1, source_target_pairs={{0,3},{1,4},{2,5},{3,6},{4,7},{5,8},{6,9},{7,10},{8,11},{9,12},{10... | collective-permute-start | bytes 3145736 | tf_op jit(solution)/shard_map/ppermute | solution.py:37
  38.1 3.8 %collective-permute-start.3 = (bf16[2,2,64,2048]{3,2,1,0:T(8,128)(2,1)}, bf16[2,2,64,2048]{3,2,1,0:T(8,128)(2,1)S(1)}, u32[]{:S(2)}, u32[]{:S(2)}) collective-permute-start(bf16[2,2,64,2048]{3,2,1,0:T(8,128)(2,1)} %pad_maximum_fusion), channel_id=1, source_target_pairs={{0,2},{1,3},{2,4},{3,5},{4,6},{5,7},{6,8},{7,9},{8,10},{9,11},{10,... | collective-permute-start | bytes 3145736 | tf_op jit(solution)/shard_map/ppermute | solution.py:37
  41.9 1.9 %collective-permute-start.4 = (bf16[2,2,64,2048]{3,2,1,0:T(8,128)(2,1)}, bf16[2,2,64,2048]{3,2,1,0:T(8,128)(2,1)}, u32[]{:S(2)}, u32[]{:S(2)}) collective-permute-start(bf16[2,2,64,2048]{3,2,1,0:T(8,128)(2,1)} %pad_maximum_fusion), channel_id=1, source_target_pairs={{0,1},{1,2},{2,3},{3,4},{4,5},{5,6},{6,7},{7,8},{8,9},{9,10},{10,1... | collective-permute-start | bytes 3145736 | tf_op jit(solution)/shard_map/ppermute | solution.py:37
  43.9 2.7 %collective-permute-start.1 = (bf16[2,64,2048]{2,1,0:T(8,128)(2,1)}, bf16[2,64,2048]{2,1,0:T(8,128)(2,1)}, u32[]{:S(2)}, u32[]{:S(2)}) collective-permute-start(bf16[2,64,2048]{2,1,0:T(8,128)(2,1)} %collective-permute-done.refs_4_), channel_id=1, source_target_pairs={{0,4},{1,5},{2,6},{3,7},{4,8},{5,9},{6,10},{7,11},{8,12},{9,13},{1... | collective-permute-start | bytes 1572872 | tf_op jit(solution)/shard_map/ppermute | solution.py:37
  46.6 2.8 %fusion.33 = f32[1024,1024]{1,0:T(8,128)} fusion(bf16[1024,160]{1,0:T(8,128)(2,1)S(1)} %bitcast.58), kind=kOutput, calls=%fused_computation.49 | convolution fusion | flops 33554432 | bytes 4521984 | tf_op jit(solution)/shard_map/ihd,jhd->hij/dot_general | solution.py:144
  50.0 15.1 %all-to-all-start.1 = ((f32[32,5,128]{2,1,0:T(8,128)}), f32[32,5,128]{2,1,0:T(8,128)S(1)}, u32[]{:S(2)}, u32[]{:S(2)}) async-start(f32[32,5,128]{2,1,0:T(8,128)} %reshape.105), calls=%async_computation.1 | async-start | bytes 262144 | tf_op jit(solution)/shard_map/all_to_all | solution.py:107
  65.2 5.2 %fusion = f32[128,1024]{1,0:T(8,128)} fusion(f32[1024,1024]{1,0:T(8,128)} %fusion.33, bf16[1024,160]{1,0:T(8,128)(2,1)S(1)} %bitcast.59), kind=kOutput, calls=%fused_computation | convolution fusion | flops 1617952768 | bytes 4980736 | tf_op jit(solution)/shard_map/hij,jhe->ihe/dot_general | solution.py:149
  71.2 5.2 %all-to-all-done.1 = f32[32,5,128]{2,1,0:T(8,128)S(1)} async-done(((f32[32,5,128]{2,1,0:T(8,128)}), f32[32,5,128]{2,1,0:T(8,128)S(1)}, u32[]{:S(2)}, u32[]{:S(2)}) %all-to-all-start.1) | async-done | bytes 81952 | tf_op jit(solution)/shard_map/all_to_all | solution.py:107
  77.1 6.5 %all-to-all-start.2 = ((f32[32,5,128]{2,1,0:T(8,128)}), f32[32,5,128]{2,1,0:T(8,128)}, u32[]{:S(2)}, u32[]{:S(2)}) async-start(f32[32,5,128]{2,1,0:T(8,128)} %reduce-window_subtract_fusion), calls=%async_computation.2 | async-start | bytes 262144 | tf_op jit(solution)/shard_map/all_to_all | solution.py:109
  84.4 10.7 %all-to-all-done.2 = f32[32,5,128]{2,1,0:T(8,128)} async-done(((f32[32,5,128]{2,1,0:T(8,128)}), f32[32,5,128]{2,1,0:T(8,128)}, u32[]{:S(2)}, u32[]{:S(2)}) %all-to-all-start.2) | async-done | bytes 81952 | tf_op jit(solution)/shard_map/all_to_all | solution.py:109
  95.0 0.9 reshape.106
  95.9 1.7 %multiply_reduce_fusion = (f32[1024]{0:T(1024)S(1)}, f32[1,128,1024]{2,1,0:T(8,128)S(1)}) fusion(f32[128,1024]{1,0:T(8,128)} %fusion, f32[160,128]{1,0:T(8,128)S(1)} %reshape.106, f32[1024,160]{0,1:T(8,128)S(1)} %convolution_multiply_fusion), kind=kOutput, calls=%fused_computation.22 | convolution fusion | flops 252050432 | bytes 1789952 | tf_op jit(solution)/shard_map/ihf,hfe->ihe/dot_general | solution.py:140
  98.6 24.9 %all-to-all-start.3 = ((bf16[16,64,128]{2,1,0:T(8,128)(2,1)}), bf16[16,64,128]{2,1,0:T(8,128)(2,1)S(1)}, u32[]{:S(2)}, u32[]{:S(2)}) async-start(bf16[16,64,128]{2,1,0:T(8,128)(2,1)} %bitcast.18), calls=%async_computation.3 | async-start | bytes 524288 | tf_op jit(solution)/shard_map/all_to_all | solution.py:157
  123.5 7.6 %all-to-all-done.3 = bf16[16,64,128]{2,1,0:T(8,128)(2,1)S(1)} async-done(((bf16[16,64,128]{2,1,0:T(8,128)(2,1)}), bf16[16,64,128]{2,1,0:T(8,128)(2,1)S(1)}, u32[]{:S(2)}, u32[]{:S(2)}) %all-to-all-start.3) | async-done | bytes 262176 | tf_op jit(solution)/shard_map/all_to_all | solution.py:157
  132.0 0.9 copy-done.1
  133.3 8.5 %shard_map.122 = bf16[64,2048]{1,0:T(8,128)(2,1)} custom-call(s32[1]{0:T(128)} %bitcast.21.pos_ref, bf16[64,2048]{1,0:T(8,128)(2,1)} %q_ref.1, bf16[64,2048]{1,0:T(8,128)(2,1)} %k_ref.1, bf16[64,2048]{1,0:T(8,128)(2,1)} %v_ref.1, bf16[2,64,2048]{2,1,0:T(8,128)(2,1)} %collective-permute-done.1.refs_0_, bf16[2,2,64,2048]{3,2,1,0:T(8,128)(2,1)} %copy-done.1, ...), custom_call_target="tpu_custom_call" | custom-call | tf_op jit(solution)/shard_map/pallas_call | solution.py:84
  (38 shorter events, 10.2 us)
Async XLA Ops:
  0.6 20.3 %copy-start = (f32[2048]{0:T(1024)S(1)}, f32[2048]{0:T(1024)}, u32[]{:S(2)}) copy-start(f32[2048]{0:T(1024)} %param.14) | copy-start | bytes 24580
  0.6 30.8 %copy-start.5 = (f32[17,160]{1,0:T(8,128)S(1)}, f32[17,160]{1,0:T(8,128)}, u32[]{:S(2)}) copy-start(f32[17,160]{1,0:T(8,128)} %constant.57.clone) | copy-start | bytes 32644
  0.7 31.5 %copy-start.3 = (f32[17,160]{1,0:T(8,128)S(1)}, f32[17,160]{1,0:T(8,128)}, u32[]{:S(2)}) copy-start(f32[17,160]{1,0:T(8,128)} %constant.58.clone) | copy-start | bytes 32644
  1.8 11.5 %collective-permute-start = (bf16[2,64,2048]{2,1,0:T(8,128)(2,1)S(1)}, bf16[2,64,2048]{2,1,0:T(8,128)(2,1)}, u32[]{:S(2)}, u32[]{:S(2)}) collective-permute-start(bf16[2,64,2048]{2,1,0:T(8,128)(2,1)S(1)} %get-tuple-element.11), channel_id=1, source_target_pairs={{0,4},{1,5},{2,6},{3,7},{4,8},{5,9},{6,10},{7,11},{8,12},{9,13},{1... | collective-permute-start | bytes 1572872 | tf_op jit(solution)/shard_map/ppermute | solution.py:37
  14.2 16.9 %all-to-all-start = ((bf16[64,16,160]{2,0,1:T(8,128)(2,1)}), bf16[64,16,160]{2,0,1:T(8,128)(2,1)S(1)}, u32[]{:S(2)}, u32[]{:S(2)}) async-start(bf16[64,16,160]{2,0,1:T(8,128)(2,1)} %copy.38), calls=%async_computation | async-start | bytes 1048576 | tf_op jit(solution)/shard_map/all_to_all | solution.py:127
  35.6 96.4 %collective-permute-start.2 = (bf16[2,2,64,2048]{3,2,1,0:T(8,128)(2,1)}, bf16[2,2,64,2048]{3,2,1,0:T(8,128)(2,1)S(1)}, u32[]{:S(2)}, u32[]{:S(2)}) collective-permute-start(bf16[2,2,64,2048]{3,2,1,0:T(8,128)(2,1)} %pad_maximum_fusion), channel_id=1, source_target_pairs={{0,3},{1,4},{2,5},{3,6},{4,7},{5,8},{6,9},{7,10},{8,11},{9,12},{10... | collective-permute-start | bytes 3145736 | tf_op jit(solution)/shard_map/ppermute | solution.py:37
  38.1 93.9 %collective-permute-start.3 = (bf16[2,2,64,2048]{3,2,1,0:T(8,128)(2,1)}, bf16[2,2,64,2048]{3,2,1,0:T(8,128)(2,1)S(1)}, u32[]{:S(2)}, u32[]{:S(2)}) collective-permute-start(bf16[2,2,64,2048]{3,2,1,0:T(8,128)(2,1)} %pad_maximum_fusion), channel_id=1, source_target_pairs={{0,2},{1,3},{2,4},{3,5},{4,6},{5,7},{6,8},{7,9},{8,10},{9,11},{10,... | collective-permute-start | bytes 3145736 | tf_op jit(solution)/shard_map/ppermute | solution.py:37
  41.9 90.1 %collective-permute-start.4 = (bf16[2,2,64,2048]{3,2,1,0:T(8,128)(2,1)}, bf16[2,2,64,2048]{3,2,1,0:T(8,128)(2,1)}, u32[]{:S(2)}, u32[]{:S(2)}) collective-permute-start(bf16[2,2,64,2048]{3,2,1,0:T(8,128)(2,1)} %pad_maximum_fusion), channel_id=1, source_target_pairs={{0,1},{1,2},{2,3},{3,4},{4,5},{5,6},{6,7},{7,8},{8,9},{9,10},{10,1... | collective-permute-start | bytes 3145736 | tf_op jit(solution)/shard_map/ppermute | solution.py:37
  43.9 88.1 %collective-permute-start.1 = (bf16[2,64,2048]{2,1,0:T(8,128)(2,1)}, bf16[2,64,2048]{2,1,0:T(8,128)(2,1)}, u32[]{:S(2)}, u32[]{:S(2)}) collective-permute-start(bf16[2,64,2048]{2,1,0:T(8,128)(2,1)} %collective-permute-done.refs_4_), channel_id=1, source_target_pairs={{0,4},{1,5},{2,6},{3,7},{4,8},{5,9},{6,10},{7,11},{8,12},{9,13},{1... | collective-permute-start | bytes 1572872 | tf_op jit(solution)/shard_map/ppermute | solution.py:37
  50.0 26.4 %all-to-all-start.1 = ((f32[32,5,128]{2,1,0:T(8,128)}), f32[32,5,128]{2,1,0:T(8,128)S(1)}, u32[]{:S(2)}, u32[]{:S(2)}) async-start(f32[32,5,128]{2,1,0:T(8,128)} %reshape.105), calls=%async_computation.1 | async-start | bytes 262144 | tf_op jit(solution)/shard_map/all_to_all | solution.py:107
  65.2 5.2 %copy-start.4 = (f32[17,160]{1,0:T(8,128)S(1)}, f32[17,160]{1,0:T(8,128)}, u32[]{:S(2)}) copy-start(f32[17,160]{1,0:T(8,128)} %constant.59.clone) | copy-start | bytes 32644
  77.1 17.9 %all-to-all-start.2 = ((f32[32,5,128]{2,1,0:T(8,128)}), f32[32,5,128]{2,1,0:T(8,128)}, u32[]{:S(2)}, u32[]{:S(2)}) async-start(f32[32,5,128]{2,1,0:T(8,128)} %reduce-window_subtract_fusion), calls=%async_computation.2 | async-start | bytes 262144 | tf_op jit(solution)/shard_map/all_to_all | solution.py:109
  98.6 32.4 %all-to-all-start.3 = ((bf16[16,64,128]{2,1,0:T(8,128)(2,1)}), bf16[16,64,128]{2,1,0:T(8,128)(2,1)S(1)}, u32[]{:S(2)}, u32[]{:S(2)}) async-start(bf16[16,64,128]{2,1,0:T(8,128)(2,1)} %bitcast.18), calls=%async_computation.3 | async-start | bytes 524288 | tf_op jit(solution)/shard_map/all_to_all | solution.py:157
  132.0 1.0 copy-start.1
  132.0 1.3 copy-start.2

commit v17 on v14

--- a/solution.py
+++ b/solution.py
@@ -99,15 +99,16 @@
     )
 
 
-def groups_before(total):
+def groups_before(total, tag):
     outer = ("y", "z")
     outer_count = lax.axis_size(outer)
     shape = total.shape
     dealt = total.reshape(outer_count, -1, shape[-1])
     held = lax.all_to_all(dealt, outer, split_axis=0, concat_axis=0, tiled=True)
+    held, tag = lax.optimization_barrier((held, tag))
     prefix = jnp.cumsum(held, axis=0) - held
     back = lax.all_to_all(prefix, outer, split_axis=0, concat_axis=0, tiled=True)
-    return back.reshape(shape)
+    return back.reshape(shape), tag
 
 
 def linear_heads(linear_query, linear_key, linear_value, lin_gain, held):
@@ -135,7 +136,7 @@
     total = jnp.einsum(
         "jhf,jhe->hfe", sym_features(key_lin, False), value_lin, precision=lax.Precision.HIGHEST
     )
-    before = groups_before(total)
+    before, (query_bf, key_bf, value_lin) = groups_before(total, (query_bf, key_bf, value_lin))
     from_state = jnp.einsum(
         "ihf,hfe->ihe", sym_features(query_lin, True), before, precision=lax.Precision.HIGHEST
     )

time: 121 us -> 125 us (1.033)
  waiting for transfers between devices: 20.7 us -> 14.3 us
  starting transfers between devices: 60.3 us -> 66.5 us
  local copies, waits for them, and re-layouts: 8.88 us -> 11.3 us
    all_to_all x1, starting transfers between devices: 16.6 us -> 20.3 us  [linear_heads(): back = lax.all_to_all(out, GROUP, split_axis=0, concat_axis=2, tiled=True)]
    all_to_all x1, waiting for transfers between devices: 9.65 us -> 6.3 us  [groups_before(): held = lax.all_to_all(dealt, outer, split_axis=0, concat_axis=0, tiled=True)]
    all_to_all x1, waiting for transfers between devices: 8.36 us -> 5.31 us  [groups_before(): lax.all_to_all(prefix, outer, split_axis=0, concat_axis=0, tiled=True)]
    all_to_all x1, starting transfers between devices: 3.86 us -> 5.63 us  [groups_before(): lax.all_to_all(prefix, outer, split_axis=0, concat_axis=0, tiled=True)]
    another operation x1, local copies, waits for them, and re-layouts: 0.01 us -> 1.55 us
    unnamed x15 -> x17, local copies, waits for them, and re-layouts: 3.87 us -> 3.83 us
  transfers between devices with their start and end apart: 9 -> 9, of which waited for: 3 -> 3; matrix products, arithmetic and copies ran while one was open for 22% -> 25% of each run, Pallas kernels for 7% -> 7%
where the time goes in v17:
time: 125 us; the launch traced here: 124 us
  starting transfers between devices  66.5 us (53%)
  matrix products  16.1 us (13%)
  waiting for transfers between devices  14.3 us (11%)
  local copies, waits for them, and re-layouts  11.3 us (9%)
  Pallas kernels  8.51 us (7%)
  other arithmetic  6.39 us (5%)
    all_to_all x1, starting transfers between devices, linear_heads(): back = lax.all_to_all(out, GROUP, split_axis=0, concat_axis=2, tiled=True)  20.3 us
    ppermute x5, starting transfers between devices, passed_along(): return lax.ppermute(shard, axis, pairs)  18.8 us
    all_to_all x1, starting transfers between devices, groups_before(): held = lax.all_to_all(dealt, outer, split_axis=0, concat_axis=0, tiled=True)  15.1 us
    pallas_call x1, Pallas kernels, window_attention(): pl.pallas_call(window_kernel, out_shape=jax.ShapeDtypeStruct((rows, chann...  8.51 us
    all_to_all x1, starting transfers between devices, linear_heads(): got = lax.all_to_all(packed, GROUP, split_axis=1, concat_axis=0, tiled=True)  6.73 us
    dot_general x4, matrix products, sym_features(): jnp.einsum('jhi,if->jhf', ext, jnp.asarray(table), precision=lax.Precisio...  6.69 us
    all_to_all x1, waiting for transfers between devices, groups_before(): held = lax.all_to_all(dealt, outer, split_axis=0, concat_axis=0, tiled=True)  6.3 us
    all_to_all x1, starting transfers between devices, groups_before(): lax.all_to_all(prefix, outer, split_axis=0, concat_axis=0, tiled=True)  5.63 us
  transfers between devices with their start and end apart: 9, of which 3 were waited for; matrix products, arithmetic and copies ran while one was open for 25% of the time, Pallas kernels for 7%

profile of v17, /device:TPU:1, one launch (start us, length us, event | category | flops | bytes accessed | tf_op | source)
XLA Modules:
  0.0 124.0 jit_solution(4990548203386443561)
XLA Ops:
  1.8 5.4 %collective-permute-start = (bf16[2,64,2048]{2,1,0:T(8,128)(2,1)S(1)}, bf16[2,64,2048]{2,1,0:T(8,128)(2,1)}, u32[]{:S(2)}, u32[]{:S(2)}) collective-permute-start(bf16[2,64,2048]{2,1,0:T(8,128)(2,1)S(1)} %get-tuple-element.15), channel_id=1, source_target_pairs={{0,4},{1,5},{2,6},{3,7},{4,8},{5,9},{6,10},{7,11},{8,12},{9,13},{1... | collective-permute-start | bytes 1572872 | tf_op jit(solution)/shard_map/ppermute | solution.py:37
  9.4 1.2 %pad_maximum_fusion.1 = bf16[64,16,160]{2,0,1:T(8,128)(2,1)} fusion(bf16[64,16,128]{2,0,1:T(8,128)(2,1)S(1)} %copy_bitcast_fusion.1, bf16[64,16,16]{2,0,1:T(8,128)(2,1)S(1)} %copy.44, bf16[64,16,16]{2,0,1:T(8,128)(2,1)S(1)} %copy.43), kind=kLoop, calls=%fused_computation.21 | loop fusion | flops 983040 | bytes 655360 | tf_op jit(solution)/shard_map/concatenate | solution.py:119
  10.7 2.6 %collective-permute-done.refs_4_ = bf16[2,64,2048]{2,1,0:T(8,128)(2,1)} collective-permute-done((bf16[2,64,2048]{2,1,0:T(8,128)(2,1)S(1)}, bf16[2,64,2048]{2,1,0:T(8,128)(2,1)}, u32[]{:S(2)}, u32[]{:S(2)}) %collective-permute-start) | collective-permute-done | bytes 524320 | tf_op jit(solution)/shard_map/ppermute | solution.py:37
  13.3 6.7 %all-to-all-start = ((bf16[64,16,160]{2,0,1:T(8,128)(2,1)}), bf16[64,16,160]{2,0,1:T(8,128)(2,1)S(1)}, u32[]{:S(2)}, u32[]{:S(2)}) async-start(bf16[64,16,160]{2,0,1:T(8,128)(2,1)} %pad_maximum_fusion.1), calls=%async_computation | async-start | bytes 1048576 | tf_op jit(solution)/shard_map/all_to_all | solution.py:128
  20.7 2.1 %pad_maximum_fusion = bf16[2,2,64,2048]{3,2,1,0:T(8,128)(2,1)} fusion(bf16[1,2,64,2048]{3,2,1,0:T(8,128)(2,1)} %bitcast.30, bf16[1,2,64,2048]{3,2,1,0:T(8,128)(2,1)S(1)} %get-tuple-element.14), kind=kLoop, calls=%fused_computation.18 | loop fusion | flops 524288 | bytes 2097152 | tf_op jit(solution)/shard_map/stack | solution.py:178
  22.9 4.5 %collective-permute-start.2 = (bf16[2,2,64,2048]{3,2,1,0:T(8,128)(2,1)}, bf16[2,2,64,2048]{3,2,1,0:T(8,128)(2,1)S(1)}, u32[]{:S(2)}, u32[]{:S(2)}) collective-permute-start(bf16[2,2,64,2048]{3,2,1,0:T(8,128)(2,1)} %pad_maximum_fusion), channel_id=1, source_target_pairs={{0,3},{1,4},{2,5},{3,6},{4,7},{5,8},{6,9},{7,10},{8,11},{9,12},{10... | collective-permute-start | bytes 3145736 | tf_op jit(solution)/shard_map/ppermute | solution.py:37
  27.4 3.6 %collective-permute-start.3 = (bf16[2,2,64,2048]{3,2,1,0:T(8,128)(2,1)}, bf16[2,2,64,2048]{3,2,1,0:T(8,128)(2,1)S(1)}, u32[]{:S(2)}, u32[]{:S(2)}) collective-permute-start(bf16[2,2,64,2048]{3,2,1,0:T(8,128)(2,1)} %pad_maximum_fusion), channel_id=1, source_target_pairs={{0,2},{1,3},{2,4},{3,5},{4,6},{5,7},{6,8},{7,9},{8,10},{9,11},{10,... | collective-permute-start | bytes 3145736 | tf_op jit(solution)/shard_map/ppermute | solution.py:37
  31.0 2.5 %collective-permute-start.4 = (bf16[2,2,64,2048]{3,2,1,0:T(8,128)(2,1)}, bf16[2,2,64,2048]{3,2,1,0:T(8,128)(2,1)}, u32[]{:S(2)}, u32[]{:S(2)}) collective-permute-start(bf16[2,2,64,2048]{3,2,1,0:T(8,128)(2,1)} %pad_maximum_fusion), channel_id=1, source_target_pairs={{0,1},{1,2},{2,3},{3,4},{4,5},{5,6},{6,7},{7,8},{8,9},{9,10},{10,1... | collective-permute-start | bytes 3145736 | tf_op jit(solution)/shard_map/ppermute | solution.py:37
  33.5 2.8 %collective-permute-start.1 = (bf16[2,64,2048]{2,1,0:T(8,128)(2,1)}, bf16[2,64,2048]{2,1,0:T(8,128)(2,1)}, u32[]{:S(2)}, u32[]{:S(2)}) collective-permute-start(bf16[2,64,2048]{2,1,0:T(8,128)(2,1)} %collective-permute-done.refs_4_), channel_id=1, source_target_pairs={{0,4},{1,5},{2,6},{3,7},{4,8},{5,9},{6,10},{7,11},{8,12},{9,13},{1... | collective-permute-start | bytes 1572872 | tf_op jit(solution)/shard_map/ppermute | solution.py:37
  38.2 1.7 %fusion.11 = f32[160,1024]{1,0:T(8,128)} fusion(f32[1024,160]{0,1:T(8,128)S(1)} %fusion.20, f32[17,160]{1,0:T(8,128)S(1)} %copy-done.5, f32[1024,1,16]{2,0,1:T(8,128)S(1)} %get-tuple-element.17), kind=kOutput, calls=%fused_computation.14 | convolution fusion | flops 33587200 | bytes 1387136 | tf_op jit(solution)/shard_map/jhi,if->jhf/dot_general | solution.py:44
  40.0 2.2 %dot_general.28 = f32[32,5,1024]{2,1,0:T(8,128)} reshape(f32[160,1024]{1,0:T(8,128)} %fusion.11) | data formatting | bytes 1310720 | tf_op jit(solution)/shard_map/jhf,jhe->hfe/dot_general | solution.py:136
  42.1 2.0 %fusion.13 = f32[32,5,128]{2,0,1:T(8,128)S(1)} fusion(f32[32,5,1024]{2,1,0:T(8,128)} %dot_general.28, bf16[1024,160]{1,0:T(8,128)(2,1)S(1)} %bitcast.78), kind=kOutput, calls=%fused_computation.19 | convolution fusion | flops 251658240 | bytes 999424 | tf_op jit(solution)/shard_map/jhf,jhe->hfe/dot_general | solution.py:136
  44.9 15.1 %all-to-all-start.1 = ((f32[32,5,128]{2,1,0:T(8,128)}), f32[32,5,128]{2,1,0:T(8,128)S(1)}, u32[]{:S(2)}, u32[]{:S(2)}) async-start(f32[32,5,128]{2,1,0:T(8,128)} %copy.47), calls=%async_computation.1 | async-start | bytes 262144 | tf_op jit(solution)/shard_map/all_to_all | solution.py:107
  59.9 1.6 %fusion.16 = f32[1024,160]{0,1:T(8,128)S(1)} fusion(f32[17,160]{1,0:T(8,128)} %constant.59.clone, f32[1024,1,16]{2,0,1:T(8,128)S(1)} %get-tuple-element.16), kind=kOutput, calls=%fused_computation.24 | convolution fusion | flops 33423360 | bytes 731776 | tf_op jit(solution)/shard_map/jhi,if->jhf/dot_general | solution.py:44
  61.5 2.5 %convolution_multiply_fusion = f32[1024,160]{0,1:T(8,128)} fusion(f32[1024,160]{0,1:T(8,128)S(1)} %fusion.16, f32[17,160]{1,0:T(8,128)} %constant.58.clone, f32[1024,1,16]{2,0,1:T(8,128)S(1)} %get-tuple-element.16), kind=kOutput, calls=%fused_computation.12 | convolution fusion | flops 33587200 | bytes 1387136 | tf_op jit(solution)/shard_map/jhi,if->jhf/dot_general | solution.py:44
  65.0 6.3 %all-to-all-done.1 = f32[32,5,128]{2,1,0:T(8,128)S(1)} async-done(((f32[32,5,128]{2,1,0:T(8,128)}), f32[32,5,128]{2,1,0:T(8,128)S(1)}, u32[]{:S(2)}, u32[]{:S(2)}) %all-to-all-start.1) | async-done | bytes 81952 | tf_op jit(solution)/shard_map/all_to_all | solution.py:107
  71.9 5.6 %all-to-all-start.2 = ((f32[32,5,128]{2,1,0:T(8,128)}), f32[32,5,128]{2,1,0:T(8,128)}, u32[]{:S(2)}, u32[]{:S(2)}) async-start(f32[32,5,128]{2,1,0:T(8,128)} %reduce-window_subtract_fusion), calls=%async_computation.2 | async-start | bytes 262144 | tf_op jit(solution)/shard_map/all_to_all | solution.py:110
  77.6 1.8 %fusion.27 = f32[1024,1024]{1,0:T(8,128)S(1)} fusion(bf16[1024,1,16]{2,0,1:T(8,128)(2,1)} %get-tuple-element.11, bf16[1024,1,16]{2,0,1:T(8,128)(2,1)} %get-tuple-element.10), kind=kOutput, calls=%fused_computation.42 | convolution fusion | flops 33554432 | bytes 4259840 | tf_op jit(solution)/shard_map/ihd,jhd->hij/dot_general | solution.py:144
  79.4 4.1 %fusion = f32[128,1024]{1,0:T(8,128)S(1)} fusion(f32[1024,1024]{1,0:T(8,128)S(1)} %fusion.27, f32[1024,1,128]{2,0,1:T(8,128)S(1)} %copy-done.4), kind=kOutput, calls=%fused_computation | convolution fusion | flops 1617952768 | bytes 5242880 | tf_op jit(solution)/shard_map/hij,jhe->ihe/dot_general | solution.py:149
  83.5 5.3 %all-to-all-done.2 = f32[32,5,128]{2,1,0:T(8,128)} async-done(((f32[32,5,128]{2,1,0:T(8,128)}), f32[32,5,128]{2,1,0:T(8,128)}, u32[]{:S(2)}, u32[]{:S(2)}) %all-to-all-start.2) | async-done | bytes 81952 | tf_op jit(solution)/shard_map/all_to_all | solution.py:110
  88.8 1.6 %reshape.119 = f32[160,128]{1,0:T(8,128)} reshape(f32[32,5,128]{2,1,0:T(8,128)} %all-to-all-done.2) | data formatting | bytes 163840 | tf_op jit(solution)/shard_map/reshape.34
  90.3 1.6 %multiply_reduce_fusion = (f32[1024]{0:T(1024)S(1)}, f32[1,128,1024]{2,1,0:T(8,128)S(1)}) fusion(f32[128,1024]{1,0:T(8,128)S(1)} %fusion, f32[160,128]{1,0:T(8,128)} %reshape.119, f32[1024,160]{0,1:T(8,128)S(1)} %copy-done.3), kind=kOutput, calls=%fused_computation.31 | convolution fusion | flops 252050432 | bytes 1789952 | tf_op jit(solution)/shard_map/ihf,hfe->ihe/dot_general | solution.py:140
  92.9 20.3 %all-to-all-start.3 = ((bf16[16,64,128]{2,1,0:T(8,128)(2,1)}), bf16[16,64,128]{2,1,0:T(8,128)(2,1)S(1)}, u32[]{:S(2)}, u32[]{:S(2)}) async-start(bf16[16,64,128]{2,1,0:T(8,128)(2,1)} %bitcast.25), calls=%async_computation.3 | async-start | bytes 524288 | tf_op jit(solution)/shard_map/all_to_all | solution.py:157
  114.5 8.5 %shard_map.122 = bf16[64,2048]{1,0:T(8,128)(2,1)} custom-call(s32[1]{0:T(128)} %bitcast.28.pos_ref, bf16[64,2048]{1,0:T(8,128)(2,1)} %q_ref.1, bf16[64,2048]{1,0:T(8,128)(2,1)} %k_ref.1, bf16[64,2048]{1,0:T(8,128)(2,1)} %v_ref.1, bf16[2,64,2048]{2,1,0:T(8,128)(2,1)} %collective-permute-done.1.refs_0_, bf16[2,2,64,2048]{3,2,1,0:T(8,128)(2,1)} %copy-done.1, ...), custom_call_target="tpu_custom_call" | custom-call | tf_op jit(solution)/shard_map/pallas_call | solution.py:84
  (38 shorter events, 11.5 us)
Async XLA Ops:
  0.6 8.7 %copy-start = (bf16[64,2048]{1,0:T(8,128)(2,1)S(1)}, bf16[64,2048]{1,0:T(8,128)(2,1)}, u32[]{:S(2)}) copy-start(bf16[64,2048]{1,0:T(8,128)(2,1)} %param.13) | copy-start | bytes 786436
  1.8 11.5 %collective-permute-start = (bf16[2,64,2048]{2,1,0:T(8,128)(2,1)S(1)}, bf16[2,64,2048]{2,1,0:T(8,128)(2,1)}, u32[]{:S(2)}, u32[]{:S(2)}) collective-permute-start(bf16[2,64,2048]{2,1,0:T(8,128)(2,1)S(1)} %get-tuple-element.15), channel_id=1, source_target_pairs={{0,4},{1,5},{2,6},{3,7},{4,8},{5,9},{6,10},{7,11},{8,12},{9,13},{1... | collective-permute-start | bytes 1572872 | tf_op jit(solution)/shard_map/ppermute | solution.py:37
  8.1 29.3 %copy-start.6 = (f32[17,160]{1,0:T(8,128)S(1)}, f32[17,160]{1,0:T(8,128)}, u32[]{:S(2)}) copy-start(f32[17,160]{1,0:T(8,128)} %constant.57.clone) | copy-start | bytes 32644
  9.4 28.8 %copy-start.5 = (f32[17,160]{1,0:T(8,128)S(1)}, f32[17,160]{1,0:T(8,128)}, u32[]{:S(2)}) copy-start(f32[17,160]{1,0:T(8,128)} %constant.58.clone) | copy-start | bytes 32644
  13.3 23.0 %all-to-all-start = ((bf16[64,16,160]{2,0,1:T(8,128)(2,1)}), bf16[64,16,160]{2,0,1:T(8,128)(2,1)S(1)}, u32[]{:S(2)}, u32[]{:S(2)}) async-start(bf16[64,16,160]{2,0,1:T(8,128)(2,1)} %pad_maximum_fusion.1), calls=%async_computation | async-start | bytes 1048576 | tf_op jit(solution)/shard_map/all_to_all | solution.py:128
  22.9 90.4 %collective-permute-start.2 = (bf16[2,2,64,2048]{3,2,1,0:T(8,128)(2,1)}, bf16[2,2,64,2048]{3,2,1,0:T(8,128)(2,1)S(1)}, u32[]{:S(2)}, u32[]{:S(2)}) collective-permute-start(bf16[2,2,64,2048]{3,2,1,0:T(8,128)(2,1)} %pad_maximum_fusion), channel_id=1, source_target_pairs={{0,3},{1,4},{2,5},{3,6},{4,7},{5,8},{6,9},{7,10},{8,11},{9,12},{10... | collective-permute-start | bytes 3145736 | tf_op jit(solution)/shard_map/ppermute | solution.py:37
  27.4 85.9 %collective-permute-start.3 = (bf16[2,2,64,2048]{3,2,1,0:T(8,128)(2,1)}, bf16[2,2,64,2048]{3,2,1,0:T(8,128)(2,1)S(1)}, u32[]{:S(2)}, u32[]{:S(2)}) collective-permute-start(bf16[2,2,64,2048]{3,2,1,0:T(8,128)(2,1)} %pad_maximum_fusion), channel_id=1, source_target_pairs={{0,2},{1,3},{2,4},{3,5},{4,6},{5,7},{6,8},{7,9},{8,10},{9,11},{10,... | collective-permute-start | bytes 3145736 | tf_op jit(solution)/shard_map/ppermute | solution.py:37
  31.0 82.3 %collective-permute-start.4 = (bf16[2,2,64,2048]{3,2,1,0:T(8,128)(2,1)}, bf16[2,2,64,2048]{3,2,1,0:T(8,128)(2,1)}, u32[]{:S(2)}, u32[]{:S(2)}) collective-permute-start(bf16[2,2,64,2048]{3,2,1,0:T(8,128)(2,1)} %pad_maximum_fusion), channel_id=1, source_target_pairs={{0,1},{1,2},{2,3},{3,4},{4,5},{5,6},{6,7},{7,8},{8,9},{9,10},{10,1... | collective-permute-start | bytes 3145736 | tf_op jit(solution)/shard_map/ppermute | solution.py:37
  33.5 79.7 %collective-permute-start.1 = (bf16[2,64,2048]{2,1,0:T(8,128)(2,1)}, bf16[2,64,2048]{2,1,0:T(8,128)(2,1)}, u32[]{:S(2)}, u32[]{:S(2)}) collective-permute-start(bf16[2,64,2048]{2,1,0:T(8,128)(2,1)} %collective-permute-done.refs_4_), channel_id=1, source_target_pairs={{0,4},{1,5},{2,6},{3,7},{4,8},{5,9},{6,10},{7,11},{8,12},{9,13},{1... | collective-permute-start | bytes 1572872 | tf_op jit(solution)/shard_map/ppermute | solution.py:37
  44.9 26.4 %all-to-all-start.1 = ((f32[32,5,128]{2,1,0:T(8,128)}), f32[32,5,128]{2,1,0:T(8,128)S(1)}, u32[]{:S(2)}, u32[]{:S(2)}) async-start(f32[32,5,128]{2,1,0:T(8,128)} %copy.47), calls=%async_computation.1 | async-start | bytes 262144 | tf_op jit(solution)/shard_map/all_to_all | solution.py:107
  71.9 16.8 %all-to-all-start.2 = ((f32[32,5,128]{2,1,0:T(8,128)}), f32[32,5,128]{2,1,0:T(8,128)}, u32[]{:S(2)}, u32[]{:S(2)}) async-start(f32[32,5,128]{2,1,0:T(8,128)} %reduce-window_subtract_fusion), calls=%async_computation.2 | async-start | bytes 262144 | tf_op jit(solution)/shard_map/all_to_all | solution.py:110
  77.6 1.8 %copy-start.4 = (f32[1024,1,128]{2,0,1:T(8,128)S(1)}, f32[1024,1,128]{2,0,1:T(8,128)}, u32[]{:S(2)}) copy-start(f32[1024,1,128]{2,0,1:T(8,128)} %bitcast_convert_fusion) | copy-start | bytes 1572868
  79.4 10.9 %copy-start.3 = (f32[1024,160]{0,1:T(8,128)S(1)}, f32[1024,160]{0,1:T(8,128)}, u32[]{:S(2)}) copy-start(f32[1024,160]{0,1:T(8,128)} %convolution_multiply_fusion) | copy-start | bytes 1966084
  92.9 30.2 %all-to-all-start.3 = ((bf16[16,64,128]{2,1,0:T(8,128)(2,1)}), bf16[16,64,128]{2,1,0:T(8,128)(2,1)S(1)}, u32[]{:S(2)}, u32[]{:S(2)}) async-start(bf16[16,64,128]{2,1,0:T(8,128)(2,1)} %bitcast.25), calls=%async_computation.3 | async-start | bytes 524288 | tf_op jit(solution)/shard_map/all_to_all | solution.py:157
  113.2 1.0 copy-start.1
  113.2 1.3 %copy-start.2 = (bf16[2,2,64,2048]{3,2,1,0:T(8,128)(2,1)}, bf16[2,2,64,2048]{3,2,1,0:T(8,128)(2,1)S(1)}, u32[]{:S(2)}) copy-start(bf16[2,2,64,2048]{3,2,1,0:T(8,128)(2,1)S(1)} %collective-permute-done.3.refs_2_.refs_6_) | copy-start | bytes 3145732

commit v18 on v14

--- a/solution.py
+++ b/solution.py
@@ -71,7 +71,7 @@
 
 def window_attention(pos, query, key, value, arrived, picks):
     rows, channels = query.shape
-    lanes = 4 * SDIM
+    lanes = 2 * SDIM
     steps = channels // lanes
     flat = pl.BlockSpec((rows, lanes), lambda g, p: (0, g))
     single = pl.BlockSpec((2, rows, lanes), lambda g, p: (0, 0, g))

time: 121 us -> 122 us (level)
  transfers between devices with their start and end apart: 9 -> 9, of which waited for: 3 -> 3; matrix products, arithmetic and copies ran while one was open for 22% -> 21% of each run, Pallas kernels for 7% -> 8%
where the time goes in v18:
time: 122 us; the launch traced here: 121 us
  starting transfers between devices  60.3 us (49%)
  waiting for transfers between devices  20.7 us (17%)
  matrix products  14.9 us (12%)
  Pallas kernels  9.54 us (8%)
  local copies, waits for them, and re-layouts  8.88 us (7%)
  other arithmetic  5.43 us (4%)
    ppermute x5, starting transfers between devices, passed_along(): return lax.ppermute(shard, axis, pairs)  18 us
    all_to_all x1, starting transfers between devices, linear_heads(): back = lax.all_to_all(out, GROUP, split_axis=0, concat_axis=2, tiled=True)  16.6 us
    all_to_all x1, starting transfers between devices, groups_before(): held = lax.all_to_all(dealt, outer, split_axis=0, concat_axis=0, tiled=True)  15.1 us
    all_to_all x1, waiting for transfers between devices, groups_before(): held = lax.all_to_all(dealt, outer, split_axis=0, concat_axis=0, tiled=True)  9.65 us
    pallas_call x1, Pallas kernels, window_attention(): pl.pallas_call(window_kernel, out_shape=jax.ShapeDtypeStruct((rows, chann...  9.54 us
    all_to_all x1, waiting for transfers between devices, groups_before(): lax.all_to_all(prefix, outer, split_axis=0, concat_axis=0, tiled=True)  8.36 us
    dot_general x4, matrix products, sym_features(): jnp.einsum('jhi,if->jhf', ext, jnp.asarray(table), precision=lax.Precisio...  7.13 us
    all_to_all x1, starting transfers between devices, linear_heads(): got = lax.all_to_all(packed, GROUP, split_axis=1, concat_axis=0, tiled=True)  6.73 us
  transfers between devices with their start and end apart: 9, of which 3 were waited for; matrix products, arithmetic and copies ran while one was open for 21% of the time, Pallas kernels for 8%

profile of v18, /device:TPU:1, one launch (start us, length us, event | category | flops | bytes accessed | tf_op | source)
XLA Modules:
  0.0 120.6 jit_solution(9944035161054388761)
XLA Ops:
  0.6 1.1 fusion.40
  1.8 5.4 %collective-permute-start = (bf16[2,64,2048]{2,1,0:T(8,128)(2,1)S(1)}, bf16[2,64,2048]{2,1,0:T(8,128)(2,1)}, u32[]{:S(2)}, u32[]{:S(2)}) collective-permute-start(bf16[2,64,2048]{2,1,0:T(8,128)(2,1)S(1)} %get-tuple-element.7), channel_id=1, source_target_pairs={{0,4},{1,5},{2,6},{3,7},{4,8},{5,9},{6,10},{7,11},{8,12},{9,13},{1... | collective-permute-start | bytes 1572872 | tf_op jit(solution)/shard_map/ppermute | solution.py:37
  9.4 1.2 %pad_maximum_fusion.1 = bf16[64,16,160]{2,0,1:T(8,128)(2,1)} fusion(bf16[64,16,128]{2,0,1:T(8,128)(2,1)S(1)} %copy_bitcast_fusion.1, bf16[64,16,16]{2,0,1:T(8,128)(2,1)S(1)} %copy.44, bf16[64,16,16]{2,0,1:T(8,128)(2,1)S(1)} %copy.43), kind=kLoop, calls=%fused_computation.21 | loop fusion | flops 983040 | bytes 655360 | tf_op jit(solution)/shard_map/concatenate | solution.py:118
  10.6 2.7 %collective-permute-done.refs_4_ = bf16[2,64,2048]{2,1,0:T(8,128)(2,1)} collective-permute-done((bf16[2,64,2048]{2,1,0:T(8,128)(2,1)S(1)}, bf16[2,64,2048]{2,1,0:T(8,128)(2,1)}, u32[]{:S(2)}, u32[]{:S(2)}) %collective-permute-start) | collective-permute-done | bytes 524320 | tf_op jit(solution)/shard_map/ppermute | solution.py:37
  13.3 6.7 %all-to-all-start = ((bf16[64,16,160]{2,0,1:T(8,128)(2,1)}), bf16[64,16,160]{2,0,1:T(8,128)(2,1)S(1)}, u32[]{:S(2)}, u32[]{:S(2)}) async-start(bf16[64,16,160]{2,0,1:T(8,128)(2,1)} %pad_maximum_fusion.1), calls=%async_computation | async-start | bytes 1048576 | tf_op jit(solution)/shard_map/all_to_all | solution.py:127
  20.7 3.5 %collective-permute-start.1 = (bf16[2,64,2048]{2,1,0:T(8,128)(2,1)}, bf16[2,64,2048]{2,1,0:T(8,128)(2,1)}, u32[]{:S(2)}, u32[]{:S(2)}) collective-permute-start(bf16[2,64,2048]{2,1,0:T(8,128)(2,1)} %collective-permute-done.refs_4_), channel_id=1, source_target_pairs={{0,4},{1,5},{2,6},{3,7},{4,8},{5,9},{6,10},{7,11},{8,12},{9,13},{1... | collective-permute-start | bytes 1572872 | tf_op jit(solution)/shard_map/ppermute | solution.py:37
  24.3 2.1 %pad_maximum_fusion = bf16[2,2,64,2048]{3,2,1,0:T(8,128)(2,1)} fusion(bf16[1,2,64,2048]{3,2,1,0:T(8,128)(2,1)} %bitcast.24, bf16[1,2,64,2048]{3,2,1,0:T(8,128)(2,1)S(1)} %get-tuple-element.6), kind=kLoop, calls=%fused_computation.18 | loop fusion | flops 524288 | bytes 2097152 | tf_op jit(solution)/shard_map/stack | solution.py:177
  26.4 4.3 %collective-permute-start.2 = (bf16[2,2,64,2048]{3,2,1,0:T(8,128)(2,1)}, bf16[2,2,64,2048]{3,2,1,0:T(8,128)(2,1)S(1)}, u32[]{:S(2)}, u32[]{:S(2)}) collective-permute-start(bf16[2,2,64,2048]{3,2,1,0:T(8,128)(2,1)} %pad_maximum_fusion), channel_id=1, source_target_pairs={{0,3},{1,4},{2,5},{3,6},{4,7},{5,8},{6,9},{7,10},{8,11},{9,12},{10... | collective-permute-start | bytes 3145736 | tf_op jit(solution)/shard_map/ppermute | solution.py:37
  30.7 2.3 %collective-permute-start.3 = (bf16[2,2,64,2048]{3,2,1,0:T(8,128)(2,1)}, bf16[2,2,64,2048]{3,2,1,0:T(8,128)(2,1)S(1)}, u32[]{:S(2)}, u32[]{:S(2)}) collective-permute-start(bf16[2,2,64,2048]{3,2,1,0:T(8,128)(2,1)} %pad_maximum_fusion), channel_id=1, source_target_pairs={{0,2},{1,3},{2,4},{3,5},{4,6},{5,7},{6,8},{7,9},{8,10},{9,11},{10,... | collective-permute-start | bytes 3145736 | tf_op jit(solution)/shard_map/ppermute | solution.py:37
  33.0 2.5 %collective-permute-start.4 = (bf16[2,2,64,2048]{3,2,1,0:T(8,128)(2,1)}, bf16[2,2,64,2048]{3,2,1,0:T(8,128)(2,1)}, u32[]{:S(2)}, u32[]{:S(2)}) collective-permute-start(bf16[2,2,64,2048]{3,2,1,0:T(8,128)(2,1)} %pad_maximum_fusion), channel_id=1, source_target_pairs={{0,1},{1,2},{2,3},{3,4},{4,5},{5,6},{6,7},{7,8},{8,9},{9,10},{10,1... | collective-permute-start | bytes 3145736 | tf_op jit(solution)/shard_map/ppermute | solution.py:37
  36.5 3.0 %fusion = f32[128,1024]{1,0:T(8,128)} fusion(f32[1024,1024]{1,0:T(8,128)S(1)} %fusion.27, bf16[1024,160]{1,0:T(8,128)(2,1)S(1)} %bitcast.62), kind=kOutput, calls=%fused_computation | convolution fusion | flops 1617952768 | bytes 4980736 | tf_op jit(solution)/shard_map/hij,jhe->ihe/dot_general | solution.py:148
  40.4 1.8 %fusion.11 = f32[160,1024]{1,0:T(8,128)} fusion(f32[1024,160]{0,1:T(8,128)S(1)} %fusion.19, f32[17,160]{1,0:T(8,128)S(1)} %copy-done.3, f32[1024,1,16]{2,0,1:T(8,128)S(1)} %get-tuple-element.9), kind=kOutput, calls=%fused_computation.14 | convolution fusion | flops 33587200 | bytes 1387136 | tf_op jit(solution)/shard_map/jhi,if->jhf/dot_general | solution.py:44
  42.2 2.2 %dot_general.30 = f32[32,5,1024]{2,1,0:T(8,128)} reshape(f32[160,1024]{1,0:T(8,128)} %fusion.11) | data formatting | bytes 1310720 | tf_op jit(solution)/shard_map/jhf,jhe->hfe/dot_general | solution.py:135
  44.3 2.0 %fusion.13 = f32[32,5,128]{2,0,1:T(8,128)S(1)} fusion(f32[32,5,1024]{2,1,0:T(8,128)} %dot_general.30, bf16[1024,160]{1,0:T(8,128)(2,1)S(1)} %bitcast.63), kind=kOutput, calls=%fused_computation.19 | convolution fusion | flops 251658240 | bytes 999424 | tf_op jit(solution)/shard_map/jhf,jhe->hfe/dot_general | solution.py:135
  47.1 15.1 %all-to-all-start.1 = ((f32[32,5,128]{2,1,0:T(8,128)}), f32[32,5,128]{2,1,0:T(8,128)S(1)}, u32[]{:S(2)}, u32[]{:S(2)}) async-start(f32[32,5,128]{2,1,0:T(8,128)} %copy.47), calls=%async_computation.1 | async-start | bytes 262144 | tf_op jit(solution)/shard_map/all_to_all | solution.py:107
  62.2 1.7 %fusion.16 = f32[1024,160]{0,1:T(8,128)} fusion(f32[17,160]{1,0:T(8,128)S(1)} %copy-done.4, f32[1024,1,16]{2,0,1:T(8,128)S(1)} %get-tuple-element.8), kind=kOutput, calls=%fused_computation.24 | convolution fusion | flops 33423360 | bytes 731776 | tf_op jit(solution)/shard_map/jhi,if->jhf/dot_general | solution.py:44
  63.9 9.6 %all-to-all-done.1 = f32[32,5,128]{2,1,0:T(8,128)S(1)} async-done(((f32[32,5,128]{2,1,0:T(8,128)}), f32[32,5,128]{2,1,0:T(8,128)S(1)}, u32[]{:S(2)}, u32[]{:S(2)}) %all-to-all-start.1) | async-done | bytes 81952 | tf_op jit(solution)/shard_map/all_to_all | solution.py:107
  74.2 3.9 %all-to-all-start.2 = ((f32[32,5,128]{2,1,0:T(8,128)}), f32[32,5,128]{2,1,0:T(8,128)S(1)}, u32[]{:S(2)}, u32[]{:S(2)}) async-start(f32[32,5,128]{2,1,0:T(8,128)} %reduce-window_subtract_fusion), calls=%async_computation.2 | async-start | bytes 262144 | tf_op jit(solution)/shard_map/all_to_all | solution.py:109
  78.1 2.8 %convolution_multiply_fusion = f32[1024,160]{0,1:T(8,128)} fusion(f32[1024,160]{0,1:T(8,128)} %fusion.16, f32[17,160]{1,0:T(8,128)S(1)} %copy-done.3, f32[1024,1,16]{2,0,1:T(8,128)S(1)} %get-tuple-element.8), kind=kOutput, calls=%fused_computation.12 | convolution fusion | flops 33587200 | bytes 1387136 | tf_op jit(solution)/shard_map/jhi,if->jhf/dot_general | solution.py:44
  80.9 8.4 %all-to-all-done.2 = f32[32,5,128]{2,1,0:T(8,128)S(1)} async-done(((f32[32,5,128]{2,1,0:T(8,128)}), f32[32,5,128]{2,1,0:T(8,128)S(1)}, u32[]{:S(2)}, u32[]{:S(2)}) %all-to-all-start.2) | async-done | bytes 81952 | tf_op jit(solution)/shard_map/all_to_all | solution.py:109
  89.3 1.9 %multiply_reduce_fusion = (f32[1024]{0:T(1024)S(1)}, f32[1,128,1024]{2,1,0:T(8,128)S(1)}) fusion(f32[128,1024]{1,0:T(8,128)} %fusion, f32[160,128]{1,0:T(8,128)S(1)} %reshape.105, f32[1024,160]{0,1:T(8,128)} %convolution_multiply_fusion), kind=kOutput, calls=%fused_computation.30 | convolution fusion | flops 252050432 | bytes 1789952 | tf_op jit(solution)/shard_map/ihf,hfe->ihe/dot_general | solution.py:139
  92.1 16.6 %all-to-all-start.3 = ((bf16[16,64,128]{2,1,0:T(8,128)(2,1)}), bf16[16,64,128]{2,1,0:T(8,128)(2,1)S(1)}, u32[]{:S(2)}, u32[]{:S(2)}) async-start(bf16[16,64,128]{2,1,0:T(8,128)(2,1)} %bitcast.19), calls=%async_computation.3 | async-start | bytes 524288 | tf_op jit(solution)/shard_map/all_to_all | solution.py:156
  108.8 1.0 copy-done.1
  110.1 9.5 %shard_map.122 = bf16[64,2048]{1,0:T(8,128)(2,1)} custom-call(s32[1]{0:T(128)} %bitcast.22.pos_ref, bf16[64,2048]{1,0:T(8,128)(2,1)} %q_ref.1, bf16[64,2048]{1,0:T(8,128)(2,1)} %k_ref.1, bf16[64,2048]{1,0:T(8,128)(2,1)} %v_ref.1, bf16[2,64,2048]{2,1,0:T(8,128)(2,1)} %collective-permute-done.1.refs_0_, bf16[2,2,64,2048]{3,2,1,0:T(8,128)(2,1)} %copy-done.1, ...), custom_call_target="tpu_custom_call" | custom-call | tf_op jit(solution)/shard_map/pallas_call | solution.py:84
  (34 shorter events, 8.4 us)
Async XLA Ops:
  0.6 8.7 %copy-start = (bf16[64,2048]{1,0:T(8,128)(2,1)S(1)}, bf16[64,2048]{1,0:T(8,128)(2,1)}, u32[]{:S(2)}) copy-start(bf16[64,2048]{1,0:T(8,128)(2,1)} %param.13) | copy-start | bytes 786436
  1.8 11.5 %collective-permute-start = (bf16[2,64,2048]{2,1,0:T(8,128)(2,1)S(1)}, bf16[2,64,2048]{2,1,0:T(8,128)(2,1)}, u32[]{:S(2)}, u32[]{:S(2)}) collective-permute-start(bf16[2,64,2048]{2,1,0:T(8,128)(2,1)S(1)} %get-tuple-element.7), channel_id=1, source_target_pairs={{0,4},{1,5},{2,6},{3,7},{4,8},{5,9},{6,10},{7,11},{8,12},{9,13},{1... | collective-permute-start | bytes 1572872 | tf_op jit(solution)/shard_map/ppermute | solution.py:37
  13.3 22.2 %all-to-all-start = ((bf16[64,16,160]{2,0,1:T(8,128)(2,1)}), bf16[64,16,160]{2,0,1:T(8,128)(2,1)S(1)}, u32[]{:S(2)}, u32[]{:S(2)}) async-start(bf16[64,16,160]{2,0,1:T(8,128)(2,1)} %pad_maximum_fusion.1), calls=%async_computation | async-start | bytes 1048576 | tf_op jit(solution)/shard_map/all_to_all | solution.py:127
  20.7 88.0 %collective-permute-start.1 = (bf16[2,64,2048]{2,1,0:T(8,128)(2,1)}, bf16[2,64,2048]{2,1,0:T(8,128)(2,1)}, u32[]{:S(2)}, u32[]{:S(2)}) collective-permute-start(bf16[2,64,2048]{2,1,0:T(8,128)(2,1)} %collective-permute-done.refs_4_), channel_id=1, source_target_pairs={{0,4},{1,5},{2,6},{3,7},{4,8},{5,9},{6,10},{7,11},{8,12},{9,13},{1... | collective-permute-start | bytes 1572872 | tf_op jit(solution)/shard_map/ppermute | solution.py:37
  26.4 82.4 %collective-permute-start.2 = (bf16[2,2,64,2048]{3,2,1,0:T(8,128)(2,1)}, bf16[2,2,64,2048]{3,2,1,0:T(8,128)(2,1)S(1)}, u32[]{:S(2)}, u32[]{:S(2)}) collective-permute-start(bf16[2,2,64,2048]{3,2,1,0:T(8,128)(2,1)} %pad_maximum_fusion), channel_id=1, source_target_pairs={{0,3},{1,4},{2,5},{3,6},{4,7},{5,8},{6,9},{7,10},{8,11},{9,12},{10... | collective-permute-start | bytes 3145736 | tf_op jit(solution)/shard_map/ppermute | solution.py:37
  30.7 78.1 %collective-permute-start.3 = (bf16[2,2,64,2048]{3,2,1,0:T(8,128)(2,1)}, bf16[2,2,64,2048]{3,2,1,0:T(8,128)(2,1)S(1)}, u32[]{:S(2)}, u32[]{:S(2)}) collective-permute-start(bf16[2,2,64,2048]{3,2,1,0:T(8,128)(2,1)} %pad_maximum_fusion), channel_id=1, source_target_pairs={{0,2},{1,3},{2,4},{3,5},{4,6},{5,7},{6,8},{7,9},{8,10},{9,11},{10,... | collective-permute-start | bytes 3145736 | tf_op jit(solution)/shard_map/ppermute | solution.py:37
  33.0 75.7 %collective-permute-start.4 = (bf16[2,2,64,2048]{3,2,1,0:T(8,128)(2,1)}, bf16[2,2,64,2048]{3,2,1,0:T(8,128)(2,1)}, u32[]{:S(2)}, u32[]{:S(2)}) collective-permute-start(bf16[2,2,64,2048]{3,2,1,0:T(8,128)(2,1)} %pad_maximum_fusion), channel_id=1, source_target_pairs={{0,1},{1,2},{2,3},{3,4},{4,5},{5,6},{6,7},{7,8},{8,9},{9,10},{10,1... | collective-permute-start | bytes 3145736 | tf_op jit(solution)/shard_map/ppermute | solution.py:37
  36.5 3.1 %copy-start.5 = (f32[17,160]{1,0:T(8,128)S(1)}, f32[17,160]{1,0:T(8,128)}, u32[]{:S(2)}) copy-start(f32[17,160]{1,0:T(8,128)} %constant.57.clone) | copy-start | bytes 32644
  36.5 3.9 %copy-start.3 = (f32[17,160]{1,0:T(8,128)S(1)}, f32[17,160]{1,0:T(8,128)}, u32[]{:S(2)}) copy-start(f32[17,160]{1,0:T(8,128)} %constant.58.clone) | copy-start | bytes 32644
  39.5 22.6 %copy-start.4 = (f32[17,160]{1,0:T(8,128)S(1)}, f32[17,160]{1,0:T(8,128)}, u32[]{:S(2)}) copy-start(f32[17,160]{1,0:T(8,128)} %constant.59.clone) | copy-start | bytes 32644
  47.1 26.4 %all-to-all-start.1 = ((f32[32,5,128]{2,1,0:T(8,128)}), f32[32,5,128]{2,1,0:T(8,128)S(1)}, u32[]{:S(2)}, u32[]{:S(2)}) async-start(f32[32,5,128]{2,1,0:T(8,128)} %copy.47), calls=%async_computation.1 | async-start | bytes 262144 | tf_op jit(solution)/shard_map/all_to_all | solution.py:107
  74.2 15.0 %all-to-all-start.2 = ((f32[32,5,128]{2,1,0:T(8,128)}), f32[32,5,128]{2,1,0:T(8,128)S(1)}, u32[]{:S(2)}, u32[]{:S(2)}) async-start(f32[32,5,128]{2,1,0:T(8,128)} %reduce-window_subtract_fusion), calls=%async_computation.2 | async-start | bytes 262144 | tf_op jit(solution)/shard_map/all_to_all | solution.py:109
  92.1 27.5 %all-to-all-start.3 = ((bf16[16,64,128]{2,1,0:T(8,128)(2,1)}), bf16[16,64,128]{2,1,0:T(8,128)(2,1)S(1)}, u32[]{:S(2)}, u32[]{:S(2)}) async-start(bf16[16,64,128]{2,1,0:T(8,128)(2,1)} %bitcast.19), calls=%async_computation.3 | async-start | bytes 524288 | tf_op jit(solution)/shard_map/all_to_all | solution.py:156
  108.7 1.0 copy-start.1
  108.8 1.3 %copy-start.2 = (bf16[2,2,64,2048]{3,2,1,0:T(8,128)(2,1)}, bf16[2,2,64,2048]{3,2,1,0:T(8,128)(2,1)S(1)}, u32[]{:S(2)}) copy-start(bf16[2,2,64,2048]{3,2,1,0:T(8,128)(2,1)S(1)} %collective-permute-done.3.refs_2_.refs_6_) | copy-start | bytes 3145732

commit v19 on v18

--- a/solution.py
+++ b/solution.py
@@ -71,7 +71,7 @@
 
 def window_attention(pos, query, key, value, arrived, picks):
     rows, channels = query.shape
-    lanes = 2 * SDIM
+    lanes = 8 * SDIM
     steps = channels // lanes
     flat = pl.BlockSpec((rows, lanes), lambda g, p: (0, g))
     single = pl.BlockSpec((2, rows, lanes), lambda g, p: (0, 0, g))

time: 122 us -> 120 us (0.984)
  transfers between devices with their start and end apart: 9 -> 9, of which waited for: 3 -> 3; matrix products, arithmetic and copies ran while one was open for 21% -> 22% of each run, Pallas kernels for 8% -> 7%
where the time goes in v19:
time: 120 us; the launch traced here: 119 us
  starting transfers between devices  60.3 us (50%)
  waiting for transfers between devices  20.7 us (17%)
  matrix products  14.9 us (12%)
  local copies, waits for them, and re-layouts  8.88 us (7%)
  Pallas kernels  8.44 us (7%)
  other arithmetic  5.43 us (5%)
    ppermute x5, starting transfers between devices, passed_along(): return lax.ppermute(shard, axis, pairs)  18 us
    all_to_all x1, starting transfers between devices, linear_heads(): back = lax.all_to_all(out, GROUP, split_axis=0, concat_axis=2, tiled=True)  16.6 us
    all_to_all x1, starting transfers between devices, groups_before(): held = lax.all_to_all(dealt, outer, split_axis=0, concat_axis=0, tiled=True)  15.1 us
    all_to_all x1, waiting for transfers between devices, groups_before(): held = lax.all_to_all(dealt, outer, split_axis=0, concat_axis=0, tiled=True)  9.65 us
    pallas_call x1, Pallas kernels, window_attention(): pl.pallas_call(window_kernel, out_shape=jax.ShapeDtypeStruct((rows, chann...  8.44 us
    all_to_all x1, waiting for transfers between devices, groups_before(): lax.all_to_all(prefix, outer, split_axis=0, concat_axis=0, tiled=True)  8.36 us
    dot_general x4, matrix products, sym_features(): jnp.einsum('jhi,if->jhf', ext, jnp.asarray(table), precision=lax.Precisio...  7.13 us
    all_to_all x1, starting transfers between devices, linear_heads(): got = lax.all_to_all(packed, GROUP, split_axis=1, concat_axis=0, tiled=True)  6.73 us
  transfers between devices with their start and end apart: 9, of which 3 were waited for; matrix products, arithmetic and copies ran while one was open for 22% of the time, Pallas kernels for 7%

profile of v19, /device:TPU:1, one launch (start us, length us, event | category | flops | bytes accessed | tf_op | source)
XLA Modules:
  0.0 119.5 jit_solution(12742880254630639427)
XLA Ops:
  0.6 1.1 fusion.40
  1.8 5.4 %collective-permute-start = (bf16[2,64,2048]{2,1,0:T(8,128)(2,1)S(1)}, bf16[2,64,2048]{2,1,0:T(8,128)(2,1)}, u32[]{:S(2)}, u32[]{:S(2)}) collective-permute-start(bf16[2,64,2048]{2,1,0:T(8,128)(2,1)S(1)} %get-tuple-element.7), channel_id=1, source_target_pairs={{0,4},{1,5},{2,6},{3,7},{4,8},{5,9},{6,10},{7,11},{8,12},{9,13},{1... | collective-permute-start | bytes 1572872 | tf_op jit(solution)/shard_map/ppermute | solution.py:37
  9.4 1.2 %pad_maximum_fusion.1 = bf16[64,16,160]{2,0,1:T(8,128)(2,1)} fusion(bf16[64,16,128]{2,0,1:T(8,128)(2,1)S(1)} %copy_bitcast_fusion.1, bf16[64,16,16]{2,0,1:T(8,128)(2,1)S(1)} %copy.44, bf16[64,16,16]{2,0,1:T(8,128)(2,1)S(1)} %copy.43), kind=kLoop, calls=%fused_computation.21 | loop fusion | flops 983040 | bytes 655360 | tf_op jit(solution)/shard_map/concatenate | solution.py:118
  10.6 2.7 %collective-permute-done.refs_4_ = bf16[2,64,2048]{2,1,0:T(8,128)(2,1)} collective-permute-done((bf16[2,64,2048]{2,1,0:T(8,128)(2,1)S(1)}, bf16[2,64,2048]{2,1,0:T(8,128)(2,1)}, u32[]{:S(2)}, u32[]{:S(2)}) %collective-permute-start) | collective-permute-done | bytes 524320 | tf_op jit(solution)/shard_map/ppermute | solution.py:37
  13.3 6.7 %all-to-all-start = ((bf16[64,16,160]{2,0,1:T(8,128)(2,1)}), bf16[64,16,160]{2,0,1:T(8,128)(2,1)S(1)}, u32[]{:S(2)}, u32[]{:S(2)}) async-start(bf16[64,16,160]{2,0,1:T(8,128)(2,1)} %pad_maximum_fusion.1), calls=%async_computation | async-start | bytes 1048576 | tf_op jit(solution)/shard_map/all_to_all | solution.py:127
  20.7 3.5 %collective-permute-start.1 = (bf16[2,64,2048]{2,1,0:T(8,128)(2,1)}, bf16[2,64,2048]{2,1,0:T(8,128)(2,1)}, u32[]{:S(2)}, u32[]{:S(2)}) collective-permute-start(bf16[2,64,2048]{2,1,0:T(8,128)(2,1)} %collective-permute-done.refs_4_), channel_id=1, source_target_pairs={{0,4},{1,5},{2,6},{3,7},{4,8},{5,9},{6,10},{7,11},{8,12},{9,13},{1... | collective-permute-start | bytes 1572872 | tf_op jit(solution)/shard_map/ppermute | solution.py:37
  24.3 2.1 %pad_maximum_fusion = bf16[2,2,64,2048]{3,2,1,0:T(8,128)(2,1)} fusion(bf16[1,2,64,2048]{3,2,1,0:T(8,128)(2,1)} %bitcast.24, bf16[1,2,64,2048]{3,2,1,0:T(8,128)(2,1)S(1)} %get-tuple-element.6), kind=kLoop, calls=%fused_computation.18 | loop fusion | flops 524288 | bytes 2097152 | tf_op jit(solution)/shard_map/stack | solution.py:177
  26.4 4.3 %collective-permute-start.2 = (bf16[2,2,64,2048]{3,2,1,0:T(8,128)(2,1)}, bf16[2,2,64,2048]{3,2,1,0:T(8,128)(2,1)S(1)}, u32[]{:S(2)}, u32[]{:S(2)}) collective-permute-start(bf16[2,2,64,2048]{3,2,1,0:T(8,128)(2,1)} %pad_maximum_fusion), channel_id=1, source_target_pairs={{0,3},{1,4},{2,5},{3,6},{4,7},{5,8},{6,9},{7,10},{8,11},{9,12},{10... | collective-permute-start | bytes 3145736 | tf_op jit(solution)/shard_map/ppermute | solution.py:37
  30.7 2.3 %collective-permute-start.3 = (bf16[2,2,64,2048]{3,2,1,0:T(8,128)(2,1)}, bf16[2,2,64,2048]{3,2,1,0:T(8,128)(2,1)S(1)}, u32[]{:S(2)}, u32[]{:S(2)}) collective-permute-start(bf16[2,2,64,2048]{3,2,1,0:T(8,128)(2,1)} %pad_maximum_fusion), channel_id=1, source_target_pairs={{0,2},{1,3},{2,4},{3,5},{4,6},{5,7},{6,8},{7,9},{8,10},{9,11},{10,... | collective-permute-start | bytes 3145736 | tf_op jit(solution)/shard_map/ppermute | solution.py:37
  33.0 2.5 %collective-permute-start.4 = (bf16[2,2,64,2048]{3,2,1,0:T(8,128)(2,1)}, bf16[2,2,64,2048]{3,2,1,0:T(8,128)(2,1)}, u32[]{:S(2)}, u32[]{:S(2)}) collective-permute-start(bf16[2,2,64,2048]{3,2,1,0:T(8,128)(2,1)} %pad_maximum_fusion), channel_id=1, source_target_pairs={{0,1},{1,2},{2,3},{3,4},{4,5},{5,6},{6,7},{7,8},{8,9},{9,10},{10,1... | collective-permute-start | bytes 3145736 | tf_op jit(solution)/shard_map/ppermute | solution.py:37
  36.5 3.0 %fusion = f32[128,1024]{1,0:T(8,128)} fusion(f32[1024,1024]{1,0:T(8,128)S(1)} %fusion.27, bf16[1024,160]{1,0:T(8,128)(2,1)S(1)} %bitcast.62), kind=kOutput, calls=%fused_computation | convolution fusion | flops 1617952768 | bytes 4980736 | tf_op jit(solution)/shard_map/hij,jhe->ihe/dot_general | solution.py:148
  40.4 1.8 %fusion.11 = f32[160,1024]{1,0:T(8,128)} fusion(f32[1024,160]{0,1:T(8,128)S(1)} %fusion.19, f32[17,160]{1,0:T(8,128)S(1)} %copy-done.3, f32[1024,1,16]{2,0,1:T(8,128)S(1)} %get-tuple-element.9), kind=kOutput, calls=%fused_computation.14 | convolution fusion | flops 33587200 | bytes 1387136 | tf_op jit(solution)/shard_map/jhi,if->jhf/dot_general | solution.py:44
  42.2 2.2 %dot_general.30 = f32[32,5,1024]{2,1,0:T(8,128)} reshape(f32[160,1024]{1,0:T(8,128)} %fusion.11) | data formatting | bytes 1310720 | tf_op jit(solution)/shard_map/jhf,jhe->hfe/dot_general | solution.py:135
  44.3 2.0 %fusion.13 = f32[32,5,128]{2,0,1:T(8,128)S(1)} fusion(f32[32,5,1024]{2,1,0:T(8,128)} %dot_general.30, bf16[1024,160]{1,0:T(8,128)(2,1)S(1)} %bitcast.63), kind=kOutput, calls=%fused_computation.19 | convolution fusion | flops 251658240 | bytes 999424 | tf_op jit(solution)/shard_map/jhf,jhe->hfe/dot_general | solution.py:135
  47.1 15.1 %all-to-all-start.1 = ((f32[32,5,128]{2,1,0:T(8,128)}), f32[32,5,128]{2,1,0:T(8,128)S(1)}, u32[]{:S(2)}, u32[]{:S(2)}) async-start(f32[32,5,128]{2,1,0:T(8,128)} %copy.47), calls=%async_computation.1 | async-start | bytes 262144 | tf_op jit(solution)/shard_map/all_to_all | solution.py:107
  62.2 1.7 %fusion.16 = f32[1024,160]{0,1:T(8,128)} fusion(f32[17,160]{1,0:T(8,128)S(1)} %copy-done.4, f32[1024,1,16]{2,0,1:T(8,128)S(1)} %get-tuple-element.8), kind=kOutput, calls=%fused_computation.24 | convolution fusion | flops 33423360 | bytes 731776 | tf_op jit(solution)/shard_map/jhi,if->jhf/dot_general | solution.py:44
  63.9 9.6 %all-to-all-done.1 = f32[32,5,128]{2,1,0:T(8,128)S(1)} async-done(((f32[32,5,128]{2,1,0:T(8,128)}), f32[32,5,128]{2,1,0:T(8,128)S(1)}, u32[]{:S(2)}, u32[]{:S(2)}) %all-to-all-start.1) | async-done | bytes 81952 | tf_op jit(solution)/shard_map/all_to_all | solution.py:107
  74.2 3.9 %all-to-all-start.2 = ((f32[32,5,128]{2,1,0:T(8,128)}), f32[32,5,128]{2,1,0:T(8,128)S(1)}, u32[]{:S(2)}, u32[]{:S(2)}) async-start(f32[32,5,128]{2,1,0:T(8,128)} %reduce-window_subtract_fusion), calls=%async_computation.2 | async-start | bytes 262144 | tf_op jit(solution)/shard_map/all_to_all | solution.py:109
  78.1 2.8 %convolution_multiply_fusion = f32[1024,160]{0,1:T(8,128)} fusion(f32[1024,160]{0,1:T(8,128)} %fusion.16, f32[17,160]{1,0:T(8,128)S(1)} %copy-done.3, f32[1024,1,16]{2,0,1:T(8,128)S(1)} %get-tuple-element.8), kind=kOutput, calls=%fused_computation.12 | convolution fusion | flops 33587200 | bytes 1387136 | tf_op jit(solution)/shard_map/jhi,if->jhf/dot_general | solution.py:44
  80.9 8.4 %all-to-all-done.2 = f32[32,5,128]{2,1,0:T(8,128)S(1)} async-done(((f32[32,5,128]{2,1,0:T(8,128)}), f32[32,5,128]{2,1,0:T(8,128)S(1)}, u32[]{:S(2)}, u32[]{:S(2)}) %all-to-all-start.2) | async-done | bytes 81952 | tf_op jit(solution)/shard_map/all_to_all | solution.py:109
  89.3 1.9 %multiply_reduce_fusion = (f32[1024]{0:T(1024)S(1)}, f32[1,128,1024]{2,1,0:T(8,128)S(1)}) fusion(f32[128,1024]{1,0:T(8,128)} %fusion, f32[160,128]{1,0:T(8,128)S(1)} %reshape.105, f32[1024,160]{0,1:T(8,128)} %convolution_multiply_fusion), kind=kOutput, calls=%fused_computation.30 | convolution fusion | flops 252050432 | bytes 1789952 | tf_op jit(solution)/shard_map/ihf,hfe->ihe/dot_general | solution.py:139
  92.1 16.6 %all-to-all-start.3 = ((bf16[16,64,128]{2,1,0:T(8,128)(2,1)}), bf16[16,64,128]{2,1,0:T(8,128)(2,1)S(1)}, u32[]{:S(2)}, u32[]{:S(2)}) async-start(bf16[16,64,128]{2,1,0:T(8,128)(2,1)} %bitcast.19), calls=%async_computation.3 | async-start | bytes 524288 | tf_op jit(solution)/shard_map/all_to_all | solution.py:156
  108.8 1.0 copy-done.1
  110.1 8.4 %shard_map.122 = bf16[64,2048]{1,0:T(8,128)(2,1)} custom-call(s32[1]{0:T(128)} %bitcast.22.pos_ref, bf16[64,2048]{1,0:T(8,128)(2,1)} %q_ref.1, bf16[64,2048]{1,0:T(8,128)(2,1)} %k_ref.1, bf16[64,2048]{1,0:T(8,128)(2,1)} %v_ref.1, bf16[2,64,2048]{2,1,0:T(8,128)(2,1)} %collective-permute-done.1.refs_0_, bf16[2,2,64,2048]{3,2,1,0:T(8,128)(2,1)} %copy-done.1, ...), custom_call_target="tpu_custom_call" | custom-call | tf_op jit(solution)/shard_map/pallas_call | solution.py:84
  (34 shorter events, 8.4 us)
Async XLA Ops:
  0.6 8.7 %copy-start = (bf16[64,2048]{1,0:T(8,128)(2,1)S(1)}, bf16[64,2048]{1,0:T(8,128)(2,1)}, u32[]{:S(2)}) copy-start(bf16[64,2048]{1,0:T(8,128)(2,1)} %param.13) | copy-start | bytes 786436
  1.8 11.5 %collective-permute-start = (bf16[2,64,2048]{2,1,0:T(8,128)(2,1)S(1)}, bf16[2,64,2048]{2,1,0:T(8,128)(2,1)}, u32[]{:S(2)}, u32[]{:S(2)}) collective-permute-start(bf16[2,64,2048]{2,1,0:T(8,128)(2,1)S(1)} %get-tuple-element.7), channel_id=1, source_target_pairs={{0,4},{1,5},{2,6},{3,7},{4,8},{5,9},{6,10},{7,11},{8,12},{9,13},{1... | collective-permute-start | bytes 1572872 | tf_op jit(solution)/shard_map/ppermute | solution.py:37
  13.3 22.2 %all-to-all-start = ((bf16[64,16,160]{2,0,1:T(8,128)(2,1)}), bf16[64,16,160]{2,0,1:T(8,128)(2,1)S(1)}, u32[]{:S(2)}, u32[]{:S(2)}) async-start(bf16[64,16,160]{2,0,1:T(8,128)(2,1)} %pad_maximum_fusion.1), calls=%async_computation | async-start | bytes 1048576 | tf_op jit(solution)/shard_map/all_to_all | solution.py:127
  20.7 88.0 %collective-permute-start.1 = (bf16[2,64,2048]{2,1,0:T(8,128)(2,1)}, bf16[2,64,2048]{2,1,0:T(8,128)(2,1)}, u32[]{:S(2)}, u32[]{:S(2)}) collective-permute-start(bf16[2,64,2048]{2,1,0:T(8,128)(2,1)} %collective-permute-done.refs_4_), channel_id=1, source_target_pairs={{0,4},{1,5},{2,6},{3,7},{4,8},{5,9},{6,10},{7,11},{8,12},{9,13},{1... | collective-permute-start | bytes 1572872 | tf_op jit(solution)/shard_map/ppermute | solution.py:37
  26.4 82.4 %collective-permute-start.2 = (bf16[2,2,64,2048]{3,2,1,0:T(8,128)(2,1)}, bf16[2,2,64,2048]{3,2,1,0:T(8,128)(2,1)S(1)}, u32[]{:S(2)}, u32[]{:S(2)}) collective-permute-start(bf16[2,2,64,2048]{3,2,1,0:T(8,128)(2,1)} %pad_maximum_fusion), channel_id=1, source_target_pairs={{0,3},{1,4},{2,5},{3,6},{4,7},{5,8},{6,9},{7,10},{8,11},{9,12},{10... | collective-permute-start | bytes 3145736 | tf_op jit(solution)/shard_map/ppermute | solution.py:37
  30.7 78.1 %collective-permute-start.3 = (bf16[2,2,64,2048]{3,2,1,0:T(8,128)(2,1)}, bf16[2,2,64,2048]{3,2,1,0:T(8,128)(2,1)S(1)}, u32[]{:S(2)}, u32[]{:S(2)}) collective-permute-start(bf16[2,2,64,2048]{3,2,1,0:T(8,128)(2,1)} %pad_maximum_fusion), channel_id=1, source_target_pairs={{0,2},{1,3},{2,4},{3,5},{4,6},{5,7},{6,8},{7,9},{8,10},{9,11},{10,... | collective-permute-start | bytes 3145736 | tf_op jit(solution)/shard_map/ppermute | solution.py:37
  33.0 75.7 %collective-permute-start.4 = (bf16[2,2,64,2048]{3,2,1,0:T(8,128)(2,1)}, bf16[2,2,64,2048]{3,2,1,0:T(8,128)(2,1)}, u32[]{:S(2)}, u32[]{:S(2)}) collective-permute-start(bf16[2,2,64,2048]{3,2,1,0:T(8,128)(2,1)} %pad_maximum_fusion), channel_id=1, source_target_pairs={{0,1},{1,2},{2,3},{3,4},{4,5},{5,6},{6,7},{7,8},{8,9},{9,10},{10,1... | collective-permute-start | bytes 3145736 | tf_op jit(solution)/shard_map/ppermute | solution.py:37
  36.5 3.1 %copy-start.5 = (f32[17,160]{1,0:T(8,128)S(1)}, f32[17,160]{1,0:T(8,128)}, u32[]{:S(2)}) copy-start(f32[17,160]{1,0:T(8,128)} %constant.57.clone) | copy-start | bytes 32644
  36.5 3.9 %copy-start.3 = (f32[17,160]{1,0:T(8,128)S(1)}, f32[17,160]{1,0:T(8,128)}, u32[]{:S(2)}) copy-start(f32[17,160]{1,0:T(8,128)} %constant.58.clone) | copy-start | bytes 32644
  39.5 22.6 %copy-start.4 = (f32[17,160]{1,0:T(8,128)S(1)}, f32[17,160]{1,0:T(8,128)}, u32[]{:S(2)}) copy-start(f32[17,160]{1,0:T(8,128)} %constant.59.clone) | copy-start | bytes 32644
  47.1 26.4 %all-to-all-start.1 = ((f32[32,5,128]{2,1,0:T(8,128)}), f32[32,5,128]{2,1,0:T(8,128)S(1)}, u32[]{:S(2)}, u32[]{:S(2)}) async-start(f32[32,5,128]{2,1,0:T(8,128)} %copy.47), calls=%async_computation.1 | async-start | bytes 262144 | tf_op jit(solution)/shard_map/all_to_all | solution.py:107
  74.2 15.0 %all-to-all-start.2 = ((f32[32,5,128]{2,1,0:T(8,128)}), f32[32,5,128]{2,1,0:T(8,128)S(1)}, u32[]{:S(2)}, u32[]{:S(2)}) async-start(f32[32,5,128]{2,1,0:T(8,128)} %reduce-window_subtract_fusion), calls=%async_computation.2 | async-start | bytes 262144 | tf_op jit(solution)/shard_map/all_to_all | solution.py:109
  92.1 26.4 %all-to-all-start.3 = ((bf16[16,64,128]{2,1,0:T(8,128)(2,1)}), bf16[16,64,128]{2,1,0:T(8,128)(2,1)S(1)}, u32[]{:S(2)}, u32[]{:S(2)}) async-start(bf16[16,64,128]{2,1,0:T(8,128)(2,1)} %bitcast.19), calls=%async_computation.3 | async-start | bytes 524288 | tf_op jit(solution)/shard_map/all_to_all | solution.py:156
  108.7 1.0 copy-start.1
  108.8 1.3 %copy-start.2 = (bf16[2,2,64,2048]{3,2,1,0:T(8,128)(2,1)}, bf16[2,2,64,2048]{3,2,1,0:T(8,128)(2,1)S(1)}, u32[]{:S(2)}) copy-start(bf16[2,2,64,2048]{3,2,1,0:T(8,128)(2,1)S(1)} %collective-permute-done.3.refs_2_.refs_6_) | copy-start | bytes 3145732
